TPU v7x, 32 devices: a whole 2x2x4 slice. The times are simulated.
32 devices in a mesh: groups: 2 (over x), ctx: 8 (over z, y), head: 2 (over core).
Axes of the slice: x: 2, y: 2, z: 4, core: 2. Of those that a mesh axis runs over, the one named last changes fastest.
Arguments:
- query_matrix: bfloat16 [6144, 4096], P(('groups', 'ctx', 'head')), parts along dimension 0, may hold values from -6 to 6
- key_matrix: bfloat16 [6144, 1024], P(('groups', 'ctx', 'head')), parts along dimension 0, may hold values from -6 to 6
- value_matrix: bfloat16 [6144, 1024], P(('groups', 'ctx', 'head')), parts along dimension 0, may hold values from -6 to 6
- fwd_output: bfloat16 [6144, 4096], P(('groups', 'ctx', 'head')), parts along dimension 0, may hold values from -6 to 6
- output_gradient: bfloat16 [6144, 4096], P(('groups', 'ctx', 'head')), parts along dimension 0, may hold values from -6 to 6
- block_docs: int32 [48], P('groups'), parts along dimension 0, may hold values from 0 to 11, never falling along the last dimension, each value on 1 to 6 neighbouring positions
Outputs:
- query_grad: bfloat16 [6144, 4096], P(('groups', 'ctx', 'head')), parts along dimension 0
- key_grad: bfloat16 [6144, 1024], P(('groups', 'ctx', 'head')), parts along dimension 0
- value_grad: bfloat16 [6144, 1024], P(('groups', 'ctx', 'head')), parts along dimension 0
There are 2 independent parts, one for each index of `groups`. A program takes and returns all parts, laid end to end along the dimension named above; each array names one. Nothing has to cross between parts.
Inputs may be any that keep to these rules, and one draw needn't show every extreme that they name: `block_docs`: never falls along the sequence; every document covers 1 to 6 blocks, and one covers exactly 6.
All inputs are finite; a program needn't handle non-finite values.
Results may differ from a plain program's by a relative error of at most 0.005.
Values may be sent and summed in bfloat16 or wider, within the bound.
No kernel may reach another device: no remote copies, remote signals or barrier semaphores. Data moves between devices by JAX's collectives and lax.ppermute only.
A program may use at most 128 MiB of HBM per device.

v0:
```python
import jax
import jax.numpy as jnp
from jax import lax
from jax.sharding import PartitionSpec as P

HEAD_SIZE = 128
BLK = 128
REACH = 2


def shifted(block, axis, distance):
    devices = range(lax.axis_size(axis))
    route = [(i - distance, i) for i in devices if i - distance in devices]
    return lax.ppermute(block, axis, route)


def from_behind(value, axis, by):
    peers = lax.axis_size(axis)
    return lax.ppermute(value, axis, [(i, (i + by) % peers) for i in range(peers)])


def per_device(query_matrix, key_matrix, value_matrix, fwd_output, output_gradient, block_docs):
    queries, key_part, value_part, grads, outputs = (
        lax.all_to_all(query_matrix, "head", split_axis=1, concat_axis=0, tiled=True),
        lax.all_to_all(key_matrix, "head", split_axis=1, concat_axis=0, tiled=True),
        lax.all_to_all(value_matrix, "head", split_axis=1, concat_axis=0, tiled=True),
        lax.all_to_all(output_gradient, "head", split_axis=1, concat_axis=0, tiled=True),
        lax.all_to_all(fwd_output, "head", split_axis=1, concat_axis=0, tiled=True),
    )
    heads_here = outputs.shape[1] // HEAD_SIZE
    output_dot_gradient = jnp.sum(
        grads.reshape(outputs.shape[0], heads_here, HEAD_SIZE).astype(jnp.float32)
        * outputs.reshape(outputs.shape[0], heads_here, HEAD_SIZE).astype(jnp.float32),
        axis=2,
    )
    window_extent = queries.shape[0]
    kv_heads = key_part.shape[1] // HEAD_SIZE
    q_heads = queries.shape[1] // HEAD_SIZE
    query_group = q_heads // kv_heads
    scale = HEAD_SIZE ** (-0.5)
    place = lax.axis_index("ctx")
    blocks_here = window_extent // BLK
    query_docs = jnp.repeat(
        lax.dynamic_slice_in_dim(block_docs, place * blocks_here, blocks_here, 0), BLK
    )
    query4 = queries.reshape(window_extent, kv_heads, query_group, HEAD_SIZE)
    grad4 = grads.reshape(window_extent, kv_heads, query_group, HEAD_SIZE)
    delta4 = jnp.transpose(
        output_dot_gradient.reshape(window_extent, kv_heads, query_group), (1, 2, 0)
    )[..., None]
    positions = jnp.arange(window_extent, dtype=jnp.int32)
    lower = positions[None, :] <= positions[:, None]

    def mask_for(distance):
        owner = place - distance
        key_docs = jnp.repeat(
            lax.dynamic_slice_in_dim(
                block_docs, jnp.maximum(owner, 0) * blocks_here, blocks_here, 0
            ),
            BLK,
        )
        mask = (query_docs[:, None] == key_docs[None, :]) & (owner >= 0)
        if distance == 0:
            mask = mask & lower
        return mask

    def raw_scores(keys_now):
        return scale * jnp.einsum(
            "qgrd,kgd->grqk",
            query4,
            keys_now.reshape(window_extent, kv_heads, HEAD_SIZE),
            preferred_element_type=jnp.float32,
        )

    def add_stats(stats, distance, keys_now):
        top, total = stats
        mask = mask_for(distance)
        masked = jnp.where(mask, raw_scores(keys_now), -1e30)
        new_top = jnp.maximum(top, jnp.max(masked, axis=3, keepdims=True))
        total = total * jnp.exp(top - new_top) + jnp.sum(
            jnp.where(mask, jnp.exp(masked - new_top), 0.0), axis=3, keepdims=True
        )
        return (new_top, total)

    def grads_for(distance, keys_now, vals_now, lse):
        mask = mask_for(distance)

        def compute(unused):
            keys3 = keys_now.reshape(window_extent, kv_heads, HEAD_SIZE)
            masked = jnp.where(mask, raw_scores(keys_now), -1e30)
            probs = jnp.where(mask, jnp.exp(masked - lse), 0.0)
            probs_low = probs.astype(jnp.bfloat16)
            dprob = jnp.einsum(
                "qgrd,kgd->grqk",
                grad4,
                vals_now.reshape(window_extent, kv_heads, HEAD_SIZE),
                preferred_element_type=jnp.float32,
            )
            dscore = (probs * (dprob - delta4)).astype(jnp.bfloat16)
            part_q = scale * jnp.einsum(
                "grqk,kgd->qgrd", dscore, keys3, preferred_element_type=jnp.float32
            )
            partial_key_gradient = scale * jnp.einsum(
                "grqk,qgrd->kgd", dscore, query4, preferred_element_type=jnp.float32
            )
            partial_value_gradient = jnp.einsum(
                "grqk,qgrd->kgd", probs_low, grad4, preferred_element_type=jnp.float32
            )
            return (
                part_q.reshape(window_extent, q_heads * HEAD_SIZE),
                partial_key_gradient.reshape(window_extent, kv_heads * HEAD_SIZE),
                partial_value_gradient.reshape(window_extent, kv_heads * HEAD_SIZE),
            )

        def nothing(unused):
            return (
                jnp.zeros((window_extent, q_heads * HEAD_SIZE), jnp.float32),
                jnp.zeros((window_extent, kv_heads * HEAD_SIZE), jnp.float32),
                jnp.zeros((window_extent, kv_heads * HEAD_SIZE), jnp.float32),
            )

        return lax.cond(jnp.any(mask), compute, nothing, 0)

    start_stats = (
        jnp.full((kv_heads, query_group, window_extent, 1), -1e30, jnp.float32),
        jnp.zeros((kv_heads, query_group, window_extent, 1), jnp.float32),
    )
    stats = add_stats(start_stats, 0, key_part)
    keys_now = key_part
    for distance in range(1, REACH + 1):
        keys_now = shifted(keys_now, "ctx", 1)
        stats = add_stats(stats, distance, keys_now)
    lse = stats[0] + jnp.log(stats[1])
    query_sum, travel_k, travel_v = grads_for(0, key_part, value_part, lse)
    pair_now = (key_part, value_part)
    for distance in range(1, REACH + 1):
        pair_now = shifted((pair_now[0], pair_now[1]), "ctx", 1)
        travel_k, travel_v = from_behind((travel_k, travel_v), "ctx", 1)
        part_q, partial_key_gradient, partial_value_gradient = grads_for(
            distance, pair_now[0], pair_now[1], lse
        )
        query_sum = query_sum + part_q
        travel_k = travel_k + partial_key_gradient
        travel_v = travel_v + partial_value_gradient
    key_sum, value_sum = (
        from_behind(travel_k.astype(jnp.bfloat16), "ctx", -REACH).astype(travel_k.dtype),
        from_behind(travel_v.astype(jnp.bfloat16), "ctx", -REACH).astype(travel_v.dtype),
    )
    return (
        lax.all_to_all(
            query_sum.astype(jnp.bfloat16), "head", split_axis=0, concat_axis=1, tiled=True
        ),
        lax.all_to_all(
            key_sum.astype(jnp.bfloat16), "head", split_axis=0, concat_axis=1, tiled=True
        ),
        lax.all_to_all(
            value_sum.astype(jnp.bfloat16), "head", split_axis=0, concat_axis=1, tiled=True
        ),
    )


def solution(mesh):
    return jax.shard_map(
        per_device,
        mesh=mesh,
        in_specs=(
            P(("groups", "ctx", "head"), None),
            P(("groups", "ctx", "head"), None),
            P(("groups", "ctx", "head"), None),
            P(("groups", "ctx", "head"), None),
            P(("groups", "ctx", "head"), None),
            P("groups"),
        ),
        out_specs=(
            P(("groups", "ctx", "head"), None),
            P(("groups", "ctx", "head"), None),
            P(("groups", "ctx", "head"), None),
        ),
        check_vma=False,
    )
```

profile of v0, /device:TPU:0, one launch (start us, length us, event | category | flops | bytes accessed | tf_op | source)
XLA Modules:
  0.0 306.5 jit_solution(12168523319416741571)
XLA Ops:
  1.7 4.2 %all_to_all.140 = bf16[192,2,512]{2,0,1:T(8,128)(2,1)S(1)} all-to-all(bf16[192,2,512]{2,0,1:T(8,128)(2,1)S(1)} %bitcast.333), channel_id=1, replica_groups=mesh['groups'=2,'ctx'=8,'head'=2] {'head'}, dimensions={1} | all-to-all | bytes 786432 | tf_op jit(solution)/shard_map/all_to_all | solution.py:25
  5.9 5.7 %collective-permute-start = (bf16[384,512]{1,0:T(8,128)(2,1)S(1)}, bf16[384,512]{1,0:T(8,128)(2,1)}, u32[]{:S(2)}, u32[]{:S(2)}) collective-permute-start(bf16[384,512]{1,0:T(8,128)(2,1)S(1)} %bitcast.318), channel_id=1, source_target_pairs={{0,2},{2,4},{4,6},{6,8},{8,10},{10,12},{12,14},{1,3},{3,5},{5,7},{... | collective-permute-start | bytes 1179656 | tf_op jit(solution)/shard_map/ppermute | solution.py:14
  11.5 2.7 copy.362
  14.3 3.7 %all-to-all-start.1 = ((bf16[192,2,2048]{2,0,1:T(8,128)(2,1)}), bf16[192,2,2048]{2,0,1:T(8,128)(2,1)S(1)}, u32[]{:S(2)}, u32[]{:S(2)}) async-start(bf16[192,2,2048]{2,0,1:T(8,128)(2,1)} %bitcast.294), calls=%async_computation.1 | async-start | bytes 3145728 | tf_op jit(solution)/shard_map/all_to_all | solution.py:24
  24.6 3.7 %all-to-all-start.3 = ((bf16[192,2,2048]{2,0,1:T(8,128)(2,1)}), bf16[192,2,2048]{2,0,1:T(8,128)(2,1)S(1)}, u32[]{:S(2)}, u32[]{:S(2)}) async-start(bf16[192,2,2048]{2,0,1:T(8,128)(2,1)} %bitcast.308), calls=%async_computation.3 | async-start | bytes 3145728 | tf_op jit(solution)/shard_map/all_to_all | solution.py:27
  28.3 2.8 reshape.216
  31.1 2.7 copy.360
  33.9 4.6 %all-to-all-start.4 = ((bf16[192,2,2048]{2,0,1:T(8,128)(2,1)}), bf16[192,2,2048]{2,0,1:T(8,128)(2,1)}, u32[]{:S(2)}, u32[]{:S(2)}) async-start(bf16[192,2,2048]{2,0,1:T(8,128)(2,1)} %bitcast.309), calls=%async_computation.4 | async-start | bytes 3145728 | tf_op jit(solution)/shard_map/all_to_all | solution.py:28
  38.5 2.8 reshape.220
  41.3 4.2 %all-to-all-start.2 = ((bf16[192,2,512]{2,0,1:T(8,128)(2,1)}), bf16[192,2,512]{2,0,1:T(8,128)(2,1)}, u32[]{:S(2)}, u32[]{:S(2)}) async-start(bf16[192,2,512]{2,0,1:T(8,128)(2,1)} %bitcast.330), calls=%async_computation.2 | async-start | bytes 786432 | tf_op jit(solution)/shard_map/all_to_all | solution.py:26
  50.3 3.5 %reduce_sum.48 = f32[384,16]{1,0:T(8,128)} reduce(f32[384,16,128]{2,1,0:T(8,128)} %bitcast.303, f32[]{:T(128)} %constant.47.clone.1), dimensions={2}, to_apply=%region_7.8 | reduce | flops 780288 | bytes 3170308 | tf_op jit(solution)/shard_map/reduce_sum | solution.py:31
  56.7 7.2 %fusion.42 = (f32[4,4,384]{2,1,0:T(4,128)}, f32[4,384,384,4]{2,1,3,0:T(8,128)}) fusion(pred[384,384]{0,1:T(8,128)(4,1)} %get-tuple-element.202, bf16[384,4,4,128]{3,2,1,0:T(4,128)(2,1)S(1)} %reshape.216, bf16[384,4,128,1]{2,1,0,3:T(4,128)(2,1)} %bitcast.323), kind=kOutput, calls=%fused_computation.57 | convolution fusion | flops 611051520 | bytes 11575296 | tf_op jit(solution)/shard_map/qgrd,kgd->grqk/dot_general | solution.py:68
  65.9 3.9 %collective-permute-start.1 = (bf16[384,512]{1,0:T(8,128)(2,1)}, bf16[384,512]{1,0:T(8,128)(2,1)}, u32[]{:S(2)}, u32[]{:S(2)}) collective-permute-start(bf16[384,512]{1,0:T(8,128)(2,1)} %collective-permute-done), channel_id=1, source_target_pairs={{0,2},{2,4},{4,6},{6,8},{8,10},{10,12},{12,14},{1,3},{3,5},{5,7},{... | collective-permute-start | bytes 1179656 | tf_op jit(solution)/shard_map/ppermute | solution.py:14
  69.8 7.4 %fusion.43 = (f32[4,4,384]{2,1,0:T(4,128)}, f32[4,384,384,4]{2,1,3,0:T(8,128)}) fusion(pred[384,384]{0,1:T(8,128)(4,1)} %get-tuple-element.203, bf16[384,4,128,1]{0,2,3,1:T(8,128)(2,1)} %bitcast.324, bf16[384,4,4,128]{3,2,1,0:T(4,128)(2,1)S(1)} %reshape.216), kind=kOutput, calls=%fused_computation.58 | convolution fusion | flops 611051520 | bytes 11575296 | tf_op jit(solution)/shard_map/qgrd,kgd->grqk/dot_general | solution.py:68
  79.8 8.1 %fusion.44 = (f32[4,4,384]{2,1,0:T(4,128)S(1)}, f32[4,384,384,4]{2,1,3,0:T(8,128)}) fusion(pred[384,384]{0,1:T(8,128)(4,1)} %get-tuple-element.204, bf16[384,4,128,1]{0,2,3,1:T(8,128)(2,1)} %bitcast.325, bf16[384,4,4,128]{3,2,1,0:T(4,128)(2,1)S(1)} %reshape.216), kind=kOutput, calls=%fused_computation.59 | convolution fusion | flops 611051520 | bytes 11575296 | tf_op jit(solution)/shard_map/qgrd,kgd->grqk/dot_general | solution.py:68
  89.4 3.3 %select_reduce_fusion.2 = f32[4,4,384]{2,1,0:T(4,128)S(1)} fusion(f32[4,384,384,4]{2,1,3,0:T(8,128)S(1)} %bitcast.298, f32[4,4,384]{2,1,0:T(4,128)S(1)} %get-tuple-element.201, pred[384,384]{0,1:T(8,128)(4,1)} %get-tuple-element.202), kind=kLoop, calls=%fused_computation.56 | loop fusion | flops 11790336 | bytes 9633792 | tf_op jit(solution)/shard_map/reduce_sum | solution.py:80
  99.5 27.4 %conditional.3 = (f32[384,512]{0,1:T(8,128)}, f32[384,512]{0,1:T(8,128)}, f32[384,2048]{1,0:T(8,128)}) conditional(s32[]{:T(128)} %convert_element_type.51, () %tuple.32, (pred[384,384]{0,1:T(8,128)(4,1)}, bf16[384,512]{1,0:T(8,128)(2,1)S(1)}, bf16[384,4,4,128]{3,2,1,0:T(4,128)(2,1)S(1)}, f32[4,4,384,1]{2,1,0,3:T(4,128)}, ...), branch_computations={%region_8.9_spmd, %region_9.10_spmd} | conditional | flops 3049193472 | bytes 85696728 | solution.py:122
  107.8 3.0 fusion.67
  110.8 3.7 %fusion.6 = f32[4,384,128,1]{1,2,3,0:T(8,128)} fusion(bf16[384,4,4,128]{0,3,2,1:T(8,128)(2,1)S(1)} %copy-done.12, f32[4,384,384,4]{2,1,3,0:T(8,128)S(1)} %fusion.67, f32[4,4,384]{2,1,0:T(4,128)S(1)} %bitcast.351, pred[384,384]{0,1:T(8,128)(4,1)S(1)} %copy-done.10), kind=kOutput, calls=%fused_computation.8 | convolution fusion | flops 615776256 | bytes 11968512 | tf_op jit(solution)/shard_map/cond/branch_1_fun/grqk,qgrd->kgd/dot_general | solution.py:106
  114.6 3.7 %fusion.1 = bf16[4,4,384,384]{2,3,1,0:T(8,128)(2,1)S(1)} fusion(f32[4,384,384,4]{2,1,3,0:T(8,128)S(1)} %fusion.67, f32[4,4,384]{2,1,0:T(4,128)S(1)} %bitcast.348, f32[4,4,384]{2,1,0:T(4,128)S(1)} %bitcast.352, pred[384,384]{0,1:T(8,128)(4,1)S(1)} %copy-done.10, bf16[384,4,4,128]{0,3,2,1:T(8,128)(2,1)S(1)} %copy-done.12, ...), kind=kOutput, calls=%fused_computation.2 | convolution fusion | flops 620494848 | bytes 16318464 | tf_op jit(solution)/shard_map/cond/branch_1_fun/qgrd,kgd->grqk/dot_general | solution.py:93
  120.7 2.7 convolution_multiply_fusion
  123.4 3.6 %copy.311 = f32[384,2048]{1,0:T(8,128)} copy(f32[384,2048]{0,1:T(8,128)} %bitcast.304) | data formatting | bytes 6291456 | tf_op jit(solution)/shard_map/cond | solution.py:122
  136.4 3.3 %collective-permute-start.2 = (bf16[384,512]{1,0:T(8,128)(2,1)}, bf16[384,512]{1,0:T(8,128)(2,1)}, u32[]{:S(2)}, u32[]{:S(2)}) collective-permute-start(bf16[384,512]{1,0:T(8,128)(2,1)} %bitcast.80), channel_id=1, source_target_pairs={{0,2},{2,4},{4,6},{6,8},{8,10},{10,12},{12,14},{1,3},{3,5},{5,7},{... | collective-permute-start | bytes 1179656 | tf_op jit(solution)/shard_map/ppermute | solution.py:14
  140.4 33.4 %collective-permute-done.2 = bf16[384,512]{1,0:T(8,128)(2,1)} collective-permute-done((bf16[384,512]{1,0:T(8,128)(2,1)}, bf16[384,512]{1,0:T(8,128)(2,1)}, u32[]{:S(2)}, u32[]{:S(2)}) %collective-permute-start.2) | collective-permute-done | bytes 393248 | tf_op jit(solution)/shard_map/ppermute | solution.py:14
  173.9 4.2 %conditional.4 = (f32[384,2048]{1,0:T(8,128)}, f32[384,512]{1,0:T(8,128)}, f32[384,512]{1,0:T(8,128)}) conditional(s32[]{:T(128)} %convert_element_type.55, () %tuple.34, (pred[384,384]{0,1:T(8,128)(4,1)}, bf16[384,512]{1,0:T(8,128)(2,1)}, bf16[384,4,4,128]{3,2,1,0:T(4,128)(2,1)S(1)}, f32[4,4,384,1]{2,1,0,3:T(4,128)}, bf16[384,512]{1,0:T(8,128)(2,1)}, ...), branch_computations={%region_11.12_spmd, %region_12.13_spmd} | conditional | flops 3049193472 | bytes 87269568 | solution.py:122
  185.4 3.4 %collective-permute-start.8 = (f32[384,512]{1,0:T(8,128)}, f32[384,512]{1,0:T(8,128)}, u32[]{:S(2)}, u32[]{:S(2)}) collective-permute-start(f32[384,512]{1,0:T(8,128)} %add.91), channel_id=1, source_target_pairs={{0,2},{2,4},{4,6},{6,8},{8,10},{10,12},{12,14},{14,0},{1,3},{3,5},... | collective-permute-start | bytes 2359304 | tf_op jit(solution)/shard_map/ppermute | solution.py:19
  191.3 33.0 %collective-permute-done.3 = bf16[384,512]{1,0:T(8,128)(2,1)S(1)} collective-permute-done((bf16[384,512]{1,0:T(8,128)(2,1)}, bf16[384,512]{1,0:T(8,128)(2,1)S(1)}, u32[]{:S(2)}, u32[]{:S(2)}) %collective-permute-start.3) | collective-permute-done | bytes 393248 | tf_op jit(solution)/shard_map/ppermute | solution.py:14
  228.1 56.3 %collective-permute-start.6 = (bf16[384,512]{1,0:T(8,128)(2,1)S(1)}, bf16[384,512]{1,0:T(8,128)(2,1)S(1)}, u32[]{:S(2)}, u32[]{:S(2)}) collective-permute-start(bf16[384,512]{1,0:T(8,128)(2,1)S(1)} %add_convert_fusion.2), channel_id=1, source_target_pairs={{0,12},{2,14},{4,0},{6,2},{8,4},{10,6},{12,8},{14,10},{1,13},{3,15... | collective-permute-start | bytes 1179656 | tf_op jit(solution)/shard_map/ppermute | solution.py:19
  285.7 4.5 %add_convert_fusion = bf16[384,2048]{1,0:T(8,128)(2,1)S(1)} fusion(f32[384,2048]{1,0:T(8,128)} %get-tuple-element.193, f32[384,2048]{1,0:T(8,128)} %get-tuple-element.189, f32[384,2048]{1,0:T(8,128)} %get-tuple-element.190), kind=kLoop, calls=%fused_computation.61 | loop fusion | flops 2359296 | bytes 11010048 | tf_op jit(solution)/shard_map/convert_element_type | solution.py:151
  290.2 5.0 %all_to_all.141 = bf16[2,192,2048]{2,1,0:T(8,128)(2,1)S(1)} all-to-all(bf16[2,192,2048]{2,1,0:T(8,128)(2,1)S(1)} %bitcast.311), channel_id=1, replica_groups=mesh['groups'=2,'ctx'=8,'head'=2] {'head'}, dimensions={0} | all-to-all | bytes 3145728 | tf_op jit(solution)/shard_map/all_to_all | solution.py:150
  296.5 4.0 %all_to_all.142 = bf16[2,192,512]{2,1,0:T(8,128)(2,1)S(1)} all-to-all(bf16[2,192,512]{2,1,0:T(8,128)(2,1)S(1)} %bitcast.338), channel_id=1, replica_groups=mesh['groups'=2,'ctx'=8,'head'=2] {'head'}, dimensions={0} | all-to-all | bytes 786432 | tf_op jit(solution)/shard_map/all_to_all | solution.py:153
  301.4 4.0 %all_to_all.143 = bf16[2,192,512]{2,1,0:T(8,128)(2,1)S(1)} all-to-all(bf16[2,192,512]{2,1,0:T(8,128)(2,1)S(1)} %bitcast.339), channel_id=1, replica_groups=mesh['groups'=2,'ctx'=8,'head'=2] {'head'}, dimensions={0} | all-to-all | bytes 786432 | tf_op jit(solution)/shard_map/all_to_all | solution.py:156
  (102 shorter events, 71.0 us)
Async XLA Ops:
  0.6 19.9 %copy-start.26 = (s32[24]{0:T(128)S(1)}, s32[24]{0:T(128)}, u32[]{:S(2)}) copy-start(s32[24]{0:T(128)} %param.17) | copy-start | bytes 292
  1.7 21.6 %copy-start.11 = (bf16[192,4096]{1,0:T(8,128)(2,1)S(1)}, bf16[192,4096]{1,0:T(8,128)(2,1)}, u32[]{:S(2)}) copy-start(bf16[192,4096]{1,0:T(8,128)(2,1)} %param.16) | copy-start | bytes 4718596
  5.9 58.1 %collective-permute-start = (bf16[384,512]{1,0:T(8,128)(2,1)S(1)}, bf16[384,512]{1,0:T(8,128)(2,1)}, u32[]{:S(2)}, u32[]{:S(2)}) collective-permute-start(bf16[384,512]{1,0:T(8,128)(2,1)S(1)} %bitcast.318), channel_id=1, source_target_pairs={{0,2},{2,4},{4,6},{6,8},{8,10},{10,12},{12,14},{1,3},{3,5},{5,7},{... | collective-permute-start | bytes 1179656 | tf_op jit(solution)/shard_map/ppermute | solution.py:14
  14.3 10.3 %all-to-all-start.1 = ((bf16[192,2,2048]{2,0,1:T(8,128)(2,1)}), bf16[192,2,2048]{2,0,1:T(8,128)(2,1)S(1)}, u32[]{:S(2)}, u32[]{:S(2)}) async-start(bf16[192,2,2048]{2,0,1:T(8,128)(2,1)} %bitcast.294), calls=%async_computation.1 | async-start | bytes 3145728 | tf_op jit(solution)/shard_map/all_to_all | solution.py:24
  24.6 3.7 %copy-start.4 = (bf16[192,2,2048]{2,0,1:T(8,128)(2,1)}, bf16[192,2,2048]{2,0,1:T(8,128)(2,1)S(1)}, u32[]{:S(2)}) copy-start(bf16[192,2,2048]{2,0,1:T(8,128)(2,1)S(1)} %all-to-all-done.1) | copy-start | bytes 4718596
  24.6 9.3 %all-to-all-start.3 = ((bf16[192,2,2048]{2,0,1:T(8,128)(2,1)}), bf16[192,2,2048]{2,0,1:T(8,128)(2,1)S(1)}, u32[]{:S(2)}, u32[]{:S(2)}) async-start(bf16[192,2,2048]{2,0,1:T(8,128)(2,1)} %bitcast.308), calls=%async_computation.3 | async-start | bytes 3145728 | tf_op jit(solution)/shard_map/all_to_all | solution.py:27
  33.9 4.6 %copy-start.1 = (bf16[192,2,2048]{2,0,1:T(8,128)(2,1)}, bf16[192,2,2048]{2,0,1:T(8,128)(2,1)S(1)}, u32[]{:S(2)}) copy-start(bf16[192,2,2048]{2,0,1:T(8,128)(2,1)S(1)} %all-to-all-done.3) | copy-start | bytes 4718596
  33.9 7.5 %all-to-all-start.4 = ((bf16[192,2,2048]{2,0,1:T(8,128)(2,1)}), bf16[192,2,2048]{2,0,1:T(8,128)(2,1)}, u32[]{:S(2)}, u32[]{:S(2)}) async-start(bf16[192,2,2048]{2,0,1:T(8,128)(2,1)} %bitcast.309), calls=%async_computation.4 | async-start | bytes 3145728 | tf_op jit(solution)/shard_map/all_to_all | solution.py:28
  41.3 58.0 %all-to-all-start.2 = ((bf16[192,2,512]{2,0,1:T(8,128)(2,1)}), bf16[192,2,512]{2,0,1:T(8,128)(2,1)}, u32[]{:S(2)}, u32[]{:S(2)}) async-start(bf16[192,2,512]{2,0,1:T(8,128)(2,1)} %bitcast.330), calls=%async_computation.2 | async-start | bytes 786432 | tf_op jit(solution)/shard_map/all_to_all | solution.py:26
  65.9 12.0 %collective-permute-start.1 = (bf16[384,512]{1,0:T(8,128)(2,1)}, bf16[384,512]{1,0:T(8,128)(2,1)}, u32[]{:S(2)}, u32[]{:S(2)}) collective-permute-start(bf16[384,512]{1,0:T(8,128)(2,1)} %collective-permute-done), channel_id=1, source_target_pairs={{0,2},{2,4},{4,6},{6,8},{8,10},{10,12},{12,14},{1,3},{3,5},{5,7},{... | collective-permute-start | bytes 1179656 | tf_op jit(solution)/shard_map/ppermute | solution.py:14
  79.8 9.5 %slice-start = ((s8[9437184]{0:T(1024)(128)(4,1)}), s8[4194304]{0:T(1024)(128)(4,1)S(1)}, s32[]{:S(2)}) async-start(s8[9437184]{0:T(1024)(128)(4,1)} %bitcast.297), calls=%async_computation.8 | async-start | bytes 8388608
  79.8 9.5 %slice-start.1 = ((s8[9437184]{0:T(1024)(128)(4,1)}), s8[4194304]{0:T(1024)(128)(4,1)S(1)}, s32[]{:S(2)}) async-start(s8[9437184]{0:T(1024)(128)(4,1)} %bitcast.297), calls=%async_computation.9 | async-start | bytes 8388608
  79.8 9.5 %slice-start.2 = ((s8[9437184]{0:T(1024)(128)(4,1)}), s8[1048576]{0:T(1024)(128)(4,1)S(1)}, s32[]{:S(2)}) async-start(s8[9437184]{0:T(1024)(128)(4,1)} %bitcast.297), calls=%async_computation.10 | async-start | bytes 2097152
  79.8 12.8 %slice-start.3 = ((s8[9437184]{0:T(1024)(128)(4,1)}), s8[4194304]{0:T(1024)(128)(4,1)S(1)}, s32[]{:S(2)}) async-start(s8[9437184]{0:T(1024)(128)(4,1)} %bitcast.299), calls=%async_computation.11 | async-start | bytes 8388608
  79.8 12.8 %slice-start.4 = ((s8[9437184]{0:T(1024)(128)(4,1)}), s8[4194304]{0:T(1024)(128)(4,1)S(1)}, s32[]{:S(2)}) async-start(s8[9437184]{0:T(1024)(128)(4,1)} %bitcast.299), calls=%async_computation.12 | async-start | bytes 8388608
  89.4 3.3 %slice-start.5 = ((s8[9437184]{0:T(1024)(128)(4,1)}), s8[1048576]{0:T(1024)(128)(4,1)S(1)}, s32[]{:S(2)}) async-start(s8[9437184]{0:T(1024)(128)(4,1)} %bitcast.299), calls=%async_computation.13 | async-start | bytes 2097152
  89.4 3.3 %copy-start.8 = (pred[384,384]{0,1:T(8,128)(4,1)S(1)}, pred[384,384]{0,1:T(8,128)(4,1)}, u32[]{:S(2)}) copy-start(pred[384,384]{0,1:T(8,128)(4,1)} %get-tuple-element.203) | copy-start | bytes 442372
  92.7 3.7 %copy-start = (f32[4,384,384,4]{2,1,3,0:T(8,128)S(1)}, f32[4,384,384,4]{2,1,3,0:T(8,128)}, u32[]{:S(2)}) copy-start(f32[4,384,384,4]{2,1,3,0:T(8,128)} %get-tuple-element.210) | copy-start | bytes 28311556
  92.7 3.7 %copy-start.6 = (pred[384,384]{0,1:T(8,128)(4,1)S(1)}, pred[384,384]{0,1:T(8,128)(4,1)}, u32[]{:S(2)}) copy-start(pred[384,384]{0,1:T(8,128)(4,1)} %get-tuple-element.204) | copy-start | bytes 442372
  107.8 3.0 copy-start.12
  107.8 3.0 copy-start.23
  110.8 3.8 %copy-start.15 = (bf16[384,4,128]{2,1,0:T(4,128)(2,1)S(1)}, bf16[384,4,128]{2,1,0:T(4,128)(2,1)}, u32[]{:S(2)}) copy-start(bf16[384,4,128]{2,1,0:T(4,128)(2,1)} %reshape.196) | copy-start | bytes 1179652 | tf_op jit(solution)/shard_map/cond
  110.8 3.8 %copy-start.20 = (f32[4,4,384,1]{2,1,0,3:T(4,128)S(1)}, f32[4,4,384,1]{2,1,0,3:T(4,128)}, u32[]{:S(2)}) copy-start(f32[4,4,384,1]{2,1,0,3:T(4,128)} %get-tuple-element.48) | copy-start | bytes 73732 | tf_op jit(solution)/shard_map/cond
  114.6 3.7 %copy-start.2 = (bf16[384,4,4,128]{0,3,2,1:T(8,128)(2,1)S(1)}, bf16[384,4,4,128]{0,3,2,1:T(8,128)(2,1)}, u32[]{:S(2)}) copy-start(bf16[384,4,4,128]{0,3,2,1:T(8,128)(2,1)} %copy.239) | copy-start | bytes 4718596 | tf_op jit(solution)/shard_map/cond
  129.2 48.8 %collective-permute-start.4 = (f32[384,512]{1,0:T(8,128)}, f32[384,512]{1,0:T(8,128)}, u32[]{:S(2)}, u32[]{:S(2)}) collective-permute-start(f32[384,512]{1,0:T(8,128)} %copy.251), channel_id=1, source_target_pairs={{0,2},{2,4},{4,6},{6,8},{8,10},{10,12},{12,14},{14,0},{1,3},{3,5},... | collective-permute-start | bytes 2359304 | tf_op jit(solution)/shard_map/ppermute | solution.py:19
  134.0 49.0 %collective-permute-start.7 = (f32[384,512]{1,0:T(8,128)}, f32[384,512]{1,0:T(8,128)}, u32[]{:S(2)}, u32[]{:S(2)}) collective-permute-start(f32[384,512]{1,0:T(8,128)} %copy.255), channel_id=1, source_target_pairs={{0,2},{2,4},{4,6},{6,8},{8,10},{10,12},{12,14},{14,0},{1,3},{3,5},... | collective-permute-start | bytes 2359304 | tf_op jit(solution)/shard_map/ppermute | solution.py:19
  136.4 37.5 %collective-permute-start.2 = (bf16[384,512]{1,0:T(8,128)(2,1)}, bf16[384,512]{1,0:T(8,128)(2,1)}, u32[]{:S(2)}, u32[]{:S(2)}) collective-permute-start(bf16[384,512]{1,0:T(8,128)(2,1)} %bitcast.80), channel_id=1, source_target_pairs={{0,2},{2,4},{4,6},{6,8},{8,10},{10,12},{12,14},{1,3},{3,5},{5,7},{... | collective-permute-start | bytes 1179656 | tf_op jit(solution)/shard_map/ppermute | solution.py:14
  180.5 46.3 %collective-permute-start.5 = (f32[384,512]{1,0:T(8,128)}, f32[384,512]{1,0:T(8,128)}, u32[]{:S(2)}, u32[]{:S(2)}) collective-permute-start(f32[384,512]{1,0:T(8,128)} %add.89), channel_id=1, source_target_pairs={{0,2},{2,4},{4,6},{6,8},{8,10},{10,12},{12,14},{14,0},{1,3},{3,5},... | collective-permute-start | bytes 2359304 | tf_op jit(solution)/shard_map/ppermute | solution.py:19
  185.4 98.9 %collective-permute-start.8 = (f32[384,512]{1,0:T(8,128)}, f32[384,512]{1,0:T(8,128)}, u32[]{:S(2)}, u32[]{:S(2)}) collective-permute-start(f32[384,512]{1,0:T(8,128)} %add.91), channel_id=1, source_target_pairs={{0,2},{2,4},{4,6},{6,8},{8,10},{10,12},{12,14},{14,0},{1,3},{3,5},... | collective-permute-start | bytes 2359304 | tf_op jit(solution)/shard_map/ppermute | solution.py:19
  188.8 35.6 %collective-permute-start.3 = (bf16[384,512]{1,0:T(8,128)(2,1)}, bf16[384,512]{1,0:T(8,128)(2,1)S(1)}, u32[]{:S(2)}, u32[]{:S(2)}) collective-permute-start(bf16[384,512]{1,0:T(8,128)(2,1)} %collective-permute-done.2), channel_id=1, source_target_pairs={{0,2},{2,4},{4,6},{6,8},{8,10},{10,12},{12,14},{1,3},{3,5},{5,7},{... | collective-permute-start | bytes 1179656 | tf_op jit(solution)/shard_map/ppermute | solution.py:14
  228.1 68.4 %collective-permute-start.6 = (bf16[384,512]{1,0:T(8,128)(2,1)S(1)}, bf16[384,512]{1,0:T(8,128)(2,1)S(1)}, u32[]{:S(2)}, u32[]{:S(2)}) collective-permute-start(bf16[384,512]{1,0:T(8,128)(2,1)S(1)} %add_convert_fusion.2), channel_id=1, source_target_pairs={{0,12},{2,14},{4,0},{6,2},{8,4},{10,6},{12,8},{14,10},{1,13},{3,15... | collective-permute-start | bytes 1179656 | tf_op jit(solution)/shard_map/ppermute | solution.py:19
  285.6 15.8 %collective-permute-start.9 = (bf16[384,512]{1,0:T(8,128)(2,1)S(1)}, bf16[384,512]{1,0:T(8,128)(2,1)S(1)}, u32[]{:S(2)}, u32[]{:S(2)}) collective-permute-start(bf16[384,512]{1,0:T(8,128)(2,1)S(1)} %add_convert_fusion.1), channel_id=1, source_target_pairs={{0,12},{2,14},{4,0},{6,2},{8,4},{10,6},{12,8},{14,10},{1,13},{3,15... | collective-permute-start | bytes 1179656 | tf_op jit(solution)/shard_map/ppermute | solution.py:19
  (4 other events, 9.6 us)
where the time goes:
time: 312 us; the launch traced here: 306 us
  starting transfers between devices  98 us (31%)
  waiting for transfers between devices  67.2 us (22%)
  local copies, waits for them, and re-layouts  52.5 us (17%)
  matrix products  38.2 us (12%)
  other arithmetic  29.5 us (9%)
  blocking collectives  17.3 us (6%)
  between operations  3.29 us (1%)
    ppermute x4, waiting for transfers between devices, shifted(): return lax.ppermute(block, axis, route)  67.2 us
    ppermute x6, starting transfers between devices, from_behind(): lax.ppermute(value, axis, [(i, (i + by) % peers) for i in range(peers)])  67.1 us
    dot_general x4, matrix products, raw_scores(): jnp.einsum('qgrd,kgd->grqk', query4, keys_now.reshape(window_extent, kv_h...  25.7 us
    ppermute x4, starting transfers between devices, shifted(): return lax.ppermute(block, axis, route)  14.8 us
    another operation x9, local copies, waits for them, and re-layouts  12.5 us
    cond x3, local copies, waits for them, and re-layouts, grads_for(): return lax.cond(jnp.any(mask), compute, nothing, 0)  8.17 us
    reduce_sum x3, other arithmetic, add_stats(): jnp.sum(jnp.where(mask, jnp.exp(masked - new_top), 0.0), axis=3, keepdims...  7.86 us
  transfers between devices with their start and end apart: 14, of which 3 were waited for; matrix products, arithmetic and copies ran while one was open for 28% of the time, Pallas kernels for 0%

commit v1 on v0

v1 whole, which is shorter than its diff:
```python
import functools

import jax
import jax.numpy as jnp
from jax import lax
from jax.experimental import pallas as pl
from jax.experimental.pallas import tpu as pltpu
from jax.sharding import PartitionSpec as P

HEAD_SIZE = 128
BLK = 128
REACH = 2
DOC_MOST = 6


def shifted(block, axis, distance):
    devices = range(lax.axis_size(axis))
    route = [(i - distance, i) for i in devices if i - distance in devices]
    return lax.ppermute(block, axis, route)


def attention_kernel(qdoc_ref, kdoc_ref, q_ref, do_ref, o_ref, k_ref, v_ref,
                     dq_ref, dk_ref, dv_ref, *, query_group, query_blocks, key_offset):
    scale = HEAD_SIZE ** (-0.5)
    window = DOC_MOST * BLK
    dk_ref[...] = jnp.zeros_like(dk_ref)
    dv_ref[...] = jnp.zeros_like(dv_ref)
    for qb in range(query_blocks):
        rows = pl.ds(qb * BLK, BLK)
        k0 = key_offset + (qb + 1 - DOC_MOST) * BLK
        kwin = k_ref[pl.ds(k0, window), :]
        vwin = v_ref[pl.ds(k0, window), :]
        qs = jnp.concatenate(
            [q_ref[rows, pl.ds(r * HEAD_SIZE, HEAD_SIZE)] for r in range(query_group)], axis=0)
        dos = jnp.concatenate(
            [do_ref[rows, pl.ds(r * HEAD_SIZE, HEAD_SIZE)] for r in range(query_group)], axis=0)
        outs = jnp.concatenate(
            [o_ref[rows, pl.ds(r * HEAD_SIZE, HEAD_SIZE)] for r in range(query_group)], axis=0)
        delta = jnp.sum(dos.astype(jnp.float32) * outs.astype(jnp.float32), axis=1, keepdims=True)
        qd = qdoc_ref[rows, :]
        kd = kdoc_ref[:, pl.ds(k0, window)]
        qpos = lax.broadcasted_iota(jnp.int32, (BLK, window), 0) + (key_offset + qb * BLK)
        kpos = lax.broadcasted_iota(jnp.int32, (BLK, window), 1) + k0
        allowed = (qd == kd) & (kpos <= qpos)
        mask = jnp.concatenate([allowed] * query_group, axis=0)
        scores = scale * lax.dot_general(
            qs, kwin, (((1,), (1,)), ((), ())), preferred_element_type=jnp.float32)
        masked = jnp.where(mask, scores, -1e30)
        top = jnp.max(masked, axis=1, keepdims=True)
        total = jnp.sum(jnp.where(mask, jnp.exp(masked - top), 0.0), axis=1, keepdims=True)
        lse = top + jnp.log(total)
        probs = jnp.where(mask, jnp.exp(masked - lse), 0.0)
        dprob = lax.dot_general(
            dos, vwin, (((1,), (1,)), ((), ())), preferred_element_type=jnp.float32)
        dscore = (probs * (dprob - delta)).astype(jnp.bfloat16)
        dq = scale * jnp.dot(dscore, kwin, preferred_element_type=jnp.float32)
        for r in range(query_group):
            dq_ref[rows, pl.ds(r * HEAD_SIZE, HEAD_SIZE)] = (
                dq[r * BLK:(r + 1) * BLK].astype(dq_ref.dtype))
        dk_ref[pl.ds(k0, window), :] += scale * lax.dot_general(
            dscore, qs, (((0,), (0,)), ((), ())), preferred_element_type=jnp.float32)
        dv_ref[pl.ds(k0, window), :] += lax.dot_general(
            probs.astype(jnp.bfloat16), dos, (((0,), (0,)), ((), ())),
            preferred_element_type=jnp.float32)


def local_backward(qdoc, kdoc, queries, grads, outputs, keys, values):
    rows, q_cols = queries.shape
    key_rows, kv_cols = keys.shape
    kv_heads = kv_cols // HEAD_SIZE
    query_group = q_cols // HEAD_SIZE // kv_heads
    group_cols = query_group * HEAD_SIZE
    kernel = functools.partial(
        attention_kernel, query_group=query_group, query_blocks=rows // BLK,
        key_offset=key_rows - rows)
    q_spec = pl.BlockSpec((rows, group_cols), lambda g: (0, g))
    k_spec = pl.BlockSpec((key_rows, HEAD_SIZE), lambda g: (0, g))
    return pl.pallas_call(
        kernel,
        grid=(kv_heads,),
        in_specs=[
            pl.BlockSpec((rows, 1), lambda g: (0, 0)),
            pl.BlockSpec((1, key_rows), lambda g: (0, 0)),
            q_spec, q_spec, q_spec, k_spec, k_spec,
        ],
        out_specs=[q_spec, k_spec, k_spec],
        out_shape=[
            jax.ShapeDtypeStruct((rows, q_cols), jnp.bfloat16),
            jax.ShapeDtypeStruct((key_rows, kv_cols), jnp.float32),
            jax.ShapeDtypeStruct((key_rows, kv_cols), jnp.float32),
        ],
        compiler_params=pltpu.CompilerParams(
            dimension_semantics=("arbitrary",), vmem_limit_bytes=48 * 1024 * 1024),
    )(qdoc, kdoc, queries, grads, outputs, keys, values)


def per_device(query_matrix, key_matrix, value_matrix, fwd_output, output_gradient, block_docs):
    queries, key_part, value_part, grads, outputs = (
        lax.all_to_all(query_matrix, "head", split_axis=1, concat_axis=0, tiled=True),
        lax.all_to_all(key_matrix, "head", split_axis=1, concat_axis=0, tiled=True),
        lax.all_to_all(value_matrix, "head", split_axis=1, concat_axis=0, tiled=True),
        lax.all_to_all(output_gradient, "head", split_axis=1, concat_axis=0, tiled=True),
        lax.all_to_all(fwd_output, "head", split_axis=1, concat_axis=0, tiled=True),
    )
    window_extent = queries.shape[0]
    kv_cols = key_part.shape[1]
    place = lax.axis_index("ctx")
    blocks_here = window_extent // BLK

    def docs_of(owner):
        docs = lax.dynamic_slice_in_dim(block_docs, jnp.maximum(owner, 0) * blocks_here, blocks_here, 0)
        return jnp.where(owner >= 0, docs, -1)

    pair = jnp.concatenate([key_part, value_part], axis=1)
    behind = [shifted(pair, "ctx", distance) for distance in range(REACH, 0, -1)]
    keys = jnp.concatenate([b[:, :kv_cols] for b in behind] + [key_part], axis=0)
    values = jnp.concatenate([b[:, kv_cols:] for b in behind] + [value_part], axis=0)
    key_docs = jnp.concatenate([docs_of(place - distance) for distance in range(REACH, -1, -1)])
    kdoc = jnp.repeat(key_docs, BLK)[None, :]
    qdoc = jnp.repeat(docs_of(place), BLK)[:, None]

    query_sum, key_partial, value_partial = local_backward(
        qdoc, kdoc, queries, grads, outputs, keys, values)

    both = jnp.concatenate([key_partial, value_partial], axis=1)
    total = both[REACH * window_extent:]
    for distance in range(1, REACH + 1):
        begin = (REACH - distance) * window_extent
        total = total + shifted(both[begin:begin + window_extent], "ctx", -distance)
    key_sum = total[:, :kv_cols].astype(jnp.bfloat16)
    value_sum = total[:, kv_cols:].astype(jnp.bfloat16)
    return (
        lax.all_to_all(query_sum, "head", split_axis=0, concat_axis=1, tiled=True),
        lax.all_to_all(key_sum, "head", split_axis=0, concat_axis=1, tiled=True),
        lax.all_to_all(value_sum, "head", split_axis=0, concat_axis=1, tiled=True),
    )


def solution(mesh):
    return jax.shard_map(
        per_device,
        mesh=mesh,
        in_specs=(
            P(("groups", "ctx", "head"), None),
            P(("groups", "ctx", "head"), None),
            P(("groups", "ctx", "head"), None),
            P(("groups", "ctx", "head"), None),
            P(("groups", "ctx", "head"), None),
            P("groups"),
        ),
        out_specs=(
            P(("groups", "ctx", "head"), None),
            P(("groups", "ctx", "head"), None),
            P(("groups", "ctx", "head"), None),
        ),
        check_vma=False,
    )
```

time: 312 us -> 178 us (0.57); the launches traced: 306 us -> 177 us
  starting transfers between devices: 98 us -> 19.2 us
  matrix products: 38.2 us -> 0 us
  local copies, waits for them, and re-layouts: 52.5 us -> 16.5 us
  other arithmetic: 29.5 us -> 1.95 us
  Pallas kernels: 0 us -> 23.6 us
  waiting for transfers between devices: 67.2 us -> 84.4 us
  blocking collectives: 17.3 us -> 31 us
    ppermute x6 -> x0, starting transfers between devices: 67.1 us -> none  [from_behind(): lax.ppermute(value, axis, [(i, (i + by) % peers) for i in range(peers)])]
    dot_general x8 -> x0, matrix products: 38.2 us -> none  [the longest x4 25.7 us: raw_scores(): jnp.einsum('qgrd,kgd->grqk', query4, keys_now.reshape(window_extent, kv_h...]
    pallas_call x0 -> x1, Pallas kernels: none -> 23.6 us  [local_backward(): pl.pallas_call(kernel, grid=(kv_heads,), in_specs=[pl.BlockSpec((rows, 1)...]
    ppermute x4, waiting for transfers between devices: 67.2 us -> 82.9 us  [shifted(): return lax.ppermute(block, axis, route)]
    all_to_all x4 -> x6, blocking collectives: 17.3 us -> 31 us  [the longest x1 7.96 us: per_device(): lax.all_to_all(fwd_output, 'head', split_axis=1, concat_axis=0, tiled=True)]
    another operation x9 -> x0, local copies, waits for them, and re-layouts: 12.5 us -> none
    reduce_sum x4 -> x0, other arithmetic: 11.3 us -> none  [the longest x3 7.86 us: add_stats(): jnp.sum(jnp.where(mask, jnp.exp(masked - new_top), 0.0), axis=3, keepdims...]
    reshape x5 -> x0, local copies, waits for them, and re-layouts: 9.81 us -> none  [the longest x1 2.82 us: per_device(): query4 = queries.reshape(window_extent, kv_heads, query_group, HEAD_SIZE)]
  transfers between devices with their start and end apart: 14 -> 6, of which waited for: 3 -> 5; matrix products, arithmetic and copies ran while one was open for 28% -> 6% of each run, Pallas kernels for 0% -> 0%
where the time goes in v1:
time: 178 us; the launch traced here: 177 us
  waiting for transfers between devices  84.4 us (47%)
  blocking collectives  31 us (17%)
  Pallas kernels  23.6 us (13%)
  starting transfers between devices  19.2 us (11%)
  local copies, waits for them, and re-layouts  16.5 us (9%)
  other arithmetic  1.95 us (1%)
    ppermute x4, waiting for transfers between devices, shifted(): return lax.ppermute(block, axis, route)  82.9 us
    pallas_call x1, Pallas kernels, local_backward(): pl.pallas_call(kernel, grid=(kv_heads,), in_specs=[pl.BlockSpec((rows, 1)...  23.6 us
    ppermute x4, starting transfers between devices, shifted(): return lax.ppermute(block, axis, route)  11.9 us
    all_to_all x1, blocking collectives, per_device(): lax.all_to_all(fwd_output, 'head', split_axis=1, concat_axis=0, tiled=True)  7.96 us
    all_to_all x1, blocking collectives, per_device(): lax.all_to_all(output_gradient, 'head', split_axis=1, concat_axis=0, tile...  5.96 us
    all_to_all x1, blocking collectives, per_device(): lax.all_to_all(query_sum, 'head', split_axis=0, concat_axis=1, tiled=True)  5 us
    all_to_all x1, blocking collectives, per_device(): lax.all_to_all(key_sum, 'head', split_axis=0, concat_axis=1, tiled=True)  4.05 us
    all_to_all x1, blocking collectives, per_device(): lax.all_to_all(value_matrix, 'head', split_axis=1, concat_axis=0, tiled=T...  4.04 us
  transfers between devices with their start and end apart: 6, of which 5 were waited for; matrix products, arithmetic and copies ran while one was open for 6% of the time, Pallas kernels for 0%

profile of v1, /device:TPU:0, one launch (start us, length us, event | category | flops | bytes accessed | tf_op | source)
XLA Modules:
  0.0 177.4 jit_solution(10770885569006824596)
XLA Ops:
  0.6 1.8 %copy.48 = bf16[24,2,8,512]{3,2,0,1:T(8,128)(2,1)} copy(bf16[24,2,8,512]{3,2,1,0:T(8,128)(2,1)} %bitcast.82) | data formatting | bytes 786432 | tf_op jit(solution)/shard_map/all_to_all | solution.py:100
  2.5 3.5 %all-to-all-start.3 = ((bf16[192,2,512]{2,0,1:T(8,128)(2,1)}), bf16[192,2,512]{2,0,1:T(8,128)(2,1)S(1)}, u32[]{:S(2)}, u32[]{:S(2)}) async-start(bf16[192,2,512]{2,0,1:T(8,128)(2,1)} %bitcast.57), calls=%async_computation.3 | async-start | bytes 786432 | tf_op jit(solution)/shard_map/all_to_all | solution.py:100
  6.0 1.6 all-to-all-done.3
  7.6 4.0 %all_to_all.152 = bf16[192,2,512]{2,0,1:T(8,128)(2,1)S(1)} all-to-all(bf16[192,2,512]{2,0,1:T(8,128)(2,1)S(1)} %bitcast.77), channel_id=1, replica_groups=mesh['groups'=2,'ctx'=8,'head'=2] {'head'}, dimensions={1} | all-to-all | bytes 786432 | tf_op jit(solution)/shard_map/all_to_all | solution.py:101
  11.6 0.7 copy-done.2
  12.5 5.8 %collective-permute-start.1 = (bf16[384,1024]{1,0:T(8,128)(2,1)S(1)}, bf16[384,1024]{1,0:T(8,128)(2,1)}, u32[]{:S(2)}, u32[]{:S(2)}) collective-permute-start(bf16[384,1024]{1,0:T(8,128)(2,1)S(1)} %pad_maximum_fusion.2), channel_id=1, source_target_pairs={{0,2},{2,4},{4,6},{6,8},{8,10},{10,12},{12,14},{1,3},{3,5},{5,7},{... | collective-permute-start | bytes 2359304 | tf_op jit(solution)/shard_map/ppermute | solution.py:19
  18.2 3.5 %collective-permute-start = (bf16[384,1024]{1,0:T(8,128)(2,1)S(1)}, bf16[384,1024]{1,0:T(8,128)(2,1)}, u32[]{:S(2)}, u32[]{:S(2)}) collective-permute-start(bf16[384,1024]{1,0:T(8,128)(2,1)S(1)} %pad_maximum_fusion.2), channel_id=1, source_target_pairs={{0,4},{2,6},{4,8},{6,10},{8,12},{10,14},{1,5},{3,7},{5,9},{7,11},{... | collective-permute-start | bytes 2359304 | tf_op jit(solution)/shard_map/ppermute | solution.py:19
  21.8 1.2 copy.46
  23.0 3.8 %all-to-all-start = ((bf16[192,2,2048]{2,0,1:T(8,128)(2,1)}), bf16[192,2,2048]{2,0,1:T(8,128)(2,1)S(1)}, u32[]{:S(2)}, u32[]{:S(2)}) async-start(bf16[192,2,2048]{2,0,1:T(8,128)(2,1)} %bitcast.55), calls=%async_computation | async-start | bytes 3145728 | tf_op jit(solution)/shard_map/all_to_all | solution.py:99
  27.3 2.8 %copy.44 = bf16[24,2,8,2048]{3,2,0,1:T(8,128)(2,1)} copy(bf16[24,2,8,2048]{3,2,1,0:T(8,128)(2,1)} %bitcast.74) | data formatting | bytes 3145728 | tf_op jit(solution)/shard_map/all_to_all | solution.py:103
  30.2 1.3 copy.45
  31.4 3.0 %collective-permute-done.1 = bf16[384,1024]{1,0:T(8,128)(2,1)} collective-permute-done((bf16[384,1024]{1,0:T(8,128)(2,1)S(1)}, bf16[384,1024]{1,0:T(8,128)(2,1)}, u32[]{:S(2)}, u32[]{:S(2)}) %collective-permute-start.1) | collective-permute-done | bytes 786464 | tf_op jit(solution)/shard_map/ppermute | solution.py:19
  34.4 1.2 fusion.5
  35.6 2.0 %collective-permute-done = bf16[384,1024]{1,0:T(8,128)(2,1)} collective-permute-done((bf16[384,1024]{1,0:T(8,128)(2,1)S(1)}, bf16[384,1024]{1,0:T(8,128)(2,1)}, u32[]{:S(2)}, u32[]{:S(2)}) %collective-permute-start) | collective-permute-done | bytes 786464 | tf_op jit(solution)/shard_map/ppermute | solution.py:19
  37.7 1.2 fusion.4
  38.8 1.2 pad_maximum_fusion
  40.0 8.0 %all_to_all.153 = bf16[192,2,2048]{2,0,1:T(8,128)(2,1)} all-to-all(bf16[192,2,2048]{2,0,1:T(8,128)(2,1)} %bitcast.65), channel_id=1, replica_groups=mesh['groups'=2,'ctx'=8,'head'=2] {'head'}, dimensions={1} | all-to-all | bytes 3145728 | tf_op jit(solution)/shard_map/all_to_all | solution.py:103
  48.0 6.0 %all_to_all.154 = bf16[192,2,2048]{2,0,1:T(8,128)(2,1)} all-to-all(bf16[192,2,2048]{2,0,1:T(8,128)(2,1)S(1)} %bitcast.64), channel_id=1, replica_groups=mesh['groups'=2,'ctx'=8,'head'=2] {'head'}, dimensions={1} | all-to-all | bytes 3145728 | tf_op jit(solution)/shard_map/all_to_all | solution.py:102
  53.9 23.6 %shard_map.85 = (bf16[384,2048]{1,0:T(8,128)(2,1)S(1)}, f32[1152,512]{1,0:T(8,128)}, f32[1152,512]{1,0:T(8,128)}) custom-call(s32[384,1]{1,0:T(8,128)S(1)} %bitcast.62, s32[1,1152]{1,0:T(1,128)S(1)} %bitcast.63, bf16[384,2048]{1,0:T(8,128)(2,1)S(1)} %bitcast.60, bf16[384,2048]{1,0:T(8,128)(2,1)} %bitcast.68, bf16[384,2048]{1,0:T(8,128)(2,1)} %bitcast.67, ...), custom_call_target="tpu_custom_call" | custom-call | tf_op jit(solution)/shard_map/pallas_call | solution.py:78
  77.5 2.0 %constant_dynamic-update-slice_fusion.1 = f32[1152,1024]{1,0:T(8,128)S(1)} fusion(f32[1152,512]{1,0:T(8,128)} %get-tuple-element.7), kind=kLoop, calls=%fused_computation.12 | loop fusion | bytes 4718592
  80.1 0.4 fusion.2
  80.5 1.3 collective-permute-start.2
  81.8 1.3 collective-permute-start.3
  83.1 5.0 %all_to_all.155 = bf16[2,192,2048]{2,1,0:T(8,128)(2,1)S(1)} all-to-all(bf16[2,192,2048]{2,1,0:T(8,128)(2,1)S(1)} %bitcast.61), channel_id=1, replica_groups=mesh['groups'=2,'ctx'=8,'head'=2] {'head'}, dimensions={0} | all-to-all | bytes 3145728 | tf_op jit(solution)/shard_map/all_to_all | solution.py:133
  88.1 1.2 copy.31
  89.4 42.9 %collective-permute-done.2 = f32[384,1024]{1,0:T(8,128)S(1)} collective-permute-done((f32[384,1024]{1,0:T(8,128)S(1)}, f32[384,1024]{1,0:T(8,128)S(1)}, u32[]{:S(2)}, u32[]{:S(2)}) %collective-permute-start.2) | collective-permute-done | bytes 1572896 | tf_op jit(solution)/shard_map/ppermute | solution.py:19
  132.3 34.9 %collective-permute-done.3 = f32[384,1024]{1,0:T(8,128)S(1)} collective-permute-done((f32[384,1024]{1,0:T(8,128)S(1)}, f32[384,1024]{1,0:T(8,128)S(1)}, u32[]{:S(2)}, u32[]{:S(2)}) %collective-permute-start.3) | collective-permute-done | bytes 1572896 | tf_op jit(solution)/shard_map/ppermute | solution.py:19
  167.2 0.5 fusion.1
  167.8 4.0 %all_to_all.156 = bf16[2,192,512]{2,1,0:T(8,128)(2,1)S(1)} all-to-all(bf16[2,192,512]{2,1,0:T(8,128)(2,1)S(1)} %bitcast.81), channel_id=1, replica_groups=mesh['groups'=2,'ctx'=8,'head'=2] {'head'}, dimensions={0} | all-to-all | bytes 786432 | tf_op jit(solution)/shard_map/all_to_all | solution.py:134
  171.8 0.8 copy.32
  172.6 4.0 %all_to_all.157 = bf16[2,192,512]{2,1,0:T(8,128)(2,1)S(1)} all-to-all(bf16[2,192,512]{2,1,0:T(8,128)(2,1)S(1)} %bitcast.80), channel_id=1, replica_groups=mesh['groups'=2,'ctx'=8,'head'=2] {'head'}, dimensions={0} | all-to-all | bytes 786432 | tf_op jit(solution)/shard_map/all_to_all | solution.py:135
  176.7 0.8 copy.33
  (29 shorter events, 1.3 us)
Async XLA Ops:
  0.6 5.3 %copy-start.7 = (bf16[192,1024]{1,0:T(8,128)(2,1)S(1)}, bf16[192,1024]{1,0:T(8,128)(2,1)}, u32[]{:S(2)}) copy-start(bf16[192,1024]{1,0:T(8,128)(2,1)} %param.8) | copy-start | bytes 1179652
  2.5 5.1 %all-to-all-start.3 = ((bf16[192,2,512]{2,0,1:T(8,128)(2,1)}), bf16[192,2,512]{2,0,1:T(8,128)(2,1)S(1)}, u32[]{:S(2)}, u32[]{:S(2)}) async-start(bf16[192,2,512]{2,0,1:T(8,128)(2,1)} %bitcast.57), calls=%async_computation.3 | async-start | bytes 786432 | tf_op jit(solution)/shard_map/all_to_all | solution.py:100
  5.9 15.8 %copy-start.5 = (bf16[192,4096]{1,0:T(8,128)(2,1)S(1)}, bf16[192,4096]{1,0:T(8,128)(2,1)}, u32[]{:S(2)}) copy-start(bf16[192,4096]{1,0:T(8,128)(2,1)} %param.6) | copy-start | bytes 4718596
  11.6 0.7 copy-start.2
  12.5 22.0 %collective-permute-start.1 = (bf16[384,1024]{1,0:T(8,128)(2,1)S(1)}, bf16[384,1024]{1,0:T(8,128)(2,1)}, u32[]{:S(2)}, u32[]{:S(2)}) collective-permute-start(bf16[384,1024]{1,0:T(8,128)(2,1)S(1)} %pad_maximum_fusion.2), channel_id=1, source_target_pairs={{0,2},{2,4},{4,6},{6,8},{8,10},{10,12},{12,14},{1,3},{3,5},{5,7},{... | collective-permute-start | bytes 2359304 | tf_op jit(solution)/shard_map/ppermute | solution.py:19
  18.2 19.4 %collective-permute-start = (bf16[384,1024]{1,0:T(8,128)(2,1)S(1)}, bf16[384,1024]{1,0:T(8,128)(2,1)}, u32[]{:S(2)}, u32[]{:S(2)}) collective-permute-start(bf16[384,1024]{1,0:T(8,128)(2,1)S(1)} %pad_maximum_fusion.2), channel_id=1, source_target_pairs={{0,4},{2,6},{4,8},{6,10},{8,12},{10,14},{1,5},{3,7},{5,9},{7,11},{... | collective-permute-start | bytes 2359304 | tf_op jit(solution)/shard_map/ppermute | solution.py:19
  23.0 3.8 %copy-start.8 = (s32[24]{0:T(128)S(1)}, s32[24]{0:T(128)}, u32[]{:S(2)}) copy-start(s32[24]{0:T(128)} %param.11) | copy-start | bytes 292
  23.0 17.0 %all-to-all-start = ((bf16[192,2,2048]{2,0,1:T(8,128)(2,1)}), bf16[192,2,2048]{2,0,1:T(8,128)(2,1)S(1)}, u32[]{:S(2)}, u32[]{:S(2)}) async-start(bf16[192,2,2048]{2,0,1:T(8,128)(2,1)} %bitcast.55), calls=%async_computation | async-start | bytes 3145728 | tf_op jit(solution)/shard_map/all_to_all | solution.py:99
  27.3 2.9 %copy-start.6 = (bf16[192,4096]{1,0:T(8,128)(2,1)S(1)}, bf16[192,4096]{1,0:T(8,128)(2,1)}, u32[]{:S(2)}) copy-start(bf16[192,4096]{1,0:T(8,128)(2,1)} %param.10) | copy-start | bytes 4718596
  31.4 7.4 %copy-start.3 = (bf16[192,2,512]{2,0,1:T(8,128)(2,1)S(1)}, bf16[192,2,512]{2,0,1:T(8,128)(2,1)}, u32[]{:S(2)}) copy-start(bf16[192,2,512]{2,0,1:T(8,128)(2,1)} %copy-done.2) | copy-start | bytes 1179652
  40.0 8.0 %copy-start.1 = (bf16[24,2,8,2048]{3,2,0,1:T(8,128)(2,1)S(1)}, bf16[24,2,8,2048]{3,2,0,1:T(8,128)(2,1)}, u32[]{:S(2)}) copy-start(bf16[24,2,8,2048]{3,2,0,1:T(8,128)(2,1)} %copy.45) | copy-start | bytes 4718596
  48.0 6.0 %copy-start = (bf16[1152,512]{1,0:T(8,128)(2,1)S(1)}, bf16[1152,512]{1,0:T(8,128)(2,1)}, u32[]{:S(2)}) copy-start(bf16[1152,512]{1,0:T(8,128)(2,1)} %get-tuple-element.21.v_ref) | copy-start | bytes 3538948
  77.5 2.4 %copy-start.4 = (f32[1152,512]{1,0:T(8,128)S(1)}, f32[1152,512]{1,0:T(8,128)}, u32[]{:S(2)}) copy-start(f32[1152,512]{1,0:T(8,128)} %get-tuple-element.8) | copy-start | bytes 7077892
  80.5 51.8 %collective-permute-start.2 = (f32[384,1024]{1,0:T(8,128)S(1)}, f32[384,1024]{1,0:T(8,128)S(1)}, u32[]{:S(2)}, u32[]{:S(2)}) collective-permute-start(f32[384,1024]{1,0:T(8,128)S(1)} %get-tuple-element.9), channel_id=1, source_target_pairs={{2,0},{4,2},{6,4},{8,6},{10,8},{12,10},{14,12},{3,1},{5,3},{7,5},{... | collective-permute-start | bytes 4718600 | tf_op jit(solution)/shard_map/ppermute | solution.py:19
  81.8 85.3 %collective-permute-start.3 = (f32[384,1024]{1,0:T(8,128)S(1)}, f32[384,1024]{1,0:T(8,128)S(1)}, u32[]{:S(2)}, u32[]{:S(2)}) collective-permute-start(f32[384,1024]{1,0:T(8,128)S(1)} %get-tuple-element.10), channel_id=1, source_target_pairs={{4,0},{6,2},{8,4},{10,6},{12,8},{14,10},{5,1},{7,3},{9,5},{11,7},{... | collective-permute-start | bytes 4718600 | tf_op jit(solution)/shard_map/ppermute | solution.py:19

commit v2 on v1

--- a/solution.py
+++ b/solution.py
@@ -19,7 +19,7 @@
     return lax.ppermute(block, axis, route)
 
 
-def attention_kernel(qdoc_ref, kdoc_ref, q_ref, do_ref, o_ref, k_ref, v_ref,
+def attention_kernel(qdoc_ref, kdoc_ref, q_ref, do_ref, delta_ref, k_ref, v_ref,
                      dq_ref, dk_ref, dv_ref, *, query_group, query_blocks, key_offset):
     scale = HEAD_SIZE ** (-0.5)
     window = DOC_MOST * BLK
@@ -34,9 +34,8 @@
             [q_ref[rows, pl.ds(r * HEAD_SIZE, HEAD_SIZE)] for r in range(query_group)], axis=0)
         dos = jnp.concatenate(
             [do_ref[rows, pl.ds(r * HEAD_SIZE, HEAD_SIZE)] for r in range(query_group)], axis=0)
-        outs = jnp.concatenate(
-            [o_ref[rows, pl.ds(r * HEAD_SIZE, HEAD_SIZE)] for r in range(query_group)], axis=0)
-        delta = jnp.sum(dos.astype(jnp.float32) * outs.astype(jnp.float32), axis=1, keepdims=True)
+        delta = jnp.concatenate(
+            [delta_ref[0, rows, pl.ds(r, 1)] for r in range(query_group)], axis=0)
         qd = qdoc_ref[rows, :]
         kd = kdoc_ref[:, pl.ds(k0, window)]
         qpos = lax.broadcasted_iota(jnp.int32, (BLK, window), 0) + (key_offset + qb * BLK)
@@ -64,7 +63,7 @@
             preferred_element_type=jnp.float32)
 
 
-def local_backward(qdoc, kdoc, queries, grads, outputs, keys, values):
+def local_backward(qdoc, kdoc, queries, grads, delta, keys, values):
     rows, q_cols = queries.shape
     key_rows, kv_cols = keys.shape
     kv_heads = kv_cols // HEAD_SIZE
@@ -81,7 +80,9 @@
         in_specs=[
             pl.BlockSpec((rows, 1), lambda g: (0, 0)),
             pl.BlockSpec((1, key_rows), lambda g: (0, 0)),
-            q_spec, q_spec, q_spec, k_spec, k_spec,
+            q_spec, q_spec,
+            pl.BlockSpec((1, rows, query_group), lambda g: (g, 0, 0)),
+            k_spec, k_spec,
         ],
         out_specs=[q_spec, k_spec, k_spec],
         out_shape=[
@@ -91,19 +92,29 @@
         ],
         compiler_params=pltpu.CompilerParams(
             dimension_semantics=("arbitrary",), vmem_limit_bytes=48 * 1024 * 1024),
-    )(qdoc, kdoc, queries, grads, outputs, keys, values)
+    )(qdoc, kdoc, queries, grads, delta, keys, values)
 
 
 def per_device(query_matrix, key_matrix, value_matrix, fwd_output, output_gradient, block_docs):
-    queries, key_part, value_part, grads, outputs = (
+    tokens, q_cols = query_matrix.shape
+    all_heads = q_cols // HEAD_SIZE
+    delta_here = jnp.sum(
+        output_gradient.reshape(tokens, all_heads, HEAD_SIZE).astype(jnp.float32)
+        * fwd_output.reshape(tokens, all_heads, HEAD_SIZE).astype(jnp.float32),
+        axis=2,
+    )
+    queries, key_part, value_part, grads, delta_heads = (
         lax.all_to_all(query_matrix, "head", split_axis=1, concat_axis=0, tiled=True),
         lax.all_to_all(key_matrix, "head", split_axis=1, concat_axis=0, tiled=True),
         lax.all_to_all(value_matrix, "head", split_axis=1, concat_axis=0, tiled=True),
         lax.all_to_all(output_gradient, "head", split_axis=1, concat_axis=0, tiled=True),
-        lax.all_to_all(fwd_output, "head", split_axis=1, concat_axis=0, tiled=True),
+        lax.all_to_all(delta_here, "head", split_axis=1, concat_axis=0, tiled=True),
     )
     window_extent = queries.shape[0]
     kv_cols = key_part.shape[1]
+    kv_heads = kv_cols // HEAD_SIZE
+    delta = jnp.transpose(
+        delta_heads.reshape(window_extent, kv_heads, delta_heads.shape[1] // kv_heads), (1, 0, 2))
     place = lax.axis_index("ctx")
     blocks_here = window_extent // BLK
 
@@ -120,13 +131,19 @@
     qdoc = jnp.repeat(docs_of(place), BLK)[:, None]
 
     query_sum, key_partial, value_partial = local_backward(
-        qdoc, kdoc, queries, grads, outputs, keys, values)
+        qdoc, kdoc, queries, grads, delta, keys, values)
 
     both = jnp.concatenate([key_partial, value_partial], axis=1)
-    total = both[REACH * window_extent:]
+    own = REACH * window_extent
+    total = both[own:]
+    reached = own + BLK - DOC_MOST * BLK
     for distance in range(1, REACH + 1):
         begin = (REACH - distance) * window_extent
-        total = total + shifted(both[begin:begin + window_extent], "ctx", -distance)
+        start = max(begin, reached)
+        if start >= begin + window_extent:
+            continue
+        sent = shifted(both[start:begin + window_extent].astype(jnp.bfloat16), "ctx", -distance)
+        total = total.at[start - begin:].add(sent.astype(jnp.float32))
     key_sum = total[:, :kv_cols].astype(jnp.bfloat16)
     value_sum = total[:, kv_cols:].astype(jnp.bfloat16)
     return (

time: 178 us -> 133 us (0.75)
  waiting for transfers between devices: 84.4 us -> 39.2 us
  blocking collectives: 31 us -> 25.1 us
  starting transfers between devices: 19.2 us -> 23.2 us
    ppermute x4, waiting for transfers between devices: 82.9 us -> 37.6 us  [shifted(): return lax.ppermute(block, axis, route)]
    all_to_all x1 -> x0, blocking collectives: 7.96 us -> none  [per_device(): lax.all_to_all(fwd_output, 'head', split_axis=1, concat_axis=0, tiled=True)]
    all_to_all x0 -> x1, starting transfers between devices: none -> 3.25 us  [per_device(): lax.all_to_all(delta_here, 'head', split_axis=1, concat_axis=0, tiled=True)]
    all_to_all x1, local copies, waits for them, and re-layouts: 2.84 us -> 0.03 us  [per_device(): lax.all_to_all(delta_here, 'head', split_axis=1, concat_axis=0, tiled=True)]
    all_to_all x1, blocking collectives: 5.96 us -> 7.85 us  [per_device(): lax.all_to_all(output_gradient, 'head', split_axis=1, concat_axis=0, tile...]
  transfers between devices with their start and end apart: 6 -> 7, of which waited for: 5 -> 3; matrix products, arithmetic and copies ran while one was open for 6% -> 9% of each run, Pallas kernels for 0% -> 0%
where the time goes in v2:
time: 133 us; the launch traced here: 132 us
  waiting for transfers between devices  39.2 us (29%)
  blocking collectives  25.1 us (19%)
  Pallas kernels  23.9 us (18%)
  starting transfers between devices  23.2 us (17%)
  local copies, waits for them, and re-layouts  15.9 us (12%)
  other arithmetic  3.58 us (3%)
    ppermute x4, waiting for transfers between devices, shifted(): return lax.ppermute(block, axis, route)  37.6 us
    pallas_call x1, Pallas kernels, local_backward(): pl.pallas_call(kernel, grid=(kv_heads,), in_specs=[pl.BlockSpec((rows, 1)...  23.9 us
    ppermute x4, starting transfers between devices, shifted(): return lax.ppermute(block, axis, route)  11.9 us
    all_to_all x1, blocking collectives, per_device(): lax.all_to_all(output_gradient, 'head', split_axis=1, concat_axis=0, tile...  7.85 us
    all_to_all x1, blocking collectives, per_device(): lax.all_to_all(query_sum, 'head', split_axis=0, concat_axis=1, tiled=True)  5 us
    all_to_all x1, starting transfers between devices, per_device(): lax.all_to_all(query_matrix, 'head', split_axis=1, concat_axis=0, tiled=T...  4.62 us
    all_to_all x1, blocking collectives, per_device(): lax.all_to_all(value_matrix, 'head', split_axis=1, concat_axis=0, tiled=T...  4.17 us
    all_to_all x1, blocking collectives, per_device(): lax.all_to_all(key_sum, 'head', split_axis=0, concat_axis=1, tiled=True)  4.05 us
  transfers between devices with their start and end apart: 7, of which 3 were waited for; matrix products, arithmetic and copies ran while one was open for 9% of the time, Pallas kernels for 0%

profile of v2, /device:TPU:0, one launch (start us, length us, event | category | flops | bytes accessed | tf_op | source)
XLA Modules:
  0.0 131.8 jit_solution(4819837145524837963)
XLA Ops:
  0.6 1.8 %copy.57 = bf16[24,2,8,512]{3,2,0,1:T(8,128)(2,1)} copy(bf16[24,2,8,512]{3,2,1,0:T(8,128)(2,1)} %bitcast.81) | data formatting | bytes 786432 | tf_op jit(solution)/shard_map/all_to_all | solution.py:108
  2.5 3.5 %all-to-all-start.3 = ((bf16[192,2,512]{2,0,1:T(8,128)(2,1)}), bf16[192,2,512]{2,0,1:T(8,128)(2,1)S(1)}, u32[]{:S(2)}, u32[]{:S(2)}) async-start(bf16[192,2,512]{2,0,1:T(8,128)(2,1)} %bitcast.58), calls=%async_computation.3 | async-start | bytes 786432 | tf_op jit(solution)/shard_map/all_to_all | solution.py:108
  6.0 1.6 %all-to-all-done.3 = bf16[192,2,512]{2,0,1:T(8,128)(2,1)S(1)} async-done(((bf16[192,2,512]{2,0,1:T(8,128)(2,1)}), bf16[192,2,512]{2,0,1:T(8,128)(2,1)S(1)}, u32[]{:S(2)}, u32[]{:S(2)}) %all-to-all-start.3) | async-done | bytes 393248 | tf_op jit(solution)/shard_map/all_to_all | solution.py:108
  7.6 4.2 %all_to_all.149 = bf16[192,2,512]{2,0,1:T(8,128)(2,1)S(1)} all-to-all(bf16[192,2,512]{2,0,1:T(8,128)(2,1)S(1)} %bitcast.76), channel_id=1, replica_groups=mesh['groups'=2,'ctx'=8,'head'=2] {'head'}, dimensions={1} | all-to-all | bytes 786432 | tf_op jit(solution)/shard_map/all_to_all | solution.py:109
  11.7 1.0 pad_maximum_fusion.2
  12.8 5.8 %collective-permute-start.1 = (bf16[384,1024]{1,0:T(8,128)(2,1)}, bf16[384,1024]{1,0:T(8,128)(2,1)}, u32[]{:S(2)}, u32[]{:S(2)}) collective-permute-start(bf16[384,1024]{1,0:T(8,128)(2,1)} %pad_maximum_fusion.2), channel_id=1, source_target_pairs={{0,2},{2,4},{4,6},{6,8},{8,10},{10,12},{12,14},{1,3},{3,5},{5,7},{... | collective-permute-start | bytes 2359304 | tf_op jit(solution)/shard_map/ppermute | solution.py:19
  18.5 3.5 %collective-permute-start = (bf16[384,1024]{1,0:T(8,128)(2,1)}, bf16[384,1024]{1,0:T(8,128)(2,1)}, u32[]{:S(2)}, u32[]{:S(2)}) collective-permute-start(bf16[384,1024]{1,0:T(8,128)(2,1)} %pad_maximum_fusion.2), channel_id=1, source_target_pairs={{0,4},{2,6},{4,8},{6,10},{8,12},{10,14},{1,5},{3,7},{5,9},{7,11},{... | collective-permute-start | bytes 2359304 | tf_op jit(solution)/shard_map/ppermute | solution.py:19
  22.1 0.4 multiply_bitcast_fusion
  22.5 0.5 copy.47
  23.0 0.9 reduce_sum.9
  23.9 0.7 copy.28
  24.6 3.3 %all-to-all-start.2 = ((f32[192,2,16]{0,2,1:T(8,128)}), f32[192,2,16]{0,2,1:T(8,128)S(1)}, u32[]{:S(2)}, u32[]{:S(2)}) async-start(f32[192,2,16]{0,2,1:T(8,128)} %bitcast.4), calls=%async_computation.2 | async-start | bytes 65536 | tf_op jit(solution)/shard_map/all_to_all | solution.py:111
  28.4 2.8 %copy.55 = bf16[24,2,8,2048]{3,2,0,1:T(8,128)(2,1)} copy(bf16[24,2,8,2048]{3,2,1,0:T(8,128)(2,1)} %bitcast.74) | data formatting | bytes 3145728 | tf_op jit(solution)/shard_map/all_to_all | solution.py:107
  31.2 1.3 copy.54
  32.5 4.6 %all-to-all-start = ((bf16[192,2,2048]{2,0,1:T(8,128)(2,1)}), bf16[192,2,2048]{2,0,1:T(8,128)(2,1)}, u32[]{:S(2)}, u32[]{:S(2)}) async-start(bf16[192,2,2048]{2,0,1:T(8,128)(2,1)} %bitcast.56), calls=%async_computation | async-start | bytes 3145728 | tf_op jit(solution)/shard_map/all_to_all | solution.py:107
  37.3 0.3 copy.30
  37.6 1.2 fusion.3
  38.8 1.2 fusion.2
  40.2 7.8 %all_to_all.150 = bf16[192,2,2048]{2,0,1:T(8,128)(2,1)} all-to-all(bf16[192,2,2048]{2,0,1:T(8,128)(2,1)} %bitcast.66), channel_id=1, replica_groups=mesh['groups'=2,'ctx'=8,'head'=2] {'head'}, dimensions={1} | all-to-all | bytes 3145728 | tf_op jit(solution)/shard_map/all_to_all | solution.py:110
  48.1 23.9 %shard_map.90 = (bf16[384,2048]{1,0:T(8,128)(2,1)S(1)}, f32[1152,512]{1,0:T(8,128)}, f32[1152,512]{1,0:T(8,128)}) custom-call(s32[384,1]{1,0:T(8,128)S(1)} %bitcast.63, s32[1,1152]{1,0:T(1,128)S(1)} %bitcast.64, bf16[384,2048]{1,0:T(8,128)(2,1)} %bitcast.1.q_ref, bf16[384,2048]{1,0:T(8,128)(2,1)} %bitcast.69, f32[4,384,4]{2,1,0:T(8,128)S(1)} %bitcast.61, ...), custom_call_target="tpu_custom_call" | custom-call | tf_op jit(solution)/shard_map/pallas_call | solution.py:77
  71.9 2.1 %constant_dynamic-update-slice_fusion.1 = f32[1152,1024]{1,0:T(8,128)S(1)} fusion(f32[1152,512]{1,0:T(8,128)} %get-tuple-element.39), kind=kLoop, calls=%fused_computation.12 | loop fusion | bytes 4718592
  74.6 0.4 convert.8
  75.0 1.3 collective-permute-start.2
  76.3 1.3 collective-permute-start.3
  77.6 5.0 %all_to_all.151 = bf16[2,192,2048]{2,1,0:T(8,128)(2,1)S(1)} all-to-all(bf16[2,192,2048]{2,1,0:T(8,128)(2,1)S(1)} %bitcast.62), channel_id=1, replica_groups=mesh['groups'=2,'ctx'=8,'head'=2] {'head'}, dimensions={0} | all-to-all | bytes 3145728 | tf_op jit(solution)/shard_map/all_to_all | solution.py:150
  82.6 1.2 copy.41
  83.9 25.4 %collective-permute-done.2 = bf16[384,1024]{1,0:T(8,128)(2,1)S(1)} collective-permute-done((bf16[384,1024]{1,0:T(8,128)(2,1)S(1)}, bf16[384,1024]{1,0:T(8,128)(2,1)S(1)}, u32[]{:S(2)}, u32[]{:S(2)}) %collective-permute-start.2) | collective-permute-done | bytes 786464 | tf_op jit(solution)/shard_map/ppermute | solution.py:19
  109.6 12.2 %collective-permute-done.3 = bf16[256,1024]{1,0:T(8,128)(2,1)S(1)} collective-permute-done((bf16[256,1024]{1,0:T(8,128)(2,1)S(1)}, bf16[256,1024]{1,0:T(8,128)(2,1)S(1)}, u32[]{:S(2)}, u32[]{:S(2)}) %collective-permute-start.3) | collective-permute-done | bytes 524320 | tf_op jit(solution)/shard_map/ppermute | solution.py:19
  122.2 4.0 %all_to_all.152 = bf16[2,192,512]{2,1,0:T(8,128)(2,1)S(1)} all-to-all(bf16[2,192,512]{2,1,0:T(8,128)(2,1)S(1)} %bitcast.80), channel_id=1, replica_groups=mesh['groups'=2,'ctx'=8,'head'=2] {'head'}, dimensions={0} | all-to-all | bytes 786432 | tf_op jit(solution)/shard_map/all_to_all | solution.py:151
  126.2 0.8 copy.42
  127.0 4.0 %all_to_all.153 = bf16[2,192,512]{2,1,0:T(8,128)(2,1)S(1)} all-to-all(bf16[2,192,512]{2,1,0:T(8,128)(2,1)S(1)} %bitcast.79), channel_id=1, replica_groups=mesh['groups'=2,'ctx'=8,'head'=2] {'head'}, dimensions={0} | all-to-all | bytes 786432 | tf_op jit(solution)/shard_map/all_to_all | solution.py:152
  131.1 0.8 copy.43
  (42 shorter events, 2.1 us)
Async XLA Ops:
  0.6 5.3 %copy-start.8 = (bf16[192,1024]{1,0:T(8,128)(2,1)S(1)}, bf16[192,1024]{1,0:T(8,128)(2,1)}, u32[]{:S(2)}) copy-start(bf16[192,1024]{1,0:T(8,128)(2,1)} %param.14) | copy-start | bytes 1179652
  2.5 5.1 %all-to-all-start.3 = ((bf16[192,2,512]{2,0,1:T(8,128)(2,1)}), bf16[192,2,512]{2,0,1:T(8,128)(2,1)S(1)}, u32[]{:S(2)}, u32[]{:S(2)}) async-start(bf16[192,2,512]{2,0,1:T(8,128)(2,1)} %bitcast.58), calls=%async_computation.3 | async-start | bytes 786432 | tf_op jit(solution)/shard_map/all_to_all | solution.py:108
  5.9 16.1 %copy-start = (bf16[192,4096]{1,0:T(8,128)(2,1)S(1)}, bf16[192,4096]{1,0:T(8,128)(2,1)}, u32[]{:S(2)}) copy-start(bf16[192,4096]{1,0:T(8,128)(2,1)} %param.16) | copy-start | bytes 4718596
  7.6 14.5 %copy-start.2 = (bf16[192,2,512]{2,0,1:T(8,128)(2,1)}, bf16[192,2,512]{2,0,1:T(8,128)(2,1)S(1)}, u32[]{:S(2)}) copy-start(bf16[192,2,512]{2,0,1:T(8,128)(2,1)S(1)} %all-to-all-done.3) | copy-start | bytes 1179652
  7.6 14.5 %copy-start.7 = (bf16[192,4096]{1,0:T(8,128)(2,1)S(1)}, bf16[192,4096]{1,0:T(8,128)(2,1)}, u32[]{:S(2)}) copy-start(bf16[192,4096]{1,0:T(8,128)(2,1)} %param.15) | copy-start | bytes 4718596
  11.7 6.8 %copy-start.4 = (bf16[192,2,512]{2,0,1:T(8,128)(2,1)}, bf16[192,2,512]{2,0,1:T(8,128)(2,1)S(1)}, u32[]{:S(2)}) copy-start(bf16[192,2,512]{2,0,1:T(8,128)(2,1)S(1)} %all_to_all.149) | copy-start | bytes 1179652
  12.8 24.8 %collective-permute-start.1 = (bf16[384,1024]{1,0:T(8,128)(2,1)}, bf16[384,1024]{1,0:T(8,128)(2,1)}, u32[]{:S(2)}, u32[]{:S(2)}) collective-permute-start(bf16[384,1024]{1,0:T(8,128)(2,1)} %pad_maximum_fusion.2), channel_id=1, source_target_pairs={{0,2},{2,4},{4,6},{6,8},{8,10},{10,12},{12,14},{1,3},{3,5},{5,7},{... | collective-permute-start | bytes 2359304 | tf_op jit(solution)/shard_map/ppermute | solution.py:19
  18.5 20.3 %collective-permute-start = (bf16[384,1024]{1,0:T(8,128)(2,1)}, bf16[384,1024]{1,0:T(8,128)(2,1)}, u32[]{:S(2)}, u32[]{:S(2)}) collective-permute-start(bf16[384,1024]{1,0:T(8,128)(2,1)} %pad_maximum_fusion.2), channel_id=1, source_target_pairs={{0,4},{2,6},{4,8},{6,10},{8,12},{10,14},{1,5},{3,7},{5,9},{7,11},{... | collective-permute-start | bytes 2359304 | tf_op jit(solution)/shard_map/ppermute | solution.py:19
  23.0 4.9 %copy-start.9 = (s32[24]{0:T(128)S(1)}, s32[24]{0:T(128)}, u32[]{:S(2)}) copy-start(s32[24]{0:T(128)} %param.17) | copy-start | bytes 292
  24.6 7.9 %all-to-all-start.2 = ((f32[192,2,16]{0,2,1:T(8,128)}), f32[192,2,16]{0,2,1:T(8,128)S(1)}, u32[]{:S(2)}, u32[]{:S(2)}) async-start(f32[192,2,16]{0,2,1:T(8,128)} %bitcast.4), calls=%async_computation.2 | async-start | bytes 65536 | tf_op jit(solution)/shard_map/all_to_all | solution.py:111
  28.4 2.9 %copy-start.1 = (bf16[192,4096]{1,0:T(8,128)(2,1)S(1)}, bf16[192,4096]{1,0:T(8,128)(2,1)}, u32[]{:S(2)}) copy-start(bf16[192,4096]{1,0:T(8,128)(2,1)} %param.16) | copy-start | bytes 4718596
  32.5 7.7 %all-to-all-start = ((bf16[192,2,2048]{2,0,1:T(8,128)(2,1)}), bf16[192,2,2048]{2,0,1:T(8,128)(2,1)}, u32[]{:S(2)}, u32[]{:S(2)}) async-start(bf16[192,2,2048]{2,0,1:T(8,128)(2,1)} %bitcast.56), calls=%async_computation | async-start | bytes 3145728 | tf_op jit(solution)/shard_map/all_to_all | solution.py:107
  37.6 2.5 %copy-start.3 = (bf16[192,2,512]{2,0,1:T(8,128)(2,1)S(1)}, bf16[192,2,512]{2,0,1:T(8,128)(2,1)}, u32[]{:S(2)}) copy-start(bf16[192,2,512]{2,0,1:T(8,128)(2,1)} %copy-done.2) | copy-start | bytes 1179652
  37.6 2.5 %copy-start.5 = (bf16[192,2,512]{2,0,1:T(8,128)(2,1)S(1)}, bf16[192,2,512]{2,0,1:T(8,128)(2,1)}, u32[]{:S(2)}) copy-start(bf16[192,2,512]{2,0,1:T(8,128)(2,1)} %copy-done.4) | copy-start | bytes 1179652
  71.9 2.4 %copy-start.6 = (f32[1152,512]{1,0:T(8,128)S(1)}, f32[1152,512]{1,0:T(8,128)}, u32[]{:S(2)}) copy-start(f32[1152,512]{1,0:T(8,128)} %get-tuple-element.40) | copy-start | bytes 7077892
  75.0 34.3 %collective-permute-start.2 = (bf16[384,1024]{1,0:T(8,128)(2,1)S(1)}, bf16[384,1024]{1,0:T(8,128)(2,1)S(1)}, u32[]{:S(2)}, u32[]{:S(2)}) collective-permute-start(bf16[384,1024]{1,0:T(8,128)(2,1)S(1)} %slice.79), channel_id=1, source_target_pairs={{2,0},{4,2},{6,4},{8,6},{10,8},{12,10},{14,12},{3,1},{5,3},{7,5},{... | collective-permute-start | bytes 2359304 | tf_op jit(solution)/shard_map/ppermute | solution.py:19
  76.3 45.4 %collective-permute-start.3 = (bf16[256,1024]{1,0:T(8,128)(2,1)S(1)}, bf16[256,1024]{1,0:T(8,128)(2,1)S(1)}, u32[]{:S(2)}, u32[]{:S(2)}) collective-permute-start(bf16[256,1024]{1,0:T(8,128)(2,1)S(1)} %slice.81), channel_id=1, source_target_pairs={{4,0},{6,2},{8,4},{10,6},{12,8},{14,10},{5,1},{7,3},{9,5},{11,7},{... | collective-permute-start | bytes 1572872 | tf_op jit(solution)/shard_map/ppermute | solution.py:19

commit v3 on v2

--- a/solution.py
+++ b/solution.py
@@ -11,6 +11,7 @@
 BLK = 128
 REACH = 2
 DOC_MOST = 6
+CHUNKS = 2
 
 
 def shifted(block, axis, distance):
@@ -97,60 +98,82 @@
 
 def per_device(query_matrix, key_matrix, value_matrix, fwd_output, output_gradient, block_docs):
     tokens, q_cols = query_matrix.shape
+    kv_all = key_matrix.shape[1]
     all_heads = q_cols // HEAD_SIZE
+    peers = lax.axis_size("head")
     delta_here = jnp.sum(
         output_gradient.reshape(tokens, all_heads, HEAD_SIZE).astype(jnp.float32)
         * fwd_output.reshape(tokens, all_heads, HEAD_SIZE).astype(jnp.float32),
         axis=2,
     )
-    queries, key_part, value_part, grads, delta_heads = (
-        lax.all_to_all(query_matrix, "head", split_axis=1, concat_axis=0, tiled=True),
-        lax.all_to_all(key_matrix, "head", split_axis=1, concat_axis=0, tiled=True),
-        lax.all_to_all(value_matrix, "head", split_axis=1, concat_axis=0, tiled=True),
-        lax.all_to_all(output_gradient, "head", split_axis=1, concat_axis=0, tiled=True),
-        lax.all_to_all(delta_here, "head", split_axis=1, concat_axis=0, tiled=True),
-    )
-    window_extent = queries.shape[0]
-    kv_cols = key_part.shape[1]
-    kv_heads = kv_cols // HEAD_SIZE
-    delta = jnp.transpose(
-        delta_heads.reshape(window_extent, kv_heads, delta_heads.shape[1] // kv_heads), (1, 0, 2))
+    window_extent = tokens * peers
     place = lax.axis_index("ctx")
     blocks_here = window_extent // BLK
+    own = REACH * window_extent
+    skip = own + BLK - DOC_MOST * BLK
 
     def docs_of(owner):
         docs = lax.dynamic_slice_in_dim(block_docs, jnp.maximum(owner, 0) * blocks_here, blocks_here, 0)
         return jnp.where(owner >= 0, docs, -1)
 
-    pair = jnp.concatenate([key_part, value_part], axis=1)
-    behind = [shifted(pair, "ctx", distance) for distance in range(REACH, 0, -1)]
-    keys = jnp.concatenate([b[:, :kv_cols] for b in behind] + [key_part], axis=0)
-    values = jnp.concatenate([b[:, kv_cols:] for b in behind] + [value_part], axis=0)
     key_docs = jnp.concatenate([docs_of(place - distance) for distance in range(REACH, -1, -1)])
-    kdoc = jnp.repeat(key_docs, BLK)[None, :]
+    kdoc = jnp.repeat(key_docs, BLK)[skip:][None, :]
     qdoc = jnp.repeat(docs_of(place), BLK)[:, None]
 
-    query_sum, key_partial, value_partial = local_backward(
-        qdoc, kdoc, queries, grads, delta, keys, values)
+    def chunk_of(x, j):
+        rows, cols = x.shape
+        per = cols // peers // CHUNKS
+        return x.reshape(rows, peers, CHUNKS, per)[:, :, j, :].reshape(rows, peers * per)
 
-    both = jnp.concatenate([key_partial, value_partial], axis=1)
-    own = REACH * window_extent
-    total = both[own:]
-    reached = own + BLK - DOC_MOST * BLK
-    for distance in range(1, REACH + 1):
-        begin = (REACH - distance) * window_extent
-        start = max(begin, reached)
-        if start >= begin + window_extent:
-            continue
-        sent = shifted(both[start:begin + window_extent].astype(jnp.bfloat16), "ctx", -distance)
-        total = total.at[start - begin:].add(sent.astype(jnp.float32))
-    key_sum = total[:, :kv_cols].astype(jnp.bfloat16)
-    value_sum = total[:, kv_cols:].astype(jnp.bfloat16)
-    return (
-        lax.all_to_all(query_sum, "head", split_axis=0, concat_axis=1, tiled=True),
-        lax.all_to_all(key_sum, "head", split_axis=0, concat_axis=1, tiled=True),
-        lax.all_to_all(value_sum, "head", split_axis=0, concat_axis=1, tiled=True),
-    )
+    def exchange(x):
+        return lax.all_to_all(x, "head", split_axis=1, concat_axis=0, tiled=True)
+
+    q_parts, k_parts, v_parts = [], [], []
+    for j in range(CHUNKS):
+        with jax.named_scope(f"chunk{j}"):
+            queries = exchange(chunk_of(query_matrix, j))
+            grads = exchange(chunk_of(output_gradient, j))
+            key_part = exchange(chunk_of(key_matrix, j))
+            value_part = exchange(chunk_of(value_matrix, j))
+            delta_heads = exchange(chunk_of(delta_here, j))
+            kv_cols = key_part.shape[1]
+            kv_heads = kv_cols // HEAD_SIZE
+            delta = jnp.transpose(
+                delta_heads.reshape(window_extent, kv_heads, delta_heads.shape[1] // kv_heads),
+                (1, 0, 2))
+            pair = jnp.concatenate([key_part, value_part], axis=1)
+            behind = []
+            for distance in range(REACH, 0, -1):
+                begin = (REACH - distance) * window_extent
+                first = max(skip - begin, 0)
+                if first < window_extent:
+                    behind.append(shifted(pair[first:], "ctx", distance))
+            keys = jnp.concatenate([b[:, :kv_cols] for b in behind] + [key_part], axis=0)
+            values = jnp.concatenate([b[:, kv_cols:] for b in behind] + [value_part], axis=0)
+
+            query_sum, key_partial, value_partial = local_backward(
+                qdoc, kdoc, queries, grads, delta, keys, values)
+
+            both = jnp.concatenate([key_partial, value_partial], axis=1)
+            total = both[own - skip:]
+            for distance in range(1, REACH + 1):
+                begin = (REACH - distance) * window_extent
+                start = max(begin, skip)
+                if start >= begin + window_extent:
+                    continue
+                sent = shifted(
+                    both[start - skip:begin + window_extent - skip].astype(jnp.bfloat16),
+                    "ctx", -distance)
+                total = total.at[start - begin:].add(sent.astype(jnp.float32))
+            q_parts.append(query_sum)
+            k_parts.append(total[:, :kv_cols].astype(jnp.bfloat16))
+            v_parts.append(total[:, kv_cols:].astype(jnp.bfloat16))
+
+    def back(parts):
+        return lax.all_to_all(
+            jnp.concatenate(parts, axis=1), "head", split_axis=0, concat_axis=1, tiled=True)
+
+    return back(q_parts), back(k_parts), back(v_parts)
 
 
 def solution(mesh):

time: 133 us -> 163 us (1.23)
  local copies, waits for them, and re-layouts: 15.9 us -> 40.9 us
  waiting for transfers between devices: 39.2 us -> 14.3 us
  starting transfers between devices: 23.2 us -> 41.9 us
  blocking collectives: 25.1 us -> 32.1 us
  other arithmetic: 3.58 us -> 8.32 us
    ppermute x4 -> x8, waiting for transfers between devices: 37.6 us -> 14.2 us  [shifted(): return lax.ppermute(block, axis, route)]
    unnamed x27 -> x64, local copies, waits for them, and re-layouts: 3.26 us -> 14.1 us
    slice x3 -> x11, local copies, waits for them, and re-layouts: 0.14 us -> 10.4 us  [the longest x4 8.73 us: chunk_of(): x.reshape(rows, peers, CHUNKS, per)[:, :, j, :].reshape(rows, peers * per)]
    all_to_all x3 -> x6, starting transfers between devices: 11.3 us -> 20.7 us  [exchange(): return lax.all_to_all(x, 'head', split_axis=1, concat_axis=0, tiled=True)]
    ppermute x4 -> x8, starting transfers between devices: 11.9 us -> 21.2 us  [shifted(): return lax.ppermute(block, axis, route)]
    all_to_all x5 -> x7, blocking collectives: 25.1 us -> 32.1 us  [the longest x4 19 us: exchange(): return lax.all_to_all(x, 'head', split_axis=1, concat_axis=0, tiled=True)]
    reshape x0 -> x4, local copies, waits for them, and re-layouts: none -> 5.65 us  [chunk_of(): x.reshape(rows, peers, CHUNKS, per)[:, :, j, :].reshape(rows, peers * per)]
    all_to_all x8 -> x6, local copies, waits for them, and re-layouts: 8.81 us -> 3.47 us  [the longest x3 2.82 us: back(): lax.all_to_all(jnp.concatenate(parts, axis=1), 'head', split_axis=0, conc...]
  transfers between devices with their start and end apart: 7 -> 14, of which waited for: 3 -> 3; matrix products, arithmetic and copies ran while one was open for 9% -> 24% of each run, Pallas kernels for 0% -> 14%
where the time goes in v3:
time: 163 us; the launch traced here: 161 us
  starting transfers between devices  41.9 us (26%)
  local copies, waits for them, and re-layouts  40.9 us (25%)
  blocking collectives  32.1 us (20%)
  Pallas kernels  22.4 us (14%)
  waiting for transfers between devices  14.3 us (9%)
  other arithmetic  8.32 us (5%)
    pallas_call x2, Pallas kernels, local_backward(): pl.pallas_call(kernel, grid=(kv_heads,), in_specs=[pl.BlockSpec((rows, 1)...  22.4 us
    ppermute x8, starting transfers between devices, shifted(): return lax.ppermute(block, axis, route)  21.2 us
    all_to_all x6, starting transfers between devices, exchange(): return lax.all_to_all(x, 'head', split_axis=1, concat_axis=0, tiled=True)  20.7 us
    all_to_all x4, blocking collectives, exchange(): return lax.all_to_all(x, 'head', split_axis=1, concat_axis=0, tiled=True)  19 us
    ppermute x8, waiting for transfers between devices, shifted(): return lax.ppermute(block, axis, route)  14.2 us
    unnamed x64, local copies, waits for them, and re-layouts  14.1 us
    all_to_all x3, blocking collectives, back(): lax.all_to_all(jnp.concatenate(parts, axis=1), 'head', split_axis=0, conc...  13.1 us
    slice x4, local copies, waits for them, and re-layouts, chunk_of(): x.reshape(rows, peers, CHUNKS, per)[:, :, j, :].reshape(rows, peers * per)  8.73 us
  transfers between devices with their start and end apart: 14, of which 3 were waited for; matrix products, arithmetic and copies ran while one was open for 24% of the time, Pallas kernels for 14%

profile of v3, /device:TPU:0, one launch (start us, length us, event | category | flops | bytes accessed | tf_op | source)
XLA Modules:
  0.0 161.1 jit_solution(15721671453234367944)
XLA Ops:
  0.6 1.3 reshape.194
  3.2 3.4 %all-to-all-start.3 = ((bf16[192,2,256]{2,0,1:T(8,128)(2,1)}), bf16[192,2,256]{2,0,1:T(8,128)(2,1)S(1)}, u32[]{:S(2)}, u32[]{:S(2)}) async-start(bf16[192,2,256]{2,0,1:T(8,128)(2,1)} %bitcast.82), calls=%async_computation.3 | async-start | bytes 393216 | tf_op jit(solution)/shard_map/chunk0/all_to_all | solution.py:129
  8.3 4.0 %all_to_all.241 = bf16[192,2,256]{2,0,1:T(8,128)(2,1)S(1)} all-to-all(bf16[192,2,256]{2,0,1:T(8,128)(2,1)S(1)} %bitcast.117), channel_id=1, replica_groups=mesh['groups'=2,'ctx'=8,'head'=2] {'head'}, dimensions={1} | all-to-all | bytes 393216 | tf_op jit(solution)/shard_map/chunk0/all_to_all | solution.py:129
  13.2 5.6 %collective-permute-start.1 = (bf16[384,512]{1,0:T(8,128)(2,1)}, bf16[384,512]{1,0:T(8,128)(2,1)}, u32[]{:S(2)}, u32[]{:S(2)}) collective-permute-start(bf16[384,512]{1,0:T(8,128)(2,1)} %pad_maximum_fusion.5), channel_id=1, source_target_pairs={{0,2},{2,4},{4,6},{6,8},{8,10},{10,12},{12,14},{1,3},{3,5},{5,7},{... | collective-permute-start | bytes 1179656 | tf_op jit(solution)/shard_map/chunk0/ppermute | solution.py:20
  19.5 3.5 %collective-permute-start = (bf16[256,512]{1,0:T(8,128)(2,1)}, bf16[256,512]{1,0:T(8,128)(2,1)}, u32[]{:S(2)}, u32[]{:S(2)}) collective-permute-start(bf16[256,512]{1,0:T(8,128)(2,1)} %fusion.3), channel_id=1, source_target_pairs={{0,4},{2,6},{4,8},{6,10},{8,12},{10,14},{1,5},{3,7},{5,9},{7,11},{... | collective-permute-start | bytes 786440 | tf_op jit(solution)/shard_map/chunk0/ppermute | solution.py:20
  23.7 3.4 %all-to-all-start.8 = ((bf16[192,2,256]{2,0,1:T(8,128)(2,1)}), bf16[192,2,256]{2,0,1:T(8,128)(2,1)S(1)}, u32[]{:S(2)}, u32[]{:S(2)}) async-start(bf16[192,2,256]{2,0,1:T(8,128)(2,1)} %bitcast.80), calls=%async_computation.8 | async-start | bytes 393216 | tf_op jit(solution)/shard_map/chunk1/all_to_all | solution.py:129
  27.2 1.8 %multiply_bitcast_fusion = f32[24,8,32,128]{3,1,2,0:T(8,128)S(1)} fusion(bf16[192,4096]{1,0:T(8,128)(2,1)} %param.21, bf16[192,4096]{1,0:T(8,128)(2,1)S(1)} %copy-done.7), kind=kLoop, calls=%fused_computation | loop fusion | flops 2359296 | bytes 6291456
  32.2 3.9 %all_to_all.242 = bf16[192,2,256]{2,0,1:T(8,128)(2,1)S(1)} all-to-all(bf16[192,2,256]{2,0,1:T(8,128)(2,1)S(1)} %bitcast.118), channel_id=1, replica_groups=mesh['groups'=2,'ctx'=8,'head'=2] {'head'}, dimensions={1} | all-to-all | bytes 393216 | tf_op jit(solution)/shard_map/chunk1/all_to_all | solution.py:129
  36.1 3.2 %all-to-all-start.2 = ((f32[192,2,8]{0,2,1:T(8,128)}), f32[192,2,8]{0,2,1:T(8,128)S(1)}, u32[]{:S(2)}, u32[]{:S(2)}) async-start(f32[192,2,8]{0,2,1:T(8,128)} %get-tuple-element.99), calls=%async_computation.2 | async-start | bytes 32768 | tf_op jit(solution)/shard_map/chunk0/all_to_all | solution.py:129
  40.1 4.2 %collective-permute-start.3 = (bf16[384,512]{1,0:T(8,128)(2,1)}, bf16[384,512]{1,0:T(8,128)(2,1)}, u32[]{:S(2)}, u32[]{:S(2)}) collective-permute-start(bf16[384,512]{1,0:T(8,128)(2,1)} %pad_maximum_fusion.6), channel_id=1, source_target_pairs={{0,2},{2,4},{4,6},{6,8},{8,10},{10,12},{12,14},{1,3},{3,5},{5,7},{... | collective-permute-start | bytes 1179656 | tf_op jit(solution)/shard_map/chunk1/ppermute | solution.py:20
  45.0 2.7 %collective-permute-start.2 = (bf16[256,512]{1,0:T(8,128)(2,1)}, bf16[256,512]{1,0:T(8,128)(2,1)}, u32[]{:S(2)}, u32[]{:S(2)}) collective-permute-start(bf16[256,512]{1,0:T(8,128)(2,1)} %fusion.2), channel_id=1, source_target_pairs={{0,4},{2,6},{4,8},{6,10},{8,12},{10,14},{1,5},{3,7},{5,9},{7,11},{... | collective-permute-start | bytes 786440 | tf_op jit(solution)/shard_map/chunk1/ppermute | solution.py:20
  48.9 2.9 %reshape.190 = bf16[192,2,2,1024]{3,2,1,0:T(2,128)(2,1)S(1)} reshape(bf16[192,4096]{1,0:T(8,128)(2,1)} %param.18) | data formatting | bytes 3145728 | tf_op jit(solution)/shard_map/chunk0/reshape | solution.py:126
  51.8 3.4 %fusion.5 = (bf16[192,2,1,1024]{3,2,1,0:T(2,128)(2,1)}, bf16[192,2,1,1024]{3,2,1,0:T(2,128)(2,1)}) fusion(bf16[192,2,2,1024]{3,2,1,0:T(2,128)(2,1)S(1)} %reshape.190), kind=kLoop, calls=%fused_computation.43 | loop fusion | bytes 3145728 | tf_op jit(solution)/shard_map/chunk0/slice | solution.py:126
  55.3 3.5 %fusion.4 = (bf16[192,2,1,1024]{3,2,1,0:T(2,128)(2,1)}, bf16[192,2,1,1024]{3,2,1,0:T(2,128)(2,1)}) fusion(bf16[192,2,2,1024]{3,2,1,0:T(2,128)(2,1)S(1)} %reshape.191), kind=kLoop, calls=%fused_computation.42 | loop fusion | bytes 3145728 | tf_op jit(solution)/shard_map/chunk0/slice | solution.py:126
  59.9 3.2 %all-to-all-start.7 = ((f32[192,2,8]{0,2,1:T(8,128)}), f32[192,2,8]{0,2,1:T(8,128)S(1)}, u32[]{:S(2)}, u32[]{:S(2)}) async-start(f32[192,2,8]{0,2,1:T(8,128)} %get-tuple-element.100), calls=%async_computation.7 | async-start | bytes 32768 | tf_op jit(solution)/shard_map/chunk1/all_to_all | solution.py:129
  64.2 1.3 copy.81
  65.5 1.3 copy.80
  66.8 3.7 %all-to-all-start = ((bf16[192,2,1024]{2,0,1:T(8,128)(2,1)}), bf16[192,2,1024]{2,0,1:T(8,128)(2,1)S(1)}, u32[]{:S(2)}, u32[]{:S(2)}) async-start(bf16[192,2,1024]{2,0,1:T(8,128)(2,1)} %bitcast.78), calls=%async_computation | async-start | bytes 1572864 | tf_op jit(solution)/shard_map/chunk0/all_to_all | solution.py:129
  71.6 1.3 copy.79
  73.0 1.3 copy.78
  75.3 1.6 %fusion.13 = (bf16[256,256]{1,0:T(8,128)(2,1)S(1)}, bf16[256,256]{1,0:T(8,128)(2,1)}) fusion(bf16[256,512]{1,0:T(8,128)(2,1)} %collective-permute-done.2), kind=kLoop, calls=%fused_computation.51 | loop fusion | bytes 524288 | tf_op jit(solution)/shard_map/chunk1/slice | solution.py:152
  78.1 5.5 %all_to_all.243 = bf16[192,2,1024]{2,0,1:T(8,128)(2,1)S(1)} all-to-all(bf16[192,2,1024]{2,0,1:T(8,128)(2,1)} %bitcast.111), channel_id=1, replica_groups=mesh['groups'=2,'ctx'=8,'head'=2] {'head'}, dimensions={1} | all-to-all | bytes 1572864 | tf_op jit(solution)/shard_map/chunk0/all_to_all | solution.py:129
  83.6 3.7 %all-to-all-start.5 = ((bf16[192,2,1024]{2,0,1:T(8,128)(2,1)}), bf16[192,2,1024]{2,0,1:T(8,128)(2,1)S(1)}, u32[]{:S(2)}, u32[]{:S(2)}) async-start(bf16[192,2,1024]{2,0,1:T(8,128)(2,1)} %bitcast.110), calls=%async_computation.5 | async-start | bytes 1572864 | tf_op jit(solution)/shard_map/chunk1/all_to_all | solution.py:129
  89.3 11.2 %chunk0.1 = (bf16[384,1024]{1,0:T(8,128)(2,1)S(1)}, f32[1024,256]{1,0:T(8,128)S(1)}, f32[1024,256]{1,0:T(8,128)S(1)}) custom-call(s32[384,1]{1,0:T(8,128)S(1)} %bitcast.88, s32[1,1024]{1,0:T(1,128)S(1)} %bitcast.92, bf16[384,1024]{1,0:T(8,128)(2,1)S(1)} %bitcast.84, bf16[384,1024]{1,0:T(8,128)(2,1)S(1)} %bitcast.86, f32[2,384,4]{2,1,0:T(8,128)S(1)} %bitcast.91, ...), custom_call_target="tpu_custom_call" | custom-call | tf_op jit(solution)/shard_map/chunk0/pallas_call | solution.py:78
  106.8 5.6 %all_to_all.244 = bf16[192,2,1024]{2,0,1:T(8,128)(2,1)S(1)} all-to-all(bf16[192,2,1024]{2,0,1:T(8,128)(2,1)} %bitcast.109), channel_id=1, replica_groups=mesh['groups'=2,'ctx'=8,'head'=2] {'head'}, dimensions={1} | all-to-all | bytes 1572864 | tf_op jit(solution)/shard_map/chunk1/all_to_all | solution.py:129
  112.5 11.2 %chunk1.1 = (bf16[384,1024]{1,0:T(8,128)(2,1)S(1)}, f32[1024,256]{1,0:T(8,128)S(1)}, f32[1024,256]{1,0:T(8,128)S(1)}) custom-call(s32[384,1]{1,0:T(8,128)S(1)} %bitcast.89, s32[1,1024]{1,0:T(1,128)S(1)} %bitcast.93, bf16[384,1024]{1,0:T(8,128)(2,1)S(1)} %bitcast.85, bf16[384,1024]{1,0:T(8,128)(2,1)S(1)} %bitcast.87, f32[2,384,4]{2,1,0:T(8,128)S(1)} %bitcast.90, ...), custom_call_target="tpu_custom_call" | custom-call | tf_op jit(solution)/shard_map/chunk1/pallas_call | solution.py:78
  128.9 5.0 %all_to_all.245 = bf16[2,192,2048]{2,1,0:T(8,128)(2,1)S(1)} all-to-all(bf16[2,192,2048]{2,1,0:T(8,128)(2,1)S(1)} %bitcast.95), channel_id=1, replica_groups=mesh['groups'=2,'ctx'=8,'head'=2] {'head'}, dimensions={0} | all-to-all | bytes 3145728 | tf_op jit(solution)/shard_map/all_to_all | solution.py:173
  135.2 1.3 slice_add_fusion.1
  137.7 2.5 %collective-permute-done.6 = bf16[384,512]{1,0:T(8,128)(2,1)S(1)} collective-permute-done((bf16[384,512]{1,0:T(8,128)(2,1)S(1)}, bf16[384,512]{1,0:T(8,128)(2,1)S(1)}, u32[]{:S(2)}, u32[]{:S(2)}) %collective-permute-start.6) | collective-permute-done | bytes 393248 | tf_op jit(solution)/shard_map/chunk1/ppermute | solution.py:20
  140.3 10.8 %collective-permute-done.7 = bf16[256,512]{1,0:T(8,128)(2,1)S(1)} collective-permute-done((bf16[256,512]{1,0:T(8,128)(2,1)S(1)}, bf16[256,512]{1,0:T(8,128)(2,1)S(1)}, u32[]{:S(2)}, u32[]{:S(2)}) %collective-permute-start.7) | collective-permute-done | bytes 262176 | tf_op jit(solution)/shard_map/chunk1/ppermute | solution.py:20
  151.4 4.0 %all_to_all.246 = bf16[2,192,512]{2,1,0:T(8,128)(2,1)S(1)} all-to-all(bf16[2,192,512]{2,1,0:T(8,128)(2,1)S(1)} %bitcast.113), channel_id=1, replica_groups=mesh['groups'=2,'ctx'=8,'head'=2] {'head'}, dimensions={0} | all-to-all | bytes 786432 | tf_op jit(solution)/shard_map/all_to_all | solution.py:173
  156.2 4.0 %all_to_all.247 = bf16[2,192,512]{2,1,0:T(8,128)(2,1)S(1)} all-to-all(bf16[2,192,512]{2,1,0:T(8,128)(2,1)S(1)} %bitcast.114), channel_id=1, replica_groups=mesh['groups'=2,'ctx'=8,'head'=2] {'head'}, dimensions={0} | all-to-all | bytes 786432 | tf_op jit(solution)/shard_map/all_to_all | solution.py:173
  (123 shorter events, 34.2 us)
Async XLA Ops:
  0.6 6.0 %copy-start.22 = (bf16[192,1024]{1,0:T(8,128)(2,1)S(1)}, bf16[192,1024]{1,0:T(8,128)(2,1)}, u32[]{:S(2)}) copy-start(bf16[192,1024]{1,0:T(8,128)(2,1)} %param.20) | copy-start | bytes 1179652
  3.2 5.1 %all-to-all-start.3 = ((bf16[192,2,256]{2,0,1:T(8,128)(2,1)}), bf16[192,2,256]{2,0,1:T(8,128)(2,1)S(1)}, u32[]{:S(2)}, u32[]{:S(2)}) async-start(bf16[192,2,256]{2,0,1:T(8,128)(2,1)} %bitcast.82), calls=%async_computation.3 | async-start | bytes 393216 | tf_op jit(solution)/shard_map/chunk0/all_to_all | solution.py:129
  8.3 18.9 %copy-start.7 = (bf16[192,4096]{1,0:T(8,128)(2,1)S(1)}, bf16[192,4096]{1,0:T(8,128)(2,1)}, u32[]{:S(2)}) copy-start(bf16[192,4096]{1,0:T(8,128)(2,1)} %param.22) | copy-start | bytes 4718596
  8.3 18.9 %copy-start.15 = (bf16[192,2,256]{2,0,1:T(8,128)(2,1)}, bf16[192,2,256]{2,0,1:T(8,128)(2,1)S(1)}, u32[]{:S(2)}) copy-start(bf16[192,2,256]{2,0,1:T(8,128)(2,1)S(1)} %all-to-all-done.3) | copy-start | bytes 589828
  12.3 6.5 %copy-start.19 = (bf16[192,2,256]{2,0,1:T(8,128)(2,1)}, bf16[192,2,256]{2,0,1:T(8,128)(2,1)S(1)}, u32[]{:S(2)}) copy-start(bf16[192,2,256]{2,0,1:T(8,128)(2,1)S(1)} %all_to_all.241) | copy-start | bytes 589828
  13.2 63.8 %collective-permute-start.1 = (bf16[384,512]{1,0:T(8,128)(2,1)}, bf16[384,512]{1,0:T(8,128)(2,1)}, u32[]{:S(2)}, u32[]{:S(2)}) collective-permute-start(bf16[384,512]{1,0:T(8,128)(2,1)} %pad_maximum_fusion.5), channel_id=1, source_target_pairs={{0,2},{2,4},{4,6},{6,8},{8,10},{10,12},{12,14},{1,3},{3,5},{5,7},{... | collective-permute-start | bytes 1179656 | tf_op jit(solution)/shard_map/chunk0/ppermute | solution.py:20
  19.5 54.8 %collective-permute-start = (bf16[256,512]{1,0:T(8,128)(2,1)}, bf16[256,512]{1,0:T(8,128)(2,1)}, u32[]{:S(2)}, u32[]{:S(2)}) collective-permute-start(bf16[256,512]{1,0:T(8,128)(2,1)} %fusion.3), channel_id=1, source_target_pairs={{0,4},{2,6},{4,8},{6,10},{8,12},{10,14},{1,5},{3,7},{5,9},{7,11},{... | collective-permute-start | bytes 786440 | tf_op jit(solution)/shard_map/chunk0/ppermute | solution.py:20
  23.7 8.5 %all-to-all-start.8 = ((bf16[192,2,256]{2,0,1:T(8,128)(2,1)}), bf16[192,2,256]{2,0,1:T(8,128)(2,1)S(1)}, u32[]{:S(2)}, u32[]{:S(2)}) async-start(bf16[192,2,256]{2,0,1:T(8,128)(2,1)} %bitcast.80), calls=%async_computation.8 | async-start | bytes 393216 | tf_op jit(solution)/shard_map/chunk1/all_to_all | solution.py:129
  30.4 17.3 %copy-start.8 = (bf16[192,4096]{1,0:T(8,128)(2,1)S(1)}, bf16[192,4096]{1,0:T(8,128)(2,1)}, u32[]{:S(2)}) copy-start(bf16[192,4096]{1,0:T(8,128)(2,1)} %param.22) | copy-start | bytes 4718596
  32.2 16.8 %copy-start.13 = (bf16[192,2,256]{2,0,1:T(8,128)(2,1)}, bf16[192,2,256]{2,0,1:T(8,128)(2,1)S(1)}, u32[]{:S(2)}) copy-start(bf16[192,2,256]{2,0,1:T(8,128)(2,1)S(1)} %all-to-all-done.8) | copy-start | bytes 589828
  36.1 11.7 %copy-start.17 = (bf16[192,2,256]{2,0,1:T(8,128)(2,1)}, bf16[192,2,256]{2,0,1:T(8,128)(2,1)S(1)}, u32[]{:S(2)}) copy-start(bf16[192,2,256]{2,0,1:T(8,128)(2,1)S(1)} %all_to_all.242) | copy-start | bytes 589828
  36.1 23.8 %all-to-all-start.2 = ((f32[192,2,8]{0,2,1:T(8,128)}), f32[192,2,8]{0,2,1:T(8,128)S(1)}, u32[]{:S(2)}, u32[]{:S(2)}) async-start(f32[192,2,8]{0,2,1:T(8,128)} %get-tuple-element.99), calls=%async_computation.2 | async-start | bytes 32768 | tf_op jit(solution)/shard_map/chunk0/all_to_all | solution.py:129
  40.1 65.5 %collective-permute-start.3 = (bf16[384,512]{1,0:T(8,128)(2,1)}, bf16[384,512]{1,0:T(8,128)(2,1)}, u32[]{:S(2)}, u32[]{:S(2)}) collective-permute-start(bf16[384,512]{1,0:T(8,128)(2,1)} %pad_maximum_fusion.6), channel_id=1, source_target_pairs={{0,2},{2,4},{4,6},{6,8},{8,10},{10,12},{12,14},{1,3},{3,5},{5,7},{... | collective-permute-start | bytes 1179656 | tf_op jit(solution)/shard_map/chunk1/ppermute | solution.py:20
  45.0 30.3 %collective-permute-start.2 = (bf16[256,512]{1,0:T(8,128)(2,1)}, bf16[256,512]{1,0:T(8,128)(2,1)}, u32[]{:S(2)}, u32[]{:S(2)}) collective-permute-start(bf16[256,512]{1,0:T(8,128)(2,1)} %fusion.2), channel_id=1, source_target_pairs={{0,4},{2,6},{4,8},{6,10},{8,12},{10,14},{1,5},{3,7},{5,9},{7,11},{... | collective-permute-start | bytes 786440 | tf_op jit(solution)/shard_map/chunk1/ppermute | solution.py:20
  55.3 8.9 %copy-start.11 = (bf16[192,2,1,1024]{3,2,1,0:T(2,128)(2,1)S(1)}, bf16[192,2,1,1024]{3,2,1,0:T(2,128)(2,1)}, u32[]{:S(2)}) copy-start(bf16[192,2,1,1024]{3,2,1,0:T(2,128)(2,1)} %get-tuple-element.81) | copy-start | bytes 2359300
  58.7 6.8 %copy-start.12 = (bf16[192,2,1,1024]{3,2,1,0:T(2,128)(2,1)S(1)}, bf16[192,2,1,1024]{3,2,1,0:T(2,128)(2,1)}, u32[]{:S(2)}) copy-start(bf16[192,2,1,1024]{3,2,1,0:T(2,128)(2,1)} %get-tuple-element.79) | copy-start | bytes 2359300
  59.9 7.0 %all-to-all-start.7 = ((f32[192,2,8]{0,2,1:T(8,128)}), f32[192,2,8]{0,2,1:T(8,128)S(1)}, u32[]{:S(2)}, u32[]{:S(2)}) async-start(f32[192,2,8]{0,2,1:T(8,128)} %get-tuple-element.100), calls=%async_computation.7 | async-start | bytes 32768 | tf_op jit(solution)/shard_map/chunk1/all_to_all | solution.py:129
  66.8 4.7 %copy-start.9 = (bf16[192,2,1,1024]{3,2,1,0:T(2,128)(2,1)S(1)}, bf16[192,2,1,1024]{3,2,1,0:T(2,128)(2,1)}, u32[]{:S(2)}) copy-start(bf16[192,2,1,1024]{3,2,1,0:T(2,128)(2,1)} %get-tuple-element.82) | copy-start | bytes 2359300
  66.8 11.3 %all-to-all-start = ((bf16[192,2,1024]{2,0,1:T(8,128)(2,1)}), bf16[192,2,1024]{2,0,1:T(8,128)(2,1)S(1)}, u32[]{:S(2)}, u32[]{:S(2)}) async-start(bf16[192,2,1024]{2,0,1:T(8,128)(2,1)} %bitcast.78), calls=%async_computation | async-start | bytes 1572864 | tf_op jit(solution)/shard_map/chunk0/all_to_all | solution.py:129
  73.0 5.0 %copy-start.16 = (bf16[192,2,256]{2,0,1:T(8,128)(2,1)S(1)}, bf16[192,2,256]{2,0,1:T(8,128)(2,1)}, u32[]{:S(2)}) copy-start(bf16[192,2,256]{2,0,1:T(8,128)(2,1)} %copy-done.15) | copy-start | bytes 589828
  73.0 5.0 %copy-start.20 = (bf16[192,2,256]{2,0,1:T(8,128)(2,1)S(1)}, bf16[192,2,256]{2,0,1:T(8,128)(2,1)}, u32[]{:S(2)}) copy-start(bf16[192,2,256]{2,0,1:T(8,128)(2,1)} %copy-done.19) | copy-start | bytes 589828
  83.6 23.2 %all-to-all-start.5 = ((bf16[192,2,1024]{2,0,1:T(8,128)(2,1)}), bf16[192,2,1024]{2,0,1:T(8,128)(2,1)S(1)}, u32[]{:S(2)}, u32[]{:S(2)}) async-start(bf16[192,2,1024]{2,0,1:T(8,128)(2,1)} %bitcast.110), calls=%async_computation.5 | async-start | bytes 1572864 | tf_op jit(solution)/shard_map/chunk1/all_to_all | solution.py:129
  102.8 3.9 %copy-start.14 = (bf16[192,2,256]{2,0,1:T(8,128)(2,1)S(1)}, bf16[192,2,256]{2,0,1:T(8,128)(2,1)}, u32[]{:S(2)}) copy-start(bf16[192,2,256]{2,0,1:T(8,128)(2,1)} %copy-done.13) | copy-start | bytes 589828
  102.8 3.9 %copy-start.18 = (bf16[192,2,256]{2,0,1:T(8,128)(2,1)S(1)}, bf16[192,2,256]{2,0,1:T(8,128)(2,1)}, u32[]{:S(2)}) copy-start(bf16[192,2,256]{2,0,1:T(8,128)(2,1)} %copy-done.17) | copy-start | bytes 589828
  102.8 3.9 %copy-start.21 = (bf16[256,256]{1,0:T(8,128)(2,1)S(1)}, bf16[256,256]{1,0:T(8,128)(2,1)}, u32[]{:S(2)}) copy-start(bf16[256,256]{1,0:T(8,128)(2,1)} %get-tuple-element.98) | copy-start | bytes 393220
  104.3 30.9 %collective-permute-start.4 = (bf16[384,512]{1,0:T(8,128)(2,1)}, bf16[384,512]{1,0:T(8,128)(2,1)}, u32[]{:S(2)}, u32[]{:S(2)}) collective-permute-start(bf16[384,512]{1,0:T(8,128)(2,1)} %slice.225), channel_id=1, source_target_pairs={{2,0},{4,2},{6,4},{8,6},{10,8},{12,10},{14,12},{3,1},{5,3},{7,5},{... | collective-permute-start | bytes 1179656 | tf_op jit(solution)/shard_map/chunk0/ppermute | solution.py:20
  106.7 5.8 %copy-start.1 = (s32[1,384]{0,1:T(8,128)S(1)}, s32[1,384]{0,1:T(8,128)}, u32[]{:S(2)}) copy-start(s32[1,384]{0,1:T(8,128)} %copy.67) | copy-start | bytes 4612
  106.7 5.7 %copy-start.2 = (f32[384,2,4]{2,0,1:T(8,128)S(1)}, f32[384,2,4]{2,0,1:T(8,128)}, u32[]{:S(2)}) copy-start(f32[384,2,4]{2,0,1:T(8,128)} %copy.48) | copy-start | bytes 36868
  124.0 4.8 %copy-start.5 = (bf16[384,1024]{1,0:T(8,128)(2,1)S(1)}, bf16[384,1024]{1,0:T(8,128)(2,1)}, u32[]{:S(2)}) copy-start(bf16[384,1024]{1,0:T(8,128)(2,1)} %copy-done.4) | copy-start | bytes 2359300
  124.9 12.6 %collective-permute-start.5 = (bf16[256,512]{1,0:T(8,128)(2,1)S(1)}, bf16[256,512]{1,0:T(8,128)(2,1)S(1)}, u32[]{:S(2)}, u32[]{:S(2)}) collective-permute-start(bf16[256,512]{1,0:T(8,128)(2,1)S(1)} %copy-done.23), channel_id=1, source_target_pairs={{4,0},{6,2},{8,4},{10,6},{12,8},{14,10},{5,1},{7,3},{9,5},{11,7},{... | collective-permute-start | bytes 786440 | tf_op jit(solution)/shard_map/chunk0/ppermute | solution.py:20
  126.2 14.0 %collective-permute-start.6 = (bf16[384,512]{1,0:T(8,128)(2,1)S(1)}, bf16[384,512]{1,0:T(8,128)(2,1)S(1)}, u32[]{:S(2)}, u32[]{:S(2)}) collective-permute-start(bf16[384,512]{1,0:T(8,128)(2,1)S(1)} %slice.230), channel_id=1, source_target_pairs={{2,0},{4,2},{6,4},{8,6},{10,8},{12,10},{14,12},{3,1},{5,3},{7,5},{... | collective-permute-start | bytes 1179656 | tf_op jit(solution)/shard_map/chunk1/ppermute | solution.py:20
  127.5 23.6 %collective-permute-start.7 = (bf16[256,512]{1,0:T(8,128)(2,1)S(1)}, bf16[256,512]{1,0:T(8,128)(2,1)S(1)}, u32[]{:S(2)}, u32[]{:S(2)}) collective-permute-start(bf16[256,512]{1,0:T(8,128)(2,1)S(1)} %slice.232), channel_id=1, source_target_pairs={{4,0},{6,2},{8,4},{10,6},{12,8},{14,10},{5,1},{7,3},{9,5},{11,7},{... | collective-permute-start | bytes 786440 | tf_op jit(solution)/shard_map/chunk1/ppermute | solution.py:20
  (7 other events, 10.1 us)

commit v4 on v1

--- a/solution.py
+++ b/solution.py
@@ -64,8 +64,8 @@
             preferred_element_type=jnp.float32)
 
 
-def local_backward(qdoc, kdoc, queries, grads, outputs, keys, values):
-    rows, q_cols = queries.shape
+def local_backward(qdoc, kdoc, fused, q_cols, keys, values):
+    rows = fused.shape[0]
     key_rows, kv_cols = keys.shape
     kv_heads = kv_cols // HEAD_SIZE
     query_group = q_cols // HEAD_SIZE // kv_heads
@@ -73,7 +73,10 @@
     kernel = functools.partial(
         attention_kernel, query_group=query_group, query_blocks=rows // BLK,
         key_offset=key_rows - rows)
-    q_spec = pl.BlockSpec((rows, group_cols), lambda g: (0, g))
+
+    def section(n):
+        return pl.BlockSpec((rows, group_cols), lambda g: (0, n * kv_heads + g))
+
     k_spec = pl.BlockSpec((key_rows, HEAD_SIZE), lambda g: (0, g))
     return pl.pallas_call(
         kernel,
@@ -81,9 +84,9 @@
         in_specs=[
             pl.BlockSpec((rows, 1), lambda g: (0, 0)),
             pl.BlockSpec((1, key_rows), lambda g: (0, 0)),
-            q_spec, q_spec, q_spec, k_spec, k_spec,
+            section(0), section(1), section(2), k_spec, k_spec,
         ],
-        out_specs=[q_spec, k_spec, k_spec],
+        out_specs=[section(0), k_spec, k_spec],
         out_shape=[
             jax.ShapeDtypeStruct((rows, q_cols), jnp.bfloat16),
             jax.ShapeDtypeStruct((key_rows, kv_cols), jnp.float32),
@@ -91,49 +94,65 @@
         ],
         compiler_params=pltpu.CompilerParams(
             dimension_semantics=("arbitrary",), vmem_limit_bytes=48 * 1024 * 1024),
-    )(qdoc, kdoc, queries, grads, outputs, keys, values)
+    )(qdoc, kdoc, fused, fused, fused, keys, values)
 
 
 def per_device(query_matrix, key_matrix, value_matrix, fwd_output, output_gradient, block_docs):
-    queries, key_part, value_part, grads, outputs = (
-        lax.all_to_all(query_matrix, "head", split_axis=1, concat_axis=0, tiled=True),
-        lax.all_to_all(key_matrix, "head", split_axis=1, concat_axis=0, tiled=True),
-        lax.all_to_all(value_matrix, "head", split_axis=1, concat_axis=0, tiled=True),
-        lax.all_to_all(output_gradient, "head", split_axis=1, concat_axis=0, tiled=True),
-        lax.all_to_all(fwd_output, "head", split_axis=1, concat_axis=0, tiled=True),
-    )
-    window_extent = queries.shape[0]
-    kv_cols = key_part.shape[1]
+    tokens, q_all = query_matrix.shape
+    kv_all = key_matrix.shape[1]
+    peers = lax.axis_size("head")
+    q_cols, kv_cols = q_all // peers, kv_all // peers
+    sections = (query_matrix, output_gradient, fwd_output, key_matrix, value_matrix)
+    outgoing = jnp.concatenate(
+        [x[:, p * (x.shape[1] // peers):(p + 1) * (x.shape[1] // peers)]
+         for p in range(peers) for x in sections], axis=1)
+    fused = lax.all_to_all(outgoing, "head", split_axis=1, concat_axis=0, tiled=True)
+    window_extent = fused.shape[0]
+    key_part = fused[:, 3 * q_cols:3 * q_cols + kv_cols]
+    value_part = fused[:, 3 * q_cols + kv_cols:]
     place = lax.axis_index("ctx")
     blocks_here = window_extent // BLK
+    own = REACH * window_extent
+    skip = own + BLK - DOC_MOST * BLK
 
     def docs_of(owner):
         docs = lax.dynamic_slice_in_dim(block_docs, jnp.maximum(owner, 0) * blocks_here, blocks_here, 0)
         return jnp.where(owner >= 0, docs, -1)
 
-    pair = jnp.concatenate([key_part, value_part], axis=1)
-    behind = [shifted(pair, "ctx", distance) for distance in range(REACH, 0, -1)]
+    pair = fused[:, 3 * q_cols:]
+    behind = []
+    for distance in range(REACH, 0, -1):
+        first = max(skip - (REACH - distance) * window_extent, 0)
+        if first < window_extent:
+            behind.append(shifted(pair[first:], "ctx", distance))
     keys = jnp.concatenate([b[:, :kv_cols] for b in behind] + [key_part], axis=0)
     values = jnp.concatenate([b[:, kv_cols:] for b in behind] + [value_part], axis=0)
     key_docs = jnp.concatenate([docs_of(place - distance) for distance in range(REACH, -1, -1)])
-    kdoc = jnp.repeat(key_docs, BLK)[None, :]
+    kdoc = jnp.repeat(key_docs, BLK)[skip:][None, :]
     qdoc = jnp.repeat(docs_of(place), BLK)[:, None]
 
     query_sum, key_partial, value_partial = local_backward(
-        qdoc, kdoc, queries, grads, outputs, keys, values)
+        qdoc, kdoc, fused, q_cols, keys, values)
 
     both = jnp.concatenate([key_partial, value_partial], axis=1)
-    total = both[REACH * window_extent:]
+    total = both[own - skip:]
     for distance in range(1, REACH + 1):
         begin = (REACH - distance) * window_extent
-        total = total + shifted(both[begin:begin + window_extent], "ctx", -distance)
-    key_sum = total[:, :kv_cols].astype(jnp.bfloat16)
-    value_sum = total[:, kv_cols:].astype(jnp.bfloat16)
-    return (
-        lax.all_to_all(query_sum, "head", split_axis=0, concat_axis=1, tiled=True),
-        lax.all_to_all(key_sum, "head", split_axis=0, concat_axis=1, tiled=True),
-        lax.all_to_all(value_sum, "head", split_axis=0, concat_axis=1, tiled=True),
-    )
+        start = max(begin, skip)
+        if start >= begin + window_extent:
+            continue
+        sent = shifted(
+            both[start - skip:begin + window_extent - skip].astype(jnp.bfloat16), "ctx", -distance)
+        total = total.at[start - begin:].add(sent.astype(jnp.float32))
+    finished = jnp.concatenate([query_sum, total.astype(jnp.bfloat16)], axis=1)
+    returned = lax.all_to_all(finished, "head", split_axis=0, concat_axis=1, tiled=True)
+    width = finished.shape[1]
+
+    def gather(begin, size):
+        return jnp.concatenate(
+            [returned[:, p * width + begin:p * width + begin + size] for p in range(peers)], axis=1)
+
+    return gather(0, q_cols), gather(q_cols, kv_cols), gather(q_cols + kv_cols, kv_cols)
 
 
 def solution(mesh):

time: 178 us -> 115 us (0.65)
  waiting for transfers between devices: 84.4 us -> 53.7 us
  blocking collectives: 31 us -> 13.8 us
  local copies, waits for them, and re-layouts: 16.5 us -> 7.6 us
  starting transfers between devices: 19.2 us -> 11 us
  other arithmetic: 1.95 us -> 4.24 us
    ppermute x4, waiting for transfers between devices: 82.9 us -> 53.7 us  [shifted(): return lax.ppermute(block, axis, route)]
    all_to_all x6 -> x2, blocking collectives: 31 us -> 13.8 us  [the longest x1 8.16 us: per_device(): lax.all_to_all(outgoing, 'head', split_axis=1, concat_axis=0, tiled=True)]
    all_to_all x8 -> x2, local copies, waits for them, and re-layouts: 10 us -> 0.59 us  [the longest x1 0.4 us: per_device(): lax.all_to_all(outgoing, 'head', split_axis=1, concat_axis=0, tiled=True)]
    all_to_all x2 -> x0, starting transfers between devices: 7.27 us -> none  [the longest x1 3.8 us: per_device(): lax.all_to_all(query_matrix, 'head', split_axis=1, concat_axis=0, tiled=T...]
    concatenate x1 -> x4, other arithmetic: 0.09 us -> 3.03 us  [the longest x3 2.84 us: gather(): jnp.concatenate([returned[:, p * width + begin:p * width + begin + size]...]
    slice x2, local copies, waits for them, and re-layouts: 2.33 us -> 0.09 us  [per_device(): b[:, kv_cols:]]
    unnamed x24 -> x29, local copies, waits for them, and re-layouts: 3.44 us -> 4.99 us
  transfers between devices with their start and end apart: 6 -> 4, of which waited for: 5 -> 4; matrix products, arithmetic and copies ran while one was open for 6% -> 2% of each run, Pallas kernels for 0% -> 0%
where the time goes in v4:
time: 115 us
  waiting for transfers between devices  53.7 us (47%)
  Pallas kernels  23.7 us (21%)
  blocking collectives  13.8 us (12%)
  starting transfers between devices  11 us (10%)
  local copies, waits for them, and re-layouts  7.6 us (7%)
  other arithmetic  4.24 us (4%)
    ppermute x4, waiting for transfers between devices, shifted(): return lax.ppermute(block, axis, route)  53.7 us
    pallas_call x1, Pallas kernels, local_backward(): pl.pallas_call(kernel, grid=(kv_heads,), in_specs=[pl.BlockSpec((rows, 1)...  23.7 us
    ppermute x4, starting transfers between devices, shifted(): return lax.ppermute(block, axis, route)  11 us
    all_to_all x1, blocking collectives, per_device(): lax.all_to_all(outgoing, 'head', split_axis=1, concat_axis=0, tiled=True)  8.16 us
    all_to_all x1, blocking collectives, per_device(): lax.all_to_all(finished, 'head', split_axis=0, concat_axis=1, tiled=True)  5.63 us
    unnamed x29, local copies, waits for them, and re-layouts  4.99 us
    concatenate x3, other arithmetic, gather(): jnp.concatenate([returned[:, p * width + begin:p * width + begin + size]...  2.84 us
  transfers between devices with their start and end apart: 4, of which 4 were waited for; matrix products, arithmetic and copies ran while one was open for 2% of the time, Pallas kernels for 0%

profile of v4, /device:TPU:0, one launch (start us, length us, event | category | flops | bytes accessed | tf_op | source)
XLA Modules:
  0.0 115.1 jit_solution(15220192803213191501)
XLA Ops:
  0.7 1.4 %slice_dynamic-update-slice_fusion.5 = bf16[192,14336]{1,0:T(8,128)(2,1)S(1)} fusion(bf16[192,4096]{1,0:T(8,128)(2,1)} %param.12), kind=kLoop, calls=%fused_computation.13 | loop fusion | bytes 1572864
  2.0 1.3 %slice_dynamic-update-slice_fusion.4 = bf16[192,14336]{1,0:T(8,128)(2,1)S(1)} fusion(bf16[192,14336]{1,0:T(8,128)(2,1)S(1)} %slice_dynamic-update-slice_fusion.5, bf16[192,4096]{1,0:T(8,128)(2,1)} %param.16), kind=kLoop, calls=%fused_computation.12 | loop fusion | bytes 1572864
  3.6 0.2 copy-done.3
  4.0 0.4 copy.20
  4.4 8.2 %all_to_all.38 = bf16[192,2,7168]{2,0,1:T(8,128)(2,1)S(1)} all-to-all(bf16[192,2,7168]{2,0,1:T(8,128)(2,1)S(1)} %bitcast.27), channel_id=1, replica_groups=mesh['groups'=2,'ctx'=8,'head'=2] {'head'}, dimensions={1} | all-to-all | bytes 11010048 | tf_op jit(solution)/shard_map/all_to_all | solution.py:109
  12.6 5.0 %collective-permute-start = (bf16[256,1024]{1,0:T(8,128)(2,1)S(1)}, bf16[256,1024]{1,0:T(8,128)(2,1)S(1)}, u32[]{:S(2)}, u32[]{:S(2)}) collective-permute-start(bf16[256,1024]{1,0:T(8,128)(2,1)S(1)} %slice.151), channel_id=1, source_target_pairs={{0,4},{2,6},{4,8},{6,10},{8,12},{10,14},{1,5},{3,7},{5,9},{7,11},{... | collective-permute-start | bytes 1572872 | tf_op jit(solution)/shard_map/ppermute | solution.py:19
  17.7 3.5 %collective-permute-start.1 = (bf16[384,1024]{1,0:T(8,128)(2,1)S(1)}, bf16[384,1024]{1,0:T(8,128)(2,1)S(1)}, u32[]{:S(2)}, u32[]{:S(2)}) collective-permute-start(bf16[384,1024]{1,0:T(8,128)(2,1)S(1)} %slice.153), channel_id=1, source_target_pairs={{0,2},{2,4},{4,6},{6,8},{8,10},{10,12},{12,14},{1,3},{3,5},{5,7},{... | collective-permute-start | bytes 2359304 | tf_op jit(solution)/shard_map/ppermute | solution.py:19
  21.2 0.1 broadcast_select_fusion.1
  21.5 0.1 copy.17
  21.6 1.2 %fusion.1 = (bf16[384,512]{1,0:T(8,128)(2,1)S(1)}, bf16[384,512]{1,0:T(8,128)(2,1)S(1)}) fusion(bf16[384,7168]{1,0:T(8,128)(2,1)} %bitcast.23), kind=kLoop, calls=%fused_computation.28 | loop fusion | bytes 1572864 | tf_op jit(solution)/shard_map/slice | solution.py:112
  22.8 6.2 %collective-permute-done = bf16[256,1024]{1,0:T(8,128)(2,1)S(1)} collective-permute-done((bf16[256,1024]{1,0:T(8,128)(2,1)S(1)}, bf16[256,1024]{1,0:T(8,128)(2,1)S(1)}, u32[]{:S(2)}, u32[]{:S(2)}) %collective-permute-start) | collective-permute-done | bytes 524320 | tf_op jit(solution)/shard_map/ppermute | solution.py:19
  29.1 8.8 %collective-permute-done.1 = bf16[384,1024]{1,0:T(8,128)(2,1)S(1)} collective-permute-done((bf16[384,1024]{1,0:T(8,128)(2,1)S(1)}, bf16[384,1024]{1,0:T(8,128)(2,1)S(1)}, u32[]{:S(2)}, u32[]{:S(2)}) %collective-permute-start.1) | collective-permute-done | bytes 786464 | tf_op jit(solution)/shard_map/ppermute | solution.py:19
  38.0 0.1 pad_maximum_fusion.2
  38.2 23.7 %shard_map.90 = (bf16[384,2048]{1,0:T(8,128)(2,1)S(1)}, f32[1024,512]{1,0:T(8,128)S(1)}, f32[1024,512]{1,0:T(8,128)}) custom-call(s32[384,1]{1,0:T(8,128)S(1)} %bitcast.19, s32[1,1024]{1,0:T(1,128)S(1)} %bitcast.20, bf16[384,7168]{1,0:T(8,128)(2,1)} %bitcast.24, bf16[384,7168]{1,0:T(8,128)(2,1)} %bitcast.25, bf16[384,7168]{1,0:T(8,128)(2,1)} %bitcast.26, ...), custom_call_target="tpu_custom_call" | custom-call | tf_op jit(solution)/shard_map/pallas_call | solution.py:81
  61.9 0.2 constant_dynamic-update-slice_fusion.1
  62.1 1.4 %copy-done.1 = f32[1024,512]{1,0:T(8,128)S(1)} copy-done((f32[1024,512]{1,0:T(8,128)S(1)}, f32[1024,512]{1,0:T(8,128)}, u32[]{:S(2)}) %copy-start.1) | copy-done | bytes 2097176
  63.5 0.2 constant_dynamic-update-slice_fusion
  63.7 0.3 convert.4
  64.1 1.3 %collective-permute-start.2 = (bf16[384,1024]{1,0:T(8,128)(2,1)S(1)}, bf16[384,1024]{1,0:T(8,128)(2,1)S(1)}, u32[]{:S(2)}, u32[]{:S(2)}) collective-permute-start(bf16[384,1024]{1,0:T(8,128)(2,1)S(1)} %slice.160), channel_id=1, source_target_pairs={{2,0},{4,2},{6,4},{8,6},{10,8},{12,10},{14,12},{3,1},{5,3},{7,5},{... | collective-permute-start | bytes 2359304 | tf_op jit(solution)/shard_map/ppermute | solution.py:19
  65.4 1.3 %collective-permute-start.3 = (bf16[256,1024]{1,0:T(8,128)(2,1)S(1)}, bf16[256,1024]{1,0:T(8,128)(2,1)S(1)}, u32[]{:S(2)}, u32[]{:S(2)}) collective-permute-start(bf16[256,1024]{1,0:T(8,128)(2,1)S(1)} %slice.162), channel_id=1, source_target_pairs={{4,0},{6,2},{8,4},{10,6},{12,8},{14,10},{5,1},{7,3},{9,5},{11,7},{... | collective-permute-start | bytes 1572872 | tf_op jit(solution)/shard_map/ppermute | solution.py:19
  66.7 25.7 %collective-permute-done.2 = bf16[384,1024]{1,0:T(8,128)(2,1)S(1)} collective-permute-done((bf16[384,1024]{1,0:T(8,128)(2,1)S(1)}, bf16[384,1024]{1,0:T(8,128)(2,1)S(1)}, u32[]{:S(2)}, u32[]{:S(2)}) %collective-permute-start.2) | collective-permute-done | bytes 786464 | tf_op jit(solution)/shard_map/ppermute | solution.py:19
  92.5 0.2 slice_add_fusion
  92.7 12.9 %collective-permute-done.3 = bf16[256,1024]{1,0:T(8,128)(2,1)S(1)} collective-permute-done((bf16[256,1024]{1,0:T(8,128)(2,1)S(1)}, bf16[256,1024]{1,0:T(8,128)(2,1)S(1)}, u32[]{:S(2)}, u32[]{:S(2)}) %collective-permute-start.3) | collective-permute-done | bytes 524320 | tf_op jit(solution)/shard_map/ppermute | solution.py:19
  105.6 0.3 fusion
  105.9 0.1 convert_element_type.13
  106.0 0.2 pad_maximum_fusion
  106.2 5.6 %all_to_all.39 = bf16[2,192,3072]{2,1,0:T(8,128)(2,1)S(1)} all-to-all(bf16[2,192,3072]{2,1,0:T(8,128)(2,1)S(1)} %bitcast.30), channel_id=1, replica_groups=mesh['groups'=2,'ctx'=8,'head'=2] {'head'}, dimensions={0} | all-to-all | bytes 4718592 | tf_op jit(solution)/shard_map/all_to_all | solution.py:148
  111.8 0.2 copy.15
  112.1 0.1 fusion.3
  112.2 1.3 %pad_maximum_fusion.1 = bf16[192,4096]{1,0:T(8,128)(2,1)} fusion(bf16[192,2048]{1,0:T(8,128)(2,1)S(1)} %get-tuple-element.48, bf16[192,2048]{1,0:T(8,128)(2,1)S(1)} %get-tuple-element.47), kind=kLoop, calls=%fused_computation.3 | loop fusion | flops 3145728 | bytes 3145728 | tf_op jit(solution)/shard_map/concatenate | solution.py:152
  113.5 0.8 pad_maximum_fusion.5
  114.3 0.8 pad_maximum_fusion.4
  (34 shorter events, 0.9 us)
Async XLA Ops:
  0.6 2.9 %copy-start.2 = (bf16[192,4096]{1,0:T(8,128)(2,1)S(1)}, bf16[192,4096]{1,0:T(8,128)(2,1)}, u32[]{:S(2)}) copy-start(bf16[192,4096]{1,0:T(8,128)(2,1)} %param.12) | copy-start | bytes 4718596
  0.6 2.7 %copy-start.4 = (bf16[192,4096]{1,0:T(8,128)(2,1)S(1)}, bf16[192,4096]{1,0:T(8,128)(2,1)}, u32[]{:S(2)}) copy-start(bf16[192,4096]{1,0:T(8,128)(2,1)} %param.15) | copy-start | bytes 4718596
  0.7 2.8 %copy-start.5 = (bf16[192,1024]{1,0:T(8,128)(2,1)S(1)}, bf16[192,1024]{1,0:T(8,128)(2,1)}, u32[]{:S(2)}) copy-start(bf16[192,1024]{1,0:T(8,128)(2,1)} %param.13) | copy-start | bytes 1179652
  0.7 2.8 %copy-start.6 = (bf16[192,1024]{1,0:T(8,128)(2,1)S(1)}, bf16[192,1024]{1,0:T(8,128)(2,1)}, u32[]{:S(2)}) copy-start(bf16[192,1024]{1,0:T(8,128)(2,1)} %param.14) | copy-start | bytes 1179652
  2.0 1.8 %copy-start.3 = (bf16[192,4096]{1,0:T(8,128)(2,1)S(1)}, bf16[192,4096]{1,0:T(8,128)(2,1)}, u32[]{:S(2)}) copy-start(bf16[192,4096]{1,0:T(8,128)(2,1)} %param.16) | copy-start | bytes 4718596
  4.4 16.8 %copy-start.7 = (s32[24]{0:T(128)S(1)}, s32[24]{0:T(128)}, u32[]{:S(2)}) copy-start(s32[24]{0:T(128)} %param.17) | copy-start | bytes 292
  12.5 5.0 %copy-start = (bf16[192,2,7168]{2,0,1:T(8,128)(2,1)}, bf16[192,2,7168]{2,0,1:T(8,128)(2,1)S(1)}, u32[]{:S(2)}) copy-start(bf16[192,2,7168]{2,0,1:T(8,128)(2,1)S(1)} %all_to_all.38) | copy-start | bytes 16515076
  12.6 16.4 %collective-permute-start = (bf16[256,1024]{1,0:T(8,128)(2,1)S(1)}, bf16[256,1024]{1,0:T(8,128)(2,1)S(1)}, u32[]{:S(2)}, u32[]{:S(2)}) collective-permute-start(bf16[256,1024]{1,0:T(8,128)(2,1)S(1)} %slice.151), channel_id=1, source_target_pairs={{0,4},{2,6},{4,8},{6,10},{8,12},{10,14},{1,5},{3,7},{5,9},{7,11},{... | collective-permute-start | bytes 1572872 | tf_op jit(solution)/shard_map/ppermute | solution.py:19
  17.7 20.2 %collective-permute-start.1 = (bf16[384,1024]{1,0:T(8,128)(2,1)S(1)}, bf16[384,1024]{1,0:T(8,128)(2,1)S(1)}, u32[]{:S(2)}, u32[]{:S(2)}) collective-permute-start(bf16[384,1024]{1,0:T(8,128)(2,1)S(1)} %slice.153), channel_id=1, source_target_pairs={{0,2},{2,4},{4,6},{6,8},{8,10},{10,12},{12,14},{1,3},{3,5},{5,7},{... | collective-permute-start | bytes 2359304 | tf_op jit(solution)/shard_map/ppermute | solution.py:19
  61.9 1.6 %copy-start.1 = (f32[1024,512]{1,0:T(8,128)S(1)}, f32[1024,512]{1,0:T(8,128)}, u32[]{:S(2)}) copy-start(f32[1024,512]{1,0:T(8,128)} %get-tuple-element.40) | copy-start | bytes 6291460
  64.1 28.4 %collective-permute-start.2 = (bf16[384,1024]{1,0:T(8,128)(2,1)S(1)}, bf16[384,1024]{1,0:T(8,128)(2,1)S(1)}, u32[]{:S(2)}, u32[]{:S(2)}) collective-permute-start(bf16[384,1024]{1,0:T(8,128)(2,1)S(1)} %slice.160), channel_id=1, source_target_pairs={{2,0},{4,2},{6,4},{8,6},{10,8},{12,10},{14,12},{3,1},{5,3},{7,5},{... | collective-permute-start | bytes 2359304 | tf_op jit(solution)/shard_map/ppermute | solution.py:19
  65.4 40.2 %collective-permute-start.3 = (bf16[256,1024]{1,0:T(8,128)(2,1)S(1)}, bf16[256,1024]{1,0:T(8,128)(2,1)S(1)}, u32[]{:S(2)}, u32[]{:S(2)}) collective-permute-start(bf16[256,1024]{1,0:T(8,128)(2,1)S(1)} %slice.162), channel_id=1, source_target_pairs={{4,0},{6,2},{8,4},{10,6},{12,8},{14,10},{5,1},{7,3},{9,5},{11,7},{... | collective-permute-start | bytes 1572872 | tf_op jit(solution)/shard_map/ppermute | solution.py:19

commit v5 on v4

--- a/solution.py
+++ b/solution.py
@@ -11,6 +11,7 @@
 BLK = 128
 REACH = 2
 DOC_MOST = 6
+CHUNKS = 2
 
 
 def shifted(block, axis, distance):
@@ -64,18 +65,20 @@
             preferred_element_type=jnp.float32)
 
 
-def local_backward(qdoc, kdoc, fused, q_cols, keys, values):
+def local_backward(qdoc, kdoc, fused, q_cols, all_kv, head0, keys, values):
     rows = fused.shape[0]
     key_rows, kv_cols = keys.shape
     kv_heads = kv_cols // HEAD_SIZE
-    query_group = q_cols // HEAD_SIZE // kv_heads
+    query_group = q_cols // HEAD_SIZE // all_kv
     group_cols = query_group * HEAD_SIZE
     kernel = functools.partial(
         attention_kernel, query_group=query_group, query_blocks=rows // BLK,
         key_offset=key_rows - rows)
 
     def section(n):
-        return pl.BlockSpec((rows, group_cols), lambda g: (0, n * kv_heads + g))
+        return pl.BlockSpec((rows, group_cols), lambda g: (0, n * all_kv + head0 + g))
+
+    out_spec = pl.BlockSpec((rows, group_cols), lambda g: (0, g))
 
     k_spec = pl.BlockSpec((key_rows, HEAD_SIZE), lambda g: (0, g))
     return pl.pallas_call(
@@ -86,9 +89,9 @@
             pl.BlockSpec((1, key_rows), lambda g: (0, 0)),
             section(0), section(1), section(2), k_spec, k_spec,
         ],
-        out_specs=[section(0), k_spec, k_spec],
+        out_specs=[out_spec, k_spec, k_spec],
         out_shape=[
-            jax.ShapeDtypeStruct((rows, q_cols), jnp.bfloat16),
+            jax.ShapeDtypeStruct((rows, kv_heads * group_cols), jnp.bfloat16),
             jax.ShapeDtypeStruct((key_rows, kv_cols), jnp.float32),
             jax.ShapeDtypeStruct((key_rows, kv_cols), jnp.float32),
         ],
@@ -119,32 +122,43 @@
         docs = lax.dynamic_slice_in_dim(block_docs, jnp.maximum(owner, 0) * blocks_here, blocks_here, 0)
         return jnp.where(owner >= 0, docs, -1)
 
-    pair = fused[:, 3 * q_cols:]
-    behind = []
-    for distance in range(REACH, 0, -1):
-        first = max(skip - (REACH - distance) * window_extent, 0)
-        if first < window_extent:
-            behind.append(shifted(pair[first:], "ctx", distance))
-    keys = jnp.concatenate([b[:, :kv_cols] for b in behind] + [key_part], axis=0)
-    values = jnp.concatenate([b[:, kv_cols:] for b in behind] + [value_part], axis=0)
     key_docs = jnp.concatenate([docs_of(place - distance) for distance in range(REACH, -1, -1)])
     kdoc = jnp.repeat(key_docs, BLK)[skip:][None, :]
     qdoc = jnp.repeat(docs_of(place), BLK)[:, None]
+    all_kv = kv_cols // HEAD_SIZE
+    per = kv_cols // CHUNKS
+    q_parts, k_parts, v_parts = [], [], []
+    for j in range(CHUNKS):
+        with jax.named_scope(f"chunk{j}"):
+            key_here = key_part[:, j * per:(j + 1) * per]
+            value_here = value_part[:, j * per:(j + 1) * per]
+            pair = jnp.concatenate([key_here, value_here], axis=1)
+            behind = []
+            for distance in range(REACH, 0, -1):
+                first = max(skip - (REACH - distance) * window_extent, 0)
+                if first < window_extent:
+                    behind.append(shifted(pair[first:], "ctx", distance))
+            keys = jnp.concatenate([b[:, :per] for b in behind] + [key_here], axis=0)
+            values = jnp.concatenate([b[:, per:] for b in behind] + [value_here], axis=0)
 
-    query_sum, key_partial, value_partial = local_backward(
-        qdoc, kdoc, fused, q_cols, keys, values)
+            query_sum, key_partial, value_partial = local_backward(
+                qdoc, kdoc, fused, q_cols, all_kv, j * per // HEAD_SIZE, keys, values)
 
-    both = jnp.concatenate([key_partial, value_partial], axis=1)
-    total = both[own - skip:]
-    for distance in range(1, REACH + 1):
-        begin = (REACH - distance) * window_extent
-        start = max(begin, skip)
-        if start >= begin + window_extent:
-            continue
-        sent = shifted(
-            both[start - skip:begin + window_extent - skip].astype(jnp.bfloat16), "ctx", -distance)
-        total = total.at[start - begin:].add(sent.astype(jnp.float32))
-    finished = jnp.concatenate([query_sum, total.astype(jnp.bfloat16)], axis=1)
+            both = jnp.concatenate([key_partial, value_partial], axis=1)
+            total = both[own - skip:]
+            for distance in range(1, REACH + 1):
+                begin = (REACH - distance) * window_extent
+                start = max(begin, skip)
+                if start >= begin + window_extent:
+                    continue
+                sent = shifted(
+                    both[start - skip:begin + window_extent - skip].astype(jnp.bfloat16),
+                    "ctx", -distance)
+                total = total.at[start - begin:].add(sent.astype(jnp.float32))
+            q_parts.append(query_sum)
+            k_parts.append(total[:, :per].astype(jnp.bfloat16))
+            v_parts.append(total[:, per:].astype(jnp.bfloat16))
+    finished = jnp.concatenate(q_parts + k_parts + v_parts, axis=1)
     returned = lax.all_to_all(finished, "head", split_axis=0, concat_axis=1, tiled=True)
     width = finished.shape[1]
 

time: 115 us -> 103 us (0.90)
  waiting for transfers between devices: 53.7 us -> 28.9 us
  starting transfers between devices: 11 us -> 20.7 us
  local copies, waits for them, and re-layouts: 7.6 us -> 8.83 us
    ppermute x4 -> x8, waiting for transfers between devices: 53.7 us -> 28.9 us  [shifted(): return lax.ppermute(block, axis, route)]
    ppermute x4 -> x8, starting transfers between devices: 11 us -> 20.7 us  [shifted(): return lax.ppermute(block, axis, route)]
    unnamed x29 -> x33, local copies, waits for them, and re-layouts: 4.99 us -> 7.32 us
    slice x5, local copies, waits for them, and re-layouts: 1.35 us -> 0.14 us  [the longest x4 0.09 us: per_device(): b[:, per:]]
    pallas_call x1 -> x2, Pallas kernels: 23.7 us -> 24 us  [local_backward(): pl.pallas_call(kernel, grid=(kv_heads,), in_specs=[pl.BlockSpec((rows, 1)...]
  transfers between devices with their start and end apart: 4 -> 8, of which waited for: 4 -> 5; matrix products, arithmetic and copies ran while one was open for 2% -> 3% of each run, Pallas kernels for 0% -> 23%
where the time goes in v5:
time: 103 us; the launch traced here: 102 us
  waiting for transfers between devices  28.9 us (28%)
  Pallas kernels  24 us (23%)
  starting transfers between devices  20.7 us (20%)
  blocking collectives  13.8 us (13%)
  local copies, waits for them, and re-layouts  8.83 us (9%)
  other arithmetic  4.8 us (5%)
  between operations  1.18 us (1%)
    ppermute x8, waiting for transfers between devices, shifted(): return lax.ppermute(block, axis, route)  28.9 us
    pallas_call x2, Pallas kernels, local_backward(): pl.pallas_call(kernel, grid=(kv_heads,), in_specs=[pl.BlockSpec((rows, 1)...  24 us
    ppermute x8, starting transfers between devices, shifted(): return lax.ppermute(block, axis, route)  20.7 us
    all_to_all x1, blocking collectives, per_device(): lax.all_to_all(outgoing, 'head', split_axis=1, concat_axis=0, tiled=True)  8.16 us
    unnamed x33, local copies, waits for them, and re-layouts  7.32 us
    all_to_all x1, blocking collectives, per_device(): lax.all_to_all(finished, 'head', split_axis=0, concat_axis=1, tiled=True)  5.63 us
    concatenate x3, other arithmetic, gather(): jnp.concatenate([returned[:, p * width + begin:p * width + begin + size]...  2.84 us
  transfers between devices with their start and end apart: 8, of which 5 were waited for; matrix products, arithmetic and copies ran while one was open for 3% of the time, Pallas kernels for 23%

profile of v5, /device:TPU:0, one launch (start us, length us, event | category | flops | bytes accessed | tf_op | source)
XLA Modules:
  0.0 102.1 jit_solution(12254891284906804895)
XLA Ops:
  0.7 1.4 %slice_dynamic-update-slice_fusion.5 = bf16[192,14336]{1,0:T(8,128)(2,1)S(1)} fusion(bf16[192,4096]{1,0:T(8,128)(2,1)} %param.18), kind=kLoop, calls=%fused_computation.9 | loop fusion | bytes 1572864
  2.0 1.3 %slice_dynamic-update-slice_fusion.4 = bf16[192,14336]{1,0:T(8,128)(2,1)S(1)} fusion(bf16[192,14336]{1,0:T(8,128)(2,1)S(1)} %slice_dynamic-update-slice_fusion.5, bf16[192,4096]{1,0:T(8,128)(2,1)} %param.22), kind=kLoop, calls=%fused_computation.8 | loop fusion | bytes 1572864
  3.5 0.3 copy-done.1
  3.8 1.0 %copy-done.2 = bf16[192,4096]{1,0:T(8,128)(2,1)S(1)} copy-done((bf16[192,4096]{1,0:T(8,128)(2,1)S(1)}, bf16[192,4096]{1,0:T(8,128)(2,1)}, u32[]{:S(2)}) %copy-start.2) | copy-done | bytes 1572888
  5.0 0.4 copy.21
  5.5 8.2 %all_to_all.38 = bf16[192,2,7168]{2,0,1:T(8,128)(2,1)S(1)} all-to-all(bf16[192,2,7168]{2,0,1:T(8,128)(2,1)S(1)} %bitcast.30), channel_id=1, replica_groups=mesh['groups'=2,'ctx'=8,'head'=2] {'head'}, dimensions={1} | all-to-all | bytes 11010048 | tf_op jit(solution)/shard_map/all_to_all | solution.py:112
  13.6 2.4 %copy-done = bf16[192,2,7168]{2,0,1:T(8,128)(2,1)} copy-done((bf16[192,2,7168]{2,0,1:T(8,128)(2,1)}, bf16[192,2,7168]{2,0,1:T(8,128)(2,1)S(1)}, u32[]{:S(2)}) %copy-start) | copy-done | bytes 5505048
  16.1 5.0 %collective-permute-start.2 = (bf16[256,512]{1,0:T(8,128)(2,1)S(1)}, bf16[256,512]{1,0:T(8,128)(2,1)S(1)}, u32[]{:S(2)}, u32[]{:S(2)}) collective-permute-start(bf16[256,512]{1,0:T(8,128)(2,1)S(1)} %fusion.2), channel_id=1, source_target_pairs={{0,4},{2,6},{4,8},{6,10},{8,12},{10,14},{1,5},{3,7},{5,9},{7,11},{... | collective-permute-start | bytes 786440 | tf_op jit(solution)/shard_map/chunk1/ppermute | solution.py:20
  21.1 3.4 %collective-permute-start.3 = (bf16[384,512]{1,0:T(8,128)(2,1)S(1)}, bf16[384,512]{1,0:T(8,128)(2,1)S(1)}, u32[]{:S(2)}, u32[]{:S(2)}) collective-permute-start(bf16[384,512]{1,0:T(8,128)(2,1)S(1)} %pad_maximum_fusion.6), channel_id=1, source_target_pairs={{0,2},{2,4},{4,6},{6,8},{8,10},{10,12},{12,14},{1,3},{3,5},{5,7},{... | collective-permute-start | bytes 1179656 | tf_op jit(solution)/shard_map/chunk1/ppermute | solution.py:20
  24.6 0.7 fusion.3
  25.3 3.5 %collective-permute-start = (bf16[256,512]{1,0:T(8,128)(2,1)}, bf16[256,512]{1,0:T(8,128)(2,1)S(1)}, u32[]{:S(2)}, u32[]{:S(2)}) collective-permute-start(bf16[256,512]{1,0:T(8,128)(2,1)} %fusion.3), channel_id=1, source_target_pairs={{0,4},{2,6},{4,8},{6,10},{8,12},{10,14},{1,5},{3,7},{5,9},{7,11},{... | collective-permute-start | bytes 786440 | tf_op jit(solution)/shard_map/chunk0/ppermute | solution.py:20
  28.8 3.4 %collective-permute-start.1 = (bf16[384,512]{1,0:T(8,128)(2,1)S(1)}, bf16[384,512]{1,0:T(8,128)(2,1)S(1)}, u32[]{:S(2)}, u32[]{:S(2)}) collective-permute-start(bf16[384,512]{1,0:T(8,128)(2,1)S(1)} %pad_maximum_fusion.5), channel_id=1, source_target_pairs={{0,2},{2,4},{4,6},{6,8},{8,10},{10,12},{12,14},{1,3},{3,5},{5,7},{... | collective-permute-start | bytes 1179656 | tf_op jit(solution)/shard_map/chunk0/ppermute | solution.py:20
  32.8 1.6 %collective-permute-done = bf16[256,512]{1,0:T(8,128)(2,1)S(1)} collective-permute-done((bf16[256,512]{1,0:T(8,128)(2,1)}, bf16[256,512]{1,0:T(8,128)(2,1)S(1)}, u32[]{:S(2)}, u32[]{:S(2)}) %collective-permute-start) | collective-permute-done | bytes 262176 | tf_op jit(solution)/shard_map/chunk0/ppermute | solution.py:20
  34.6 12.0 %chunk1.1 = (bf16[384,1024]{1,0:T(8,128)(2,1)S(1)}, f32[1024,256]{1,0:T(8,128)S(1)}, f32[1024,256]{1,0:T(8,128)S(1)}) custom-call(s32[384,1]{1,0:T(8,128)S(1)} %bitcast.19, s32[1,1024]{1,0:T(1,128)S(1)} %bitcast.21, bf16[384,7168]{1,0:T(8,128)(2,1)} %bitcast.24, bf16[384,7168]{1,0:T(8,128)(2,1)} %bitcast.25, bf16[384,7168]{1,0:T(8,128)(2,1)} %bitcast.26, ...), custom_call_target="tpu_custom_call" | custom-call | tf_op jit(solution)/shard_map/chunk1/pallas_call | solution.py:84
  46.5 0.1 constant_dynamic-update-slice_fusion.3
  46.7 0.2 constant_dynamic-update-slice_fusion.2
  47.1 1.5 %collective-permute-start.6 = (bf16[384,512]{1,0:T(8,128)(2,1)S(1)}, bf16[384,512]{1,0:T(8,128)(2,1)S(1)}, u32[]{:S(2)}, u32[]{:S(2)}) collective-permute-start(bf16[384,512]{1,0:T(8,128)(2,1)S(1)} %slice.270), channel_id=1, source_target_pairs={{2,0},{4,2},{6,4},{8,6},{10,8},{12,10},{14,12},{3,1},{5,3},{7,5},{... | collective-permute-start | bytes 1179656 | tf_op jit(solution)/shard_map/chunk1/ppermute | solution.py:20
  48.7 12.0 %chunk0.1 = (bf16[384,1024]{1,0:T(8,128)(2,1)S(1)}, f32[1024,256]{1,0:T(8,128)S(1)}, f32[1024,256]{1,0:T(8,128)S(1)}) custom-call(s32[384,1]{1,0:T(8,128)S(1)} %bitcast.20, s32[1,1024]{1,0:T(1,128)S(1)} %bitcast.22, bf16[384,7168]{1,0:T(8,128)(2,1)} %bitcast.27, bf16[384,7168]{1,0:T(8,128)(2,1)} %bitcast.28, bf16[384,7168]{1,0:T(8,128)(2,1)} %bitcast.29, ...), custom_call_target="tpu_custom_call" | custom-call | tf_op jit(solution)/shard_map/chunk0/pallas_call | solution.py:84
  60.7 0.1 constant_dynamic-update-slice_fusion.1
  60.8 0.2 constant_dynamic-update-slice_fusion
  61.2 1.3 %collective-permute-start.7 = (bf16[256,512]{1,0:T(8,128)(2,1)S(1)}, bf16[256,512]{1,0:T(8,128)(2,1)S(1)}, u32[]{:S(2)}, u32[]{:S(2)}) collective-permute-start(bf16[256,512]{1,0:T(8,128)(2,1)S(1)} %slice.272), channel_id=1, source_target_pairs={{4,0},{6,2},{8,4},{10,6},{12,8},{14,10},{5,1},{7,3},{9,5},{11,7},{... | collective-permute-start | bytes 786440 | tf_op jit(solution)/shard_map/chunk1/ppermute | solution.py:20
  62.5 1.3 %collective-permute-start.4 = (bf16[384,512]{1,0:T(8,128)(2,1)S(1)}, bf16[384,512]{1,0:T(8,128)(2,1)S(1)}, u32[]{:S(2)}, u32[]{:S(2)}) collective-permute-start(bf16[384,512]{1,0:T(8,128)(2,1)S(1)} %slice.265), channel_id=1, source_target_pairs={{2,0},{4,2},{6,4},{8,6},{10,8},{12,10},{14,12},{3,1},{5,3},{7,5},{... | collective-permute-start | bytes 1179656 | tf_op jit(solution)/shard_map/chunk0/ppermute | solution.py:20
  63.8 1.3 %collective-permute-start.5 = (bf16[256,512]{1,0:T(8,128)(2,1)S(1)}, bf16[256,512]{1,0:T(8,128)(2,1)S(1)}, u32[]{:S(2)}, u32[]{:S(2)}) collective-permute-start(bf16[256,512]{1,0:T(8,128)(2,1)S(1)} %slice.267), channel_id=1, source_target_pairs={{4,0},{6,2},{8,4},{10,6},{12,8},{14,10},{5,1},{7,3},{9,5},{11,7},{... | collective-permute-start | bytes 786440 | tf_op jit(solution)/shard_map/chunk0/ppermute | solution.py:20
  65.2 0.5 collective-permute-done.6
  65.9 15.5 %collective-permute-done.7 = bf16[256,512]{1,0:T(8,128)(2,1)S(1)} collective-permute-done((bf16[256,512]{1,0:T(8,128)(2,1)S(1)}, bf16[256,512]{1,0:T(8,128)(2,1)S(1)}, u32[]{:S(2)}, u32[]{:S(2)}) %collective-permute-start.7) | collective-permute-done | bytes 262176 | tf_op jit(solution)/shard_map/chunk1/ppermute | solution.py:20
  81.6 0.2 collective-permute-done.4
  82.0 11.0 %collective-permute-done.5 = bf16[256,512]{1,0:T(8,128)(2,1)S(1)} collective-permute-done((bf16[256,512]{1,0:T(8,128)(2,1)S(1)}, bf16[256,512]{1,0:T(8,128)(2,1)S(1)}, u32[]{:S(2)}, u32[]{:S(2)}) %collective-permute-start.5) | collective-permute-done | bytes 262176 | tf_op jit(solution)/shard_map/chunk0/ppermute | solution.py:20
  93.2 5.6 %all_to_all.39 = bf16[2,192,3072]{2,1,0:T(8,128)(2,1)S(1)} all-to-all(bf16[2,192,3072]{2,1,0:T(8,128)(2,1)S(1)} %bitcast.35), channel_id=1, replica_groups=mesh['groups'=2,'ctx'=8,'head'=2] {'head'}, dimensions={0} | all-to-all | bytes 4718592 | tf_op jit(solution)/shard_map/all_to_all | solution.py:162
  98.9 0.2 copy.16
  99.3 0.8 pad_maximum_fusion.8
  100.1 0.8 pad_maximum_fusion.7
  100.9 1.3 %pad_maximum_fusion = bf16[192,4096]{1,0:T(8,128)(2,1)} fusion(bf16[192,2048]{1,0:T(8,128)(2,1)S(1)} %get-tuple-element.88, bf16[192,2048]{1,0:T(8,128)(2,1)S(1)} %get-tuple-element.87), kind=kLoop, calls=%fused_computation.1 | loop fusion | flops 3145728 | bytes 3145728 | tf_op jit(solution)/shard_map/concatenate | solution.py:166
  (59 shorter events, 2.5 us)
Async XLA Ops:
  0.6 2.7 %copy-start.3 = (bf16[192,4096]{1,0:T(8,128)(2,1)S(1)}, bf16[192,4096]{1,0:T(8,128)(2,1)}, u32[]{:S(2)}) copy-start(bf16[192,4096]{1,0:T(8,128)(2,1)} %param.21) | copy-start | bytes 4718596
  0.6 2.8 %copy-start.4 = (bf16[192,1024]{1,0:T(8,128)(2,1)S(1)}, bf16[192,1024]{1,0:T(8,128)(2,1)}, u32[]{:S(2)}) copy-start(bf16[192,1024]{1,0:T(8,128)(2,1)} %param.19) | copy-start | bytes 1179652
  0.7 2.8 %copy-start.5 = (bf16[192,1024]{1,0:T(8,128)(2,1)S(1)}, bf16[192,1024]{1,0:T(8,128)(2,1)}, u32[]{:S(2)}) copy-start(bf16[192,1024]{1,0:T(8,128)(2,1)} %param.20) | copy-start | bytes 1179652
  2.0 1.8 %copy-start.1 = (bf16[192,4096]{1,0:T(8,128)(2,1)S(1)}, bf16[192,4096]{1,0:T(8,128)(2,1)}, u32[]{:S(2)}) copy-start(bf16[192,4096]{1,0:T(8,128)(2,1)} %param.18) | copy-start | bytes 4718596
  3.4 1.5 %copy-start.2 = (bf16[192,4096]{1,0:T(8,128)(2,1)S(1)}, bf16[192,4096]{1,0:T(8,128)(2,1)}, u32[]{:S(2)}) copy-start(bf16[192,4096]{1,0:T(8,128)(2,1)} %param.22) | copy-start | bytes 4718596
  13.6 2.4 %copy-start = (bf16[192,2,7168]{2,0,1:T(8,128)(2,1)}, bf16[192,2,7168]{2,0,1:T(8,128)(2,1)S(1)}, u32[]{:S(2)}) copy-start(bf16[192,2,7168]{2,0,1:T(8,128)(2,1)S(1)} %all_to_all.38) | copy-start | bytes 16515076
  13.6 18.6 %copy-start.6 = (s32[24]{0:T(128)S(1)}, s32[24]{0:T(128)}, u32[]{:S(2)}) copy-start(s32[24]{0:T(128)} %param.23) | copy-start | bytes 292
  16.1 16.6 %collective-permute-start.2 = (bf16[256,512]{1,0:T(8,128)(2,1)S(1)}, bf16[256,512]{1,0:T(8,128)(2,1)S(1)}, u32[]{:S(2)}, u32[]{:S(2)}) collective-permute-start(bf16[256,512]{1,0:T(8,128)(2,1)S(1)} %fusion.2), channel_id=1, source_target_pairs={{0,4},{2,6},{4,8},{6,10},{8,12},{10,14},{1,5},{3,7},{5,9},{7,11},{... | collective-permute-start | bytes 786440 | tf_op jit(solution)/shard_map/chunk1/ppermute | solution.py:20
  21.1 13.2 %collective-permute-start.3 = (bf16[384,512]{1,0:T(8,128)(2,1)S(1)}, bf16[384,512]{1,0:T(8,128)(2,1)S(1)}, u32[]{:S(2)}, u32[]{:S(2)}) collective-permute-start(bf16[384,512]{1,0:T(8,128)(2,1)S(1)} %pad_maximum_fusion.6), channel_id=1, source_target_pairs={{0,2},{2,4},{4,6},{6,8},{8,10},{10,12},{12,14},{1,3},{3,5},{5,7},{... | collective-permute-start | bytes 1179656 | tf_op jit(solution)/shard_map/chunk1/ppermute | solution.py:20
  25.3 9.0 %collective-permute-start = (bf16[256,512]{1,0:T(8,128)(2,1)}, bf16[256,512]{1,0:T(8,128)(2,1)S(1)}, u32[]{:S(2)}, u32[]{:S(2)}) collective-permute-start(bf16[256,512]{1,0:T(8,128)(2,1)} %fusion.3), channel_id=1, source_target_pairs={{0,4},{2,6},{4,8},{6,10},{8,12},{10,14},{1,5},{3,7},{5,9},{7,11},{... | collective-permute-start | bytes 786440 | tf_op jit(solution)/shard_map/chunk0/ppermute | solution.py:20
  28.8 19.8 %collective-permute-start.1 = (bf16[384,512]{1,0:T(8,128)(2,1)S(1)}, bf16[384,512]{1,0:T(8,128)(2,1)S(1)}, u32[]{:S(2)}, u32[]{:S(2)}) collective-permute-start(bf16[384,512]{1,0:T(8,128)(2,1)S(1)} %pad_maximum_fusion.5), channel_id=1, source_target_pairs={{0,2},{2,4},{4,6},{6,8},{8,10},{10,12},{12,14},{1,3},{3,5},{5,7},{... | collective-permute-start | bytes 1179656 | tf_op jit(solution)/shard_map/chunk0/ppermute | solution.py:20
  47.1 18.7 %collective-permute-start.6 = (bf16[384,512]{1,0:T(8,128)(2,1)S(1)}, bf16[384,512]{1,0:T(8,128)(2,1)S(1)}, u32[]{:S(2)}, u32[]{:S(2)}) collective-permute-start(bf16[384,512]{1,0:T(8,128)(2,1)S(1)} %slice.270), channel_id=1, source_target_pairs={{2,0},{4,2},{6,4},{8,6},{10,8},{12,10},{14,12},{3,1},{5,3},{7,5},{... | collective-permute-start | bytes 1179656 | tf_op jit(solution)/shard_map/chunk1/ppermute | solution.py:20
  61.2 20.2 %collective-permute-start.7 = (bf16[256,512]{1,0:T(8,128)(2,1)S(1)}, bf16[256,512]{1,0:T(8,128)(2,1)S(1)}, u32[]{:S(2)}, u32[]{:S(2)}) collective-permute-start(bf16[256,512]{1,0:T(8,128)(2,1)S(1)} %slice.272), channel_id=1, source_target_pairs={{4,0},{6,2},{8,4},{10,6},{12,8},{14,10},{5,1},{7,3},{9,5},{11,7},{... | collective-permute-start | bytes 786440 | tf_op jit(solution)/shard_map/chunk1/ppermute | solution.py:20
  62.5 19.3 %collective-permute-start.4 = (bf16[384,512]{1,0:T(8,128)(2,1)S(1)}, bf16[384,512]{1,0:T(8,128)(2,1)S(1)}, u32[]{:S(2)}, u32[]{:S(2)}) collective-permute-start(bf16[384,512]{1,0:T(8,128)(2,1)S(1)} %slice.265), channel_id=1, source_target_pairs={{2,0},{4,2},{6,4},{8,6},{10,8},{12,10},{14,12},{3,1},{5,3},{7,5},{... | collective-permute-start | bytes 1179656 | tf_op jit(solution)/shard_map/chunk0/ppermute | solution.py:20
  63.8 29.1 %collective-permute-start.5 = (bf16[256,512]{1,0:T(8,128)(2,1)S(1)}, bf16[256,512]{1,0:T(8,128)(2,1)S(1)}, u32[]{:S(2)}, u32[]{:S(2)}) collective-permute-start(bf16[256,512]{1,0:T(8,128)(2,1)S(1)} %slice.267), channel_id=1, source_target_pairs={{4,0},{6,2},{8,4},{10,6},{12,8},{14,10},{5,1},{7,3},{9,5},{11,7},{... | collective-permute-start | bytes 786440 | tf_op jit(solution)/shard_map/chunk0/ppermute | solution.py:20

commit v6 on v5

v6 whole, which is shorter than its diff:
```python
import functools

import jax
import jax.numpy as jnp
from jax import lax
from jax.experimental import pallas as pl
from jax.experimental.pallas import tpu as pltpu
from jax.sharding import PartitionSpec as P

HEAD_SIZE = 128
BLK = 128
REACH = 2
DOC_MOST = 6
CHUNKS = 2


def shifted(block, axis, distance):
    devices = range(lax.axis_size(axis))
    route = [(i - distance, i) for i in devices if i - distance in devices]
    return lax.ppermute(block, axis, route)


def attention_kernel(bdoc_ref, qdoc_ref, kdoc_ref, q_ref, do_ref, o_ref, k_ref, v_ref,
                     dq_ref, dk_ref, dv_ref, s_scr, m_scr, l_scr, dq_scr,
                     *, query_group, query_blocks, key_offset):
    scale = HEAD_SIZE ** (-0.5)
    dk_ref[...] = jnp.zeros_like(dk_ref)
    dv_ref[...] = jnp.zeros_like(dv_ref)
    for qb in range(query_blocks):
        rows = pl.ds(qb * BLK, BLK)
        first = key_offset // BLK + qb + 1 - DOC_MOST
        qs = jnp.concatenate(
            [q_ref[rows, pl.ds(r * HEAD_SIZE, HEAD_SIZE)] for r in range(query_group)], axis=0)
        dos = jnp.concatenate(
            [do_ref[rows, pl.ds(r * HEAD_SIZE, HEAD_SIZE)] for r in range(query_group)], axis=0)
        outs = jnp.concatenate(
            [o_ref[rows, pl.ds(r * HEAD_SIZE, HEAD_SIZE)] for r in range(query_group)], axis=0)
        delta = jnp.sum(dos.astype(jnp.float32) * outs.astype(jnp.float32), axis=1, keepdims=True)
        qd = qdoc_ref[rows, :]
        query_doc = bdoc_ref[qb]

        def mask_of(kb):
            kd = kdoc_ref[:, pl.ds(kb * BLK, BLK)]
            qpos = lax.broadcasted_iota(jnp.int32, (BLK, BLK), 0) + (key_offset + qb * BLK)
            kpos = lax.broadcasted_iota(jnp.int32, (BLK, BLK), 1) + kb * BLK
            allowed = (qd == kd) & (kpos <= qpos)
            return jnp.concatenate([allowed] * query_group, axis=0)

        m_scr[...] = jnp.full(m_scr.shape, -1e30, jnp.float32)
        l_scr[...] = jnp.zeros(l_scr.shape, jnp.float32)
        dq_scr[...] = jnp.zeros(dq_scr.shape, jnp.float32)
        for b in range(DOC_MOST):
            kb = first + b

            @pl.when(bdoc_ref[query_blocks + kb] == query_doc)
            def _():
                kblk = k_ref[pl.ds(kb * BLK, BLK), :]
                scores = scale * lax.dot_general(
                    qs, kblk, (((1,), (1,)), ((), ())), preferred_element_type=jnp.float32)
                masked = jnp.where(mask_of(kb), scores, -1e30)
                s_scr[b] = masked
                m_scr[...] = jnp.maximum(m_scr[...], jnp.max(masked, axis=1, keepdims=True))

        for b in range(DOC_MOST):
            kb = first + b

            @pl.when(bdoc_ref[query_blocks + kb] == query_doc)
            def _():
                l_scr[...] += jnp.sum(
                    jnp.where(mask_of(kb), jnp.exp(s_scr[b] - m_scr[...]), 0.0),
                    axis=1, keepdims=True)

        lse = m_scr[...] + jnp.log(l_scr[...])
        for b in range(DOC_MOST):
            kb = first + b

            @pl.when(bdoc_ref[query_blocks + kb] == query_doc)
            def _():
                kblk = k_ref[pl.ds(kb * BLK, BLK), :]
                vblk = v_ref[pl.ds(kb * BLK, BLK), :]
                probs = jnp.where(mask_of(kb), jnp.exp(s_scr[b] - lse), 0.0)
                dprob = lax.dot_general(
                    dos, vblk, (((1,), (1,)), ((), ())), preferred_element_type=jnp.float32)
                dscore = (probs * (dprob - delta)).astype(jnp.bfloat16)
                dq_scr[...] += jnp.dot(dscore, kblk, preferred_element_type=jnp.float32)
                dk_ref[pl.ds(kb * BLK, BLK), :] += scale * lax.dot_general(
                    dscore, qs, (((0,), (0,)), ((), ())), preferred_element_type=jnp.float32)
                dv_ref[pl.ds(kb * BLK, BLK), :] += lax.dot_general(
                    probs.astype(jnp.bfloat16), dos, (((0,), (0,)), ((), ())),
                    preferred_element_type=jnp.float32)

        dq = scale * dq_scr[...]
        for r in range(query_group):
            dq_ref[rows, pl.ds(r * HEAD_SIZE, HEAD_SIZE)] = (
                dq[r * BLK:(r + 1) * BLK].astype(dq_ref.dtype))


def local_backward(bdoc, qdoc, kdoc, fused, q_cols, all_kv, head0, keys, values):
    rows = fused.shape[0]
    key_rows, kv_cols = keys.shape
    kv_heads = kv_cols // HEAD_SIZE
    query_group = q_cols // HEAD_SIZE // all_kv
    group_cols = query_group * HEAD_SIZE
    kernel = functools.partial(
        attention_kernel, query_group=query_group, query_blocks=rows // BLK,
        key_offset=key_rows - rows)

    def section(n):
        return pl.BlockSpec((rows, group_cols), lambda g, bd: (0, n * all_kv + head0 + g))

    out_spec = pl.BlockSpec((rows, group_cols), lambda g, bd: (0, g))

    k_spec = pl.BlockSpec((key_rows, HEAD_SIZE), lambda g, bd: (0, g))
    stacked = query_group * BLK
    grid_spec = pltpu.PrefetchScalarGridSpec(
        num_scalar_prefetch=1,
        grid=(kv_heads,),
        in_specs=[
            pl.BlockSpec((rows, 1), lambda g, bd: (0, 0)),
            pl.BlockSpec((1, key_rows), lambda g, bd: (0, 0)),
            section(0), section(1), section(2), k_spec, k_spec,
        ],
        out_specs=[out_spec, k_spec, k_spec],
        scratch_shapes=[
            pltpu.VMEM((DOC_MOST, stacked, BLK), jnp.float32),
            pltpu.VMEM((stacked, 1), jnp.float32),
            pltpu.VMEM((stacked, 1), jnp.float32),
            pltpu.VMEM((stacked, HEAD_SIZE), jnp.float32),
        ],
    )
    return pl.pallas_call(
        kernel,
        grid_spec=grid_spec,
        out_shape=[
            jax.ShapeDtypeStruct((rows, kv_heads * group_cols), jnp.bfloat16),
            jax.ShapeDtypeStruct((key_rows, kv_cols), jnp.float32),
            jax.ShapeDtypeStruct((key_rows, kv_cols), jnp.float32),
        ],
        compiler_params=pltpu.CompilerParams(
            dimension_semantics=("arbitrary",), vmem_limit_bytes=48 * 1024 * 1024),
    )(bdoc, qdoc, kdoc, fused, fused, fused, keys, values)


def per_device(query_matrix, key_matrix, value_matrix, fwd_output, output_gradient, block_docs):
    _, q_all = query_matrix.shape
    kv_all = key_matrix.shape[1]
    peers = lax.axis_size("head")
    q_cols, kv_cols = q_all // peers, kv_all // peers
    sections = (query_matrix, output_gradient, fwd_output, key_matrix, value_matrix)
    outgoing = jnp.concatenate(
        [x[:, p * (x.shape[1] // peers):(p + 1) * (x.shape[1] // peers)]
         for p in range(peers) for x in sections], axis=1)
    fused = lax.all_to_all(outgoing, "head", split_axis=1, concat_axis=0, tiled=True)
    window_extent = fused.shape[0]
    key_part = fused[:, 3 * q_cols:3 * q_cols + kv_cols]
    value_part = fused[:, 3 * q_cols + kv_cols:]
    place = lax.axis_index("ctx")
    blocks_here = window_extent // BLK
    own = REACH * window_extent
    skip = own + BLK - DOC_MOST * BLK

    def docs_of(owner):
        docs = lax.dynamic_slice_in_dim(block_docs, jnp.maximum(owner, 0) * blocks_here, blocks_here, 0)
        return jnp.where(owner >= 0, docs, -1)

    key_docs = jnp.concatenate([docs_of(place - distance) for distance in range(REACH, -1, -1)])
    kdoc = jnp.repeat(key_docs, BLK)[skip:][None, :]
    qdoc = jnp.repeat(docs_of(place), BLK)[:, None]
    bdoc = jnp.concatenate([docs_of(place), key_docs[skip // BLK:]])
    all_kv = kv_cols // HEAD_SIZE
    per = kv_cols // CHUNKS
    q_parts, k_parts, v_parts = [], [], []
    for j in range(CHUNKS):
        key_here = key_part[:, j * per:(j + 1) * per]
        value_here = value_part[:, j * per:(j + 1) * per]
        pair = jnp.concatenate([key_here, value_here], axis=1)
        behind = []
        for distance in range(REACH, 0, -1):
            first = max(skip - (REACH - distance) * window_extent, 0)
            if first < window_extent:
                behind.append(shifted(pair[first:], "ctx", distance))
        keys = jnp.concatenate([b[:, :per] for b in behind] + [key_here], axis=0)
        values = jnp.concatenate([b[:, per:] for b in behind] + [value_here], axis=0)

        query_sum, key_partial, value_partial = local_backward(
            bdoc, qdoc, kdoc, fused, q_cols, all_kv, j * per // HEAD_SIZE, keys, values)

        both = jnp.concatenate([key_partial, value_partial], axis=1)
        total = both[own - skip:]
        for distance in range(1, REACH + 1):
            begin = (REACH - distance) * window_extent
            start = max(begin, skip)
            if start >= begin + window_extent:
                continue
            sent = shifted(
                both[start - skip:begin + window_extent - skip].astype(jnp.bfloat16),
                "ctx", -distance)
            total = total.at[start - begin:].add(sent.astype(jnp.float32))
        q_parts.append(query_sum)
        k_parts.append(total[:, :per].astype(jnp.bfloat16))
        v_parts.append(total[:, per:].astype(jnp.bfloat16))
    finished = jnp.concatenate(q_parts + k_parts + v_parts, axis=1)
    returned = lax.all_to_all(finished, "head", split_axis=0, concat_axis=1, tiled=True)
    width = finished.shape[1]

    def gather(begin, size):
        return jnp.concatenate(
            [returned[:, p * width + begin:p * width + begin + size] for p in range(peers)], axis=1)

    return gather(0, q_cols), gather(q_cols, kv_cols), gather(q_cols + kv_cols, kv_cols)


def solution(mesh):
    return jax.shard_map(
        per_device,
        mesh=mesh,
        in_specs=(
            P(("groups", "ctx", "head"), None),
            P(("groups", "ctx", "head"), None),
            P(("groups", "ctx", "head"), None),
            P(("groups", "ctx", "head"), None),
            P(("groups", "ctx", "head"), None),
            P("groups"),
        ),
        out_specs=(
            P(("groups", "ctx", "head"), None),
            P(("groups", "ctx", "head"), None),
            P(("groups", "ctx", "head"), None),
        ),
        check_vma=False,
    )
```

time: 103 us -> 141 us (1.37)
  the two profiles are of different devices: /device:TPU:0 before, /device:TPU:19 now
where the time goes in v6:
time: 141 us
  waiting for transfers between devices  53.5 us (38%)
  Pallas kernels  32 us (23%)
  starting transfers between devices  23.7 us (17%)
  blocking collectives  16.6 us (12%)
  local copies, waits for them, and re-layouts  8.77 us (6%)
  other arithmetic  4.87 us (3%)
    ppermute x8, waiting for transfers between devices, shifted(): return lax.ppermute(block, axis, route)  53.5 us
    pallas_call x2, Pallas kernels, local_backward(): pl.pallas_call(kernel, grid_spec=grid_spec, out_shape=[jax.ShapeDtypeStru...  32 us
    ppermute x8, starting transfers between devices, shifted(): return lax.ppermute(block, axis, route)  23.7 us
    all_to_all x1, blocking collectives, per_device(): lax.all_to_all(outgoing, 'head', split_axis=1, concat_axis=0, tiled=True)  8.46 us
    all_to_all x1, blocking collectives, per_device(): lax.all_to_all(finished, 'head', split_axis=0, concat_axis=1, tiled=True)  8.16 us
    unnamed x33, local copies, waits for them, and re-layouts  7.29 us
    concatenate x3, other arithmetic, gather(): jnp.concatenate([returned[:, p * width + begin:p * width + begin + size]...  2.84 us
  transfers between devices with their start and end apart: 8, of which 6 were waited for; matrix products, arithmetic and copies ran while one was open for 2% of the time, Pallas kernels for 23%

profile of v6, /device:TPU:19, one launch (start us, length us, event | category | flops | bytes accessed | tf_op | source)
XLA Modules:
  0.0 140.7 jit_solution(4429138867192437034)
XLA Ops:
  0.7 1.4 slice_dynamic-update-slice_fusion.5
  2.0 1.3 slice_dynamic-update-slice_fusion.4
  3.5 0.3 copy-done.1
  3.8 1.0 copy-done.2
  5.0 0.4 copy.21
  5.5 8.5 %all_to_all.38 = bf16[192,2,7168]{2,0,1:T(8,128)(2,1)S(1)} all-to-all(bf16[192,2,7168]{2,0,1:T(8,128)(2,1)S(1)} %bitcast.30), channel_id=1, replica_groups=mesh['groups'=2,'ctx'=8,'head'=2] {'head'}, dimensions={1} | all-to-all | bytes 11010048 | tf_op jit(solution)/shard_map/all_to_all | solution.py:153
  13.9 2.4 %copy-done = bf16[192,2,7168]{2,0,1:T(8,128)(2,1)} copy-done((bf16[192,2,7168]{2,0,1:T(8,128)(2,1)}, bf16[192,2,7168]{2,0,1:T(8,128)(2,1)S(1)}, u32[]{:S(2)}) %copy-start) | copy-done | bytes 5505048
  16.4 3.2 %collective-permute-start.2 = (bf16[256,512]{1,0:T(8,128)(2,1)S(1)}, bf16[256,512]{1,0:T(8,128)(2,1)S(1)}, u32[]{:S(2)}, u32[]{:S(2)}) collective-permute-start(bf16[256,512]{1,0:T(8,128)(2,1)S(1)} %fusion.2), channel_id=1, source_target_pairs={{0,4},{2,6},{4,8},{6,10},{8,12},{10,14},{1,5},{3,7},{5,9},{7,11},{... | collective-permute-start | bytes 786440 | tf_op jit(solution)/shard_map/ppermute | solution.py:20
  19.6 3.1 %collective-permute-start.3 = (bf16[384,512]{1,0:T(8,128)(2,1)S(1)}, bf16[384,512]{1,0:T(8,128)(2,1)S(1)}, u32[]{:S(2)}, u32[]{:S(2)}) collective-permute-start(bf16[384,512]{1,0:T(8,128)(2,1)S(1)} %pad_maximum_fusion.6), channel_id=1, source_target_pairs={{0,2},{2,4},{4,6},{6,8},{8,10},{10,12},{12,14},{1,3},{3,5},{5,7},{... | collective-permute-start | bytes 1179656 | tf_op jit(solution)/shard_map/ppermute | solution.py:20
  22.8 0.7 fusion.3
  23.5 1.9 %collective-permute-start = (bf16[256,512]{1,0:T(8,128)(2,1)}, bf16[256,512]{1,0:T(8,128)(2,1)S(1)}, u32[]{:S(2)}, u32[]{:S(2)}) collective-permute-start(bf16[256,512]{1,0:T(8,128)(2,1)} %fusion.3), channel_id=1, source_target_pairs={{0,4},{2,6},{4,8},{6,10},{8,12},{10,14},{1,5},{3,7},{5,9},{7,11},{... | collective-permute-start | bytes 786440 | tf_op jit(solution)/shard_map/ppermute | solution.py:20
  25.5 1.9 %collective-permute-start.1 = (bf16[384,512]{1,0:T(8,128)(2,1)S(1)}, bf16[384,512]{1,0:T(8,128)(2,1)S(1)}, u32[]{:S(2)}, u32[]{:S(2)}) collective-permute-start(bf16[384,512]{1,0:T(8,128)(2,1)S(1)} %pad_maximum_fusion.5), channel_id=1, source_target_pairs={{0,2},{2,4},{4,6},{6,8},{8,10},{10,12},{12,14},{1,3},{3,5},{5,7},{... | collective-permute-start | bytes 1179656 | tf_op jit(solution)/shard_map/ppermute | solution.py:20
  27.8 0.1 copy.18
  28.0 4.5 %collective-permute-done = bf16[256,512]{1,0:T(8,128)(2,1)S(1)} collective-permute-done((bf16[256,512]{1,0:T(8,128)(2,1)}, bf16[256,512]{1,0:T(8,128)(2,1)S(1)}, u32[]{:S(2)}, u32[]{:S(2)}) %collective-permute-start) | collective-permute-done | bytes 262176 | tf_op jit(solution)/shard_map/ppermute | solution.py:20
  32.6 2.6 %collective-permute-done.3 = bf16[384,512]{1,0:T(8,128)(2,1)S(1)} collective-permute-done((bf16[384,512]{1,0:T(8,128)(2,1)S(1)}, bf16[384,512]{1,0:T(8,128)(2,1)S(1)}, u32[]{:S(2)}, u32[]{:S(2)}) %collective-permute-start.3) | collective-permute-done | bytes 393248 | tf_op jit(solution)/shard_map/ppermute | solution.py:20
  35.3 16.1 %shard_map.96 = (bf16[384,1024]{1,0:T(8,128)(2,1)S(1)}, f32[1024,256]{1,0:T(8,128)S(1)}, f32[1024,256]{1,0:T(8,128)S(1)}) custom-call(s32[11]{0:T(128)S(1)} %pad_add_fusion.1.bdoc_ref, s32[384,1]{1,0:T(8,128)S(1)} %bitcast.19, s32[1,1024]{1,0:T(1,128)S(1)} %bitcast.21, bf16[384,7168]{1,0:T(8,128)(2,1)} %bitcast.24, bf16[384,7168]{1,0:T(8,128)(2,1)} %bitcast.25, ...), custom_call_target="tpu_custom_call" | custom-call | tf_op jit(solution)/shard_map/pallas_call | solution.py:131
  51.5 0.1 constant_dynamic-update-slice_fusion.3
  51.6 0.2 constant_dynamic-update-slice_fusion.2
  52.0 7.7 %collective-permute-start.6 = (bf16[384,512]{1,0:T(8,128)(2,1)S(1)}, bf16[384,512]{1,0:T(8,128)(2,1)S(1)}, u32[]{:S(2)}, u32[]{:S(2)}) collective-permute-start(bf16[384,512]{1,0:T(8,128)(2,1)S(1)} %slice.271), channel_id=1, source_target_pairs={{2,0},{4,2},{6,4},{8,6},{10,8},{12,10},{14,12},{3,1},{5,3},{7,5},{... | collective-permute-start | bytes 1179656 | tf_op jit(solution)/shard_map/ppermute | solution.py:20
  59.9 15.9 %shard_map.95 = (bf16[384,1024]{1,0:T(8,128)(2,1)S(1)}, f32[1024,256]{1,0:T(8,128)S(1)}, f32[1024,256]{1,0:T(8,128)S(1)}) custom-call(s32[11]{0:T(128)S(1)} %pad_add_fusion.1.bdoc_ref, s32[384,1]{1,0:T(8,128)S(1)} %bitcast.20, s32[1,1024]{1,0:T(1,128)S(1)} %bitcast.22, bf16[384,7168]{1,0:T(8,128)(2,1)} %bitcast.27, bf16[384,7168]{1,0:T(8,128)(2,1)} %bitcast.28, ...), custom_call_target="tpu_custom_call" | custom-call | tf_op jit(solution)/shard_map/pallas_call | solution.py:131
  76.3 1.9 %collective-permute-start.7 = (bf16[256,512]{1,0:T(8,128)(2,1)S(1)}, bf16[256,512]{1,0:T(8,128)(2,1)S(1)}, u32[]{:S(2)}, u32[]{:S(2)}) collective-permute-start(bf16[256,512]{1,0:T(8,128)(2,1)S(1)} %slice.273), channel_id=1, source_target_pairs={{4,0},{6,2},{8,4},{10,6},{12,8},{14,10},{5,1},{7,3},{9,5},{11,7},{... | collective-permute-start | bytes 786440 | tf_op jit(solution)/shard_map/ppermute | solution.py:20
  78.2 1.9 %collective-permute-start.4 = (bf16[384,512]{1,0:T(8,128)(2,1)S(1)}, bf16[384,512]{1,0:T(8,128)(2,1)S(1)}, u32[]{:S(2)}, u32[]{:S(2)}) collective-permute-start(bf16[384,512]{1,0:T(8,128)(2,1)S(1)} %slice.266), channel_id=1, source_target_pairs={{2,0},{4,2},{6,4},{8,6},{10,8},{12,10},{14,12},{3,1},{5,3},{7,5},{... | collective-permute-start | bytes 1179656 | tf_op jit(solution)/shard_map/ppermute | solution.py:20
  80.1 1.9 %collective-permute-start.5 = (bf16[256,512]{1,0:T(8,128)(2,1)S(1)}, bf16[256,512]{1,0:T(8,128)(2,1)S(1)}, u32[]{:S(2)}, u32[]{:S(2)}) collective-permute-start(bf16[256,512]{1,0:T(8,128)(2,1)S(1)} %slice.268), channel_id=1, source_target_pairs={{4,0},{6,2},{8,4},{10,6},{12,8},{14,10},{5,1},{7,3},{9,5},{11,7},{... | collective-permute-start | bytes 786440 | tf_op jit(solution)/shard_map/ppermute | solution.py:20
  82.2 2.5 %collective-permute-done.6 = bf16[384,512]{1,0:T(8,128)(2,1)S(1)} collective-permute-done((bf16[384,512]{1,0:T(8,128)(2,1)S(1)}, bf16[384,512]{1,0:T(8,128)(2,1)S(1)}, u32[]{:S(2)}, u32[]{:S(2)}) %collective-permute-start.6) | collective-permute-done | bytes 393248 | tf_op jit(solution)/shard_map/ppermute | solution.py:20
  84.8 12.0 %collective-permute-done.7 = bf16[256,512]{1,0:T(8,128)(2,1)S(1)} collective-permute-done((bf16[256,512]{1,0:T(8,128)(2,1)S(1)}, bf16[256,512]{1,0:T(8,128)(2,1)S(1)}, u32[]{:S(2)}, u32[]{:S(2)}) %collective-permute-start.7) | collective-permute-done | bytes 262176 | tf_op jit(solution)/shard_map/ppermute | solution.py:20
  96.9 25.5 %collective-permute-done.4 = bf16[384,512]{1,0:T(8,128)(2,1)S(1)} collective-permute-done((bf16[384,512]{1,0:T(8,128)(2,1)S(1)}, bf16[384,512]{1,0:T(8,128)(2,1)S(1)}, u32[]{:S(2)}, u32[]{:S(2)}) %collective-permute-start.4) | collective-permute-done | bytes 393248 | tf_op jit(solution)/shard_map/ppermute | solution.py:20
  122.6 6.4 %collective-permute-done.5 = bf16[256,512]{1,0:T(8,128)(2,1)S(1)} collective-permute-done((bf16[256,512]{1,0:T(8,128)(2,1)S(1)}, bf16[256,512]{1,0:T(8,128)(2,1)S(1)}, u32[]{:S(2)}, u32[]{:S(2)}) %collective-permute-start.5) | collective-permute-done | bytes 262176 | tf_op jit(solution)/shard_map/ppermute | solution.py:20
  129.3 8.2 %all_to_all.39 = bf16[2,192,3072]{2,1,0:T(8,128)(2,1)S(1)} all-to-all(bf16[2,192,3072]{2,1,0:T(8,128)(2,1)S(1)} %bitcast.35), channel_id=1, replica_groups=mesh['groups'=2,'ctx'=8,'head'=2] {'head'}, dimensions={0} | all-to-all | bytes 4718592 | tf_op jit(solution)/shard_map/all_to_all | solution.py:203
  137.4 0.2 copy.16
  137.8 0.8 pad_maximum_fusion.8
  138.6 0.8 pad_maximum_fusion.7
  139.4 1.3 pad_maximum_fusion
  (60 shorter events, 2.7 us)
Async XLA Ops:
  0.6 2.7 %copy-start.3 = (bf16[192,4096]{1,0:T(8,128)(2,1)S(1)}, bf16[192,4096]{1,0:T(8,128)(2,1)}, u32[]{:S(2)}) copy-start(bf16[192,4096]{1,0:T(8,128)(2,1)} %param.21) | copy-start | bytes 4718596
  0.6 2.8 %copy-start.4 = (bf16[192,1024]{1,0:T(8,128)(2,1)S(1)}, bf16[192,1024]{1,0:T(8,128)(2,1)}, u32[]{:S(2)}) copy-start(bf16[192,1024]{1,0:T(8,128)(2,1)} %param.19) | copy-start | bytes 1179652
  0.7 2.8 %copy-start.5 = (bf16[192,1024]{1,0:T(8,128)(2,1)S(1)}, bf16[192,1024]{1,0:T(8,128)(2,1)}, u32[]{:S(2)}) copy-start(bf16[192,1024]{1,0:T(8,128)(2,1)} %param.20) | copy-start | bytes 1179652
  2.0 1.8 %copy-start.1 = (bf16[192,4096]{1,0:T(8,128)(2,1)S(1)}, bf16[192,4096]{1,0:T(8,128)(2,1)}, u32[]{:S(2)}) copy-start(bf16[192,4096]{1,0:T(8,128)(2,1)} %param.18) | copy-start | bytes 4718596
  3.4 1.5 %copy-start.2 = (bf16[192,4096]{1,0:T(8,128)(2,1)S(1)}, bf16[192,4096]{1,0:T(8,128)(2,1)}, u32[]{:S(2)}) copy-start(bf16[192,4096]{1,0:T(8,128)(2,1)} %param.22) | copy-start | bytes 4718596
  13.9 2.4 %copy-start = (bf16[192,2,7168]{2,0,1:T(8,128)(2,1)}, bf16[192,2,7168]{2,0,1:T(8,128)(2,1)S(1)}, u32[]{:S(2)}) copy-start(bf16[192,2,7168]{2,0,1:T(8,128)(2,1)S(1)} %all_to_all.38) | copy-start | bytes 16515076
  13.9 13.5 %copy-start.6 = (s32[24]{0:T(128)S(1)}, s32[24]{0:T(128)}, u32[]{:S(2)}) copy-start(s32[24]{0:T(128)} %param.23) | copy-start | bytes 292
  16.4 11.6 %collective-permute-start.2 = (bf16[256,512]{1,0:T(8,128)(2,1)S(1)}, bf16[256,512]{1,0:T(8,128)(2,1)S(1)}, u32[]{:S(2)}, u32[]{:S(2)}) collective-permute-start(bf16[256,512]{1,0:T(8,128)(2,1)S(1)} %fusion.2), channel_id=1, source_target_pairs={{0,4},{2,6},{4,8},{6,10},{8,12},{10,14},{1,5},{3,7},{5,9},{7,11},{... | collective-permute-start | bytes 786440 | tf_op jit(solution)/shard_map/ppermute | solution.py:20
  19.6 15.5 %collective-permute-start.3 = (bf16[384,512]{1,0:T(8,128)(2,1)S(1)}, bf16[384,512]{1,0:T(8,128)(2,1)S(1)}, u32[]{:S(2)}, u32[]{:S(2)}) collective-permute-start(bf16[384,512]{1,0:T(8,128)(2,1)S(1)} %pad_maximum_fusion.6), channel_id=1, source_target_pairs={{0,2},{2,4},{4,6},{6,8},{8,10},{10,12},{12,14},{1,3},{3,5},{5,7},{... | collective-permute-start | bytes 1179656 | tf_op jit(solution)/shard_map/ppermute | solution.py:20
  23.5 9.0 %collective-permute-start = (bf16[256,512]{1,0:T(8,128)(2,1)}, bf16[256,512]{1,0:T(8,128)(2,1)S(1)}, u32[]{:S(2)}, u32[]{:S(2)}) collective-permute-start(bf16[256,512]{1,0:T(8,128)(2,1)} %fusion.3), channel_id=1, source_target_pairs={{0,4},{2,6},{4,8},{6,10},{8,12},{10,14},{1,5},{3,7},{5,9},{7,11},{... | collective-permute-start | bytes 786440 | tf_op jit(solution)/shard_map/ppermute | solution.py:20
  25.5 34.3 %collective-permute-start.1 = (bf16[384,512]{1,0:T(8,128)(2,1)S(1)}, bf16[384,512]{1,0:T(8,128)(2,1)S(1)}, u32[]{:S(2)}, u32[]{:S(2)}) collective-permute-start(bf16[384,512]{1,0:T(8,128)(2,1)S(1)} %pad_maximum_fusion.5), channel_id=1, source_target_pairs={{0,2},{2,4},{4,6},{6,8},{8,10},{10,12},{12,14},{1,3},{3,5},{5,7},{... | collective-permute-start | bytes 1179656 | tf_op jit(solution)/shard_map/ppermute | solution.py:20
  52.0 32.7 %collective-permute-start.6 = (bf16[384,512]{1,0:T(8,128)(2,1)S(1)}, bf16[384,512]{1,0:T(8,128)(2,1)S(1)}, u32[]{:S(2)}, u32[]{:S(2)}) collective-permute-start(bf16[384,512]{1,0:T(8,128)(2,1)S(1)} %slice.271), channel_id=1, source_target_pairs={{2,0},{4,2},{6,4},{8,6},{10,8},{12,10},{14,12},{3,1},{5,3},{7,5},{... | collective-permute-start | bytes 1179656 | tf_op jit(solution)/shard_map/ppermute | solution.py:20
  76.3 20.5 %collective-permute-start.7 = (bf16[256,512]{1,0:T(8,128)(2,1)S(1)}, bf16[256,512]{1,0:T(8,128)(2,1)S(1)}, u32[]{:S(2)}, u32[]{:S(2)}) collective-permute-start(bf16[256,512]{1,0:T(8,128)(2,1)S(1)} %slice.273), channel_id=1, source_target_pairs={{4,0},{6,2},{8,4},{10,6},{12,8},{14,10},{5,1},{7,3},{9,5},{11,7},{... | collective-permute-start | bytes 786440 | tf_op jit(solution)/shard_map/ppermute | solution.py:20
  78.2 44.3 %collective-permute-start.4 = (bf16[384,512]{1,0:T(8,128)(2,1)S(1)}, bf16[384,512]{1,0:T(8,128)(2,1)S(1)}, u32[]{:S(2)}, u32[]{:S(2)}) collective-permute-start(bf16[384,512]{1,0:T(8,128)(2,1)S(1)} %slice.266), channel_id=1, source_target_pairs={{2,0},{4,2},{6,4},{8,6},{10,8},{12,10},{14,12},{3,1},{5,3},{7,5},{... | collective-permute-start | bytes 1179656 | tf_op jit(solution)/shard_map/ppermute | solution.py:20
  80.1 48.8 %collective-permute-start.5 = (bf16[256,512]{1,0:T(8,128)(2,1)S(1)}, bf16[256,512]{1,0:T(8,128)(2,1)S(1)}, u32[]{:S(2)}, u32[]{:S(2)}) collective-permute-start(bf16[256,512]{1,0:T(8,128)(2,1)S(1)} %slice.268), channel_id=1, source_target_pairs={{4,0},{6,2},{8,4},{10,6},{12,8},{14,10},{5,1},{7,3},{9,5},{11,7},{... | collective-permute-start | bytes 786440 | tf_op jit(solution)/shard_map/ppermute | solution.py:20

commit v7 on v5

--- a/solution.py
+++ b/solution.py
@@ -37,32 +37,33 @@
             [do_ref[rows, pl.ds(r * HEAD_SIZE, HEAD_SIZE)] for r in range(query_group)], axis=0)
         outs = jnp.concatenate(
             [o_ref[rows, pl.ds(r * HEAD_SIZE, HEAD_SIZE)] for r in range(query_group)], axis=0)
-        delta = jnp.sum(dos.astype(jnp.float32) * outs.astype(jnp.float32), axis=1, keepdims=True)
-        qd = qdoc_ref[rows, :]
-        kd = kdoc_ref[:, pl.ds(k0, window)]
-        qpos = lax.broadcasted_iota(jnp.int32, (BLK, window), 0) + (key_offset + qb * BLK)
-        kpos = lax.broadcasted_iota(jnp.int32, (BLK, window), 1) + k0
-        allowed = (qd == kd) & (kpos <= qpos)
-        mask = jnp.concatenate([allowed] * query_group, axis=0)
+        product = dos.astype(jnp.float32) * outs.astype(jnp.float32)
+        delta = jnp.sum(product.T, axis=0, keepdims=True)
+        qd = qdoc_ref[:, rows]
+        kd = kdoc_ref[pl.ds(k0, window), :]
+        qpos = lax.broadcasted_iota(jnp.int32, (window, BLK), 1) + (key_offset + qb * BLK)
+        kpos = lax.broadcasted_iota(jnp.int32, (window, BLK), 0) + k0
+        allowed = (kd == qd) & (kpos <= qpos)
+        mask = jnp.concatenate([allowed] * query_group, axis=1)
         scores = scale * lax.dot_general(
-            qs, kwin, (((1,), (1,)), ((), ())), preferred_element_type=jnp.float32)
+            kwin, qs, (((1,), (1,)), ((), ())), preferred_element_type=jnp.float32)
         masked = jnp.where(mask, scores, -1e30)
-        top = jnp.max(masked, axis=1, keepdims=True)
-        total = jnp.sum(jnp.where(mask, jnp.exp(masked - top), 0.0), axis=1, keepdims=True)
+        top = jnp.max(masked, axis=0, keepdims=True)
+        total = jnp.sum(jnp.exp(masked - top), axis=0, keepdims=True)
         lse = top + jnp.log(total)
-        probs = jnp.where(mask, jnp.exp(masked - lse), 0.0)
+        probs = jnp.exp(masked - lse)
         dprob = lax.dot_general(
-            dos, vwin, (((1,), (1,)), ((), ())), preferred_element_type=jnp.float32)
+            vwin, dos, (((1,), (1,)), ((), ())), preferred_element_type=jnp.float32)
         dscore = (probs * (dprob - delta)).astype(jnp.bfloat16)
-        dq = scale * jnp.dot(dscore, kwin, preferred_element_type=jnp.float32)
+        dq = scale * lax.dot_general(
+            dscore, kwin, (((0,), (0,)), ((), ())), preferred_element_type=jnp.float32)
         for r in range(query_group):
             dq_ref[rows, pl.ds(r * HEAD_SIZE, HEAD_SIZE)] = (
                 dq[r * BLK:(r + 1) * BLK].astype(dq_ref.dtype))
-        dk_ref[pl.ds(k0, window), :] += scale * lax.dot_general(
-            dscore, qs, (((0,), (0,)), ((), ())), preferred_element_type=jnp.float32)
-        dv_ref[pl.ds(k0, window), :] += lax.dot_general(
-            probs.astype(jnp.bfloat16), dos, (((0,), (0,)), ((), ())),
-            preferred_element_type=jnp.float32)
+        dk_ref[pl.ds(k0, window), :] += scale * jnp.dot(
+            dscore, qs, preferred_element_type=jnp.float32)
+        dv_ref[pl.ds(k0, window), :] += jnp.dot(
+            probs.astype(jnp.bfloat16), dos, preferred_element_type=jnp.float32)
 
 
 def local_backward(qdoc, kdoc, fused, q_cols, all_kv, head0, keys, values):
@@ -85,8 +86,8 @@
         kernel,
         grid=(kv_heads,),
         in_specs=[
-            pl.BlockSpec((rows, 1), lambda g: (0, 0)),
-            pl.BlockSpec((1, key_rows), lambda g: (0, 0)),
+            pl.BlockSpec((1, rows), lambda g: (0, 0)),
+            pl.BlockSpec((key_rows, 1), lambda g: (0, 0)),
             section(0), section(1), section(2), k_spec, k_spec,
         ],
         out_specs=[out_spec, k_spec, k_spec],
@@ -101,7 +102,7 @@
 
 
 def per_device(query_matrix, key_matrix, value_matrix, fwd_output, output_gradient, block_docs):
-    tokens, q_all = query_matrix.shape
+    _, q_all = query_matrix.shape
     kv_all = key_matrix.shape[1]
     peers = lax.axis_size("head")
     q_cols, kv_cols = q_all // peers, kv_all // peers
@@ -123,41 +124,40 @@
         return jnp.where(owner >= 0, docs, -1)
 
     key_docs = jnp.concatenate([docs_of(place - distance) for distance in range(REACH, -1, -1)])
-    kdoc = jnp.repeat(key_docs, BLK)[skip:][None, :]
-    qdoc = jnp.repeat(docs_of(place), BLK)[:, None]
+    kdoc = jnp.repeat(key_docs, BLK)[skip:][:, None]
+    qdoc = jnp.repeat(docs_of(place), BLK)[None, :]
     all_kv = kv_cols // HEAD_SIZE
     per = kv_cols // CHUNKS
     q_parts, k_parts, v_parts = [], [], []
     for j in range(CHUNKS):
-        with jax.named_scope(f"chunk{j}"):
-            key_here = key_part[:, j * per:(j + 1) * per]
-            value_here = value_part[:, j * per:(j + 1) * per]
-            pair = jnp.concatenate([key_here, value_here], axis=1)
-            behind = []
-            for distance in range(REACH, 0, -1):
-                first = max(skip - (REACH - distance) * window_extent, 0)
-                if first < window_extent:
-                    behind.append(shifted(pair[first:], "ctx", distance))
-            keys = jnp.concatenate([b[:, :per] for b in behind] + [key_here], axis=0)
-            values = jnp.concatenate([b[:, per:] for b in behind] + [value_here], axis=0)
+        key_here = key_part[:, j * per:(j + 1) * per]
+        value_here = value_part[:, j * per:(j + 1) * per]
+        pair = jnp.concatenate([key_here, value_here], axis=1)
+        behind = []
+        for distance in range(REACH, 0, -1):
+            first = max(skip - (REACH - distance) * window_extent, 0)
+            if first < window_extent:
+                behind.append(shifted(pair[first:], "ctx", distance))
+        keys = jnp.concatenate([b[:, :per] for b in behind] + [key_here], axis=0)
+        values = jnp.concatenate([b[:, per:] for b in behind] + [value_here], axis=0)
 
-            query_sum, key_partial, value_partial = local_backward(
-                qdoc, kdoc, fused, q_cols, all_kv, j * per // HEAD_SIZE, keys, values)
+        query_sum, key_partial, value_partial = local_backward(
+            qdoc, kdoc, fused, q_cols, all_kv, j * per // HEAD_SIZE, keys, values)
 
-            both = jnp.concatenate([key_partial, value_partial], axis=1)
-            total = both[own - skip:]
-            for distance in range(1, REACH + 1):
-                begin = (REACH - distance) * window_extent
-                start = max(begin, skip)
-                if start >= begin + window_extent:
-                    continue
-                sent = shifted(
-                    both[start - skip:begin + window_extent - skip].astype(jnp.bfloat16),
-                    "ctx", -distance)
-                total = total.at[start - begin:].add(sent.astype(jnp.float32))
-            q_parts.append(query_sum)
-            k_parts.append(total[:, :per].astype(jnp.bfloat16))
-            v_parts.append(total[:, per:].astype(jnp.bfloat16))
+        both = jnp.concatenate([key_partial, value_partial], axis=1)
+        total = both[own - skip:]
+        for distance in range(1, REACH + 1):
+            begin = (REACH - distance) * window_extent
+            start = max(begin, skip)
+            if start >= begin + window_extent:
+                continue
+            sent = shifted(
+                both[start - skip:begin + window_extent - skip].astype(jnp.bfloat16),
+                "ctx", -distance)
+            total = total.at[start - begin:].add(sent.astype(jnp.float32))
+        q_parts.append(query_sum)
+        k_parts.append(total[:, :per].astype(jnp.bfloat16))
+        v_parts.append(total[:, per:].astype(jnp.bfloat16))
     finished = jnp.concatenate(q_parts + k_parts + v_parts, axis=1)
     returned = lax.all_to_all(finished, "head", split_axis=0, concat_axis=1, tiled=True)
     width = finished.shape[1]

time: 103 us -> 103 us (level)
  local copies, waits for them, and re-layouts: 8.83 us -> 9.89 us
    unnamed x33 -> x32, local copies, waits for them, and re-layouts: 7.32 us -> 7.19 us
  transfers between devices with their start and end apart: 8 -> 8, of which waited for: 5 -> 5; matrix products, arithmetic and copies ran while one was open for 3% -> 4% of each run, Pallas kernels for 23% -> 23%
where the time goes in v7:
time: 103 us
  waiting for transfers between devices  28 us (27%)
  Pallas kernels  23.6 us (23%)
  starting transfers between devices  21.4 us (21%)
  blocking collectives  13.8 us (13%)
  local copies, waits for them, and re-layouts  9.89 us (10%)
  other arithmetic  4.79 us (5%)
  between operations  1.17 us (1%)
    ppermute x8, waiting for transfers between devices, shifted(): return lax.ppermute(block, axis, route)  28 us
    pallas_call x2, Pallas kernels, local_backward(): pl.pallas_call(kernel, grid=(kv_heads,), in_specs=[pl.BlockSpec((1, rows)...  23.6 us
    ppermute x8, starting transfers between devices, shifted(): return lax.ppermute(block, axis, route)  21.4 us
    all_to_all x1, blocking collectives, per_device(): lax.all_to_all(outgoing, 'head', split_axis=1, concat_axis=0, tiled=True)  8.16 us
    unnamed x32, local copies, waits for them, and re-layouts  7.19 us
    all_to_all x1, blocking collectives, per_device(): lax.all_to_all(finished, 'head', split_axis=0, concat_axis=1, tiled=True)  5.63 us
    concatenate x3, other arithmetic, gather(): jnp.concatenate([returned[:, p * width + begin:p * width + begin + size]...  2.84 us
  transfers between devices with their start and end apart: 8, of which 5 were waited for; matrix products, arithmetic and copies ran while one was open for 4% of the time, Pallas kernels for 23%

profile of v7, /device:TPU:0, one launch (start us, length us, event | category | flops | bytes accessed | tf_op | source)
XLA Modules:
  0.0 102.6 jit_solution(16332984631032570163)
XLA Ops:
  0.7 1.4 %slice_dynamic-update-slice_fusion.5 = bf16[192,14336]{1,0:T(8,128)(2,1)S(1)} fusion(bf16[192,4096]{1,0:T(8,128)(2,1)} %param.18), kind=kLoop, calls=%fused_computation.9 | loop fusion | bytes 1572864
  2.0 1.3 %slice_dynamic-update-slice_fusion.4 = bf16[192,14336]{1,0:T(8,128)(2,1)S(1)} fusion(bf16[192,14336]{1,0:T(8,128)(2,1)S(1)} %slice_dynamic-update-slice_fusion.5, bf16[192,4096]{1,0:T(8,128)(2,1)} %param.22), kind=kLoop, calls=%fused_computation.8 | loop fusion | bytes 1572864
  3.5 0.3 copy-done.1
  3.8 1.0 %copy-done.2 = bf16[192,4096]{1,0:T(8,128)(2,1)S(1)} copy-done((bf16[192,4096]{1,0:T(8,128)(2,1)S(1)}, bf16[192,4096]{1,0:T(8,128)(2,1)}, u32[]{:S(2)}) %copy-start.2) | copy-done | bytes 1572888
  5.0 0.4 copy.20
  5.5 8.2 %all_to_all.38 = bf16[192,2,7168]{2,0,1:T(8,128)(2,1)S(1)} all-to-all(bf16[192,2,7168]{2,0,1:T(8,128)(2,1)S(1)} %bitcast.27), channel_id=1, replica_groups=mesh['groups'=2,'ctx'=8,'head'=2] {'head'}, dimensions={1} | all-to-all | bytes 11010048 | tf_op jit(solution)/shard_map/all_to_all | solution.py:113
  13.6 2.4 %copy-done = bf16[192,2,7168]{2,0,1:T(8,128)(2,1)} copy-done((bf16[192,2,7168]{2,0,1:T(8,128)(2,1)}, bf16[192,2,7168]{2,0,1:T(8,128)(2,1)S(1)}, u32[]{:S(2)}) %copy-start) | copy-done | bytes 5505048
  16.1 5.0 %collective-permute-start.2 = (bf16[256,512]{1,0:T(8,128)(2,1)S(1)}, bf16[256,512]{1,0:T(8,128)(2,1)S(1)}, u32[]{:S(2)}, u32[]{:S(2)}) collective-permute-start(bf16[256,512]{1,0:T(8,128)(2,1)S(1)} %fusion.2), channel_id=1, source_target_pairs={{0,4},{2,6},{4,8},{6,10},{8,12},{10,14},{1,5},{3,7},{5,9},{7,11},{... | collective-permute-start | bytes 786440 | tf_op jit(solution)/shard_map/ppermute | solution.py:20
  21.1 3.4 %collective-permute-start.3 = (bf16[384,512]{1,0:T(8,128)(2,1)S(1)}, bf16[384,512]{1,0:T(8,128)(2,1)S(1)}, u32[]{:S(2)}, u32[]{:S(2)}) collective-permute-start(bf16[384,512]{1,0:T(8,128)(2,1)S(1)} %pad_maximum_fusion.6), channel_id=1, source_target_pairs={{0,2},{2,4},{4,6},{6,8},{8,10},{10,12},{12,14},{1,3},{3,5},{5,7},{... | collective-permute-start | bytes 1179656 | tf_op jit(solution)/shard_map/ppermute | solution.py:20
  24.6 0.7 fusion.3
  25.3 4.2 %collective-permute-start = (bf16[256,512]{1,0:T(8,128)(2,1)}, bf16[256,512]{1,0:T(8,128)(2,1)}, u32[]{:S(2)}, u32[]{:S(2)}) collective-permute-start(bf16[256,512]{1,0:T(8,128)(2,1)} %fusion.3), channel_id=1, source_target_pairs={{0,4},{2,6},{4,8},{6,10},{8,12},{10,14},{1,5},{3,7},{5,9},{7,11},{... | collective-permute-start | bytes 786440 | tf_op jit(solution)/shard_map/ppermute | solution.py:20
  29.5 3.4 %collective-permute-start.1 = (bf16[384,512]{1,0:T(8,128)(2,1)S(1)}, bf16[384,512]{1,0:T(8,128)(2,1)S(1)}, u32[]{:S(2)}, u32[]{:S(2)}) collective-permute-start(bf16[384,512]{1,0:T(8,128)(2,1)S(1)} %pad_maximum_fusion.5), channel_id=1, source_target_pairs={{0,2},{2,4},{4,6},{6,8},{8,10},{10,12},{12,14},{1,3},{3,5},{5,7},{... | collective-permute-start | bytes 1179656 | tf_op jit(solution)/shard_map/ppermute | solution.py:20
  33.3 0.2 copy.12.kdoc_ref
  33.6 0.7 collective-permute-done
  34.3 1.0 fusion.10
  35.5 11.8 %shard_map.96 = (bf16[384,1024]{1,0:T(8,128)(2,1)S(1)}, f32[1024,256]{1,0:T(8,128)S(1)}, f32[1024,256]{1,0:T(8,128)S(1)}) custom-call(s32[1,384]{1,0:T(1,128)S(1)} %bitcast.18, s32[1024,1]{1,0:T(8,128)S(1)} %copy.12.kdoc_ref, bf16[384,7168]{1,0:T(8,128)(2,1)} %bitcast.21, bf16[384,7168]{1,0:T(8,128)(2,1)} %bitcast.22, bf16[384,7168]{1,0:T(8,128)(2,1)} %bitcast.23, ...), custom_call_target="tpu_custom_call" | custom-call | tf_op jit(solution)/shard_map/pallas_call | solution.py:85
  47.4 0.2 constant_dynamic-update-slice_fusion.2
  47.8 1.5 %collective-permute-start.6 = (bf16[384,512]{1,0:T(8,128)(2,1)S(1)}, bf16[384,512]{1,0:T(8,128)(2,1)S(1)}, u32[]{:S(2)}, u32[]{:S(2)}) collective-permute-start(bf16[384,512]{1,0:T(8,128)(2,1)S(1)} %slice.270), channel_id=1, source_target_pairs={{2,0},{4,2},{6,4},{8,6},{10,8},{12,10},{14,12},{3,1},{5,3},{7,5},{... | collective-permute-start | bytes 1179656 | tf_op jit(solution)/shard_map/ppermute | solution.py:20
  49.4 11.8 %shard_map.95 = (bf16[384,1024]{1,0:T(8,128)(2,1)S(1)}, f32[1024,256]{1,0:T(8,128)S(1)}, f32[1024,256]{1,0:T(8,128)S(1)}) custom-call(s32[1,384]{1,0:T(1,128)S(1)} %bitcast.19, s32[1024,1]{1,0:T(8,128)S(1)} %copy.12.kdoc_ref, bf16[384,7168]{1,0:T(8,128)(2,1)} %bitcast.24, bf16[384,7168]{1,0:T(8,128)(2,1)} %bitcast.25, bf16[384,7168]{1,0:T(8,128)(2,1)} %bitcast.26, ...), custom_call_target="tpu_custom_call" | custom-call | tf_op jit(solution)/shard_map/pallas_call | solution.py:85
  61.3 0.2 constant_dynamic-update-slice_fusion
  61.7 1.3 %collective-permute-start.7 = (bf16[256,512]{1,0:T(8,128)(2,1)S(1)}, bf16[256,512]{1,0:T(8,128)(2,1)S(1)}, u32[]{:S(2)}, u32[]{:S(2)}) collective-permute-start(bf16[256,512]{1,0:T(8,128)(2,1)S(1)} %slice.272), channel_id=1, source_target_pairs={{4,0},{6,2},{8,4},{10,6},{12,8},{14,10},{5,1},{7,3},{9,5},{11,7},{... | collective-permute-start | bytes 786440 | tf_op jit(solution)/shard_map/ppermute | solution.py:20
  63.0 1.3 %collective-permute-start.4 = (bf16[384,512]{1,0:T(8,128)(2,1)S(1)}, bf16[384,512]{1,0:T(8,128)(2,1)S(1)}, u32[]{:S(2)}, u32[]{:S(2)}) collective-permute-start(bf16[384,512]{1,0:T(8,128)(2,1)S(1)} %slice.265), channel_id=1, source_target_pairs={{2,0},{4,2},{6,4},{8,6},{10,8},{12,10},{14,12},{3,1},{5,3},{7,5},{... | collective-permute-start | bytes 1179656 | tf_op jit(solution)/shard_map/ppermute | solution.py:20
  64.3 1.3 %collective-permute-start.5 = (bf16[256,512]{1,0:T(8,128)(2,1)S(1)}, bf16[256,512]{1,0:T(8,128)(2,1)S(1)}, u32[]{:S(2)}, u32[]{:S(2)}) collective-permute-start(bf16[256,512]{1,0:T(8,128)(2,1)S(1)} %slice.267), channel_id=1, source_target_pairs={{4,0},{6,2},{8,4},{10,6},{12,8},{14,10},{5,1},{7,3},{9,5},{11,7},{... | collective-permute-start | bytes 786440 | tf_op jit(solution)/shard_map/ppermute | solution.py:20
  65.7 0.8 collective-permute-done.6
  66.6 15.3 %collective-permute-done.7 = bf16[256,512]{1,0:T(8,128)(2,1)S(1)} collective-permute-done((bf16[256,512]{1,0:T(8,128)(2,1)S(1)}, bf16[256,512]{1,0:T(8,128)(2,1)S(1)}, u32[]{:S(2)}, u32[]{:S(2)}) %collective-permute-start.7) | collective-permute-done | bytes 262176 | tf_op jit(solution)/shard_map/ppermute | solution.py:20
  82.1 0.2 collective-permute-done.4
  82.4 11.0 %collective-permute-done.5 = bf16[256,512]{1,0:T(8,128)(2,1)S(1)} collective-permute-done((bf16[256,512]{1,0:T(8,128)(2,1)S(1)}, bf16[256,512]{1,0:T(8,128)(2,1)S(1)}, u32[]{:S(2)}, u32[]{:S(2)}) %collective-permute-start.5) | collective-permute-done | bytes 262176 | tf_op jit(solution)/shard_map/ppermute | solution.py:20
  93.7 5.6 %all_to_all.39 = bf16[2,192,3072]{2,1,0:T(8,128)(2,1)S(1)} all-to-all(bf16[2,192,3072]{2,1,0:T(8,128)(2,1)S(1)} %bitcast.32), channel_id=1, replica_groups=mesh['groups'=2,'ctx'=8,'head'=2] {'head'}, dimensions={0} | all-to-all | bytes 4718592 | tf_op jit(solution)/shard_map/all_to_all | solution.py:162
  99.3 0.2 copy.16
  99.8 0.8 pad_maximum_fusion.8
  100.5 0.8 pad_maximum_fusion.7
  101.3 1.3 %pad_maximum_fusion = bf16[192,4096]{1,0:T(8,128)(2,1)} fusion(bf16[192,2048]{1,0:T(8,128)(2,1)S(1)} %get-tuple-element.88, bf16[192,2048]{1,0:T(8,128)(2,1)S(1)} %get-tuple-element.87), kind=kLoop, calls=%fused_computation.1 | loop fusion | flops 3145728 | bytes 3145728 | tf_op jit(solution)/shard_map/concatenate | solution.py:166
  (59 shorter events, 2.6 us)
Async XLA Ops:
  0.6 2.7 %copy-start.3 = (bf16[192,4096]{1,0:T(8,128)(2,1)S(1)}, bf16[192,4096]{1,0:T(8,128)(2,1)}, u32[]{:S(2)}) copy-start(bf16[192,4096]{1,0:T(8,128)(2,1)} %param.21) | copy-start | bytes 4718596
  0.6 2.8 %copy-start.4 = (bf16[192,1024]{1,0:T(8,128)(2,1)S(1)}, bf16[192,1024]{1,0:T(8,128)(2,1)}, u32[]{:S(2)}) copy-start(bf16[192,1024]{1,0:T(8,128)(2,1)} %param.19) | copy-start | bytes 1179652
  0.7 2.8 %copy-start.5 = (bf16[192,1024]{1,0:T(8,128)(2,1)S(1)}, bf16[192,1024]{1,0:T(8,128)(2,1)}, u32[]{:S(2)}) copy-start(bf16[192,1024]{1,0:T(8,128)(2,1)} %param.20) | copy-start | bytes 1179652
  2.0 1.8 %copy-start.1 = (bf16[192,4096]{1,0:T(8,128)(2,1)S(1)}, bf16[192,4096]{1,0:T(8,128)(2,1)}, u32[]{:S(2)}) copy-start(bf16[192,4096]{1,0:T(8,128)(2,1)} %param.18) | copy-start | bytes 4718596
  3.4 1.5 %copy-start.2 = (bf16[192,4096]{1,0:T(8,128)(2,1)S(1)}, bf16[192,4096]{1,0:T(8,128)(2,1)}, u32[]{:S(2)}) copy-start(bf16[192,4096]{1,0:T(8,128)(2,1)} %param.22) | copy-start | bytes 4718596
  13.6 2.4 %copy-start = (bf16[192,2,7168]{2,0,1:T(8,128)(2,1)}, bf16[192,2,7168]{2,0,1:T(8,128)(2,1)S(1)}, u32[]{:S(2)}) copy-start(bf16[192,2,7168]{2,0,1:T(8,128)(2,1)S(1)} %all_to_all.38) | copy-start | bytes 16515076
  13.6 19.3 %copy-start.6 = (s32[24]{0:T(128)S(1)}, s32[24]{0:T(128)}, u32[]{:S(2)}) copy-start(s32[24]{0:T(128)} %param.23) | copy-start | bytes 292
  16.1 17.5 %collective-permute-start.2 = (bf16[256,512]{1,0:T(8,128)(2,1)S(1)}, bf16[256,512]{1,0:T(8,128)(2,1)S(1)}, u32[]{:S(2)}, u32[]{:S(2)}) collective-permute-start(bf16[256,512]{1,0:T(8,128)(2,1)S(1)} %fusion.2), channel_id=1, source_target_pairs={{0,4},{2,6},{4,8},{6,10},{8,12},{10,14},{1,5},{3,7},{5,9},{7,11},{... | collective-permute-start | bytes 786440 | tf_op jit(solution)/shard_map/ppermute | solution.py:20
  21.1 14.2 %collective-permute-start.3 = (bf16[384,512]{1,0:T(8,128)(2,1)S(1)}, bf16[384,512]{1,0:T(8,128)(2,1)S(1)}, u32[]{:S(2)}, u32[]{:S(2)}) collective-permute-start(bf16[384,512]{1,0:T(8,128)(2,1)S(1)} %pad_maximum_fusion.6), channel_id=1, source_target_pairs={{0,2},{2,4},{4,6},{6,8},{8,10},{10,12},{12,14},{1,3},{3,5},{5,7},{... | collective-permute-start | bytes 1179656 | tf_op jit(solution)/shard_map/ppermute | solution.py:20
  25.3 9.1 %collective-permute-start = (bf16[256,512]{1,0:T(8,128)(2,1)}, bf16[256,512]{1,0:T(8,128)(2,1)}, u32[]{:S(2)}, u32[]{:S(2)}) collective-permute-start(bf16[256,512]{1,0:T(8,128)(2,1)} %fusion.3), channel_id=1, source_target_pairs={{0,4},{2,6},{4,8},{6,10},{8,12},{10,14},{1,5},{3,7},{5,9},{7,11},{... | collective-permute-start | bytes 786440 | tf_op jit(solution)/shard_map/ppermute | solution.py:20
  29.5 19.8 %collective-permute-start.1 = (bf16[384,512]{1,0:T(8,128)(2,1)S(1)}, bf16[384,512]{1,0:T(8,128)(2,1)S(1)}, u32[]{:S(2)}, u32[]{:S(2)}) collective-permute-start(bf16[384,512]{1,0:T(8,128)(2,1)S(1)} %pad_maximum_fusion.5), channel_id=1, source_target_pairs={{0,2},{2,4},{4,6},{6,8},{8,10},{10,12},{12,14},{1,3},{3,5},{5,7},{... | collective-permute-start | bytes 1179656 | tf_op jit(solution)/shard_map/ppermute | solution.py:20
  47.8 18.7 %collective-permute-start.6 = (bf16[384,512]{1,0:T(8,128)(2,1)S(1)}, bf16[384,512]{1,0:T(8,128)(2,1)S(1)}, u32[]{:S(2)}, u32[]{:S(2)}) collective-permute-start(bf16[384,512]{1,0:T(8,128)(2,1)S(1)} %slice.270), channel_id=1, source_target_pairs={{2,0},{4,2},{6,4},{8,6},{10,8},{12,10},{14,12},{3,1},{5,3},{7,5},{... | collective-permute-start | bytes 1179656 | tf_op jit(solution)/shard_map/ppermute | solution.py:20
  61.7 20.2 %collective-permute-start.7 = (bf16[256,512]{1,0:T(8,128)(2,1)S(1)}, bf16[256,512]{1,0:T(8,128)(2,1)S(1)}, u32[]{:S(2)}, u32[]{:S(2)}) collective-permute-start(bf16[256,512]{1,0:T(8,128)(2,1)S(1)} %slice.272), channel_id=1, source_target_pairs={{4,0},{6,2},{8,4},{10,6},{12,8},{14,10},{5,1},{7,3},{9,5},{11,7},{... | collective-permute-start | bytes 786440 | tf_op jit(solution)/shard_map/ppermute | solution.py:20
  63.0 19.3 %collective-permute-start.4 = (bf16[384,512]{1,0:T(8,128)(2,1)S(1)}, bf16[384,512]{1,0:T(8,128)(2,1)S(1)}, u32[]{:S(2)}, u32[]{:S(2)}) collective-permute-start(bf16[384,512]{1,0:T(8,128)(2,1)S(1)} %slice.265), channel_id=1, source_target_pairs={{2,0},{4,2},{6,4},{8,6},{10,8},{12,10},{14,12},{3,1},{5,3},{7,5},{... | collective-permute-start | bytes 1179656 | tf_op jit(solution)/shard_map/ppermute | solution.py:20
  64.3 29.1 %collective-permute-start.5 = (bf16[256,512]{1,0:T(8,128)(2,1)S(1)}, bf16[256,512]{1,0:T(8,128)(2,1)S(1)}, u32[]{:S(2)}, u32[]{:S(2)}) collective-permute-start(bf16[256,512]{1,0:T(8,128)(2,1)S(1)} %slice.267), channel_id=1, source_target_pairs={{4,0},{6,2},{8,4},{10,6},{12,8},{14,10},{5,1},{7,3},{9,5},{11,7},{... | collective-permute-start | bytes 786440 | tf_op jit(solution)/shard_map/ppermute | solution.py:20

commit v8 on v5

--- a/solution.py
+++ b/solution.py
@@ -65,10 +65,10 @@
             preferred_element_type=jnp.float32)
 
 
-def local_backward(qdoc, kdoc, fused, q_cols, all_kv, head0, keys, values):
+def local_backward(qdoc, kdoc, fused, q_cols, all_kv, head0, keys, values, kv_heads):
     rows = fused.shape[0]
-    key_rows, kv_cols = keys.shape
-    kv_heads = kv_cols // HEAD_SIZE
+    key_rows = keys.shape[0]
+    kv_cols = kv_heads * HEAD_SIZE
     query_group = q_cols // HEAD_SIZE // all_kv
     group_cols = query_group * HEAD_SIZE
     kernel = functools.partial(
@@ -80,7 +80,8 @@
 
     out_spec = pl.BlockSpec((rows, group_cols), lambda g: (0, g))
 
-    k_spec = pl.BlockSpec((key_rows, HEAD_SIZE), lambda g: (0, g))
+    k_spec = pl.BlockSpec((key_rows, HEAD_SIZE), lambda g: (0, head0 + g))
+    part_spec = pl.BlockSpec((key_rows, HEAD_SIZE), lambda g: (0, g))
     return pl.pallas_call(
         kernel,
         grid=(kv_heads,),
@@ -89,7 +90,7 @@
             pl.BlockSpec((1, key_rows), lambda g: (0, 0)),
             section(0), section(1), section(2), k_spec, k_spec,
         ],
-        out_specs=[out_spec, k_spec, k_spec],
+        out_specs=[out_spec, part_spec, part_spec],
         out_shape=[
             jax.ShapeDtypeStruct((rows, kv_heads * group_cols), jnp.bfloat16),
             jax.ShapeDtypeStruct((key_rows, kv_cols), jnp.float32),
@@ -101,7 +102,7 @@
 
 
 def per_device(query_matrix, key_matrix, value_matrix, fwd_output, output_gradient, block_docs):
-    tokens, q_all = query_matrix.shape
+    _, q_all = query_matrix.shape
     kv_all = key_matrix.shape[1]
     peers = lax.axis_size("head")
     q_cols, kv_cols = q_all // peers, kv_all // peers
@@ -127,37 +128,50 @@
     qdoc = jnp.repeat(docs_of(place), BLK)[:, None]
     all_kv = kv_cols // HEAD_SIZE
     per = kv_cols // CHUNKS
+    core = lax.axis_index("head")
+    ctx_size = lax.axis_size("ctx")
+
+    def half(x, which):
+        return lax.dynamic_slice_in_dim(x, which * kv_cols, kv_cols, 1)
+
+    straight = jnp.concatenate([half(key_matrix, core), half(value_matrix, core)], axis=1)
+    across = jnp.concatenate([half(key_matrix, 1 - core), half(value_matrix, 1 - core)], axis=1)
+    behind_k, behind_v = [], []
+    for distance in range(REACH, 0, -1):
+        first = max(skip - (REACH - distance) * window_extent, 0)
+        if first >= window_extent:
+            continue
+        mine = shifted(straight, "ctx", distance)
+        other = lax.ppermute(across, ("ctx", "head"), [
+            (c * peers + p, (c + distance) * peers + (peers - 1 - p))
+            for c in range(ctx_size - distance) for p in range(peers)])
+        lead = jnp.where(core == 0, mine, other)
+        tail = jnp.where(core == 0, other, mine)
+        whole = jnp.concatenate([lead, tail], axis=0)[first:]
+        behind_k.append(whole[:, :kv_cols])
+        behind_v.append(whole[:, kv_cols:])
+    keys = jnp.concatenate(behind_k + [key_part], axis=0)
+    values = jnp.concatenate(behind_v + [value_part], axis=0)
     q_parts, k_parts, v_parts = [], [], []
     for j in range(CHUNKS):
-        with jax.named_scope(f"chunk{j}"):
-            key_here = key_part[:, j * per:(j + 1) * per]
-            value_here = value_part[:, j * per:(j + 1) * per]
-            pair = jnp.concatenate([key_here, value_here], axis=1)
-            behind = []
-            for distance in range(REACH, 0, -1):
-                first = max(skip - (REACH - distance) * window_extent, 0)
-                if first < window_extent:
-                    behind.append(shifted(pair[first:], "ctx", distance))
-            keys = jnp.concatenate([b[:, :per] for b in behind] + [key_here], axis=0)
-            values = jnp.concatenate([b[:, per:] for b in behind] + [value_here], axis=0)
-
-            query_sum, key_partial, value_partial = local_backward(
-                qdoc, kdoc, fused, q_cols, all_kv, j * per // HEAD_SIZE, keys, values)
-
-            both = jnp.concatenate([key_partial, value_partial], axis=1)
-            total = both[own - skip:]
-            for distance in range(1, REACH + 1):
-                begin = (REACH - distance) * window_extent
-                start = max(begin, skip)
-                if start >= begin + window_extent:
-                    continue
-                sent = shifted(
-                    both[start - skip:begin + window_extent - skip].astype(jnp.bfloat16),
-                    "ctx", -distance)
-                total = total.at[start - begin:].add(sent.astype(jnp.float32))
-            q_parts.append(query_sum)
-            k_parts.append(total[:, :per].astype(jnp.bfloat16))
-            v_parts.append(total[:, per:].astype(jnp.bfloat16))
+        query_sum, key_partial, value_partial = local_backward(
+            qdoc, kdoc, fused, q_cols, all_kv, j * per // HEAD_SIZE, keys, values,
+            per // HEAD_SIZE)
+
+        both = jnp.concatenate([key_partial, value_partial], axis=1)
+        total = both[own - skip:]
+        for distance in range(1, REACH + 1):
+            begin = (REACH - distance) * window_extent
+            start = max(begin, skip)
+            if start >= begin + window_extent:
+                continue
+            sent = shifted(
+                both[start - skip:begin + window_extent - skip].astype(jnp.bfloat16),
+                "ctx", -distance)
+            total = total.at[start - begin:].add(sent.astype(jnp.float32))
+        q_parts.append(query_sum)
+        k_parts.append(total[:, :per].astype(jnp.bfloat16))
+        v_parts.append(total[:, per:].astype(jnp.bfloat16))
     finished = jnp.concatenate(q_parts + k_parts + v_parts, axis=1)
     returned = lax.all_to_all(finished, "head", split_axis=0, concat_axis=1, tiled=True)
     width = finished.shape[1]

time: 103 us -> 119 us (1.16)
  the two profiles are of different devices: /device:TPU:0 before, /device:TPU:15 now
where the time goes in v8:
time: 119 us; the launch traced here: 118 us
  waiting for transfers between devices  36.5 us (31%)
  starting transfers between devices  26.9 us (23%)
  Pallas kernels  24 us (20%)
  local copies, waits for them, and re-layouts  19.4 us (16%)
  blocking collectives  6.52 us (5%)
  other arithmetic  3.66 us (3%)
    ppermute x6, waiting for transfers between devices, shifted(): return lax.ppermute(block, axis, route)  31.5 us
    pallas_call x2, Pallas kernels, local_backward(): pl.pallas_call(kernel, grid=(kv_heads,), in_specs=[pl.BlockSpec((rows, 1)...  24 us
    ppermute x6, starting transfers between devices, shifted(): return lax.ppermute(block, axis, route)  13.2 us
    unnamed x30, local copies, waits for them, and re-layouts  10.5 us
    all_to_all x1, starting transfers between devices, per_device(): lax.all_to_all(outgoing, 'head', split_axis=1, concat_axis=0, tiled=True)  7.12 us
    ppermute x2, starting transfers between devices, per_device(): lax.ppermute(across, ('ctx', 'head'), [(c * peers + p, (c + distance) * p...  6.63 us
    all_to_all x1, blocking collectives, per_device(): lax.all_to_all(finished, 'head', split_axis=0, concat_axis=1, tiled=True)  6.52 us
    all_to_all x1, local copies, waits for them, and re-layouts, per_device(): lax.all_to_all(outgoing, 'head', split_axis=1, concat_axis=0, tiled=True)  5.36 us
  transfers between devices with their start and end apart: 9, of which 4 were waited for; matrix products, arithmetic and copies ran while one was open for 7% of the time, Pallas kernels for 0%

profile of v8, /device:TPU:15, one launch (start us, length us, event | category | flops | bytes accessed | tf_op | source)
XLA Modules:
  0.0 118.0 jit_solution(5708585569919109911)
XLA Ops:
  0.7 2.3 %slice_dynamic-update-slice_fusion.5 = bf16[192,14336]{1,0:T(8,128)(2,1)} fusion(bf16[192,4096]{1,0:T(8,128)(2,1)} %param.18), kind=kLoop, calls=%fused_computation.18 | loop fusion | bytes 1572864
  2.9 2.2 %slice_dynamic-update-slice_fusion.4 = bf16[192,14336]{1,0:T(8,128)(2,1)} fusion(bf16[192,14336]{1,0:T(8,128)(2,1)} %slice_dynamic-update-slice_fusion.5, bf16[192,4096]{1,0:T(8,128)(2,1)} %param.22), kind=kLoop, calls=%fused_computation.17 | loop fusion | bytes 1572864
  5.1 0.9 slice_dynamic-update-slice_fusion.3
  6.1 0.7 slice_dynamic-update-slice_fusion.13
  6.8 0.7 slice_dynamic-update-slice_fusion.12
  7.5 1.0 slice_dynamic-update-slice_fusion.2
  8.5 1.0 slice_dynamic-update-slice_fusion.1
  9.5 1.0 slice_dynamic-update-slice_fusion
  10.6 0.7 constant_dynamic-slice_fusion.3
  11.3 0.8 constant_dynamic-slice_fusion.2
  12.1 3.7 %collective-permute-start.3 = (bf16[192,1024]{1,0:T(8,128)(2,1)S(1)}, bf16[192,1024]{1,0:T(8,128)(2,1)S(1)}, u32[]{:S(2)}, u32[]{:S(2)}) collective-permute-start(bf16[192,1024]{1,0:T(8,128)(2,1)S(1)} %pad_maximum_fusion.5), channel_id=1, source_target_pairs={{0,3},{1,2},{2,5},{3,4},{4,7},{5,6},{6,9},{7,8},{8,11},{9,10},{10,... | collective-permute-start | bytes 1179656 | tf_op jit(solution)/shard_map/ppermute | solution.py:145
  15.8 2.9 %collective-permute-start.1 = (bf16[192,1024]{1,0:T(8,128)(2,1)S(1)}, bf16[192,1024]{1,0:T(8,128)(2,1)S(1)}, u32[]{:S(2)}, u32[]{:S(2)}) collective-permute-start(bf16[192,1024]{1,0:T(8,128)(2,1)S(1)} %pad_maximum_fusion.5), channel_id=1, source_target_pairs={{0,5},{1,4},{2,7},{3,6},{4,9},{5,8},{6,11},{7,10},{8,13},{9,12},{1... | collective-permute-start | bytes 1179656 | tf_op jit(solution)/shard_map/ppermute | solution.py:145
  18.8 3.1 %collective-permute-start.2 = (bf16[192,1024]{1,0:T(8,128)(2,1)S(1)}, bf16[192,1024]{1,0:T(8,128)(2,1)S(1)}, u32[]{:S(2)}, u32[]{:S(2)}) collective-permute-start(bf16[192,1024]{1,0:T(8,128)(2,1)S(1)} %pad_maximum_fusion.4), channel_id=1, source_target_pairs={{0,2},{2,4},{4,6},{6,8},{8,10},{10,12},{12,14},{1,3},{3,5},{5,7},{... | collective-permute-start | bytes 1179656 | tf_op jit(solution)/shard_map/ppermute | solution.py:20
  22.0 1.9 %collective-permute-start = (bf16[192,1024]{1,0:T(8,128)(2,1)S(1)}, bf16[192,1024]{1,0:T(8,128)(2,1)S(1)}, u32[]{:S(2)}, u32[]{:S(2)}) collective-permute-start(bf16[192,1024]{1,0:T(8,128)(2,1)S(1)} %pad_maximum_fusion.4), channel_id=1, source_target_pairs={{0,4},{2,6},{4,8},{6,10},{8,12},{10,14},{1,5},{3,7},{5,9},{7,11},{... | collective-permute-start | bytes 1179656 | tf_op jit(solution)/shard_map/ppermute | solution.py:20
  23.9 5.4 %copy.21 = bf16[24,2,8,7168]{3,2,0,1:T(8,128)(2,1)} copy(bf16[24,2,8,7168]{3,2,1,0:T(8,128)(2,1)} %bitcast.6) | data formatting | bytes 11010048 | tf_op jit(solution)/shard_map/all_to_all | solution.py:113
  29.3 7.1 %all-to-all-start = ((bf16[192,2,7168]{2,0,1:T(8,128)(2,1)}), bf16[192,2,7168]{2,0,1:T(8,128)(2,1)}, u32[]{:S(2)}, u32[]{:S(2)}) async-start(bf16[192,2,7168]{2,0,1:T(8,128)(2,1)} %bitcast.23), calls=%async_computation | async-start | bytes 11010048 | tf_op jit(solution)/shard_map/all_to_all | solution.py:113
  36.5 4.9 %all-to-all-done = bf16[192,2,7168]{2,0,1:T(8,128)(2,1)} async-done(((bf16[192,2,7168]{2,0,1:T(8,128)(2,1)}), bf16[192,2,7168]{2,0,1:T(8,128)(2,1)}, u32[]{:S(2)}, u32[]{:S(2)}) %all-to-all-start) | async-done | bytes 5505056 | tf_op jit(solution)/shard_map/all_to_all | solution.py:113
  41.4 1.2 fusion.7
  43.0 7.9 %collective-permute-done = bf16[192,1024]{1,0:T(8,128)(2,1)S(1)} collective-permute-done((bf16[192,1024]{1,0:T(8,128)(2,1)S(1)}, bf16[192,1024]{1,0:T(8,128)(2,1)S(1)}, u32[]{:S(2)}, u32[]{:S(2)}) %collective-permute-start) | collective-permute-done | bytes 393248 | tf_op jit(solution)/shard_map/ppermute | solution.py:20
  51.0 0.2 fusion.1
  51.2 12.0 %shard_map.96 = (bf16[384,1024]{1,0:T(8,128)(2,1)S(1)}, f32[1024,256]{1,0:T(8,128)S(1)}, f32[1024,256]{1,0:T(8,128)S(1)}) custom-call(s32[384,1]{1,0:T(8,128)S(1)} %bitcast.19, s32[1,1024]{1,0:T(1,128)S(1)} %bitcast.21, bf16[384,7168]{1,0:T(8,128)(2,1)} %bitcast.2.q_ref.do_ref.o_ref, bf16[384,7168]{1,0:T(8,128)(2,1)} %bitcast.2.q_ref.do_ref.o_ref, ...), custom_call_target="tpu_custom_call" | custom-call | tf_op jit(solution)/shard_map/pallas_call | solution.py:85
  63.2 12.0 %shard_map.95 = (bf16[384,1024]{1,0:T(8,128)(2,1)S(1)}, f32[1024,256]{1,0:T(8,128)S(1)}, f32[1024,256]{1,0:T(8,128)S(1)}) custom-call(s32[384,1]{1,0:T(8,128)S(1)} %bitcast.20, s32[1,1024]{1,0:T(1,128)S(1)} %bitcast.22, bf16[384,7168]{1,0:T(8,128)(2,1)} %bitcast.2.q_ref.do_ref.o_ref, bf16[384,7168]{1,0:T(8,128)(2,1)} %bitcast.2.q_ref.do_ref.o_ref, ...), custom_call_target="tpu_custom_call" | custom-call | tf_op jit(solution)/shard_map/pallas_call | solution.py:85
  75.7 1.9 %collective-permute-start.6 = (bf16[384,512]{1,0:T(8,128)(2,1)S(1)}, bf16[384,512]{1,0:T(8,128)(2,1)S(1)}, u32[]{:S(2)}, u32[]{:S(2)}) collective-permute-start(bf16[384,512]{1,0:T(8,128)(2,1)S(1)} %slice.223), channel_id=1, source_target_pairs={{2,0},{4,2},{6,4},{8,6},{10,8},{12,10},{14,12},{3,1},{5,3},{7,5},{... | collective-permute-start | bytes 1179656 | tf_op jit(solution)/shard_map/ppermute | solution.py:20
  78.1 1.9 %collective-permute-start.7 = (bf16[256,512]{1,0:T(8,128)(2,1)S(1)}, bf16[256,512]{1,0:T(8,128)(2,1)S(1)}, u32[]{:S(2)}, u32[]{:S(2)}) collective-permute-start(bf16[256,512]{1,0:T(8,128)(2,1)S(1)} %slice.225), channel_id=1, source_target_pairs={{4,0},{6,2},{8,4},{10,6},{12,8},{14,10},{5,1},{7,3},{9,5},{11,7},{... | collective-permute-start | bytes 786440 | tf_op jit(solution)/shard_map/ppermute | solution.py:20
  80.0 1.9 %collective-permute-start.5 = (bf16[256,512]{1,0:T(8,128)(2,1)S(1)}, bf16[256,512]{1,0:T(8,128)(2,1)S(1)}, u32[]{:S(2)}, u32[]{:S(2)}) collective-permute-start(bf16[256,512]{1,0:T(8,128)(2,1)S(1)} %slice.220), channel_id=1, source_target_pairs={{4,0},{6,2},{8,4},{10,6},{12,8},{14,10},{5,1},{7,3},{9,5},{11,7},{... | collective-permute-start | bytes 786440 | tf_op jit(solution)/shard_map/ppermute | solution.py:20
  82.0 2.3 %collective-permute-start.4 = (bf16[384,512]{1,0:T(8,128)(2,1)S(1)}, bf16[384,512]{1,0:T(8,128)(2,1)S(1)}, u32[]{:S(2)}, u32[]{:S(2)}) collective-permute-start(bf16[384,512]{1,0:T(8,128)(2,1)S(1)} %slice.218), channel_id=1, source_target_pairs={{2,0},{4,2},{6,4},{8,6},{10,8},{12,10},{14,12},{3,1},{5,3},{7,5},{... | collective-permute-start | bytes 1179656 | tf_op jit(solution)/shard_map/ppermute | solution.py:20
  84.4 4.3 %collective-permute-done.6 = bf16[384,512]{1,0:T(8,128)(2,1)S(1)} collective-permute-done((bf16[384,512]{1,0:T(8,128)(2,1)S(1)}, bf16[384,512]{1,0:T(8,128)(2,1)S(1)}, u32[]{:S(2)}, u32[]{:S(2)}) %collective-permute-start.6) | collective-permute-done | bytes 393248 | tf_op jit(solution)/shard_map/ppermute | solution.py:20
  89.1 19.3 %collective-permute-done.4 = bf16[384,512]{1,0:T(8,128)(2,1)S(1)} collective-permute-done((bf16[384,512]{1,0:T(8,128)(2,1)S(1)}, bf16[384,512]{1,0:T(8,128)(2,1)S(1)}, u32[]{:S(2)}, u32[]{:S(2)}) %collective-permute-start.4) | collective-permute-done | bytes 393248 | tf_op jit(solution)/shard_map/ppermute | solution.py:20
  108.8 6.5 %all_to_all.38 = bf16[2,192,3072]{2,1,0:T(8,128)(2,1)S(1)} all-to-all(bf16[2,192,3072]{2,1,0:T(8,128)(2,1)S(1)} %bitcast.27), channel_id=1, replica_groups=mesh['groups'=2,'ctx'=8,'head'=2] {'head'}, dimensions={0} | all-to-all | bytes 4718592 | tf_op jit(solution)/shard_map/all_to_all | solution.py:176
  115.4 0.2 copy.16
  115.8 1.3 %pad_maximum_fusion = bf16[192,4096]{1,0:T(8,128)(2,1)} fusion(bf16[192,2048]{1,0:T(8,128)(2,1)S(1)} %get-tuple-element.86, bf16[192,2048]{1,0:T(8,128)(2,1)S(1)} %get-tuple-element.85), kind=kLoop, calls=%fused_computation.1 | loop fusion | flops 3145728 | bytes 3145728 | tf_op jit(solution)/shard_map/concatenate | solution.py:180
  117.0 1.0 pad_maximum_fusion.6
  (53 shorter events, 2.6 us)
Async XLA Ops:
  0.6 4.5 %copy-start.2 = (bf16[192,4096]{1,0:T(8,128)(2,1)S(1)}, bf16[192,4096]{1,0:T(8,128)(2,1)}, u32[]{:S(2)}) copy-start(bf16[192,4096]{1,0:T(8,128)(2,1)} %param.21) | copy-start | bytes 4718596
  0.6 5.4 %copy-start.3 = (bf16[192,1024]{1,0:T(8,128)(2,1)S(1)}, bf16[192,1024]{1,0:T(8,128)(2,1)}, u32[]{:S(2)}) copy-start(bf16[192,1024]{1,0:T(8,128)(2,1)} %param.19) | copy-start | bytes 1179652
  0.7 6.1 %copy-start.4 = (bf16[192,1024]{1,0:T(8,128)(2,1)S(1)}, bf16[192,1024]{1,0:T(8,128)(2,1)}, u32[]{:S(2)}) copy-start(bf16[192,1024]{1,0:T(8,128)(2,1)} %param.20) | copy-start | bytes 1179652
  2.9 4.6 %copy-start = (bf16[192,4096]{1,0:T(8,128)(2,1)S(1)}, bf16[192,4096]{1,0:T(8,128)(2,1)}, u32[]{:S(2)}) copy-start(bf16[192,4096]{1,0:T(8,128)(2,1)} %param.18) | copy-start | bytes 4718596
  5.1 3.4 %copy-start.1 = (bf16[192,4096]{1,0:T(8,128)(2,1)S(1)}, bf16[192,4096]{1,0:T(8,128)(2,1)}, u32[]{:S(2)}) copy-start(bf16[192,4096]{1,0:T(8,128)(2,1)} %param.22) | copy-start | bytes 4718596
  12.1 30.8 %collective-permute-start.3 = (bf16[192,1024]{1,0:T(8,128)(2,1)S(1)}, bf16[192,1024]{1,0:T(8,128)(2,1)S(1)}, u32[]{:S(2)}, u32[]{:S(2)}) collective-permute-start(bf16[192,1024]{1,0:T(8,128)(2,1)S(1)} %pad_maximum_fusion.5), channel_id=1, source_target_pairs={{0,3},{1,2},{2,5},{3,4},{4,7},{5,6},{6,9},{7,8},{8,11},{9,10},{10,... | collective-permute-start | bytes 1179656 | tf_op jit(solution)/shard_map/ppermute | solution.py:145
  15.8 27.2 %collective-permute-start.1 = (bf16[192,1024]{1,0:T(8,128)(2,1)S(1)}, bf16[192,1024]{1,0:T(8,128)(2,1)S(1)}, u32[]{:S(2)}, u32[]{:S(2)}) collective-permute-start(bf16[192,1024]{1,0:T(8,128)(2,1)S(1)} %pad_maximum_fusion.5), channel_id=1, source_target_pairs={{0,5},{1,4},{2,7},{3,6},{4,9},{5,8},{6,11},{7,10},{8,13},{9,12},{1... | collective-permute-start | bytes 1179656 | tf_op jit(solution)/shard_map/ppermute | solution.py:145
  18.8 24.1 %collective-permute-start.2 = (bf16[192,1024]{1,0:T(8,128)(2,1)S(1)}, bf16[192,1024]{1,0:T(8,128)(2,1)S(1)}, u32[]{:S(2)}, u32[]{:S(2)}) collective-permute-start(bf16[192,1024]{1,0:T(8,128)(2,1)S(1)} %pad_maximum_fusion.4), channel_id=1, source_target_pairs={{0,2},{2,4},{4,6},{6,8},{8,10},{10,12},{12,14},{1,3},{3,5},{5,7},{... | collective-permute-start | bytes 1179656 | tf_op jit(solution)/shard_map/ppermute | solution.py:20
  22.0 28.9 %collective-permute-start = (bf16[192,1024]{1,0:T(8,128)(2,1)S(1)}, bf16[192,1024]{1,0:T(8,128)(2,1)S(1)}, u32[]{:S(2)}, u32[]{:S(2)}) collective-permute-start(bf16[192,1024]{1,0:T(8,128)(2,1)S(1)} %pad_maximum_fusion.4), channel_id=1, source_target_pairs={{0,4},{2,6},{4,8},{6,10},{8,12},{10,14},{1,5},{3,7},{5,9},{7,11},{... | collective-permute-start | bytes 1179656 | tf_op jit(solution)/shard_map/ppermute | solution.py:20
  29.2 7.1 %copy-start.5 = (s32[24]{0:T(128)S(1)}, s32[24]{0:T(128)}, u32[]{:S(2)}) copy-start(s32[24]{0:T(128)} %param.23) | copy-start | bytes 292
  29.3 12.2 %all-to-all-start = ((bf16[192,2,7168]{2,0,1:T(8,128)(2,1)}), bf16[192,2,7168]{2,0,1:T(8,128)(2,1)}, u32[]{:S(2)}, u32[]{:S(2)}) async-start(bf16[192,2,7168]{2,0,1:T(8,128)(2,1)} %bitcast.23), calls=%async_computation | async-start | bytes 11010048 | tf_op jit(solution)/shard_map/all_to_all | solution.py:113
  75.7 13.1 %collective-permute-start.6 = (bf16[384,512]{1,0:T(8,128)(2,1)S(1)}, bf16[384,512]{1,0:T(8,128)(2,1)S(1)}, u32[]{:S(2)}, u32[]{:S(2)}) collective-permute-start(bf16[384,512]{1,0:T(8,128)(2,1)S(1)} %slice.223), channel_id=1, source_target_pairs={{2,0},{4,2},{6,4},{8,6},{10,8},{12,10},{14,12},{3,1},{5,3},{7,5},{... | collective-permute-start | bytes 1179656 | tf_op jit(solution)/shard_map/ppermute | solution.py:20
  78.1 10.8 %collective-permute-start.7 = (bf16[256,512]{1,0:T(8,128)(2,1)S(1)}, bf16[256,512]{1,0:T(8,128)(2,1)S(1)}, u32[]{:S(2)}, u32[]{:S(2)}) collective-permute-start(bf16[256,512]{1,0:T(8,128)(2,1)S(1)} %slice.225), channel_id=1, source_target_pairs={{4,0},{6,2},{8,4},{10,6},{12,8},{14,10},{5,1},{7,3},{9,5},{11,7},{... | collective-permute-start | bytes 786440 | tf_op jit(solution)/shard_map/ppermute | solution.py:20
  80.0 28.5 %collective-permute-start.5 = (bf16[256,512]{1,0:T(8,128)(2,1)S(1)}, bf16[256,512]{1,0:T(8,128)(2,1)S(1)}, u32[]{:S(2)}, u32[]{:S(2)}) collective-permute-start(bf16[256,512]{1,0:T(8,128)(2,1)S(1)} %slice.220), channel_id=1, source_target_pairs={{4,0},{6,2},{8,4},{10,6},{12,8},{14,10},{5,1},{7,3},{9,5},{11,7},{... | collective-permute-start | bytes 786440 | tf_op jit(solution)/shard_map/ppermute | solution.py:20
  82.0 26.5 %collective-permute-start.4 = (bf16[384,512]{1,0:T(8,128)(2,1)S(1)}, bf16[384,512]{1,0:T(8,128)(2,1)S(1)}, u32[]{:S(2)}, u32[]{:S(2)}) collective-permute-start(bf16[384,512]{1,0:T(8,128)(2,1)S(1)} %slice.218), channel_id=1, source_target_pairs={{2,0},{4,2},{6,4},{8,6},{10,8},{12,10},{14,12},{3,1},{5,3},{7,5},{... | collective-permute-start | bytes 1179656 | tf_op jit(solution)/shard_map/ppermute | solution.py:20

commit v9 on v7

--- a/solution.py
+++ b/solution.py
@@ -37,33 +37,32 @@
             [do_ref[rows, pl.ds(r * HEAD_SIZE, HEAD_SIZE)] for r in range(query_group)], axis=0)
         outs = jnp.concatenate(
             [o_ref[rows, pl.ds(r * HEAD_SIZE, HEAD_SIZE)] for r in range(query_group)], axis=0)
-        product = dos.astype(jnp.float32) * outs.astype(jnp.float32)
-        delta = jnp.sum(product.T, axis=0, keepdims=True)
-        qd = qdoc_ref[:, rows]
-        kd = kdoc_ref[pl.ds(k0, window), :]
-        qpos = lax.broadcasted_iota(jnp.int32, (window, BLK), 1) + (key_offset + qb * BLK)
-        kpos = lax.broadcasted_iota(jnp.int32, (window, BLK), 0) + k0
-        allowed = (kd == qd) & (kpos <= qpos)
-        mask = jnp.concatenate([allowed] * query_group, axis=1)
+        delta = jnp.sum(dos.astype(jnp.float32) * outs.astype(jnp.float32), axis=1, keepdims=True)
+        qd = qdoc_ref[rows, :]
+        kd = kdoc_ref[:, pl.ds(k0, window)]
+        qpos = lax.broadcasted_iota(jnp.int32, (BLK, window), 0) + (key_offset + qb * BLK)
+        kpos = lax.broadcasted_iota(jnp.int32, (BLK, window), 1) + k0
+        allowed = (qd == kd) & (kpos <= qpos)
+        mask = jnp.concatenate([allowed] * query_group, axis=0)
         scores = scale * lax.dot_general(
-            kwin, qs, (((1,), (1,)), ((), ())), preferred_element_type=jnp.float32)
+            qs, kwin, (((1,), (1,)), ((), ())), preferred_element_type=jnp.float32)
         masked = jnp.where(mask, scores, -1e30)
-        top = jnp.max(masked, axis=0, keepdims=True)
-        total = jnp.sum(jnp.exp(masked - top), axis=0, keepdims=True)
+        top = jnp.max(masked, axis=1, keepdims=True)
+        total = jnp.sum(jnp.where(mask, jnp.exp(masked - top), 0.0), axis=1, keepdims=True)
         lse = top + jnp.log(total)
-        probs = jnp.exp(masked - lse)
+        probs = jnp.where(mask, jnp.exp(masked - lse), 0.0)
         dprob = lax.dot_general(
-            vwin, dos, (((1,), (1,)), ((), ())), preferred_element_type=jnp.float32)
+            dos, vwin, (((1,), (1,)), ((), ())), preferred_element_type=jnp.float32)
         dscore = (probs * (dprob - delta)).astype(jnp.bfloat16)
-        dq = scale * lax.dot_general(
-            dscore, kwin, (((0,), (0,)), ((), ())), preferred_element_type=jnp.float32)
+        dq = scale * jnp.dot(dscore, kwin, preferred_element_type=jnp.float32)
         for r in range(query_group):
             dq_ref[rows, pl.ds(r * HEAD_SIZE, HEAD_SIZE)] = (
                 dq[r * BLK:(r + 1) * BLK].astype(dq_ref.dtype))
-        dk_ref[pl.ds(k0, window), :] += scale * jnp.dot(
-            dscore, qs, preferred_element_type=jnp.float32)
-        dv_ref[pl.ds(k0, window), :] += jnp.dot(
-            probs.astype(jnp.bfloat16), dos, preferred_element_type=jnp.float32)
+        dk_ref[pl.ds(k0, window), :] += scale * lax.dot_general(
+            dscore, qs, (((0,), (0,)), ((), ())), preferred_element_type=jnp.float32)
+        dv_ref[pl.ds(k0, window), :] += lax.dot_general(
+            probs.astype(jnp.bfloat16), dos, (((0,), (0,)), ((), ())),
+            preferred_element_type=jnp.float32)
 
 
 def local_backward(qdoc, kdoc, fused, q_cols, all_kv, head0, keys, values):
@@ -86,8 +85,8 @@
         kernel,
         grid=(kv_heads,),
         in_specs=[
-            pl.BlockSpec((1, rows), lambda g: (0, 0)),
-            pl.BlockSpec((key_rows, 1), lambda g: (0, 0)),
+            pl.BlockSpec((rows, 1), lambda g: (0, 0)),
+            pl.BlockSpec((1, key_rows), lambda g: (0, 0)),
             section(0), section(1), section(2), k_spec, k_spec,
         ],
         out_specs=[out_spec, k_spec, k_spec],
@@ -124,8 +123,8 @@
         return jnp.where(owner >= 0, docs, -1)
 
     key_docs = jnp.concatenate([docs_of(place - distance) for distance in range(REACH, -1, -1)])
-    kdoc = jnp.repeat(key_docs, BLK)[skip:][:, None]
-    qdoc = jnp.repeat(docs_of(place), BLK)[None, :]
+    kdoc = jnp.repeat(key_docs, BLK)[skip:][None, :]
+    qdoc = jnp.repeat(docs_of(place), BLK)[:, None]
     all_kv = kv_cols // HEAD_SIZE
     per = kv_cols // CHUNKS
     q_parts, k_parts, v_parts = [], [], []
@@ -158,7 +157,9 @@
         q_parts.append(query_sum)
         k_parts.append(total[:, :per].astype(jnp.bfloat16))
         v_parts.append(total[:, per:].astype(jnp.bfloat16))
-    finished = jnp.concatenate(q_parts + k_parts + v_parts, axis=1)
+    query_back = lax.all_to_all(
+        jnp.concatenate(q_parts, axis=1), "head", split_axis=0, concat_axis=1, tiled=True)
+    finished = jnp.concatenate(k_parts + v_parts, axis=1)
     returned = lax.all_to_all(finished, "head", split_axis=0, concat_axis=1, tiled=True)
     width = finished.shape[1]
 
@@ -166,7 +167,7 @@
         return jnp.concatenate(
             [returned[:, p * width + begin:p * width + begin + size] for p in range(peers)], axis=1)
 
-    return gather(0, q_cols), gather(q_cols, kv_cols), gather(q_cols + kv_cols, kv_cols)
+    return query_back, gather(0, kv_cols), gather(kv_cols, kv_cols)
 
 
 def solution(mesh):

time: 103 us -> 98.7 us (0.958)
  waiting for transfers between devices: 28 us -> 22.6 us
  blocking collectives: 13.8 us -> 17.5 us
  local copies, waits for them, and re-layouts: 9.89 us -> 8.56 us
  other arithmetic: 4.79 us -> 3.75 us
    ppermute x8, waiting for transfers between devices: 28 us -> 22.6 us  [shifted(): return lax.ppermute(block, axis, route)]
    all_to_all x0 -> x1, blocking collectives: none -> 5 us  [per_device(): lax.all_to_all(jnp.concatenate(q_parts, axis=1), 'head', split_axis=0, co...]
    all_to_all x1, blocking collectives: 5.63 us -> 4.37 us  [per_device(): lax.all_to_all(finished, 'head', split_axis=0, concat_axis=1, tiled=True)]
    concatenate x3 -> x2, other arithmetic: 2.84 us -> 1.59 us  [gather(): jnp.concatenate([returned[:, p * width + begin:p * width + begin + size]...]
    all_to_all x0 -> x1, local copies, waits for them, and re-layouts: none -> 1.24 us  [per_device(): lax.all_to_all(jnp.concatenate(q_parts, axis=1), 'head', split_axis=0, co...]
    unnamed x32 -> x28, local copies, waits for them, and re-layouts: 7.19 us -> 6.06 us
  transfers between devices with their start and end apart: 8 -> 8, of which waited for: 5 -> 4; matrix products, arithmetic and copies ran while one was open for 4% -> 4% of each run, Pallas kernels for 23% -> 24%
where the time goes in v9:
time: 98.7 us; the launch traced here: 98.2 us
  Pallas kernels  24 us (24%)
  waiting for transfers between devices  22.6 us (23%)
  starting transfers between devices  20.7 us (21%)
  blocking collectives  17.5 us (18%)
  local copies, waits for them, and re-layouts  8.56 us (9%)
  other arithmetic  3.75 us (4%)
  between operations  1.16 us (1%)
    pallas_call x2, Pallas kernels, local_backward(): pl.pallas_call(kernel, grid=(kv_heads,), in_specs=[pl.BlockSpec((rows, 1)...  24 us
    ppermute x8, waiting for transfers between devices, shifted(): return lax.ppermute(block, axis, route)  22.6 us
    ppermute x8, starting transfers between devices, shifted(): return lax.ppermute(block, axis, route)  20.7 us
    all_to_all x1, blocking collectives, per_device(): lax.all_to_all(outgoing, 'head', split_axis=1, concat_axis=0, tiled=True)  8.16 us
    unnamed x28, local copies, waits for them, and re-layouts  6.06 us
    all_to_all x1, blocking collectives, per_device(): lax.all_to_all(jnp.concatenate(q_parts, axis=1), 'head', split_axis=0, co...  5 us
    all_to_all x1, blocking collectives, per_device(): lax.all_to_all(finished, 'head', split_axis=0, concat_axis=1, tiled=True)  4.37 us
  transfers between devices with their start and end apart: 8, of which 4 were waited for; matrix products, arithmetic and copies ran while one was open for 4% of the time, Pallas kernels for 24%

profile of v9, /device:TPU:0, one launch (start us, length us, event | category | flops | bytes accessed | tf_op | source)
XLA Modules:
  0.0 98.2 jit_solution(1316105793767172957)
XLA Ops:
  0.7 1.4 %slice_dynamic-update-slice_fusion.5 = bf16[192,14336]{1,0:T(8,128)(2,1)S(1)} fusion(bf16[192,4096]{1,0:T(8,128)(2,1)} %param.18), kind=kLoop, calls=%fused_computation.10 | loop fusion | bytes 1572864
  2.0 1.3 %slice_dynamic-update-slice_fusion.4 = bf16[192,14336]{1,0:T(8,128)(2,1)S(1)} fusion(bf16[192,14336]{1,0:T(8,128)(2,1)S(1)} %slice_dynamic-update-slice_fusion.5, bf16[192,4096]{1,0:T(8,128)(2,1)} %param.22), kind=kLoop, calls=%fused_computation.9 | loop fusion | bytes 1572864
  3.6 0.2 copy-done.2
  4.0 0.4 copy.24
  4.4 8.2 %all_to_all.57 = bf16[192,2,7168]{2,0,1:T(8,128)(2,1)S(1)} all-to-all(bf16[192,2,7168]{2,0,1:T(8,128)(2,1)S(1)} %bitcast.34), channel_id=1, replica_groups=mesh['groups'=2,'ctx'=8,'head'=2] {'head'}, dimensions={1} | all-to-all | bytes 11010048 | tf_op jit(solution)/shard_map/all_to_all | solution.py:112
  12.5 2.4 %copy-done = bf16[192,2,7168]{2,0,1:T(8,128)(2,1)} copy-done((bf16[192,2,7168]{2,0,1:T(8,128)(2,1)}, bf16[192,2,7168]{2,0,1:T(8,128)(2,1)S(1)}, u32[]{:S(2)}) %copy-start) | copy-done | bytes 5505048
  15.0 5.0 %collective-permute-start = (bf16[256,512]{1,0:T(8,128)(2,1)S(1)}, bf16[256,512]{1,0:T(8,128)(2,1)S(1)}, u32[]{:S(2)}, u32[]{:S(2)}) collective-permute-start(bf16[256,512]{1,0:T(8,128)(2,1)S(1)} %fusion.3), channel_id=1, source_target_pairs={{0,4},{2,6},{4,8},{6,10},{8,12},{10,14},{1,5},{3,7},{5,9},{7,11},{... | collective-permute-start | bytes 786440 | tf_op jit(solution)/shard_map/ppermute | solution.py:20
  20.0 3.4 %collective-permute-start.1 = (bf16[384,512]{1,0:T(8,128)(2,1)S(1)}, bf16[384,512]{1,0:T(8,128)(2,1)S(1)}, u32[]{:S(2)}, u32[]{:S(2)}) collective-permute-start(bf16[384,512]{1,0:T(8,128)(2,1)S(1)} %pad_maximum_fusion.6), channel_id=1, source_target_pairs={{0,2},{2,4},{4,6},{6,8},{8,10},{10,12},{12,14},{1,3},{3,5},{5,7},{... | collective-permute-start | bytes 1179656 | tf_op jit(solution)/shard_map/ppermute | solution.py:20
  23.5 0.7 fusion.2
  24.2 3.5 %collective-permute-start.2 = (bf16[256,512]{1,0:T(8,128)(2,1)}, bf16[256,512]{1,0:T(8,128)(2,1)S(1)}, u32[]{:S(2)}, u32[]{:S(2)}) collective-permute-start(bf16[256,512]{1,0:T(8,128)(2,1)} %fusion.2), channel_id=1, source_target_pairs={{0,4},{2,6},{4,8},{6,10},{8,12},{10,14},{1,5},{3,7},{5,9},{7,11},{... | collective-permute-start | bytes 786440 | tf_op jit(solution)/shard_map/ppermute | solution.py:20
  27.7 3.4 %collective-permute-start.3 = (bf16[384,512]{1,0:T(8,128)(2,1)S(1)}, bf16[384,512]{1,0:T(8,128)(2,1)S(1)}, u32[]{:S(2)}, u32[]{:S(2)}) collective-permute-start(bf16[384,512]{1,0:T(8,128)(2,1)S(1)} %pad_maximum_fusion.7), channel_id=1, source_target_pairs={{0,2},{2,4},{4,6},{6,8},{8,10},{10,12},{12,14},{1,3},{3,5},{5,7},{... | collective-permute-start | bytes 1179656 | tf_op jit(solution)/shard_map/ppermute | solution.py:20
  31.5 0.1 copy.21
  31.7 1.6 %collective-permute-done.2 = bf16[256,512]{1,0:T(8,128)(2,1)S(1)} collective-permute-done((bf16[256,512]{1,0:T(8,128)(2,1)}, bf16[256,512]{1,0:T(8,128)(2,1)S(1)}, u32[]{:S(2)}, u32[]{:S(2)}) %collective-permute-start.2) | collective-permute-done | bytes 262176 | tf_op jit(solution)/shard_map/ppermute | solution.py:20
  33.5 12.0 %shard_map.95 = (bf16[384,1024]{1,0:T(8,128)(2,1)S(1)}, f32[1024,256]{1,0:T(8,128)S(1)}, f32[1024,256]{1,0:T(8,128)S(1)}) custom-call(s32[384,1]{1,0:T(8,128)S(1)} %bitcast.23, s32[1,1024]{1,0:T(1,128)S(1)} %bitcast.25, bf16[384,7168]{1,0:T(8,128)(2,1)} %bitcast.28, bf16[384,7168]{1,0:T(8,128)(2,1)} %bitcast.29, bf16[384,7168]{1,0:T(8,128)(2,1)} %bitcast.30, ...), custom_call_target="tpu_custom_call" | custom-call | tf_op jit(solution)/shard_map/pallas_call | solution.py:84
  45.5 0.1 constant_dynamic-update-slice_fusion.1
  45.6 0.2 constant_dynamic-update-slice_fusion
  45.8 0.1 convert.16
  46.0 1.5 %collective-permute-start.4 = (bf16[384,512]{1,0:T(8,128)(2,1)S(1)}, bf16[384,512]{1,0:T(8,128)(2,1)S(1)}, u32[]{:S(2)}, u32[]{:S(2)}) collective-permute-start(bf16[384,512]{1,0:T(8,128)(2,1)S(1)} %slice.257), channel_id=1, source_target_pairs={{2,0},{4,2},{6,4},{8,6},{10,8},{12,10},{14,12},{3,1},{5,3},{7,5},{... | collective-permute-start | bytes 1179656 | tf_op jit(solution)/shard_map/ppermute | solution.py:20
  47.6 12.0 %shard_map.96 = (bf16[384,1024]{1,0:T(8,128)(2,1)S(1)}, f32[1024,256]{1,0:T(8,128)S(1)}, f32[1024,256]{1,0:T(8,128)S(1)}) custom-call(s32[384,1]{1,0:T(8,128)S(1)} %bitcast.24, s32[1,1024]{1,0:T(1,128)S(1)} %bitcast.26, bf16[384,7168]{1,0:T(8,128)(2,1)} %bitcast.31, bf16[384,7168]{1,0:T(8,128)(2,1)} %bitcast.32, bf16[384,7168]{1,0:T(8,128)(2,1)} %bitcast.33, ...), custom_call_target="tpu_custom_call" | custom-call | tf_op jit(solution)/shard_map/pallas_call | solution.py:84
  59.9 0.1 convert.18
  60.1 1.3 %collective-permute-start.5 = (bf16[256,512]{1,0:T(8,128)(2,1)S(1)}, bf16[256,512]{1,0:T(8,128)(2,1)S(1)}, u32[]{:S(2)}, u32[]{:S(2)}) collective-permute-start(bf16[256,512]{1,0:T(8,128)(2,1)S(1)} %slice.259), channel_id=1, source_target_pairs={{4,0},{6,2},{8,4},{10,6},{12,8},{14,10},{5,1},{7,3},{9,5},{11,7},{... | collective-permute-start | bytes 786440 | tf_op jit(solution)/shard_map/ppermute | solution.py:20
  61.4 1.3 %collective-permute-start.6 = (bf16[384,512]{1,0:T(8,128)(2,1)S(1)}, bf16[384,512]{1,0:T(8,128)(2,1)S(1)}, u32[]{:S(2)}, u32[]{:S(2)}) collective-permute-start(bf16[384,512]{1,0:T(8,128)(2,1)S(1)} %slice.262), channel_id=1, source_target_pairs={{2,0},{4,2},{6,4},{8,6},{10,8},{12,10},{14,12},{3,1},{5,3},{7,5},{... | collective-permute-start | bytes 1179656 | tf_op jit(solution)/shard_map/ppermute | solution.py:20
  62.7 1.3 %collective-permute-start.7 = (bf16[256,512]{1,0:T(8,128)(2,1)S(1)}, bf16[256,512]{1,0:T(8,128)(2,1)S(1)}, u32[]{:S(2)}, u32[]{:S(2)}) collective-permute-start(bf16[256,512]{1,0:T(8,128)(2,1)S(1)} %slice.264), channel_id=1, source_target_pairs={{4,0},{6,2},{8,4},{10,6},{12,8},{14,10},{5,1},{7,3},{9,5},{11,7},{... | collective-permute-start | bytes 786440 | tf_op jit(solution)/shard_map/ppermute | solution.py:20
  64.0 0.1 pad_maximum_fusion
  64.1 5.0 %all_to_all.58 = bf16[2,192,2048]{2,1,0:T(8,128)(2,1)S(1)} all-to-all(bf16[2,192,2048]{2,1,0:T(8,128)(2,1)S(1)} %bitcast.36), channel_id=1, replica_groups=mesh['groups'=2,'ctx'=8,'head'=2] {'head'}, dimensions={0} | all-to-all | bytes 3145728 | tf_op jit(solution)/shard_map/all_to_all | solution.py:160
  69.1 1.2 %copy.18 = bf16[2,24,8,2048]{3,2,0,1:T(8,128)(2,1)} copy(bf16[2,24,8,2048]{3,2,1,0:T(8,128)(2,1)S(1)} %bitcast.37) | data formatting | bytes 3145728 | tf_op jit(solution)/shard_map/all_to_all | solution.py:160
  70.5 9.8 %collective-permute-done.5 = bf16[256,512]{1,0:T(8,128)(2,1)S(1)} collective-permute-done((bf16[256,512]{1,0:T(8,128)(2,1)S(1)}, bf16[256,512]{1,0:T(8,128)(2,1)S(1)}, u32[]{:S(2)}, u32[]{:S(2)}) %collective-permute-start.5) | collective-permute-done | bytes 262176 | tf_op jit(solution)/shard_map/ppermute | solution.py:20
  80.5 0.2 collective-permute-done.6
  80.8 11.0 %collective-permute-done.7 = bf16[256,512]{1,0:T(8,128)(2,1)S(1)} collective-permute-done((bf16[256,512]{1,0:T(8,128)(2,1)S(1)}, bf16[256,512]{1,0:T(8,128)(2,1)S(1)}, u32[]{:S(2)}, u32[]{:S(2)}) %collective-permute-start.7) | collective-permute-done | bytes 262176 | tf_op jit(solution)/shard_map/ppermute | solution.py:20
  92.1 4.4 %all_to_all.59 = bf16[2,192,1024]{2,1,0:T(8,128)(2,1)S(1)} all-to-all(bf16[2,192,1024]{2,1,0:T(8,128)(2,1)S(1)} %bitcast.39), channel_id=1, replica_groups=mesh['groups'=2,'ctx'=8,'head'=2] {'head'}, dimensions={0} | all-to-all | bytes 1572864 | tf_op jit(solution)/shard_map/all_to_all | solution.py:163
  96.6 0.8 pad_maximum_fusion.9
  97.4 0.8 pad_maximum_fusion.8
  (57 shorter events, 2.2 us)
Async XLA Ops:
  0.6 2.9 %copy-start.1 = (bf16[192,4096]{1,0:T(8,128)(2,1)S(1)}, bf16[192,4096]{1,0:T(8,128)(2,1)}, u32[]{:S(2)}) copy-start(bf16[192,4096]{1,0:T(8,128)(2,1)} %param.18) | copy-start | bytes 4718596
  0.6 2.7 %copy-start.3 = (bf16[192,4096]{1,0:T(8,128)(2,1)S(1)}, bf16[192,4096]{1,0:T(8,128)(2,1)}, u32[]{:S(2)}) copy-start(bf16[192,4096]{1,0:T(8,128)(2,1)} %param.21) | copy-start | bytes 4718596
  0.7 2.8 %copy-start.4 = (bf16[192,1024]{1,0:T(8,128)(2,1)S(1)}, bf16[192,1024]{1,0:T(8,128)(2,1)}, u32[]{:S(2)}) copy-start(bf16[192,1024]{1,0:T(8,128)(2,1)} %param.19) | copy-start | bytes 1179652
  0.7 2.8 %copy-start.5 = (bf16[192,1024]{1,0:T(8,128)(2,1)S(1)}, bf16[192,1024]{1,0:T(8,128)(2,1)}, u32[]{:S(2)}) copy-start(bf16[192,1024]{1,0:T(8,128)(2,1)} %param.20) | copy-start | bytes 1179652
  2.0 1.8 %copy-start.2 = (bf16[192,4096]{1,0:T(8,128)(2,1)S(1)}, bf16[192,4096]{1,0:T(8,128)(2,1)}, u32[]{:S(2)}) copy-start(bf16[192,4096]{1,0:T(8,128)(2,1)} %param.22) | copy-start | bytes 4718596
  12.5 2.4 %copy-start = (bf16[192,2,7168]{2,0,1:T(8,128)(2,1)}, bf16[192,2,7168]{2,0,1:T(8,128)(2,1)S(1)}, u32[]{:S(2)}) copy-start(bf16[192,2,7168]{2,0,1:T(8,128)(2,1)S(1)} %all_to_all.57) | copy-start | bytes 16515076
  12.5 18.6 %copy-start.6 = (s32[24]{0:T(128)S(1)}, s32[24]{0:T(128)}, u32[]{:S(2)}) copy-start(s32[24]{0:T(128)} %param.23) | copy-start | bytes 292
  15.0 16.6 %collective-permute-start = (bf16[256,512]{1,0:T(8,128)(2,1)S(1)}, bf16[256,512]{1,0:T(8,128)(2,1)S(1)}, u32[]{:S(2)}, u32[]{:S(2)}) collective-permute-start(bf16[256,512]{1,0:T(8,128)(2,1)S(1)} %fusion.3), channel_id=1, source_target_pairs={{0,4},{2,6},{4,8},{6,10},{8,12},{10,14},{1,5},{3,7},{5,9},{7,11},{... | collective-permute-start | bytes 786440 | tf_op jit(solution)/shard_map/ppermute | solution.py:20
  20.0 13.2 %collective-permute-start.1 = (bf16[384,512]{1,0:T(8,128)(2,1)S(1)}, bf16[384,512]{1,0:T(8,128)(2,1)S(1)}, u32[]{:S(2)}, u32[]{:S(2)}) collective-permute-start(bf16[384,512]{1,0:T(8,128)(2,1)S(1)} %pad_maximum_fusion.6), channel_id=1, source_target_pairs={{0,2},{2,4},{4,6},{6,8},{8,10},{10,12},{12,14},{1,3},{3,5},{5,7},{... | collective-permute-start | bytes 1179656 | tf_op jit(solution)/shard_map/ppermute | solution.py:20
  24.2 9.0 %collective-permute-start.2 = (bf16[256,512]{1,0:T(8,128)(2,1)}, bf16[256,512]{1,0:T(8,128)(2,1)S(1)}, u32[]{:S(2)}, u32[]{:S(2)}) collective-permute-start(bf16[256,512]{1,0:T(8,128)(2,1)} %fusion.2), channel_id=1, source_target_pairs={{0,4},{2,6},{4,8},{6,10},{8,12},{10,14},{1,5},{3,7},{5,9},{7,11},{... | collective-permute-start | bytes 786440 | tf_op jit(solution)/shard_map/ppermute | solution.py:20
  27.7 19.8 %collective-permute-start.3 = (bf16[384,512]{1,0:T(8,128)(2,1)S(1)}, bf16[384,512]{1,0:T(8,128)(2,1)S(1)}, u32[]{:S(2)}, u32[]{:S(2)}) collective-permute-start(bf16[384,512]{1,0:T(8,128)(2,1)S(1)} %pad_maximum_fusion.7), channel_id=1, source_target_pairs={{0,2},{2,4},{4,6},{6,8},{8,10},{10,12},{12,14},{1,3},{3,5},{5,7},{... | collective-permute-start | bytes 1179656 | tf_op jit(solution)/shard_map/ppermute | solution.py:20
  46.0 24.4 %collective-permute-start.4 = (bf16[384,512]{1,0:T(8,128)(2,1)S(1)}, bf16[384,512]{1,0:T(8,128)(2,1)S(1)}, u32[]{:S(2)}, u32[]{:S(2)}) collective-permute-start(bf16[384,512]{1,0:T(8,128)(2,1)S(1)} %slice.257), channel_id=1, source_target_pairs={{2,0},{4,2},{6,4},{8,6},{10,8},{12,10},{14,12},{3,1},{5,3},{7,5},{... | collective-permute-start | bytes 1179656 | tf_op jit(solution)/shard_map/ppermute | solution.py:20
  60.1 20.2 %collective-permute-start.5 = (bf16[256,512]{1,0:T(8,128)(2,1)S(1)}, bf16[256,512]{1,0:T(8,128)(2,1)S(1)}, u32[]{:S(2)}, u32[]{:S(2)}) collective-permute-start(bf16[256,512]{1,0:T(8,128)(2,1)S(1)} %slice.259), channel_id=1, source_target_pairs={{4,0},{6,2},{8,4},{10,6},{12,8},{14,10},{5,1},{7,3},{9,5},{11,7},{... | collective-permute-start | bytes 786440 | tf_op jit(solution)/shard_map/ppermute | solution.py:20
  61.4 19.3 %collective-permute-start.6 = (bf16[384,512]{1,0:T(8,128)(2,1)S(1)}, bf16[384,512]{1,0:T(8,128)(2,1)S(1)}, u32[]{:S(2)}, u32[]{:S(2)}) collective-permute-start(bf16[384,512]{1,0:T(8,128)(2,1)S(1)} %slice.262), channel_id=1, source_target_pairs={{2,0},{4,2},{6,4},{8,6},{10,8},{12,10},{14,12},{3,1},{5,3},{7,5},{... | collective-permute-start | bytes 1179656 | tf_op jit(solution)/shard_map/ppermute | solution.py:20
  62.7 29.1 %collective-permute-start.7 = (bf16[256,512]{1,0:T(8,128)(2,1)S(1)}, bf16[256,512]{1,0:T(8,128)(2,1)S(1)}, u32[]{:S(2)}, u32[]{:S(2)}) collective-permute-start(bf16[256,512]{1,0:T(8,128)(2,1)S(1)} %slice.264), channel_id=1, source_target_pairs={{4,0},{6,2},{8,4},{10,6},{12,8},{14,10},{5,1},{7,3},{9,5},{11,7},{... | collective-permute-start | bytes 786440 | tf_op jit(solution)/shard_map/ppermute | solution.py:20

commit v10 on v9

--- a/solution.py
+++ b/solution.py
@@ -11,7 +11,8 @@
 BLK = 128
 REACH = 2
 DOC_MOST = 6
-CHUNKS = 2
+CHUNKS = 4
+ENTRY_CHUNKS = 2
 
 
 def shifted(block, axis, distance):
@@ -48,9 +49,9 @@
             qs, kwin, (((1,), (1,)), ((), ())), preferred_element_type=jnp.float32)
         masked = jnp.where(mask, scores, -1e30)
         top = jnp.max(masked, axis=1, keepdims=True)
-        total = jnp.sum(jnp.where(mask, jnp.exp(masked - top), 0.0), axis=1, keepdims=True)
+        total = jnp.sum(jnp.exp(masked - top), axis=1, keepdims=True)
         lse = top + jnp.log(total)
-        probs = jnp.where(mask, jnp.exp(masked - lse), 0.0)
+        probs = jnp.exp(masked - lse)
         dprob = lax.dot_general(
             dos, vwin, (((1,), (1,)), ((), ())), preferred_element_type=jnp.float32)
         dscore = (probs * (dprob - delta)).astype(jnp.bfloat16)
@@ -65,10 +66,10 @@
             preferred_element_type=jnp.float32)
 
 
-def local_backward(qdoc, kdoc, fused, q_cols, all_kv, head0, keys, values):
+def local_backward(qdoc, kdoc, fused, q_cols, all_kv, head0, keys, values, key_head0, kv_heads):
     rows = fused.shape[0]
-    key_rows, kv_cols = keys.shape
-    kv_heads = kv_cols // HEAD_SIZE
+    key_rows = keys.shape[0]
+    kv_cols = kv_heads * HEAD_SIZE
     query_group = q_cols // HEAD_SIZE // all_kv
     group_cols = query_group * HEAD_SIZE
     kernel = functools.partial(
@@ -80,7 +81,8 @@
 
     out_spec = pl.BlockSpec((rows, group_cols), lambda g: (0, g))
 
-    k_spec = pl.BlockSpec((key_rows, HEAD_SIZE), lambda g: (0, g))
+    k_spec = pl.BlockSpec((key_rows, HEAD_SIZE), lambda g: (0, key_head0 + g))
+    part_spec = pl.BlockSpec((key_rows, HEAD_SIZE), lambda g: (0, g))
     return pl.pallas_call(
         kernel,
         grid=(kv_heads,),
@@ -89,7 +91,7 @@
             pl.BlockSpec((1, key_rows), lambda g: (0, 0)),
             section(0), section(1), section(2), k_spec, k_spec,
         ],
-        out_specs=[out_spec, k_spec, k_spec],
+        out_specs=[out_spec, part_spec, part_spec],
         out_shape=[
             jax.ShapeDtypeStruct((rows, kv_heads * group_cols), jnp.bfloat16),
             jax.ShapeDtypeStruct((key_rows, kv_cols), jnp.float32),
@@ -127,21 +129,26 @@
     qdoc = jnp.repeat(docs_of(place), BLK)[:, None]
     all_kv = kv_cols // HEAD_SIZE
     per = kv_cols // CHUNKS
-    q_parts, k_parts, v_parts = [], [], []
-    for j in range(CHUNKS):
-        key_here = key_part[:, j * per:(j + 1) * per]
-        value_here = value_part[:, j * per:(j + 1) * per]
+    entry_per = kv_cols // ENTRY_CHUNKS
+    entries = []
+    for e in range(ENTRY_CHUNKS):
+        key_here = key_part[:, e * entry_per:(e + 1) * entry_per]
+        value_here = value_part[:, e * entry_per:(e + 1) * entry_per]
         pair = jnp.concatenate([key_here, value_here], axis=1)
         behind = []
         for distance in range(REACH, 0, -1):
             first = max(skip - (REACH - distance) * window_extent, 0)
             if first < window_extent:
                 behind.append(shifted(pair[first:], "ctx", distance))
-        keys = jnp.concatenate([b[:, :per] for b in behind] + [key_here], axis=0)
-        values = jnp.concatenate([b[:, per:] for b in behind] + [value_here], axis=0)
-
+        keys = jnp.concatenate([b[:, :entry_per] for b in behind] + [key_here], axis=0)
+        values = jnp.concatenate([b[:, entry_per:] for b in behind] + [value_here], axis=0)
+        entries.append((keys, values))
+    q_parts, k_parts, v_parts = [], [], []
+    for j in range(CHUNKS):
+        keys, values = entries[j * per // entry_per]
         query_sum, key_partial, value_partial = local_backward(
-            qdoc, kdoc, fused, q_cols, all_kv, j * per // HEAD_SIZE, keys, values)
+            qdoc, kdoc, fused, q_cols, all_kv, j * per // HEAD_SIZE, keys, values,
+            (j * per % entry_per) // HEAD_SIZE, per // HEAD_SIZE)
 
         both = jnp.concatenate([key_partial, value_partial], axis=1)
         total = both[own - skip:]
@@ -157,9 +164,7 @@
         q_parts.append(query_sum)
         k_parts.append(total[:, :per].astype(jnp.bfloat16))
         v_parts.append(total[:, per:].astype(jnp.bfloat16))
-    query_back = lax.all_to_all(
-        jnp.concatenate(q_parts, axis=1), "head", split_axis=0, concat_axis=1, tiled=True)
-    finished = jnp.concatenate(k_parts + v_parts, axis=1)
+    finished = jnp.concatenate(q_parts + k_parts + v_parts, axis=1)
     returned = lax.all_to_all(finished, "head", split_axis=0, concat_axis=1, tiled=True)
     width = finished.shape[1]
 
@@ -167,7 +172,7 @@
         return jnp.concatenate(
             [returned[:, p * width + begin:p * width + begin + size] for p in range(peers)], axis=1)
 
-    return query_back, gather(0, kv_cols), gather(kv_cols, kv_cols)
+    return gather(0, q_cols), gather(q_cols, kv_cols), gather(q_cols + kv_cols, kv_cols)
 
 
 def solution(mesh):

time: 98.7 us -> 109 us (1.10)
  waiting for transfers between devices: 22.6 us -> 30.1 us
  starting transfers between devices: 20.7 us -> 25.6 us
  blocking collectives: 17.5 us -> 13.8 us
    ppermute x8 -> x12, waiting for transfers between devices: 22.6 us -> 30.1 us  [shifted(): return lax.ppermute(block, axis, route)]
    all_to_all x1 -> x0, blocking collectives: 5 us -> none  [per_device(): lax.all_to_all(jnp.concatenate(q_parts, axis=1), 'head', split_axis=0, co...]
    ppermute x8 -> x12, starting transfers between devices: 20.7 us -> 25.6 us  [shifted(): return lax.ppermute(block, axis, route)]
    unnamed x28 -> x41, local copies, waits for them, and re-layouts: 6.06 us -> 7.39 us
    all_to_all x1, blocking collectives: 4.37 us -> 5.63 us  [per_device(): lax.all_to_all(finished, 'head', split_axis=0, concat_axis=1, tiled=True)]
    concatenate x2 -> x3, other arithmetic: 1.59 us -> 2.84 us  [gather(): jnp.concatenate([returned[:, p * width + begin:p * width + begin + size]...]
    all_to_all x1 -> x0, local copies, waits for them, and re-layouts: 1.24 us -> none  [per_device(): lax.all_to_all(jnp.concatenate(q_parts, axis=1), 'head', split_axis=0, co...]
    pallas_call x2 -> x4, Pallas kernels: 24 us -> 24.1 us  [local_backward(): pl.pallas_call(kernel, grid=(kv_heads,), in_specs=[pl.BlockSpec((rows, 1)...]
  transfers between devices with their start and end apart: 8 -> 12, of which waited for: 4 -> 6; matrix products, arithmetic and copies ran while one was open for 4% -> 2% of each run, Pallas kernels for 24% -> 11%
where the time goes in v10:
time: 109 us; the launch traced here: 108 us
  waiting for transfers between devices  30.1 us (28%)
  starting transfers between devices  25.6 us (23%)
  Pallas kernels  24.1 us (22%)
  blocking collectives  13.8 us (13%)
  local copies, waits for them, and re-layouts  8.75 us (8%)
  other arithmetic  4.6 us (4%)
  between operations  1.4 us (1%)
    ppermute x12, waiting for transfers between devices, shifted(): return lax.ppermute(block, axis, route)  30.1 us
    ppermute x12, starting transfers between devices, shifted(): return lax.ppermute(block, axis, route)  25.6 us
    pallas_call x4, Pallas kernels, local_backward(): pl.pallas_call(kernel, grid=(kv_heads,), in_specs=[pl.BlockSpec((rows, 1)...  24.1 us
    all_to_all x1, blocking collectives, per_device(): lax.all_to_all(outgoing, 'head', split_axis=1, concat_axis=0, tiled=True)  8.16 us
    unnamed x41, local copies, waits for them, and re-layouts  7.39 us
    all_to_all x1, blocking collectives, per_device(): lax.all_to_all(finished, 'head', split_axis=0, concat_axis=1, tiled=True)  5.63 us
    concatenate x3, other arithmetic, gather(): jnp.concatenate([returned[:, p * width + begin:p * width + begin + size]...  2.84 us
  transfers between devices with their start and end apart: 12, of which 6 were waited for; matrix products, arithmetic and copies ran while one was open for 2% of the time, Pallas kernels for 11%

profile of v10, /device:TPU:0, one launch (start us, length us, event | category | flops | bytes accessed | tf_op | source)
XLA Modules:
  0.0 108.4 jit_solution(8686013158365251778)
XLA Ops:
  0.7 1.4 %slice_dynamic-update-slice_fusion.5 = bf16[192,14336]{1,0:T(8,128)(2,1)S(1)} fusion(bf16[192,4096]{1,0:T(8,128)(2,1)} %param.30), kind=kLoop, calls=%fused_computation.7 | loop fusion | bytes 1572864
  2.0 1.3 %slice_dynamic-update-slice_fusion.4 = bf16[192,14336]{1,0:T(8,128)(2,1)S(1)} fusion(bf16[192,14336]{1,0:T(8,128)(2,1)S(1)} %slice_dynamic-update-slice_fusion.5, bf16[192,4096]{1,0:T(8,128)(2,1)} %param.34), kind=kLoop, calls=%fused_computation.6 | loop fusion | bytes 1572864
  3.8 1.0 copy-done.2
  5.5 8.2 %all_to_all.38 = bf16[192,2,7168]{2,0,1:T(8,128)(2,1)S(1)} all-to-all(bf16[192,2,7168]{2,0,1:T(8,128)(2,1)S(1)} %bitcast.40), channel_id=1, replica_groups=mesh['groups'=2,'ctx'=8,'head'=2] {'head'}, dimensions={1} | all-to-all | bytes 11010048 | tf_op jit(solution)/shard_map/all_to_all | solution.py:114
  13.6 2.4 %copy-done = bf16[192,2,7168]{2,0,1:T(8,128)(2,1)} copy-done((bf16[192,2,7168]{2,0,1:T(8,128)(2,1)}, bf16[192,2,7168]{2,0,1:T(8,128)(2,1)S(1)}, u32[]{:S(2)}) %copy-start) | copy-done | bytes 5505048
  16.1 5.0 %collective-permute-start.2 = (bf16[256,512]{1,0:T(8,128)(2,1)S(1)}, bf16[256,512]{1,0:T(8,128)(2,1)S(1)}, u32[]{:S(2)}, u32[]{:S(2)}) collective-permute-start(bf16[256,512]{1,0:T(8,128)(2,1)S(1)} %fusion), channel_id=1, source_target_pairs={{0,4},{2,6},{4,8},{6,10},{8,12},{10,14},{1,5},{3,7},{5,9},{7,11},{... | collective-permute-start | bytes 786440 | tf_op jit(solution)/shard_map/ppermute | solution.py:21
  21.1 3.4 %collective-permute-start.3 = (bf16[384,512]{1,0:T(8,128)(2,1)S(1)}, bf16[384,512]{1,0:T(8,128)(2,1)S(1)}, u32[]{:S(2)}, u32[]{:S(2)}) collective-permute-start(bf16[384,512]{1,0:T(8,128)(2,1)S(1)} %pad_maximum_fusion.6), channel_id=1, source_target_pairs={{0,2},{2,4},{4,6},{6,8},{8,10},{10,12},{12,14},{1,3},{3,5},{5,7},{... | collective-permute-start | bytes 1179656 | tf_op jit(solution)/shard_map/ppermute | solution.py:21
  24.6 0.7 fusion.1
  25.3 3.5 %collective-permute-start = (bf16[256,512]{1,0:T(8,128)(2,1)}, bf16[256,512]{1,0:T(8,128)(2,1)S(1)}, u32[]{:S(2)}, u32[]{:S(2)}) collective-permute-start(bf16[256,512]{1,0:T(8,128)(2,1)} %fusion.1), channel_id=1, source_target_pairs={{0,4},{2,6},{4,8},{6,10},{8,12},{10,14},{1,5},{3,7},{5,9},{7,11},{... | collective-permute-start | bytes 786440 | tf_op jit(solution)/shard_map/ppermute | solution.py:21
  28.8 3.4 %collective-permute-start.1 = (bf16[384,512]{1,0:T(8,128)(2,1)S(1)}, bf16[384,512]{1,0:T(8,128)(2,1)S(1)}, u32[]{:S(2)}, u32[]{:S(2)}) collective-permute-start(bf16[384,512]{1,0:T(8,128)(2,1)S(1)} %pad_maximum_fusion.5), channel_id=1, source_target_pairs={{0,2},{2,4},{4,6},{6,8},{8,10},{10,12},{12,14},{1,3},{3,5},{5,7},{... | collective-permute-start | bytes 1179656 | tf_op jit(solution)/shard_map/ppermute | solution.py:21
  32.8 1.6 %collective-permute-done = bf16[256,512]{1,0:T(8,128)(2,1)S(1)} collective-permute-done((bf16[256,512]{1,0:T(8,128)(2,1)}, bf16[256,512]{1,0:T(8,128)(2,1)S(1)}, u32[]{:S(2)}, u32[]{:S(2)}) %collective-permute-start) | collective-permute-done | bytes 262176 | tf_op jit(solution)/shard_map/ppermute | solution.py:21
  34.6 6.0 %shard_map.108 = (bf16[384,512]{1,0:T(8,128)(2,1)S(1)}, f32[1024,128]{1,0:T(8,128)S(1)}, f32[1024,128]{1,0:T(8,128)S(1)}) custom-call(s32[384,1]{1,0:T(8,128)S(1)} %bitcast.19, s32[1,1024]{1,0:T(1,128)S(1)} %bitcast.23, bf16[384,7168]{1,0:T(8,128)(2,1)} %bitcast.28, bf16[384,7168]{1,0:T(8,128)(2,1)} %bitcast.29, bf16[384,7168]{1,0:T(8,128)(2,1)} %bitcast.30, ...), custom_call_target="tpu_custom_call" | custom-call | tf_op jit(solution)/shard_map/pallas_call | solution.py:86
  40.7 6.0 %shard_map.107 = (bf16[384,512]{1,0:T(8,128)(2,1)S(1)}, f32[1024,128]{1,0:T(8,128)S(1)}, f32[1024,128]{1,0:T(8,128)S(1)}) custom-call(s32[384,1]{1,0:T(8,128)S(1)} %bitcast.20, s32[1,1024]{1,0:T(1,128)S(1)} %bitcast.24, bf16[384,7168]{1,0:T(8,128)(2,1)} %bitcast.31, bf16[384,7168]{1,0:T(8,128)(2,1)} %bitcast.32, bf16[384,7168]{1,0:T(8,128)(2,1)} %bitcast.33, ...), custom_call_target="tpu_custom_call" | custom-call | tf_op jit(solution)/shard_map/pallas_call | solution.py:86
  47.0 6.2 %shard_map.106 = (bf16[384,512]{1,0:T(8,128)(2,1)S(1)}, f32[1024,128]{1,0:T(8,128)S(1)}, f32[1024,128]{1,0:T(8,128)S(1)}) custom-call(s32[384,1]{1,0:T(8,128)S(1)} %bitcast.21, s32[1,1024]{1,0:T(1,128)S(1)} %bitcast.25, bf16[384,7168]{1,0:T(8,128)(2,1)} %bitcast.34, bf16[384,7168]{1,0:T(8,128)(2,1)} %bitcast.35, bf16[384,7168]{1,0:T(8,128)(2,1)} %bitcast.36, ...), custom_call_target="tpu_custom_call" | custom-call | tf_op jit(solution)/shard_map/pallas_call | solution.py:86
  53.4 6.0 %shard_map.105 = (bf16[384,512]{1,0:T(8,128)(2,1)S(1)}, f32[1024,128]{1,0:T(8,128)S(1)}, f32[1024,128]{1,0:T(8,128)S(1)}) custom-call(s32[384,1]{1,0:T(8,128)S(1)} %bitcast.22, s32[1,1024]{1,0:T(1,128)S(1)} %bitcast.26, bf16[384,7168]{1,0:T(8,128)(2,1)} %bitcast.37, bf16[384,7168]{1,0:T(8,128)(2,1)} %bitcast.38, bf16[384,7168]{1,0:T(8,128)(2,1)} %bitcast.39, ...), custom_call_target="tpu_custom_call" | custom-call | tf_op jit(solution)/shard_map/pallas_call | solution.py:86
  59.6 1.3 %collective-permute-start.10 = (bf16[384,256]{1,0:T(8,128)(2,1)S(1)}, bf16[384,256]{1,0:T(8,128)(2,1)S(1)}, u32[]{:S(2)}, u32[]{:S(2)}) collective-permute-start(bf16[384,256]{1,0:T(8,128)(2,1)S(1)} %slice.396), channel_id=1, source_target_pairs={{2,0},{4,2},{6,4},{8,6},{10,8},{12,10},{14,12},{3,1},{5,3},{7,5},{... | collective-permute-start | bytes 589832 | tf_op jit(solution)/shard_map/ppermute | solution.py:21
  60.9 1.3 %collective-permute-start.11 = (bf16[256,256]{1,0:T(8,128)(2,1)S(1)}, bf16[256,256]{1,0:T(8,128)(2,1)S(1)}, u32[]{:S(2)}, u32[]{:S(2)}) collective-permute-start(bf16[256,256]{1,0:T(8,128)(2,1)S(1)} %slice.398), channel_id=1, source_target_pairs={{4,0},{6,2},{8,4},{10,6},{12,8},{14,10},{5,1},{7,3},{9,5},{11,7},{... | collective-permute-start | bytes 393224 | tf_op jit(solution)/shard_map/ppermute | solution.py:21
  62.2 1.3 %collective-permute-start.8 = (bf16[384,256]{1,0:T(8,128)(2,1)S(1)}, bf16[384,256]{1,0:T(8,128)(2,1)S(1)}, u32[]{:S(2)}, u32[]{:S(2)}) collective-permute-start(bf16[384,256]{1,0:T(8,128)(2,1)S(1)} %slice.391), channel_id=1, source_target_pairs={{2,0},{4,2},{6,4},{8,6},{10,8},{12,10},{14,12},{3,1},{5,3},{7,5},{... | collective-permute-start | bytes 589832 | tf_op jit(solution)/shard_map/ppermute | solution.py:21
  63.5 1.3 %collective-permute-start.9 = (bf16[256,256]{1,0:T(8,128)(2,1)S(1)}, bf16[256,256]{1,0:T(8,128)(2,1)S(1)}, u32[]{:S(2)}, u32[]{:S(2)}) collective-permute-start(bf16[256,256]{1,0:T(8,128)(2,1)S(1)} %slice.393), channel_id=1, source_target_pairs={{4,0},{6,2},{8,4},{10,6},{12,8},{14,10},{5,1},{7,3},{9,5},{11,7},{... | collective-permute-start | bytes 393224 | tf_op jit(solution)/shard_map/ppermute | solution.py:21
  64.8 1.3 %collective-permute-start.6 = (bf16[384,256]{1,0:T(8,128)(2,1)S(1)}, bf16[384,256]{1,0:T(8,128)(2,1)S(1)}, u32[]{:S(2)}, u32[]{:S(2)}) collective-permute-start(bf16[384,256]{1,0:T(8,128)(2,1)S(1)} %slice.386), channel_id=1, source_target_pairs={{2,0},{4,2},{6,4},{8,6},{10,8},{12,10},{14,12},{3,1},{5,3},{7,5},{... | collective-permute-start | bytes 589832 | tf_op jit(solution)/shard_map/ppermute | solution.py:21
  66.3 9.0 %collective-permute-done.10 = bf16[384,256]{1,0:T(8,128)(2,1)S(1)} collective-permute-done((bf16[384,256]{1,0:T(8,128)(2,1)S(1)}, bf16[384,256]{1,0:T(8,128)(2,1)S(1)}, u32[]{:S(2)}, u32[]{:S(2)}) %collective-permute-start.10) | collective-permute-done | bytes 196640 | tf_op jit(solution)/shard_map/ppermute | solution.py:21
  75.3 1.3 %collective-permute-start.7 = (bf16[256,256]{1,0:T(8,128)(2,1)S(1)}, bf16[256,256]{1,0:T(8,128)(2,1)S(1)}, u32[]{:S(2)}, u32[]{:S(2)}) collective-permute-start(bf16[256,256]{1,0:T(8,128)(2,1)S(1)} %slice.388), channel_id=1, source_target_pairs={{4,0},{6,2},{8,4},{10,6},{12,8},{14,10},{5,1},{7,3},{9,5},{11,7},{... | collective-permute-start | bytes 393224 | tf_op jit(solution)/shard_map/ppermute | solution.py:21
  76.7 3.9 %collective-permute-done.11 = bf16[256,256]{1,0:T(8,128)(2,1)S(1)} collective-permute-done((bf16[256,256]{1,0:T(8,128)(2,1)S(1)}, bf16[256,256]{1,0:T(8,128)(2,1)S(1)}, u32[]{:S(2)}, u32[]{:S(2)}) %collective-permute-start.11) | collective-permute-done | bytes 131104 | tf_op jit(solution)/shard_map/ppermute | solution.py:21
  80.6 1.3 %collective-permute-start.4 = (bf16[384,256]{1,0:T(8,128)(2,1)S(1)}, bf16[384,256]{1,0:T(8,128)(2,1)S(1)}, u32[]{:S(2)}, u32[]{:S(2)}) collective-permute-start(bf16[384,256]{1,0:T(8,128)(2,1)S(1)} %slice.381), channel_id=1, source_target_pairs={{2,0},{4,2},{6,4},{8,6},{10,8},{12,10},{14,12},{3,1},{5,3},{7,5},{... | collective-permute-start | bytes 589832 | tf_op jit(solution)/shard_map/ppermute | solution.py:21
  82.0 1.3 %collective-permute-start.5 = (bf16[256,256]{1,0:T(8,128)(2,1)S(1)}, bf16[256,256]{1,0:T(8,128)(2,1)S(1)}, u32[]{:S(2)}, u32[]{:S(2)}) collective-permute-start(bf16[256,256]{1,0:T(8,128)(2,1)S(1)} %slice.383), channel_id=1, source_target_pairs={{4,0},{6,2},{8,4},{10,6},{12,8},{14,10},{5,1},{7,3},{9,5},{11,7},{... | collective-permute-start | bytes 393224 | tf_op jit(solution)/shard_map/ppermute | solution.py:21
  83.3 4.3 %collective-permute-done.9 = bf16[256,256]{1,0:T(8,128)(2,1)S(1)} collective-permute-done((bf16[256,256]{1,0:T(8,128)(2,1)S(1)}, bf16[256,256]{1,0:T(8,128)(2,1)S(1)}, u32[]{:S(2)}, u32[]{:S(2)}) %collective-permute-start.9) | collective-permute-done | bytes 131104 | tf_op jit(solution)/shard_map/ppermute | solution.py:21
  87.8 6.9 %collective-permute-done.7 = bf16[256,256]{1,0:T(8,128)(2,1)S(1)} collective-permute-done((bf16[256,256]{1,0:T(8,128)(2,1)S(1)}, bf16[256,256]{1,0:T(8,128)(2,1)S(1)}, u32[]{:S(2)}, u32[]{:S(2)}) %collective-permute-start.7) | collective-permute-done | bytes 131104 | tf_op jit(solution)/shard_map/ppermute | solution.py:21
  94.8 4.4 %collective-permute-done.5 = bf16[256,256]{1,0:T(8,128)(2,1)S(1)} collective-permute-done((bf16[256,256]{1,0:T(8,128)(2,1)S(1)}, bf16[256,256]{1,0:T(8,128)(2,1)S(1)}, u32[]{:S(2)}, u32[]{:S(2)}) %collective-permute-start.5) | collective-permute-done | bytes 131104 | tf_op jit(solution)/shard_map/ppermute | solution.py:21
  99.5 5.6 %all_to_all.39 = bf16[2,192,3072]{2,1,0:T(8,128)(2,1)S(1)} all-to-all(bf16[2,192,3072]{2,1,0:T(8,128)(2,1)S(1)} %bitcast.45), channel_id=1, replica_groups=mesh['groups'=2,'ctx'=8,'head'=2] {'head'}, dimensions={0} | all-to-all | bytes 4718592 | tf_op jit(solution)/shard_map/all_to_all | solution.py:168
  105.6 0.8 pad_maximum_fusion.8
  106.4 0.8 pad_maximum_fusion.7
  107.2 1.3 %pad_maximum_fusion = bf16[192,4096]{1,0:T(8,128)(2,1)} fusion(bf16[192,2048]{1,0:T(8,128)(2,1)S(1)} %get-tuple-element.164, bf16[192,2048]{1,0:T(8,128)(2,1)S(1)} %get-tuple-element.163), kind=kLoop, calls=%fused_computation.1 | loop fusion | flops 3145728 | bytes 3145728 | tf_op jit(solution)/shard_map/concatenate | solution.py:172
  (91 shorter events, 3.7 us)
Async XLA Ops:
  0.6 2.7 %copy-start.3 = (bf16[192,4096]{1,0:T(8,128)(2,1)S(1)}, bf16[192,4096]{1,0:T(8,128)(2,1)}, u32[]{:S(2)}) copy-start(bf16[192,4096]{1,0:T(8,128)(2,1)} %param.33) | copy-start | bytes 4718596
  0.6 2.8 %copy-start.4 = (bf16[192,1024]{1,0:T(8,128)(2,1)S(1)}, bf16[192,1024]{1,0:T(8,128)(2,1)}, u32[]{:S(2)}) copy-start(bf16[192,1024]{1,0:T(8,128)(2,1)} %param.31) | copy-start | bytes 1179652
  0.7 2.8 %copy-start.5 = (bf16[192,1024]{1,0:T(8,128)(2,1)S(1)}, bf16[192,1024]{1,0:T(8,128)(2,1)}, u32[]{:S(2)}) copy-start(bf16[192,1024]{1,0:T(8,128)(2,1)} %param.32) | copy-start | bytes 1179652
  2.0 1.8 %copy-start.1 = (bf16[192,4096]{1,0:T(8,128)(2,1)S(1)}, bf16[192,4096]{1,0:T(8,128)(2,1)}, u32[]{:S(2)}) copy-start(bf16[192,4096]{1,0:T(8,128)(2,1)} %param.30) | copy-start | bytes 4718596
  3.4 1.5 %copy-start.2 = (bf16[192,4096]{1,0:T(8,128)(2,1)S(1)}, bf16[192,4096]{1,0:T(8,128)(2,1)}, u32[]{:S(2)}) copy-start(bf16[192,4096]{1,0:T(8,128)(2,1)} %param.34) | copy-start | bytes 4718596
  13.6 2.4 %copy-start = (bf16[192,2,7168]{2,0,1:T(8,128)(2,1)}, bf16[192,2,7168]{2,0,1:T(8,128)(2,1)S(1)}, u32[]{:S(2)}) copy-start(bf16[192,2,7168]{2,0,1:T(8,128)(2,1)S(1)} %all_to_all.38) | copy-start | bytes 16515076
  13.6 18.7 %copy-start.6 = (s32[24]{0:T(128)S(1)}, s32[24]{0:T(128)}, u32[]{:S(2)}) copy-start(s32[24]{0:T(128)} %param.35) | copy-start | bytes 292
  16.1 16.6 %collective-permute-start.2 = (bf16[256,512]{1,0:T(8,128)(2,1)S(1)}, bf16[256,512]{1,0:T(8,128)(2,1)S(1)}, u32[]{:S(2)}, u32[]{:S(2)}) collective-permute-start(bf16[256,512]{1,0:T(8,128)(2,1)S(1)} %fusion), channel_id=1, source_target_pairs={{0,4},{2,6},{4,8},{6,10},{8,12},{10,14},{1,5},{3,7},{5,9},{7,11},{... | collective-permute-start | bytes 786440 | tf_op jit(solution)/shard_map/ppermute | solution.py:21
  21.1 13.2 %collective-permute-start.3 = (bf16[384,512]{1,0:T(8,128)(2,1)S(1)}, bf16[384,512]{1,0:T(8,128)(2,1)S(1)}, u32[]{:S(2)}, u32[]{:S(2)}) collective-permute-start(bf16[384,512]{1,0:T(8,128)(2,1)S(1)} %pad_maximum_fusion.6), channel_id=1, source_target_pairs={{0,2},{2,4},{4,6},{6,8},{8,10},{10,12},{12,14},{1,3},{3,5},{5,7},{... | collective-permute-start | bytes 1179656 | tf_op jit(solution)/shard_map/ppermute | solution.py:21
  25.3 9.0 %collective-permute-start = (bf16[256,512]{1,0:T(8,128)(2,1)}, bf16[256,512]{1,0:T(8,128)(2,1)S(1)}, u32[]{:S(2)}, u32[]{:S(2)}) collective-permute-start(bf16[256,512]{1,0:T(8,128)(2,1)} %fusion.1), channel_id=1, source_target_pairs={{0,4},{2,6},{4,8},{6,10},{8,12},{10,14},{1,5},{3,7},{5,9},{7,11},{... | collective-permute-start | bytes 786440 | tf_op jit(solution)/shard_map/ppermute | solution.py:21
  28.8 18.1 %collective-permute-start.1 = (bf16[384,512]{1,0:T(8,128)(2,1)S(1)}, bf16[384,512]{1,0:T(8,128)(2,1)S(1)}, u32[]{:S(2)}, u32[]{:S(2)}) collective-permute-start(bf16[384,512]{1,0:T(8,128)(2,1)S(1)} %pad_maximum_fusion.5), channel_id=1, source_target_pairs={{0,2},{2,4},{4,6},{6,8},{8,10},{10,12},{12,14},{1,3},{3,5},{5,7},{... | collective-permute-start | bytes 1179656 | tf_op jit(solution)/shard_map/ppermute | solution.py:21
  59.6 15.7 %collective-permute-start.10 = (bf16[384,256]{1,0:T(8,128)(2,1)S(1)}, bf16[384,256]{1,0:T(8,128)(2,1)S(1)}, u32[]{:S(2)}, u32[]{:S(2)}) collective-permute-start(bf16[384,256]{1,0:T(8,128)(2,1)S(1)} %slice.396), channel_id=1, source_target_pairs={{2,0},{4,2},{6,4},{8,6},{10,8},{12,10},{14,12},{3,1},{5,3},{7,5},{... | collective-permute-start | bytes 589832 | tf_op jit(solution)/shard_map/ppermute | solution.py:21
  60.9 19.7 %collective-permute-start.11 = (bf16[256,256]{1,0:T(8,128)(2,1)S(1)}, bf16[256,256]{1,0:T(8,128)(2,1)S(1)}, u32[]{:S(2)}, u32[]{:S(2)}) collective-permute-start(bf16[256,256]{1,0:T(8,128)(2,1)S(1)} %slice.398), channel_id=1, source_target_pairs={{4,0},{6,2},{8,4},{10,6},{12,8},{14,10},{5,1},{7,3},{9,5},{11,7},{... | collective-permute-start | bytes 393224 | tf_op jit(solution)/shard_map/ppermute | solution.py:21
  62.2 19.8 %collective-permute-start.8 = (bf16[384,256]{1,0:T(8,128)(2,1)S(1)}, bf16[384,256]{1,0:T(8,128)(2,1)S(1)}, u32[]{:S(2)}, u32[]{:S(2)}) collective-permute-start(bf16[384,256]{1,0:T(8,128)(2,1)S(1)} %slice.391), channel_id=1, source_target_pairs={{2,0},{4,2},{6,4},{8,6},{10,8},{12,10},{14,12},{3,1},{5,3},{7,5},{... | collective-permute-start | bytes 589832 | tf_op jit(solution)/shard_map/ppermute | solution.py:21
  63.5 24.1 %collective-permute-start.9 = (bf16[256,256]{1,0:T(8,128)(2,1)S(1)}, bf16[256,256]{1,0:T(8,128)(2,1)S(1)}, u32[]{:S(2)}, u32[]{:S(2)}) collective-permute-start(bf16[256,256]{1,0:T(8,128)(2,1)S(1)} %slice.393), channel_id=1, source_target_pairs={{4,0},{6,2},{8,4},{10,6},{12,8},{14,10},{5,1},{7,3},{9,5},{11,7},{... | collective-permute-start | bytes 393224 | tf_op jit(solution)/shard_map/ppermute | solution.py:21
  64.8 22.9 %collective-permute-start.6 = (bf16[384,256]{1,0:T(8,128)(2,1)S(1)}, bf16[384,256]{1,0:T(8,128)(2,1)S(1)}, u32[]{:S(2)}, u32[]{:S(2)}) collective-permute-start(bf16[384,256]{1,0:T(8,128)(2,1)S(1)} %slice.386), channel_id=1, source_target_pairs={{2,0},{4,2},{6,4},{8,6},{10,8},{12,10},{14,12},{3,1},{5,3},{7,5},{... | collective-permute-start | bytes 589832 | tf_op jit(solution)/shard_map/ppermute | solution.py:21
  75.3 19.3 %collective-permute-start.7 = (bf16[256,256]{1,0:T(8,128)(2,1)S(1)}, bf16[256,256]{1,0:T(8,128)(2,1)S(1)}, u32[]{:S(2)}, u32[]{:S(2)}) collective-permute-start(bf16[256,256]{1,0:T(8,128)(2,1)S(1)} %slice.388), channel_id=1, source_target_pairs={{4,0},{6,2},{8,4},{10,6},{12,8},{14,10},{5,1},{7,3},{9,5},{11,7},{... | collective-permute-start | bytes 393224 | tf_op jit(solution)/shard_map/ppermute | solution.py:21
  80.6 14.1 %collective-permute-start.4 = (bf16[384,256]{1,0:T(8,128)(2,1)S(1)}, bf16[384,256]{1,0:T(8,128)(2,1)S(1)}, u32[]{:S(2)}, u32[]{:S(2)}) collective-permute-start(bf16[384,256]{1,0:T(8,128)(2,1)S(1)} %slice.381), channel_id=1, source_target_pairs={{2,0},{4,2},{6,4},{8,6},{10,8},{12,10},{14,12},{3,1},{5,3},{7,5},{... | collective-permute-start | bytes 589832 | tf_op jit(solution)/shard_map/ppermute | solution.py:21
  82.0 17.2 %collective-permute-start.5 = (bf16[256,256]{1,0:T(8,128)(2,1)S(1)}, bf16[256,256]{1,0:T(8,128)(2,1)S(1)}, u32[]{:S(2)}, u32[]{:S(2)}) collective-permute-start(bf16[256,256]{1,0:T(8,128)(2,1)S(1)} %slice.383), channel_id=1, source_target_pairs={{4,0},{6,2},{8,4},{10,6},{12,8},{14,10},{5,1},{7,3},{9,5},{11,7},{... | collective-permute-start | bytes 393224 | tf_op jit(solution)/shard_map/ppermute | solution.py:21

commit v11 on v9

--- a/solution.py
+++ b/solution.py
@@ -20,7 +20,7 @@
     return lax.ppermute(block, axis, route)
 
 
-def attention_kernel(qdoc_ref, kdoc_ref, q_ref, do_ref, o_ref, k_ref, v_ref,
+def attention_kernel(qdoc_ref, kdoc_ref, q_ref, do_ref, d_ref, k_ref, v_ref,
                      dq_ref, dk_ref, dv_ref, *, query_group, query_blocks, key_offset):
     scale = HEAD_SIZE ** (-0.5)
     window = DOC_MOST * BLK
@@ -35,9 +35,11 @@
             [q_ref[rows, pl.ds(r * HEAD_SIZE, HEAD_SIZE)] for r in range(query_group)], axis=0)
         dos = jnp.concatenate(
             [do_ref[rows, pl.ds(r * HEAD_SIZE, HEAD_SIZE)] for r in range(query_group)], axis=0)
-        outs = jnp.concatenate(
-            [o_ref[rows, pl.ds(r * HEAD_SIZE, HEAD_SIZE)] for r in range(query_group)], axis=0)
-        delta = jnp.sum(dos.astype(jnp.float32) * outs.astype(jnp.float32), axis=1, keepdims=True)
+        pieces = d_ref[rows, :].astype(jnp.float32)
+        delta = jnp.concatenate(
+            [pieces[:, r:r + 1] + pieces[:, query_group + r:query_group + r + 1]
+             + pieces[:, 2 * query_group + r:2 * query_group + r + 1]
+             for r in range(query_group)], axis=0)
         qd = qdoc_ref[rows, :]
         kd = kdoc_ref[:, pl.ds(k0, window)]
         qpos = lax.broadcasted_iota(jnp.int32, (BLK, window), 0) + (key_offset + qb * BLK)
@@ -48,9 +50,9 @@
             qs, kwin, (((1,), (1,)), ((), ())), preferred_element_type=jnp.float32)
         masked = jnp.where(mask, scores, -1e30)
         top = jnp.max(masked, axis=1, keepdims=True)
-        total = jnp.sum(jnp.where(mask, jnp.exp(masked - top), 0.0), axis=1, keepdims=True)
+        total = jnp.sum(jnp.exp(masked - top), axis=1, keepdims=True)
         lse = top + jnp.log(total)
-        probs = jnp.where(mask, jnp.exp(masked - lse), 0.0)
+        probs = jnp.exp(masked - lse)
         dprob = lax.dot_general(
             dos, vwin, (((1,), (1,)), ((), ())), preferred_element_type=jnp.float32)
         dscore = (probs * (dprob - delta)).astype(jnp.bfloat16)
@@ -87,7 +89,10 @@
         in_specs=[
             pl.BlockSpec((rows, 1), lambda g: (0, 0)),
             pl.BlockSpec((1, key_rows), lambda g: (0, 0)),
-            section(0), section(1), section(2), k_spec, k_spec,
+            section(0), section(1),
+            pl.BlockSpec((rows, HEAD_SIZE),
+                         lambda g: (0, 2 * q_cols // HEAD_SIZE + 2 * all_kv + head0 + g)),
+            k_spec, k_spec,
         ],
         out_specs=[out_spec, k_spec, k_spec],
         out_shape=[
@@ -101,18 +106,34 @@
 
 
 def per_device(query_matrix, key_matrix, value_matrix, fwd_output, output_gradient, block_docs):
-    _, q_all = query_matrix.shape
+    tokens, q_all = query_matrix.shape
     kv_all = key_matrix.shape[1]
     peers = lax.axis_size("head")
     q_cols, kv_cols = q_all // peers, kv_all // peers
-    sections = (query_matrix, output_gradient, fwd_output, key_matrix, value_matrix)
+    all_heads = q_all // HEAD_SIZE
+    all_kv = kv_cols // HEAD_SIZE
+    group = all_heads // peers // all_kv
+    delta_here = jnp.sum(
+        output_gradient.reshape(tokens, all_heads, HEAD_SIZE).astype(jnp.float32)
+        * fwd_output.reshape(tokens, all_heads, HEAD_SIZE).astype(jnp.float32),
+        axis=2,
+    )
+    hi = lax.reduce_precision(delta_here, exponent_bits=8, mantissa_bits=7)
+    rest = delta_here - hi
+    mid = lax.reduce_precision(rest, exponent_bits=8, mantissa_bits=7)
+    pieces = jnp.stack([hi, mid, rest - mid]).astype(jnp.bfloat16)
+    pieces = pieces.reshape(3, tokens, peers, all_kv, group).transpose(1, 2, 3, 0, 4)
+    pieces = jnp.pad(pieces.reshape(tokens, peers, all_kv, 3 * group),
+                     ((0, 0), (0, 0), (0, 0), (0, HEAD_SIZE - 3 * group)))
+    pieces = pieces.reshape(tokens, peers * all_kv * HEAD_SIZE)
+    sections = (query_matrix, output_gradient, key_matrix, value_matrix, pieces)
     outgoing = jnp.concatenate(
         [x[:, p * (x.shape[1] // peers):(p + 1) * (x.shape[1] // peers)]
          for p in range(peers) for x in sections], axis=1)
     fused = lax.all_to_all(outgoing, "head", split_axis=1, concat_axis=0, tiled=True)
     window_extent = fused.shape[0]
-    key_part = fused[:, 3 * q_cols:3 * q_cols + kv_cols]
-    value_part = fused[:, 3 * q_cols + kv_cols:]
+    key_part = fused[:, 2 * q_cols:2 * q_cols + kv_cols]
+    value_part = fused[:, 2 * q_cols + kv_cols:2 * q_cols + 2 * kv_cols]
     place = lax.axis_index("ctx")
     blocks_here = window_extent // BLK
     own = REACH * window_extent
@@ -125,7 +146,6 @@
     key_docs = jnp.concatenate([docs_of(place - distance) for distance in range(REACH, -1, -1)])
     kdoc = jnp.repeat(key_docs, BLK)[skip:][None, :]
     qdoc = jnp.repeat(docs_of(place), BLK)[:, None]
-    all_kv = kv_cols // HEAD_SIZE
     per = kv_cols // CHUNKS
     q_parts, k_parts, v_parts = [], [], []
     for j in range(CHUNKS):
@@ -157,9 +177,7 @@
         q_parts.append(query_sum)
         k_parts.append(total[:, :per].astype(jnp.bfloat16))
         v_parts.append(total[:, per:].astype(jnp.bfloat16))
-    query_back = lax.all_to_all(
-        jnp.concatenate(q_parts, axis=1), "head", split_axis=0, concat_axis=1, tiled=True)
-    finished = jnp.concatenate(k_parts + v_parts, axis=1)
+    finished = jnp.concatenate(q_parts + k_parts + v_parts, axis=1)
     returned = lax.all_to_all(finished, "head", split_axis=0, concat_axis=1, tiled=True)
     width = finished.shape[1]
 
@@ -167,7 +185,7 @@
         return jnp.concatenate(
             [returned[:, p * width + begin:p * width + begin + size] for p in range(peers)], axis=1)
 
-    return query_back, gather(0, kv_cols), gather(kv_cols, kv_cols)
+    return gather(0, q_cols), gather(q_cols, kv_cols), gather(q_cols + kv_cols, kv_cols)
 
 
 def solution(mesh):

time: 98.7 us -> 103 us (1.044)
  waiting for transfers between devices: 22.6 us -> 28.9 us
  blocking collectives: 17.5 us -> 12.8 us
  other arithmetic: 3.75 us -> 8.06 us
  local copies, waits for them, and re-layouts: 8.56 us -> 7.36 us
    ppermute x8, waiting for transfers between devices: 22.6 us -> 28.9 us  [shifted(): return lax.ppermute(block, axis, route)]
    all_to_all x1 -> x0, blocking collectives: 5 us -> none  [per_device(): lax.all_to_all(jnp.concatenate(q_parts, axis=1), 'head', split_axis=0, co...]
    unnamed x0 -> x1, other arithmetic: none -> 2.31 us
    all_to_all x1, blocking collectives: 4.37 us -> 5.63 us  [per_device(): lax.all_to_all(finished, 'head', split_axis=0, concat_axis=1, tiled=True)]
    concatenate x2 -> x3, other arithmetic: 1.59 us -> 2.84 us  [gather(): jnp.concatenate([returned[:, p * width + begin:p * width + begin + size]...]
    all_to_all x1 -> x0, local copies, waits for them, and re-layouts: 1.24 us -> none  [per_device(): lax.all_to_all(jnp.concatenate(q_parts, axis=1), 'head', split_axis=0, co...]
    unnamed x28 -> x33, local copies, waits for them, and re-layouts: 6.06 us -> 5.38 us
  transfers between devices with their start and end apart: 8 -> 8, of which waited for: 4 -> 5; matrix products, arithmetic and copies ran while one was open for 4% -> 3% of each run, Pallas kernels for 24% -> 23%
where the time goes in v11:
time: 103 us
  waiting for transfers between devices  28.9 us (28%)
  Pallas kernels  23.6 us (23%)
  starting transfers between devices  20.7 us (20%)
  blocking collectives  12.8 us (12%)
  other arithmetic  8.06 us (8%)
  local copies, waits for them, and re-layouts  7.36 us (7%)
  between operations  1.24 us (1%)
    ppermute x8, waiting for transfers between devices, shifted(): return lax.ppermute(block, axis, route)  28.9 us
    pallas_call x2, Pallas kernels, local_backward(): pl.pallas_call(kernel, grid=(kv_heads,), in_specs=[pl.BlockSpec((rows, 1)...  23.6 us
    ppermute x8, starting transfers between devices, shifted(): return lax.ppermute(block, axis, route)  20.7 us
    all_to_all x1, blocking collectives, per_device(): lax.all_to_all(outgoing, 'head', split_axis=1, concat_axis=0, tiled=True)  7.21 us
    all_to_all x1, blocking collectives, per_device(): lax.all_to_all(finished, 'head', split_axis=0, concat_axis=1, tiled=True)  5.63 us
    unnamed x33, local copies, waits for them, and re-layouts  5.38 us
    concatenate x3, other arithmetic, gather(): jnp.concatenate([returned[:, p * width + begin:p * width + begin + size]...  2.84 us
    unnamed x1, other arithmetic  2.31 us
  transfers between devices with their start and end apart: 8, of which 5 were waited for; matrix products, arithmetic and copies ran while one was open for 3% of the time, Pallas kernels for 23%

profile of v11, /device:TPU:0, one launch (start us, length us, event | category | flops | bytes accessed | tf_op | source)
XLA Modules:
  0.0 102.6 jit_solution(18272762264921783850)
XLA Ops:
  0.6 2.3 %multiply_bitcast_fusion = f32[24,8,32,128]{3,1,2,0:T(8,128)S(1)} fusion(bf16[192,4096]{1,0:T(8,128)(2,1)} %param.21, bf16[192,4096]{1,0:T(8,128)(2,1)} %param.22), kind=kLoop, calls=%fused_computation.1 | loop fusion | flops 2359296 | bytes 6291456
  3.0 0.5 copy.34
  3.5 0.9 reduce_sum.11
  4.6 0.3 copy.29
  4.9 0.2 pad.14.clone
  5.1 0.3 reshape.165
  5.4 1.3 %slice_dynamic-update-slice_fusion.3 = bf16[192,11264]{1,0:T(8,128)(2,1)S(1)} fusion(bf16[192,4096]{1,0:T(8,128)(2,1)} %param.18), kind=kLoop, calls=%fused_computation.8 | loop fusion | bytes 1572864
  6.9 0.3 copy-done.2
  7.4 0.3 copy.37
  7.7 7.2 %all_to_all.38 = bf16[192,2,5632]{2,0,1:T(8,128)(2,1)S(1)} all-to-all(bf16[192,2,5632]{2,0,1:T(8,128)(2,1)S(1)} %bitcast.38), channel_id=1, replica_groups=mesh['groups'=2,'ctx'=8,'head'=2] {'head'}, dimensions={1} | all-to-all | bytes 8650752 | tf_op jit(solution)/shard_map/all_to_all | solution.py:133
  14.9 2.0 %copy-done = bf16[192,2,5632]{2,0,1:T(8,128)(2,1)} copy-done((bf16[192,2,5632]{2,0,1:T(8,128)(2,1)}, bf16[192,2,5632]{2,0,1:T(8,128)(2,1)S(1)}, u32[]{:S(2)}) %copy-start) | copy-done | bytes 4325400
  17.0 5.0 %collective-permute-start.2 = (bf16[256,512]{1,0:T(8,128)(2,1)S(1)}, bf16[256,512]{1,0:T(8,128)(2,1)S(1)}, u32[]{:S(2)}, u32[]{:S(2)}) collective-permute-start(bf16[256,512]{1,0:T(8,128)(2,1)S(1)} %fusion.2), channel_id=1, source_target_pairs={{0,4},{2,6},{4,8},{6,10},{8,12},{10,14},{1,5},{3,7},{5,9},{7,11},{... | collective-permute-start | bytes 786440 | tf_op jit(solution)/shard_map/ppermute | solution.py:20
  22.0 3.4 %collective-permute-start.3 = (bf16[384,512]{1,0:T(8,128)(2,1)S(1)}, bf16[384,512]{1,0:T(8,128)(2,1)S(1)}, u32[]{:S(2)}, u32[]{:S(2)}) collective-permute-start(bf16[384,512]{1,0:T(8,128)(2,1)S(1)} %pad_maximum_fusion.6), channel_id=1, source_target_pairs={{0,2},{2,4},{4,6},{6,8},{8,10},{10,12},{12,14},{1,3},{3,5},{5,7},{... | collective-permute-start | bytes 1179656 | tf_op jit(solution)/shard_map/ppermute | solution.py:20
  25.5 0.7 fusion.3
  26.2 3.5 %collective-permute-start = (bf16[256,512]{1,0:T(8,128)(2,1)}, bf16[256,512]{1,0:T(8,128)(2,1)S(1)}, u32[]{:S(2)}, u32[]{:S(2)}) collective-permute-start(bf16[256,512]{1,0:T(8,128)(2,1)} %fusion.3), channel_id=1, source_target_pairs={{0,4},{2,6},{4,8},{6,10},{8,12},{10,14},{1,5},{3,7},{5,9},{7,11},{... | collective-permute-start | bytes 786440 | tf_op jit(solution)/shard_map/ppermute | solution.py:20
  29.7 3.4 %collective-permute-start.1 = (bf16[384,512]{1,0:T(8,128)(2,1)S(1)}, bf16[384,512]{1,0:T(8,128)(2,1)S(1)}, u32[]{:S(2)}, u32[]{:S(2)}) collective-permute-start(bf16[384,512]{1,0:T(8,128)(2,1)S(1)} %pad_maximum_fusion.5), channel_id=1, source_target_pairs={{0,2},{2,4},{4,6},{6,8},{8,10},{10,12},{12,14},{1,3},{3,5},{5,7},{... | collective-permute-start | bytes 1179656 | tf_op jit(solution)/shard_map/ppermute | solution.py:20
  33.7 1.6 %collective-permute-done = bf16[256,512]{1,0:T(8,128)(2,1)S(1)} collective-permute-done((bf16[256,512]{1,0:T(8,128)(2,1)}, bf16[256,512]{1,0:T(8,128)(2,1)S(1)}, u32[]{:S(2)}, u32[]{:S(2)}) %collective-permute-start) | collective-permute-done | bytes 262176 | tf_op jit(solution)/shard_map/ppermute | solution.py:20
  35.5 11.8 %shard_map.96 = (bf16[384,1024]{1,0:T(8,128)(2,1)S(1)}, f32[1024,256]{1,0:T(8,128)S(1)}, f32[1024,256]{1,0:T(8,128)S(1)}) custom-call(s32[384,1]{1,0:T(8,128)S(1)} %bitcast.27, s32[1,1024]{1,0:T(1,128)S(1)} %bitcast.29, bf16[384,5632]{1,0:T(8,128)(2,1)} %bitcast.32, bf16[384,5632]{1,0:T(8,128)(2,1)} %bitcast.33, bf16[384,5632]{1,0:T(8,128)(2,1)} %bitcast.34, ...), custom_call_target="tpu_custom_call" | custom-call | tf_op jit(solution)/shard_map/pallas_call | solution.py:86
  47.8 1.5 %collective-permute-start.6 = (bf16[384,512]{1,0:T(8,128)(2,1)S(1)}, bf16[384,512]{1,0:T(8,128)(2,1)S(1)}, u32[]{:S(2)}, u32[]{:S(2)}) collective-permute-start(bf16[384,512]{1,0:T(8,128)(2,1)S(1)} %slice.272), channel_id=1, source_target_pairs={{2,0},{4,2},{6,4},{8,6},{10,8},{12,10},{14,12},{3,1},{5,3},{7,5},{... | collective-permute-start | bytes 1179656 | tf_op jit(solution)/shard_map/ppermute | solution.py:20
  49.4 11.8 %shard_map.95 = (bf16[384,1024]{1,0:T(8,128)(2,1)S(1)}, f32[1024,256]{1,0:T(8,128)S(1)}, f32[1024,256]{1,0:T(8,128)S(1)}) custom-call(s32[384,1]{1,0:T(8,128)S(1)} %bitcast.28, s32[1,1024]{1,0:T(1,128)S(1)} %bitcast.30, bf16[384,5632]{1,0:T(8,128)(2,1)} %bitcast.35, bf16[384,5632]{1,0:T(8,128)(2,1)} %bitcast.36, bf16[384,5632]{1,0:T(8,128)(2,1)} %bitcast.37, ...), custom_call_target="tpu_custom_call" | custom-call | tf_op jit(solution)/shard_map/pallas_call | solution.py:86
  61.7 1.3 %collective-permute-start.7 = (bf16[256,512]{1,0:T(8,128)(2,1)S(1)}, bf16[256,512]{1,0:T(8,128)(2,1)S(1)}, u32[]{:S(2)}, u32[]{:S(2)}) collective-permute-start(bf16[256,512]{1,0:T(8,128)(2,1)S(1)} %slice.274), channel_id=1, source_target_pairs={{4,0},{6,2},{8,4},{10,6},{12,8},{14,10},{5,1},{7,3},{9,5},{11,7},{... | collective-permute-start | bytes 786440 | tf_op jit(solution)/shard_map/ppermute | solution.py:20
  63.0 1.3 %collective-permute-start.4 = (bf16[384,512]{1,0:T(8,128)(2,1)S(1)}, bf16[384,512]{1,0:T(8,128)(2,1)S(1)}, u32[]{:S(2)}, u32[]{:S(2)}) collective-permute-start(bf16[384,512]{1,0:T(8,128)(2,1)S(1)} %slice.267), channel_id=1, source_target_pairs={{2,0},{4,2},{6,4},{8,6},{10,8},{12,10},{14,12},{3,1},{5,3},{7,5},{... | collective-permute-start | bytes 1179656 | tf_op jit(solution)/shard_map/ppermute | solution.py:20
  64.3 1.3 %collective-permute-start.5 = (bf16[256,512]{1,0:T(8,128)(2,1)S(1)}, bf16[256,512]{1,0:T(8,128)(2,1)S(1)}, u32[]{:S(2)}, u32[]{:S(2)}) collective-permute-start(bf16[256,512]{1,0:T(8,128)(2,1)S(1)} %slice.269), channel_id=1, source_target_pairs={{4,0},{6,2},{8,4},{10,6},{12,8},{14,10},{5,1},{7,3},{9,5},{11,7},{... | collective-permute-start | bytes 786440 | tf_op jit(solution)/shard_map/ppermute | solution.py:20
  65.8 0.7 collective-permute-done.6
  66.6 15.3 %collective-permute-done.7 = bf16[256,512]{1,0:T(8,128)(2,1)S(1)} collective-permute-done((bf16[256,512]{1,0:T(8,128)(2,1)S(1)}, bf16[256,512]{1,0:T(8,128)(2,1)S(1)}, u32[]{:S(2)}, u32[]{:S(2)}) %collective-permute-start.7) | collective-permute-done | bytes 262176 | tf_op jit(solution)/shard_map/ppermute | solution.py:20
  82.1 0.2 collective-permute-done.4
  82.5 11.0 %collective-permute-done.5 = bf16[256,512]{1,0:T(8,128)(2,1)S(1)} collective-permute-done((bf16[256,512]{1,0:T(8,128)(2,1)S(1)}, bf16[256,512]{1,0:T(8,128)(2,1)S(1)}, u32[]{:S(2)}, u32[]{:S(2)}) %collective-permute-start.5) | collective-permute-done | bytes 262176 | tf_op jit(solution)/shard_map/ppermute | solution.py:20
  93.8 5.6 %all_to_all.39 = bf16[2,192,3072]{2,1,0:T(8,128)(2,1)S(1)} all-to-all(bf16[2,192,3072]{2,1,0:T(8,128)(2,1)S(1)} %bitcast.44), channel_id=1, replica_groups=mesh['groups'=2,'ctx'=8,'head'=2] {'head'}, dimensions={0} | all-to-all | bytes 4718592 | tf_op jit(solution)/shard_map/all_to_all | solution.py:181
  99.4 0.2 copy.31
  99.8 0.8 pad_maximum_fusion.8
  100.6 0.8 pad_maximum_fusion.7
  101.4 1.3 %pad_maximum_fusion = bf16[192,4096]{1,0:T(8,128)(2,1)} fusion(bf16[192,2048]{1,0:T(8,128)(2,1)S(1)} %get-tuple-element.88, bf16[192,2048]{1,0:T(8,128)(2,1)S(1)} %get-tuple-element.87), kind=kLoop, calls=%fused_computation.2 | loop fusion | flops 3145728 | bytes 3145728 | tf_op jit(solution)/shard_map/concatenate | solution.py:185
  (68 shorter events, 3.3 us)
Async XLA Ops:
  4.4 2.4 %copy-start.1 = (bf16[192,4096]{1,0:T(8,128)(2,1)S(1)}, bf16[192,4096]{1,0:T(8,128)(2,1)}, u32[]{:S(2)}) copy-start(bf16[192,4096]{1,0:T(8,128)(2,1)} %param.22) | copy-start | bytes 4718596
  4.9 1.9 %copy-start.3 = (bf16[192,1024]{1,0:T(8,128)(2,1)S(1)}, bf16[192,1024]{1,0:T(8,128)(2,1)}, u32[]{:S(2)}) copy-start(bf16[192,1024]{1,0:T(8,128)(2,1)} %param.19) | copy-start | bytes 1179652
  5.1 1.7 %copy-start.4 = (bf16[192,1024]{1,0:T(8,128)(2,1)S(1)}, bf16[192,1024]{1,0:T(8,128)(2,1)}, u32[]{:S(2)}) copy-start(bf16[192,1024]{1,0:T(8,128)(2,1)} %param.20) | copy-start | bytes 1179652
  5.4 1.8 %copy-start.2 = (bf16[192,4096]{1,0:T(8,128)(2,1)S(1)}, bf16[192,4096]{1,0:T(8,128)(2,1)}, u32[]{:S(2)}) copy-start(bf16[192,4096]{1,0:T(8,128)(2,1)} %param.18) | copy-start | bytes 4718596
  14.9 2.0 %copy-start = (bf16[192,2,5632]{2,0,1:T(8,128)(2,1)}, bf16[192,2,5632]{2,0,1:T(8,128)(2,1)S(1)}, u32[]{:S(2)}) copy-start(bf16[192,2,5632]{2,0,1:T(8,128)(2,1)S(1)} %all_to_all.38) | copy-start | bytes 12976132
  14.9 18.2 %copy-start.5 = (s32[24]{0:T(128)S(1)}, s32[24]{0:T(128)}, u32[]{:S(2)}) copy-start(s32[24]{0:T(128)} %param.23) | copy-start | bytes 292
  17.0 16.6 %collective-permute-start.2 = (bf16[256,512]{1,0:T(8,128)(2,1)S(1)}, bf16[256,512]{1,0:T(8,128)(2,1)S(1)}, u32[]{:S(2)}, u32[]{:S(2)}) collective-permute-start(bf16[256,512]{1,0:T(8,128)(2,1)S(1)} %fusion.2), channel_id=1, source_target_pairs={{0,4},{2,6},{4,8},{6,10},{8,12},{10,14},{1,5},{3,7},{5,9},{7,11},{... | collective-permute-start | bytes 786440 | tf_op jit(solution)/shard_map/ppermute | solution.py:20
  22.0 13.2 %collective-permute-start.3 = (bf16[384,512]{1,0:T(8,128)(2,1)S(1)}, bf16[384,512]{1,0:T(8,128)(2,1)S(1)}, u32[]{:S(2)}, u32[]{:S(2)}) collective-permute-start(bf16[384,512]{1,0:T(8,128)(2,1)S(1)} %pad_maximum_fusion.6), channel_id=1, source_target_pairs={{0,2},{2,4},{4,6},{6,8},{8,10},{10,12},{12,14},{1,3},{3,5},{5,7},{... | collective-permute-start | bytes 1179656 | tf_op jit(solution)/shard_map/ppermute | solution.py:20
  26.2 9.0 %collective-permute-start = (bf16[256,512]{1,0:T(8,128)(2,1)}, bf16[256,512]{1,0:T(8,128)(2,1)S(1)}, u32[]{:S(2)}, u32[]{:S(2)}) collective-permute-start(bf16[256,512]{1,0:T(8,128)(2,1)} %fusion.3), channel_id=1, source_target_pairs={{0,4},{2,6},{4,8},{6,10},{8,12},{10,14},{1,5},{3,7},{5,9},{7,11},{... | collective-permute-start | bytes 786440 | tf_op jit(solution)/shard_map/ppermute | solution.py:20
  29.7 19.6 %collective-permute-start.1 = (bf16[384,512]{1,0:T(8,128)(2,1)S(1)}, bf16[384,512]{1,0:T(8,128)(2,1)S(1)}, u32[]{:S(2)}, u32[]{:S(2)}) collective-permute-start(bf16[384,512]{1,0:T(8,128)(2,1)S(1)} %pad_maximum_fusion.5), channel_id=1, source_target_pairs={{0,2},{2,4},{4,6},{6,8},{8,10},{10,12},{12,14},{1,3},{3,5},{5,7},{... | collective-permute-start | bytes 1179656 | tf_op jit(solution)/shard_map/ppermute | solution.py:20
  47.8 18.7 %collective-permute-start.6 = (bf16[384,512]{1,0:T(8,128)(2,1)S(1)}, bf16[384,512]{1,0:T(8,128)(2,1)S(1)}, u32[]{:S(2)}, u32[]{:S(2)}) collective-permute-start(bf16[384,512]{1,0:T(8,128)(2,1)S(1)} %slice.272), channel_id=1, source_target_pairs={{2,0},{4,2},{6,4},{8,6},{10,8},{12,10},{14,12},{3,1},{5,3},{7,5},{... | collective-permute-start | bytes 1179656 | tf_op jit(solution)/shard_map/ppermute | solution.py:20
  61.7 20.2 %collective-permute-start.7 = (bf16[256,512]{1,0:T(8,128)(2,1)S(1)}, bf16[256,512]{1,0:T(8,128)(2,1)S(1)}, u32[]{:S(2)}, u32[]{:S(2)}) collective-permute-start(bf16[256,512]{1,0:T(8,128)(2,1)S(1)} %slice.274), channel_id=1, source_target_pairs={{4,0},{6,2},{8,4},{10,6},{12,8},{14,10},{5,1},{7,3},{9,5},{11,7},{... | collective-permute-start | bytes 786440 | tf_op jit(solution)/shard_map/ppermute | solution.py:20
  63.0 19.3 %collective-permute-start.4 = (bf16[384,512]{1,0:T(8,128)(2,1)S(1)}, bf16[384,512]{1,0:T(8,128)(2,1)S(1)}, u32[]{:S(2)}, u32[]{:S(2)}) collective-permute-start(bf16[384,512]{1,0:T(8,128)(2,1)S(1)} %slice.267), channel_id=1, source_target_pairs={{2,0},{4,2},{6,4},{8,6},{10,8},{12,10},{14,12},{3,1},{5,3},{7,5},{... | collective-permute-start | bytes 1179656 | tf_op jit(solution)/shard_map/ppermute | solution.py:20
  64.3 29.1 %collective-permute-start.5 = (bf16[256,512]{1,0:T(8,128)(2,1)S(1)}, bf16[256,512]{1,0:T(8,128)(2,1)S(1)}, u32[]{:S(2)}, u32[]{:S(2)}) collective-permute-start(bf16[256,512]{1,0:T(8,128)(2,1)S(1)} %slice.269), channel_id=1, source_target_pairs={{4,0},{6,2},{8,4},{10,6},{12,8},{14,10},{5,1},{7,3},{9,5},{11,7},{... | collective-permute-start | bytes 786440 | tf_op jit(solution)/shard_map/ppermute | solution.py:20

commit v12 on v9

--- a/solution.py
+++ b/solution.py
@@ -12,6 +12,7 @@
 REACH = 2
 DOC_MOST = 6
 CHUNKS = 2
+SHARES = (3, 1)
 
 
 def shifted(block, axis, distance):
@@ -48,9 +49,9 @@
             qs, kwin, (((1,), (1,)), ((), ())), preferred_element_type=jnp.float32)
         masked = jnp.where(mask, scores, -1e30)
         top = jnp.max(masked, axis=1, keepdims=True)
-        total = jnp.sum(jnp.where(mask, jnp.exp(masked - top), 0.0), axis=1, keepdims=True)
+        total = jnp.sum(jnp.exp(masked - top), axis=1, keepdims=True)
         lse = top + jnp.log(total)
-        probs = jnp.where(mask, jnp.exp(masked - lse), 0.0)
+        probs = jnp.exp(masked - lse)
         dprob = lax.dot_general(
             dos, vwin, (((1,), (1,)), ((), ())), preferred_element_type=jnp.float32)
         dscore = (probs * (dprob - delta)).astype(jnp.bfloat16)
@@ -126,11 +127,13 @@
     kdoc = jnp.repeat(key_docs, BLK)[skip:][None, :]
     qdoc = jnp.repeat(docs_of(place), BLK)[:, None]
     all_kv = kv_cols // HEAD_SIZE
-    per = kv_cols // CHUNKS
+    unit = kv_cols // sum(SHARES)
     q_parts, k_parts, v_parts = [], [], []
     for j in range(CHUNKS):
-        key_here = key_part[:, j * per:(j + 1) * per]
-        value_here = value_part[:, j * per:(j + 1) * per]
+        lo = sum(SHARES[:j]) * unit
+        per = SHARES[j] * unit
+        key_here = key_part[:, lo:lo + per]
+        value_here = value_part[:, lo:lo + per]
         pair = jnp.concatenate([key_here, value_here], axis=1)
         behind = []
         for distance in range(REACH, 0, -1):
@@ -141,7 +144,7 @@
         values = jnp.concatenate([b[:, per:] for b in behind] + [value_here], axis=0)
 
         query_sum, key_partial, value_partial = local_backward(
-            qdoc, kdoc, fused, q_cols, all_kv, j * per // HEAD_SIZE, keys, values)
+            qdoc, kdoc, fused, q_cols, all_kv, lo // HEAD_SIZE, keys, values)
 
         both = jnp.concatenate([key_partial, value_partial], axis=1)
         total = both[own - skip:]
@@ -157,9 +160,7 @@
         q_parts.append(query_sum)
         k_parts.append(total[:, :per].astype(jnp.bfloat16))
         v_parts.append(total[:, per:].astype(jnp.bfloat16))
-    query_back = lax.all_to_all(
-        jnp.concatenate(q_parts, axis=1), "head", split_axis=0, concat_axis=1, tiled=True)
-    finished = jnp.concatenate(k_parts + v_parts, axis=1)
+    finished = jnp.concatenate(q_parts + k_parts + v_parts, axis=1)
     returned = lax.all_to_all(finished, "head", split_axis=0, concat_axis=1, tiled=True)
     width = finished.shape[1]
 
@@ -167,7 +168,7 @@
         return jnp.concatenate(
             [returned[:, p * width + begin:p * width + begin + size] for p in range(peers)], axis=1)
 
-    return query_back, gather(0, kv_cols), gather(kv_cols, kv_cols)
+    return gather(0, q_cols), gather(q_cols, kv_cols), gather(q_cols + kv_cols, kv_cols)
 
 
 def solution(mesh):

time: 98.7 us -> 106 us (1.074)
  waiting for transfers between devices: 22.6 us -> 36.8 us
  blocking collectives: 17.5 us -> 13.8 us
  local copies, waits for them, and re-layouts: 8.56 us -> 6.42 us
  Pallas kernels: 24 us -> 22 us
    ppermute x8, waiting for transfers between devices: 22.6 us -> 36.8 us  [shifted(): return lax.ppermute(block, axis, route)]
    all_to_all x1 -> x0, blocking collectives: 5 us -> none  [per_device(): lax.all_to_all(jnp.concatenate(q_parts, axis=1), 'head', split_axis=0, co...]
    pallas_call x2, Pallas kernels: 24 us -> 22 us  [local_backward(): pl.pallas_call(kernel, grid=(kv_heads,), in_specs=[pl.BlockSpec((rows, 1)...]
    all_to_all x1, blocking collectives: 4.37 us -> 5.63 us  [per_device(): lax.all_to_all(finished, 'head', split_axis=0, concat_axis=1, tiled=True)]
    concatenate x2 -> x3, other arithmetic: 1.59 us -> 2.84 us  [gather(): jnp.concatenate([returned[:, p * width + begin:p * width + begin + size]...]
    all_to_all x1 -> x0, local copies, waits for them, and re-layouts: 1.24 us -> none  [per_device(): lax.all_to_all(jnp.concatenate(q_parts, axis=1), 'head', split_axis=0, co...]
    unnamed x28 -> x33, local copies, waits for them, and re-layouts: 6.06 us -> 4.99 us
  transfers between devices with their start and end apart: 8 -> 8, of which waited for: 4 -> 4; matrix products, arithmetic and copies ran while one was open for 4% -> 2% of each run, Pallas kernels for 24% -> 21%
where the time goes in v12:
time: 106 us
  waiting for transfers between devices  36.8 us (35%)
  Pallas kernels  22 us (21%)
  starting transfers between devices  20.7 us (20%)
  blocking collectives  13.8 us (13%)
  local copies, waits for them, and re-layouts  6.42 us (6%)
  other arithmetic  4.71 us (4%)
  between operations  1.19 us (1%)
    ppermute x8, waiting for transfers between devices, shifted(): return lax.ppermute(block, axis, route)  36.8 us
    pallas_call x2, Pallas kernels, local_backward(): pl.pallas_call(kernel, grid=(kv_heads,), in_specs=[pl.BlockSpec((rows, 1)...  22 us
    ppermute x8, starting transfers between devices, shifted(): return lax.ppermute(block, axis, route)  20.7 us
    all_to_all x1, blocking collectives, per_device(): lax.all_to_all(outgoing, 'head', split_axis=1, concat_axis=0, tiled=True)  8.16 us
    all_to_all x1, blocking collectives, per_device(): lax.all_to_all(finished, 'head', split_axis=0, concat_axis=1, tiled=True)  5.63 us
    unnamed x33, local copies, waits for them, and re-layouts  4.99 us
    concatenate x3, other arithmetic, gather(): jnp.concatenate([returned[:, p * width + begin:p * width + begin + size]...  2.84 us
  transfers between devices with their start and end apart: 8, of which 4 were waited for; matrix products, arithmetic and copies ran while one was open for 2% of the time, Pallas kernels for 21%

profile of v12, /device:TPU:0, one launch (start us, length us, event | category | flops | bytes accessed | tf_op | source)
XLA Modules:
  0.0 105.6 jit_solution(9269574422239297750)
XLA Ops:
  0.7 1.4 %slice_dynamic-update-slice_fusion.5 = bf16[192,14336]{1,0:T(8,128)(2,1)S(1)} fusion(bf16[192,4096]{1,0:T(8,128)(2,1)} %param.18), kind=kLoop, calls=%fused_computation.12 | loop fusion | bytes 1572864
  2.0 1.3 %slice_dynamic-update-slice_fusion.4 = bf16[192,14336]{1,0:T(8,128)(2,1)S(1)} fusion(bf16[192,14336]{1,0:T(8,128)(2,1)S(1)} %slice_dynamic-update-slice_fusion.5, bf16[192,4096]{1,0:T(8,128)(2,1)} %param.22), kind=kLoop, calls=%fused_computation.11 | loop fusion | bytes 1572864
  3.5 0.3 copy-done.1
  3.8 1.0 copy-done.2
  5.0 0.4 copy.21
  5.5 8.2 %all_to_all.38 = bf16[192,2,7168]{2,0,1:T(8,128)(2,1)S(1)} all-to-all(bf16[192,2,7168]{2,0,1:T(8,128)(2,1)S(1)} %bitcast.31), channel_id=1, replica_groups=mesh['groups'=2,'ctx'=8,'head'=2] {'head'}, dimensions={1} | all-to-all | bytes 11010048 | tf_op jit(solution)/shard_map/all_to_all | solution.py:113
  13.6 0.8 fusion.3
  14.4 5.0 %collective-permute-start.2 = (bf16[256,256]{1,0:T(8,128)(2,1)}, bf16[256,256]{1,0:T(8,128)(2,1)S(1)}, u32[]{:S(2)}, u32[]{:S(2)}) collective-permute-start(bf16[256,256]{1,0:T(8,128)(2,1)} %fusion.3), channel_id=1, source_target_pairs={{0,4},{2,6},{4,8},{6,10},{8,12},{10,14},{1,5},{3,7},{5,9},{7,11},{... | collective-permute-start | bytes 393224 | tf_op jit(solution)/shard_map/ppermute | solution.py:21
  19.4 3.4 %collective-permute-start.3 = (bf16[384,256]{1,0:T(8,128)(2,1)S(1)}, bf16[384,256]{1,0:T(8,128)(2,1)S(1)}, u32[]{:S(2)}, u32[]{:S(2)}) collective-permute-start(bf16[384,256]{1,0:T(8,128)(2,1)S(1)} %pad_maximum_fusion.8), channel_id=1, source_target_pairs={{0,2},{2,4},{4,6},{6,8},{8,10},{10,12},{12,14},{1,3},{3,5},{5,7},{... | collective-permute-start | bytes 589832 | tf_op jit(solution)/shard_map/ppermute | solution.py:21
  23.0 3.5 %collective-permute-start = (bf16[256,768]{1,0:T(8,128)(2,1)S(1)}, bf16[256,768]{1,0:T(8,128)(2,1)S(1)}, u32[]{:S(2)}, u32[]{:S(2)}) collective-permute-start(bf16[256,768]{1,0:T(8,128)(2,1)S(1)} %fusion.1), channel_id=1, source_target_pairs={{0,4},{2,6},{4,8},{6,10},{8,12},{10,14},{1,5},{3,7},{5,9},{7,11},{... | collective-permute-start | bytes 1179656 | tf_op jit(solution)/shard_map/ppermute | solution.py:21
  26.5 3.5 %collective-permute-start.1 = (bf16[384,768]{1,0:T(8,128)(2,1)S(1)}, bf16[384,768]{1,0:T(8,128)(2,1)S(1)}, u32[]{:S(2)}, u32[]{:S(2)}) collective-permute-start(bf16[384,768]{1,0:T(8,128)(2,1)S(1)} %pad_maximum_fusion.3), channel_id=1, source_target_pairs={{0,2},{2,4},{4,6},{6,8},{8,10},{10,12},{12,14},{1,3},{3,5},{5,7},{... | collective-permute-start | bytes 1769480 | tf_op jit(solution)/shard_map/ppermute | solution.py:21
  30.3 0.1 copy.18
  30.7 6.0 %shard_map.96 = (bf16[384,512]{1,0:T(8,128)(2,1)S(1)}, f32[1024,128]{1,0:T(8,128)S(1)}, f32[1024,128]{1,0:T(8,128)S(1)}) custom-call(s32[384,1]{1,0:T(8,128)S(1)} %bitcast.19, s32[1,1024]{1,0:T(1,128)S(1)} %bitcast.21, bf16[384,7168]{1,0:T(8,128)(2,1)} %bitcast.25, bf16[384,7168]{1,0:T(8,128)(2,1)} %bitcast.26, bf16[384,7168]{1,0:T(8,128)(2,1)} %bitcast.27, ...), custom_call_target="tpu_custom_call" | custom-call | tf_op jit(solution)/shard_map/pallas_call | solution.py:85
  36.9 1.3 %collective-permute-start.6 = (bf16[384,256]{1,0:T(8,128)(2,1)S(1)}, bf16[384,256]{1,0:T(8,128)(2,1)S(1)}, u32[]{:S(2)}, u32[]{:S(2)}) collective-permute-start(bf16[384,256]{1,0:T(8,128)(2,1)S(1)} %slice.270), channel_id=1, source_target_pairs={{2,0},{4,2},{6,4},{8,6},{10,8},{12,10},{14,12},{3,1},{5,3},{7,5},{... | collective-permute-start | bytes 589832 | tf_op jit(solution)/shard_map/ppermute | solution.py:21
  38.2 1.5 %collective-permute-start.7 = (bf16[256,256]{1,0:T(8,128)(2,1)S(1)}, bf16[256,256]{1,0:T(8,128)(2,1)S(1)}, u32[]{:S(2)}, u32[]{:S(2)}) collective-permute-start(bf16[256,256]{1,0:T(8,128)(2,1)S(1)} %slice.272), channel_id=1, source_target_pairs={{4,0},{6,2},{8,4},{10,6},{12,8},{14,10},{5,1},{7,3},{9,5},{11,7},{... | collective-permute-start | bytes 393224 | tf_op jit(solution)/shard_map/ppermute | solution.py:21
  39.7 4.9 %collective-permute-done.6 = bf16[384,256]{1,0:T(8,128)(2,1)S(1)} collective-permute-done((bf16[384,256]{1,0:T(8,128)(2,1)S(1)}, bf16[384,256]{1,0:T(8,128)(2,1)S(1)}, u32[]{:S(2)}, u32[]{:S(2)}) %collective-permute-start.6) | collective-permute-done | bytes 196640 | tf_op jit(solution)/shard_map/ppermute | solution.py:21
  44.6 1.6 %collective-permute-done.1 = bf16[384,768]{1,0:T(8,128)(2,1)S(1)} collective-permute-done((bf16[384,768]{1,0:T(8,128)(2,1)S(1)}, bf16[384,768]{1,0:T(8,128)(2,1)S(1)}, u32[]{:S(2)}, u32[]{:S(2)}) %collective-permute-start.1) | collective-permute-done | bytes 589856 | tf_op jit(solution)/shard_map/ppermute | solution.py:21
  46.3 0.2 pad_maximum_fusion.1
  46.5 16.0 %shard_map.95 = (bf16[384,1536]{1,0:T(8,128)(2,1)S(1)}, f32[1024,384]{1,0:T(8,128)S(1)}, f32[1024,384]{1,0:T(8,128)S(1)}) custom-call(s32[384,1]{1,0:T(8,128)S(1)} %bitcast.20, s32[1,1024]{1,0:T(1,128)S(1)} %bitcast.22, bf16[384,7168]{1,0:T(8,128)(2,1)} %bitcast.28, bf16[384,7168]{1,0:T(8,128)(2,1)} %bitcast.29, bf16[384,7168]{1,0:T(8,128)(2,1)} %bitcast.30, ...), custom_call_target="tpu_custom_call" | custom-call | tf_op jit(solution)/shard_map/pallas_call | solution.py:85
  62.7 0.2 convert.16
  62.9 1.3 %collective-permute-start.4 = (bf16[384,768]{1,0:T(8,128)(2,1)S(1)}, bf16[384,768]{1,0:T(8,128)(2,1)S(1)}, u32[]{:S(2)}, u32[]{:S(2)}) collective-permute-start(bf16[384,768]{1,0:T(8,128)(2,1)S(1)} %slice.265), channel_id=1, source_target_pairs={{2,0},{4,2},{6,4},{8,6},{10,8},{12,10},{14,12},{3,1},{5,3},{7,5},{... | collective-permute-start | bytes 1769480 | tf_op jit(solution)/shard_map/ppermute | solution.py:21
  64.3 1.3 %collective-permute-start.5 = (bf16[256,768]{1,0:T(8,128)(2,1)S(1)}, bf16[256,768]{1,0:T(8,128)(2,1)S(1)}, u32[]{:S(2)}, u32[]{:S(2)}) collective-permute-start(bf16[256,768]{1,0:T(8,128)(2,1)S(1)} %slice.267), channel_id=1, source_target_pairs={{4,0},{6,2},{8,4},{10,6},{12,8},{14,10},{5,1},{7,3},{9,5},{11,7},{... | collective-permute-start | bytes 1179656 | tf_op jit(solution)/shard_map/ppermute | solution.py:21
  65.6 0.1 constant_dynamic-update-slice_fusion.5
  65.9 15.1 %collective-permute-done.4 = bf16[384,768]{1,0:T(8,128)(2,1)S(1)} collective-permute-done((bf16[384,768]{1,0:T(8,128)(2,1)S(1)}, bf16[384,768]{1,0:T(8,128)(2,1)S(1)}, u32[]{:S(2)}, u32[]{:S(2)}) %collective-permute-start.4) | collective-permute-done | bytes 589856 | tf_op jit(solution)/shard_map/ppermute | solution.py:21
  81.0 15.2 %collective-permute-done.5 = bf16[256,768]{1,0:T(8,128)(2,1)S(1)} collective-permute-done((bf16[256,768]{1,0:T(8,128)(2,1)S(1)}, bf16[256,768]{1,0:T(8,128)(2,1)S(1)}, u32[]{:S(2)}, u32[]{:S(2)}) %collective-permute-start.5) | collective-permute-done | bytes 393248 | tf_op jit(solution)/shard_map/ppermute | solution.py:21
  96.3 0.2 fusion
  96.7 5.6 %all_to_all.39 = bf16[2,192,3072]{2,1,0:T(8,128)(2,1)S(1)} all-to-all(bf16[2,192,3072]{2,1,0:T(8,128)(2,1)S(1)} %bitcast.36), channel_id=1, replica_groups=mesh['groups'=2,'ctx'=8,'head'=2] {'head'}, dimensions={0} | all-to-all | bytes 4718592 | tf_op jit(solution)/shard_map/all_to_all | solution.py:164
  102.3 0.2 copy.16
  102.6 0.1 fusion.7
  102.7 0.8 pad_maximum_fusion.5
  103.5 0.8 pad_maximum_fusion.4
  104.3 1.3 %pad_maximum_fusion = bf16[192,4096]{1,0:T(8,128)(2,1)} fusion(bf16[192,2048]{1,0:T(8,128)(2,1)S(1)} %get-tuple-element.88, bf16[192,2048]{1,0:T(8,128)(2,1)S(1)} %get-tuple-element.87), kind=kLoop, calls=%fused_computation.1 | loop fusion | flops 3145728 | bytes 3145728 | tf_op jit(solution)/shard_map/concatenate | solution.py:168
  (60 shorter events, 2.1 us)
Async XLA Ops:
  0.6 2.7 %copy-start.3 = (bf16[192,4096]{1,0:T(8,128)(2,1)S(1)}, bf16[192,4096]{1,0:T(8,128)(2,1)}, u32[]{:S(2)}) copy-start(bf16[192,4096]{1,0:T(8,128)(2,1)} %param.21) | copy-start | bytes 4718596
  0.6 2.8 %copy-start.4 = (bf16[192,1024]{1,0:T(8,128)(2,1)S(1)}, bf16[192,1024]{1,0:T(8,128)(2,1)}, u32[]{:S(2)}) copy-start(bf16[192,1024]{1,0:T(8,128)(2,1)} %param.19) | copy-start | bytes 1179652
  0.7 2.8 %copy-start.5 = (bf16[192,1024]{1,0:T(8,128)(2,1)S(1)}, bf16[192,1024]{1,0:T(8,128)(2,1)}, u32[]{:S(2)}) copy-start(bf16[192,1024]{1,0:T(8,128)(2,1)} %param.20) | copy-start | bytes 1179652
  2.0 1.8 %copy-start.1 = (bf16[192,4096]{1,0:T(8,128)(2,1)S(1)}, bf16[192,4096]{1,0:T(8,128)(2,1)}, u32[]{:S(2)}) copy-start(bf16[192,4096]{1,0:T(8,128)(2,1)} %param.18) | copy-start | bytes 4718596
  3.4 1.5 %copy-start.2 = (bf16[192,4096]{1,0:T(8,128)(2,1)S(1)}, bf16[192,4096]{1,0:T(8,128)(2,1)}, u32[]{:S(2)}) copy-start(bf16[192,4096]{1,0:T(8,128)(2,1)} %param.22) | copy-start | bytes 4718596
  13.6 9.2 %copy-start = (bf16[192,2,7168]{2,0,1:T(8,128)(2,1)}, bf16[192,2,7168]{2,0,1:T(8,128)(2,1)S(1)}, u32[]{:S(2)}) copy-start(bf16[192,2,7168]{2,0,1:T(8,128)(2,1)S(1)} %all_to_all.38) | copy-start | bytes 16515076
  13.6 16.4 %copy-start.6 = (s32[24]{0:T(128)S(1)}, s32[24]{0:T(128)}, u32[]{:S(2)}) copy-start(s32[24]{0:T(128)} %param.23) | copy-start | bytes 292
  14.4 16.1 %collective-permute-start.2 = (bf16[256,256]{1,0:T(8,128)(2,1)}, bf16[256,256]{1,0:T(8,128)(2,1)S(1)}, u32[]{:S(2)}, u32[]{:S(2)}) collective-permute-start(bf16[256,256]{1,0:T(8,128)(2,1)} %fusion.3), channel_id=1, source_target_pairs={{0,4},{2,6},{4,8},{6,10},{8,12},{10,14},{1,5},{3,7},{5,9},{7,11},{... | collective-permute-start | bytes 393224 | tf_op jit(solution)/shard_map/ppermute | solution.py:21
  19.4 11.1 %collective-permute-start.3 = (bf16[384,256]{1,0:T(8,128)(2,1)S(1)}, bf16[384,256]{1,0:T(8,128)(2,1)S(1)}, u32[]{:S(2)}, u32[]{:S(2)}) collective-permute-start(bf16[384,256]{1,0:T(8,128)(2,1)S(1)} %pad_maximum_fusion.8), channel_id=1, source_target_pairs={{0,2},{2,4},{4,6},{6,8},{8,10},{10,12},{12,14},{1,3},{3,5},{5,7},{... | collective-permute-start | bytes 589832 | tf_op jit(solution)/shard_map/ppermute | solution.py:21
  23.0 16.7 %collective-permute-start = (bf16[256,768]{1,0:T(8,128)(2,1)S(1)}, bf16[256,768]{1,0:T(8,128)(2,1)S(1)}, u32[]{:S(2)}, u32[]{:S(2)}) collective-permute-start(bf16[256,768]{1,0:T(8,128)(2,1)S(1)} %fusion.1), channel_id=1, source_target_pairs={{0,4},{2,6},{4,8},{6,10},{8,12},{10,14},{1,5},{3,7},{5,9},{7,11},{... | collective-permute-start | bytes 1179656 | tf_op jit(solution)/shard_map/ppermute | solution.py:21
  26.5 19.7 %collective-permute-start.1 = (bf16[384,768]{1,0:T(8,128)(2,1)S(1)}, bf16[384,768]{1,0:T(8,128)(2,1)S(1)}, u32[]{:S(2)}, u32[]{:S(2)}) collective-permute-start(bf16[384,768]{1,0:T(8,128)(2,1)S(1)} %pad_maximum_fusion.3), channel_id=1, source_target_pairs={{0,2},{2,4},{4,6},{6,8},{8,10},{10,12},{12,14},{1,3},{3,5},{5,7},{... | collective-permute-start | bytes 1769480 | tf_op jit(solution)/shard_map/ppermute | solution.py:21
  36.9 7.7 %collective-permute-start.6 = (bf16[384,256]{1,0:T(8,128)(2,1)S(1)}, bf16[384,256]{1,0:T(8,128)(2,1)S(1)}, u32[]{:S(2)}, u32[]{:S(2)}) collective-permute-start(bf16[384,256]{1,0:T(8,128)(2,1)S(1)} %slice.270), channel_id=1, source_target_pairs={{2,0},{4,2},{6,4},{8,6},{10,8},{12,10},{14,12},{3,1},{5,3},{7,5},{... | collective-permute-start | bytes 589832 | tf_op jit(solution)/shard_map/ppermute | solution.py:21
  38.2 26.0 %collective-permute-start.7 = (bf16[256,256]{1,0:T(8,128)(2,1)S(1)}, bf16[256,256]{1,0:T(8,128)(2,1)S(1)}, u32[]{:S(2)}, u32[]{:S(2)}) collective-permute-start(bf16[256,256]{1,0:T(8,128)(2,1)S(1)} %slice.272), channel_id=1, source_target_pairs={{4,0},{6,2},{8,4},{10,6},{12,8},{14,10},{5,1},{7,3},{9,5},{11,7},{... | collective-permute-start | bytes 393224 | tf_op jit(solution)/shard_map/ppermute | solution.py:21
  62.9 18.0 %collective-permute-start.4 = (bf16[384,768]{1,0:T(8,128)(2,1)S(1)}, bf16[384,768]{1,0:T(8,128)(2,1)S(1)}, u32[]{:S(2)}, u32[]{:S(2)}) collective-permute-start(bf16[384,768]{1,0:T(8,128)(2,1)S(1)} %slice.265), channel_id=1, source_target_pairs={{2,0},{4,2},{6,4},{8,6},{10,8},{12,10},{14,12},{3,1},{5,3},{7,5},{... | collective-permute-start | bytes 1769480 | tf_op jit(solution)/shard_map/ppermute | solution.py:21
  64.3 31.9 %collective-permute-start.5 = (bf16[256,768]{1,0:T(8,128)(2,1)S(1)}, bf16[256,768]{1,0:T(8,128)(2,1)S(1)}, u32[]{:S(2)}, u32[]{:S(2)}) collective-permute-start(bf16[256,768]{1,0:T(8,128)(2,1)S(1)} %slice.267), channel_id=1, source_target_pairs={{4,0},{6,2},{8,4},{10,6},{12,8},{14,10},{5,1},{7,3},{9,5},{11,7},{... | collective-permute-start | bytes 1179656 | tf_op jit(solution)/shard_map/ppermute | solution.py:21

commit v13 on v9

--- a/solution.py
+++ b/solution.py
@@ -48,9 +48,9 @@
             qs, kwin, (((1,), (1,)), ((), ())), preferred_element_type=jnp.float32)
         masked = jnp.where(mask, scores, -1e30)
         top = jnp.max(masked, axis=1, keepdims=True)
-        total = jnp.sum(jnp.where(mask, jnp.exp(masked - top), 0.0), axis=1, keepdims=True)
+        total = jnp.sum(jnp.exp(masked - top), axis=1, keepdims=True)
         lse = top + jnp.log(total)
-        probs = jnp.where(mask, jnp.exp(masked - lse), 0.0)
+        probs = jnp.exp(masked - lse)
         dprob = lax.dot_general(
             dos, vwin, (((1,), (1,)), ((), ())), preferred_element_type=jnp.float32)
         dscore = (probs * (dprob - delta)).astype(jnp.bfloat16)
@@ -96,7 +96,8 @@
             jax.ShapeDtypeStruct((key_rows, kv_cols), jnp.float32),
         ],
         compiler_params=pltpu.CompilerParams(
-            dimension_semantics=("arbitrary",), vmem_limit_bytes=48 * 1024 * 1024),
+            dimension_semantics=("arbitrary",), vmem_limit_bytes=48 * 1024 * 1024,
+            allow_input_fusion=[False] * 5 + [True] * 2),
     )(qdoc, kdoc, fused, fused, fused, keys, values)
 
 
@@ -157,9 +158,7 @@
         q_parts.append(query_sum)
         k_parts.append(total[:, :per].astype(jnp.bfloat16))
         v_parts.append(total[:, per:].astype(jnp.bfloat16))
-    query_back = lax.all_to_all(
-        jnp.concatenate(q_parts, axis=1), "head", split_axis=0, concat_axis=1, tiled=True)
-    finished = jnp.concatenate(k_parts + v_parts, axis=1)
+    finished = jnp.concatenate(q_parts + k_parts + v_parts, axis=1)
     returned = lax.all_to_all(finished, "head", split_axis=0, concat_axis=1, tiled=True)
     width = finished.shape[1]
 
@@ -167,7 +166,7 @@
         return jnp.concatenate(
             [returned[:, p * width + begin:p * width + begin + size] for p in range(peers)], axis=1)
 
-    return query_back, gather(0, kv_cols), gather(kv_cols, kv_cols)
+    return gather(0, q_cols), gather(q_cols, kv_cols), gather(q_cols + kv_cols, kv_cols)
 
 
 def solution(mesh):

time: 98.7 us -> 101 us (1.023)
  waiting for transfers between devices: 22.6 us -> 28.9 us
  blocking collectives: 17.5 us -> 13.8 us
  Pallas kernels: 24 us -> 22 us
  other arithmetic: 3.75 us -> 4.8 us
    ppermute x8, waiting for transfers between devices: 22.6 us -> 28.9 us  [shifted(): return lax.ppermute(block, axis, route)]
    all_to_all x1 -> x0, blocking collectives: 5 us -> none  [per_device(): lax.all_to_all(jnp.concatenate(q_parts, axis=1), 'head', split_axis=0, co...]
    pallas_call x2, Pallas kernels: 24 us -> 22 us  [local_backward(): pl.pallas_call(kernel, grid=(kv_heads,), in_specs=[pl.BlockSpec((rows, 1)...]
    unnamed x28 -> x33, local copies, waits for them, and re-layouts: 6.06 us -> 7.32 us
    all_to_all x1, blocking collectives: 4.37 us -> 5.63 us  [per_device(): lax.all_to_all(finished, 'head', split_axis=0, concat_axis=1, tiled=True)]
    concatenate x2 -> x3, other arithmetic: 1.59 us -> 2.84 us  [gather(): jnp.concatenate([returned[:, p * width + begin:p * width + begin + size]...]
    all_to_all x1 -> x0, local copies, waits for them, and re-layouts: 1.24 us -> none  [per_device(): lax.all_to_all(jnp.concatenate(q_parts, axis=1), 'head', split_axis=0, co...]
  transfers between devices with their start and end apart: 8 -> 8, of which waited for: 4 -> 5; matrix products, arithmetic and copies ran while one was open for 4% -> 3% of each run, Pallas kernels for 24% -> 22%
where the time goes in v13:
time: 101 us; the launch traced here: 100 us
  waiting for transfers between devices  28.9 us (29%)
  Pallas kernels  22 us (22%)
  starting transfers between devices  20.7 us (20%)
  blocking collectives  13.8 us (14%)
  local copies, waits for them, and re-layouts  8.83 us (9%)
  other arithmetic  4.8 us (5%)
  between operations  1.18 us (1%)
    ppermute x8, waiting for transfers between devices, shifted(): return lax.ppermute(block, axis, route)  28.9 us
    pallas_call x2, Pallas kernels, local_backward(): pl.pallas_call(kernel, grid=(kv_heads,), in_specs=[pl.BlockSpec((rows, 1)...  22 us
    ppermute x8, starting transfers between devices, shifted(): return lax.ppermute(block, axis, route)  20.7 us
    all_to_all x1, blocking collectives, per_device(): lax.all_to_all(outgoing, 'head', split_axis=1, concat_axis=0, tiled=True)  8.16 us
    unnamed x33, local copies, waits for them, and re-layouts  7.32 us
    all_to_all x1, blocking collectives, per_device(): lax.all_to_all(finished, 'head', split_axis=0, concat_axis=1, tiled=True)  5.63 us
    concatenate x3, other arithmetic, gather(): jnp.concatenate([returned[:, p * width + begin:p * width + begin + size]...  2.84 us
  transfers between devices with their start and end apart: 8, of which 5 were waited for; matrix products, arithmetic and copies ran while one was open for 3% of the time, Pallas kernels for 22%

profile of v13, /device:TPU:0, one launch (start us, length us, event | category | flops | bytes accessed | tf_op | source)
XLA Modules:
  0.0 100.2 jit_solution(15613899789797580149)
XLA Ops:
  0.7 1.4 %slice_dynamic-update-slice_fusion.5 = bf16[192,14336]{1,0:T(8,128)(2,1)S(1)} fusion(bf16[192,4096]{1,0:T(8,128)(2,1)} %param.18), kind=kLoop, calls=%fused_computation.9 | loop fusion | bytes 1572864
  2.0 1.3 %slice_dynamic-update-slice_fusion.4 = bf16[192,14336]{1,0:T(8,128)(2,1)S(1)} fusion(bf16[192,14336]{1,0:T(8,128)(2,1)S(1)} %slice_dynamic-update-slice_fusion.5, bf16[192,4096]{1,0:T(8,128)(2,1)} %param.22), kind=kLoop, calls=%fused_computation.8 | loop fusion | bytes 1572864
  3.5 0.3 copy-done.1
  3.8 1.0 %copy-done.2 = bf16[192,4096]{1,0:T(8,128)(2,1)S(1)} copy-done((bf16[192,4096]{1,0:T(8,128)(2,1)S(1)}, bf16[192,4096]{1,0:T(8,128)(2,1)}, u32[]{:S(2)}) %copy-start.2) | copy-done | bytes 1572888
  5.0 0.4 copy.21
  5.5 8.2 %all_to_all.38 = bf16[192,2,7168]{2,0,1:T(8,128)(2,1)S(1)} all-to-all(bf16[192,2,7168]{2,0,1:T(8,128)(2,1)S(1)} %bitcast.30), channel_id=1, replica_groups=mesh['groups'=2,'ctx'=8,'head'=2] {'head'}, dimensions={1} | all-to-all | bytes 11010048 | tf_op jit(solution)/shard_map/all_to_all | solution.py:113
  13.6 2.4 %copy-done = bf16[192,2,7168]{2,0,1:T(8,128)(2,1)} copy-done((bf16[192,2,7168]{2,0,1:T(8,128)(2,1)}, bf16[192,2,7168]{2,0,1:T(8,128)(2,1)S(1)}, u32[]{:S(2)}) %copy-start) | copy-done | bytes 5505048
  16.1 5.0 %collective-permute-start.2 = (bf16[256,512]{1,0:T(8,128)(2,1)S(1)}, bf16[256,512]{1,0:T(8,128)(2,1)S(1)}, u32[]{:S(2)}, u32[]{:S(2)}) collective-permute-start(bf16[256,512]{1,0:T(8,128)(2,1)S(1)} %fusion.2), channel_id=1, source_target_pairs={{0,4},{2,6},{4,8},{6,10},{8,12},{10,14},{1,5},{3,7},{5,9},{7,11},{... | collective-permute-start | bytes 786440 | tf_op jit(solution)/shard_map/ppermute | solution.py:20
  21.1 3.4 %collective-permute-start.3 = (bf16[384,512]{1,0:T(8,128)(2,1)S(1)}, bf16[384,512]{1,0:T(8,128)(2,1)S(1)}, u32[]{:S(2)}, u32[]{:S(2)}) collective-permute-start(bf16[384,512]{1,0:T(8,128)(2,1)S(1)} %pad_maximum_fusion.6), channel_id=1, source_target_pairs={{0,2},{2,4},{4,6},{6,8},{8,10},{10,12},{12,14},{1,3},{3,5},{5,7},{... | collective-permute-start | bytes 1179656 | tf_op jit(solution)/shard_map/ppermute | solution.py:20
  24.6 0.7 fusion.3
  25.3 3.5 %collective-permute-start = (bf16[256,512]{1,0:T(8,128)(2,1)}, bf16[256,512]{1,0:T(8,128)(2,1)S(1)}, u32[]{:S(2)}, u32[]{:S(2)}) collective-permute-start(bf16[256,512]{1,0:T(8,128)(2,1)} %fusion.3), channel_id=1, source_target_pairs={{0,4},{2,6},{4,8},{6,10},{8,12},{10,14},{1,5},{3,7},{5,9},{7,11},{... | collective-permute-start | bytes 786440 | tf_op jit(solution)/shard_map/ppermute | solution.py:20
  28.8 3.4 %collective-permute-start.1 = (bf16[384,512]{1,0:T(8,128)(2,1)S(1)}, bf16[384,512]{1,0:T(8,128)(2,1)S(1)}, u32[]{:S(2)}, u32[]{:S(2)}) collective-permute-start(bf16[384,512]{1,0:T(8,128)(2,1)S(1)} %pad_maximum_fusion.5), channel_id=1, source_target_pairs={{0,2},{2,4},{4,6},{6,8},{8,10},{10,12},{12,14},{1,3},{3,5},{5,7},{... | collective-permute-start | bytes 1179656 | tf_op jit(solution)/shard_map/ppermute | solution.py:20
  32.8 1.6 %collective-permute-done = bf16[256,512]{1,0:T(8,128)(2,1)S(1)} collective-permute-done((bf16[256,512]{1,0:T(8,128)(2,1)}, bf16[256,512]{1,0:T(8,128)(2,1)S(1)}, u32[]{:S(2)}, u32[]{:S(2)}) %collective-permute-start) | collective-permute-done | bytes 262176 | tf_op jit(solution)/shard_map/ppermute | solution.py:20
  34.6 11.0 %shard_map.96 = (bf16[384,1024]{1,0:T(8,128)(2,1)S(1)}, f32[1024,256]{1,0:T(8,128)S(1)}, f32[1024,256]{1,0:T(8,128)S(1)}) custom-call(s32[384,1]{1,0:T(8,128)S(1)} %bitcast.19, s32[1,1024]{1,0:T(1,128)S(1)} %bitcast.21, bf16[384,7168]{1,0:T(8,128)(2,1)} %bitcast.24, bf16[384,7168]{1,0:T(8,128)(2,1)} %bitcast.25, bf16[384,7168]{1,0:T(8,128)(2,1)} %bitcast.26, ...), custom_call_target="tpu_custom_call" | custom-call | tf_op jit(solution)/shard_map/pallas_call | solution.py:84
  45.6 0.1 constant_dynamic-update-slice_fusion.3
  45.7 0.2 constant_dynamic-update-slice_fusion.2
  46.1 1.5 %collective-permute-start.6 = (bf16[384,512]{1,0:T(8,128)(2,1)S(1)}, bf16[384,512]{1,0:T(8,128)(2,1)S(1)}, u32[]{:S(2)}, u32[]{:S(2)}) collective-permute-start(bf16[384,512]{1,0:T(8,128)(2,1)S(1)} %slice.270), channel_id=1, source_target_pairs={{2,0},{4,2},{6,4},{8,6},{10,8},{12,10},{14,12},{3,1},{5,3},{7,5},{... | collective-permute-start | bytes 1179656 | tf_op jit(solution)/shard_map/ppermute | solution.py:20
  47.7 11.0 %shard_map.95 = (bf16[384,1024]{1,0:T(8,128)(2,1)S(1)}, f32[1024,256]{1,0:T(8,128)S(1)}, f32[1024,256]{1,0:T(8,128)S(1)}) custom-call(s32[384,1]{1,0:T(8,128)S(1)} %bitcast.20, s32[1,1024]{1,0:T(1,128)S(1)} %bitcast.22, bf16[384,7168]{1,0:T(8,128)(2,1)} %bitcast.27, bf16[384,7168]{1,0:T(8,128)(2,1)} %bitcast.28, bf16[384,7168]{1,0:T(8,128)(2,1)} %bitcast.29, ...), custom_call_target="tpu_custom_call" | custom-call | tf_op jit(solution)/shard_map/pallas_call | solution.py:84
  58.7 0.1 constant_dynamic-update-slice_fusion.1
  58.9 0.2 constant_dynamic-update-slice_fusion
  59.3 1.3 %collective-permute-start.7 = (bf16[256,512]{1,0:T(8,128)(2,1)S(1)}, bf16[256,512]{1,0:T(8,128)(2,1)S(1)}, u32[]{:S(2)}, u32[]{:S(2)}) collective-permute-start(bf16[256,512]{1,0:T(8,128)(2,1)S(1)} %slice.272), channel_id=1, source_target_pairs={{4,0},{6,2},{8,4},{10,6},{12,8},{14,10},{5,1},{7,3},{9,5},{11,7},{... | collective-permute-start | bytes 786440 | tf_op jit(solution)/shard_map/ppermute | solution.py:20
  60.6 1.3 %collective-permute-start.4 = (bf16[384,512]{1,0:T(8,128)(2,1)S(1)}, bf16[384,512]{1,0:T(8,128)(2,1)S(1)}, u32[]{:S(2)}, u32[]{:S(2)}) collective-permute-start(bf16[384,512]{1,0:T(8,128)(2,1)S(1)} %slice.265), channel_id=1, source_target_pairs={{2,0},{4,2},{6,4},{8,6},{10,8},{12,10},{14,12},{3,1},{5,3},{7,5},{... | collective-permute-start | bytes 1179656 | tf_op jit(solution)/shard_map/ppermute | solution.py:20
  61.9 1.3 %collective-permute-start.5 = (bf16[256,512]{1,0:T(8,128)(2,1)S(1)}, bf16[256,512]{1,0:T(8,128)(2,1)S(1)}, u32[]{:S(2)}, u32[]{:S(2)}) collective-permute-start(bf16[256,512]{1,0:T(8,128)(2,1)S(1)} %slice.267), channel_id=1, source_target_pairs={{4,0},{6,2},{8,4},{10,6},{12,8},{14,10},{5,1},{7,3},{9,5},{11,7},{... | collective-permute-start | bytes 786440 | tf_op jit(solution)/shard_map/ppermute | solution.py:20
  63.3 1.5 %collective-permute-done.6 = bf16[384,512]{1,0:T(8,128)(2,1)S(1)} collective-permute-done((bf16[384,512]{1,0:T(8,128)(2,1)S(1)}, bf16[384,512]{1,0:T(8,128)(2,1)S(1)}, u32[]{:S(2)}, u32[]{:S(2)}) %collective-permute-start.6) | collective-permute-done | bytes 393248 | tf_op jit(solution)/shard_map/ppermute | solution.py:20
  64.9 14.6 %collective-permute-done.7 = bf16[256,512]{1,0:T(8,128)(2,1)S(1)} collective-permute-done((bf16[256,512]{1,0:T(8,128)(2,1)S(1)}, bf16[256,512]{1,0:T(8,128)(2,1)S(1)}, u32[]{:S(2)}, u32[]{:S(2)}) %collective-permute-start.7) | collective-permute-done | bytes 262176 | tf_op jit(solution)/shard_map/ppermute | solution.py:20
  79.7 0.2 collective-permute-done.4
  80.0 11.0 %collective-permute-done.5 = bf16[256,512]{1,0:T(8,128)(2,1)S(1)} collective-permute-done((bf16[256,512]{1,0:T(8,128)(2,1)S(1)}, bf16[256,512]{1,0:T(8,128)(2,1)S(1)}, u32[]{:S(2)}, u32[]{:S(2)}) %collective-permute-start.5) | collective-permute-done | bytes 262176 | tf_op jit(solution)/shard_map/ppermute | solution.py:20
  91.3 5.6 %all_to_all.39 = bf16[2,192,3072]{2,1,0:T(8,128)(2,1)S(1)} all-to-all(bf16[2,192,3072]{2,1,0:T(8,128)(2,1)S(1)} %bitcast.35), channel_id=1, replica_groups=mesh['groups'=2,'ctx'=8,'head'=2] {'head'}, dimensions={0} | all-to-all | bytes 4718592 | tf_op jit(solution)/shard_map/all_to_all | solution.py:162
  96.9 0.2 copy.16
  97.3 0.8 pad_maximum_fusion.8
  98.1 0.8 pad_maximum_fusion.7
  98.9 1.3 %pad_maximum_fusion = bf16[192,4096]{1,0:T(8,128)(2,1)} fusion(bf16[192,2048]{1,0:T(8,128)(2,1)S(1)} %get-tuple-element.88, bf16[192,2048]{1,0:T(8,128)(2,1)S(1)} %get-tuple-element.87), kind=kLoop, calls=%fused_computation.1 | loop fusion | flops 3145728 | bytes 3145728 | tf_op jit(solution)/shard_map/concatenate | solution.py:166
  (59 shorter events, 2.5 us)
Async XLA Ops:
  0.6 2.7 %copy-start.3 = (bf16[192,4096]{1,0:T(8,128)(2,1)S(1)}, bf16[192,4096]{1,0:T(8,128)(2,1)}, u32[]{:S(2)}) copy-start(bf16[192,4096]{1,0:T(8,128)(2,1)} %param.21) | copy-start | bytes 4718596
  0.6 2.8 %copy-start.4 = (bf16[192,1024]{1,0:T(8,128)(2,1)S(1)}, bf16[192,1024]{1,0:T(8,128)(2,1)}, u32[]{:S(2)}) copy-start(bf16[192,1024]{1,0:T(8,128)(2,1)} %param.19) | copy-start | bytes 1179652
  0.7 2.8 %copy-start.5 = (bf16[192,1024]{1,0:T(8,128)(2,1)S(1)}, bf16[192,1024]{1,0:T(8,128)(2,1)}, u32[]{:S(2)}) copy-start(bf16[192,1024]{1,0:T(8,128)(2,1)} %param.20) | copy-start | bytes 1179652
  2.0 1.8 %copy-start.1 = (bf16[192,4096]{1,0:T(8,128)(2,1)S(1)}, bf16[192,4096]{1,0:T(8,128)(2,1)}, u32[]{:S(2)}) copy-start(bf16[192,4096]{1,0:T(8,128)(2,1)} %param.18) | copy-start | bytes 4718596
  3.4 1.5 %copy-start.2 = (bf16[192,4096]{1,0:T(8,128)(2,1)S(1)}, bf16[192,4096]{1,0:T(8,128)(2,1)}, u32[]{:S(2)}) copy-start(bf16[192,4096]{1,0:T(8,128)(2,1)} %param.22) | copy-start | bytes 4718596
  13.6 2.4 %copy-start = (bf16[192,2,7168]{2,0,1:T(8,128)(2,1)}, bf16[192,2,7168]{2,0,1:T(8,128)(2,1)S(1)}, u32[]{:S(2)}) copy-start(bf16[192,2,7168]{2,0,1:T(8,128)(2,1)S(1)} %all_to_all.38) | copy-start | bytes 16515076
  13.6 18.6 %copy-start.6 = (s32[24]{0:T(128)S(1)}, s32[24]{0:T(128)}, u32[]{:S(2)}) copy-start(s32[24]{0:T(128)} %param.23) | copy-start | bytes 292
  16.1 16.6 %collective-permute-start.2 = (bf16[256,512]{1,0:T(8,128)(2,1)S(1)}, bf16[256,512]{1,0:T(8,128)(2,1)S(1)}, u32[]{:S(2)}, u32[]{:S(2)}) collective-permute-start(bf16[256,512]{1,0:T(8,128)(2,1)S(1)} %fusion.2), channel_id=1, source_target_pairs={{0,4},{2,6},{4,8},{6,10},{8,12},{10,14},{1,5},{3,7},{5,9},{7,11},{... | collective-permute-start | bytes 786440 | tf_op jit(solution)/shard_map/ppermute | solution.py:20
  21.1 13.2 %collective-permute-start.3 = (bf16[384,512]{1,0:T(8,128)(2,1)S(1)}, bf16[384,512]{1,0:T(8,128)(2,1)S(1)}, u32[]{:S(2)}, u32[]{:S(2)}) collective-permute-start(bf16[384,512]{1,0:T(8,128)(2,1)S(1)} %pad_maximum_fusion.6), channel_id=1, source_target_pairs={{0,2},{2,4},{4,6},{6,8},{8,10},{10,12},{12,14},{1,3},{3,5},{5,7},{... | collective-permute-start | bytes 1179656 | tf_op jit(solution)/shard_map/ppermute | solution.py:20
  25.3 9.0 %collective-permute-start = (bf16[256,512]{1,0:T(8,128)(2,1)}, bf16[256,512]{1,0:T(8,128)(2,1)S(1)}, u32[]{:S(2)}, u32[]{:S(2)}) collective-permute-start(bf16[256,512]{1,0:T(8,128)(2,1)} %fusion.3), channel_id=1, source_target_pairs={{0,4},{2,6},{4,8},{6,10},{8,12},{10,14},{1,5},{3,7},{5,9},{7,11},{... | collective-permute-start | bytes 786440 | tf_op jit(solution)/shard_map/ppermute | solution.py:20
  28.8 18.8 %collective-permute-start.1 = (bf16[384,512]{1,0:T(8,128)(2,1)S(1)}, bf16[384,512]{1,0:T(8,128)(2,1)S(1)}, u32[]{:S(2)}, u32[]{:S(2)}) collective-permute-start(bf16[384,512]{1,0:T(8,128)(2,1)S(1)} %pad_maximum_fusion.5), channel_id=1, source_target_pairs={{0,2},{2,4},{4,6},{6,8},{8,10},{10,12},{12,14},{1,3},{3,5},{5,7},{... | collective-permute-start | bytes 1179656 | tf_op jit(solution)/shard_map/ppermute | solution.py:20
  46.1 18.7 %collective-permute-start.6 = (bf16[384,512]{1,0:T(8,128)(2,1)S(1)}, bf16[384,512]{1,0:T(8,128)(2,1)S(1)}, u32[]{:S(2)}, u32[]{:S(2)}) collective-permute-start(bf16[384,512]{1,0:T(8,128)(2,1)S(1)} %slice.270), channel_id=1, source_target_pairs={{2,0},{4,2},{6,4},{8,6},{10,8},{12,10},{14,12},{3,1},{5,3},{7,5},{... | collective-permute-start | bytes 1179656 | tf_op jit(solution)/shard_map/ppermute | solution.py:20
  59.3 20.2 %collective-permute-start.7 = (bf16[256,512]{1,0:T(8,128)(2,1)S(1)}, bf16[256,512]{1,0:T(8,128)(2,1)S(1)}, u32[]{:S(2)}, u32[]{:S(2)}) collective-permute-start(bf16[256,512]{1,0:T(8,128)(2,1)S(1)} %slice.272), channel_id=1, source_target_pairs={{4,0},{6,2},{8,4},{10,6},{12,8},{14,10},{5,1},{7,3},{9,5},{11,7},{... | collective-permute-start | bytes 786440 | tf_op jit(solution)/shard_map/ppermute | solution.py:20
  60.6 19.3 %collective-permute-start.4 = (bf16[384,512]{1,0:T(8,128)(2,1)S(1)}, bf16[384,512]{1,0:T(8,128)(2,1)S(1)}, u32[]{:S(2)}, u32[]{:S(2)}) collective-permute-start(bf16[384,512]{1,0:T(8,128)(2,1)S(1)} %slice.265), channel_id=1, source_target_pairs={{2,0},{4,2},{6,4},{8,6},{10,8},{12,10},{14,12},{3,1},{5,3},{7,5},{... | collective-permute-start | bytes 1179656 | tf_op jit(solution)/shard_map/ppermute | solution.py:20
  61.9 29.1 %collective-permute-start.5 = (bf16[256,512]{1,0:T(8,128)(2,1)S(1)}, bf16[256,512]{1,0:T(8,128)(2,1)S(1)}, u32[]{:S(2)}, u32[]{:S(2)}) collective-permute-start(bf16[256,512]{1,0:T(8,128)(2,1)S(1)} %slice.267), channel_id=1, source_target_pairs={{4,0},{6,2},{8,4},{10,6},{12,8},{14,10},{5,1},{7,3},{9,5},{11,7},{... | collective-permute-start | bytes 786440 | tf_op jit(solution)/shard_map/ppermute | solution.py:20

commit v14 on v13

--- a/solution.py
+++ b/solution.py
@@ -58,11 +58,12 @@
         for r in range(query_group):
             dq_ref[rows, pl.ds(r * HEAD_SIZE, HEAD_SIZE)] = (
                 dq[r * BLK:(r + 1) * BLK].astype(dq_ref.dtype))
-        dk_ref[pl.ds(k0, window), :] += scale * lax.dot_general(
+        dk_ref[pl.ds(k0, window), :] += lax.dot_general(
             dscore, qs, (((0,), (0,)), ((), ())), preferred_element_type=jnp.float32)
         dv_ref[pl.ds(k0, window), :] += lax.dot_general(
             probs.astype(jnp.bfloat16), dos, (((0,), (0,)), ((), ())),
             preferred_element_type=jnp.float32)
+    dk_ref[...] = scale * dk_ref[...]
 
 
 def local_backward(qdoc, kdoc, fused, q_cols, all_kv, head0, keys, values):
@@ -97,7 +98,7 @@
         ],
         compiler_params=pltpu.CompilerParams(
             dimension_semantics=("arbitrary",), vmem_limit_bytes=48 * 1024 * 1024,
-            allow_input_fusion=[False] * 5 + [True] * 2),
+            allow_input_fusion=[True] * 2 + [False] * 3 + [True] * 2),
     )(qdoc, kdoc, fused, fused, fused, keys, values)
 
 

time: 101 us -> 100 us (0.990)
  no operation moved by 1% of the time
where the time goes in v14:
time: 100 us
  waiting for transfers between devices  28.9 us (29%)
  Pallas kernels  21.9 us (22%)
  starting transfers between devices  20.7 us (21%)
  blocking collectives  13.8 us (14%)
  local copies, waits for them, and re-layouts  8.83 us (9%)
  other arithmetic  4.8 us (5%)
  between operations  1.18 us (1%)
    ppermute x8, waiting for transfers between devices, shifted(): return lax.ppermute(block, axis, route)  28.9 us
    pallas_call x2, Pallas kernels, local_backward(): pl.pallas_call(kernel, grid=(kv_heads,), in_specs=[pl.BlockSpec((rows, 1)...  21.9 us
    ppermute x8, starting transfers between devices, shifted(): return lax.ppermute(block, axis, route)  20.7 us
    all_to_all x1, blocking collectives, per_device(): lax.all_to_all(outgoing, 'head', split_axis=1, concat_axis=0, tiled=True)  8.16 us
    unnamed x33, local copies, waits for them, and re-layouts  7.32 us
    all_to_all x1, blocking collectives, per_device(): lax.all_to_all(finished, 'head', split_axis=0, concat_axis=1, tiled=True)  5.63 us
    concatenate x3, other arithmetic, gather(): jnp.concatenate([returned[:, p * width + begin:p * width + begin + size]...  2.84 us
  transfers between devices with their start and end apart: 8, of which 5 were waited for; matrix products, arithmetic and copies ran while one was open for 3% of the time, Pallas kernels for 22%

profile of v14, /device:TPU:0, one launch (start us, length us, event | category | flops | bytes accessed | tf_op | source)
XLA Modules:
  0.0 100.0 jit_solution(2850788946577953640)
XLA Ops:
  0.7 1.4 %slice_dynamic-update-slice_fusion.5 = bf16[192,14336]{1,0:T(8,128)(2,1)S(1)} fusion(bf16[192,4096]{1,0:T(8,128)(2,1)} %param.18), kind=kLoop, calls=%fused_computation.9 | loop fusion | bytes 1572864
  2.0 1.3 %slice_dynamic-update-slice_fusion.4 = bf16[192,14336]{1,0:T(8,128)(2,1)S(1)} fusion(bf16[192,14336]{1,0:T(8,128)(2,1)S(1)} %slice_dynamic-update-slice_fusion.5, bf16[192,4096]{1,0:T(8,128)(2,1)} %param.22), kind=kLoop, calls=%fused_computation.8 | loop fusion | bytes 1572864
  3.5 0.3 copy-done.1
  3.8 1.0 %copy-done.2 = bf16[192,4096]{1,0:T(8,128)(2,1)S(1)} copy-done((bf16[192,4096]{1,0:T(8,128)(2,1)S(1)}, bf16[192,4096]{1,0:T(8,128)(2,1)}, u32[]{:S(2)}) %copy-start.2) | copy-done | bytes 1572888
  5.0 0.4 copy.21
  5.5 8.2 %all_to_all.38 = bf16[192,2,7168]{2,0,1:T(8,128)(2,1)S(1)} all-to-all(bf16[192,2,7168]{2,0,1:T(8,128)(2,1)S(1)} %bitcast.30), channel_id=1, replica_groups=mesh['groups'=2,'ctx'=8,'head'=2] {'head'}, dimensions={1} | all-to-all | bytes 11010048 | tf_op jit(solution)/shard_map/all_to_all | solution.py:114
  13.6 2.4 %copy-done = bf16[192,2,7168]{2,0,1:T(8,128)(2,1)} copy-done((bf16[192,2,7168]{2,0,1:T(8,128)(2,1)}, bf16[192,2,7168]{2,0,1:T(8,128)(2,1)S(1)}, u32[]{:S(2)}) %copy-start) | copy-done | bytes 5505048
  16.1 5.0 %collective-permute-start.2 = (bf16[256,512]{1,0:T(8,128)(2,1)S(1)}, bf16[256,512]{1,0:T(8,128)(2,1)S(1)}, u32[]{:S(2)}, u32[]{:S(2)}) collective-permute-start(bf16[256,512]{1,0:T(8,128)(2,1)S(1)} %fusion.2), channel_id=1, source_target_pairs={{0,4},{2,6},{4,8},{6,10},{8,12},{10,14},{1,5},{3,7},{5,9},{7,11},{... | collective-permute-start | bytes 786440 | tf_op jit(solution)/shard_map/ppermute | solution.py:20
  21.1 3.4 %collective-permute-start.3 = (bf16[384,512]{1,0:T(8,128)(2,1)S(1)}, bf16[384,512]{1,0:T(8,128)(2,1)S(1)}, u32[]{:S(2)}, u32[]{:S(2)}) collective-permute-start(bf16[384,512]{1,0:T(8,128)(2,1)S(1)} %pad_maximum_fusion.6), channel_id=1, source_target_pairs={{0,2},{2,4},{4,6},{6,8},{8,10},{10,12},{12,14},{1,3},{3,5},{5,7},{... | collective-permute-start | bytes 1179656 | tf_op jit(solution)/shard_map/ppermute | solution.py:20
  24.6 0.7 fusion.3
  25.3 3.5 %collective-permute-start = (bf16[256,512]{1,0:T(8,128)(2,1)}, bf16[256,512]{1,0:T(8,128)(2,1)S(1)}, u32[]{:S(2)}, u32[]{:S(2)}) collective-permute-start(bf16[256,512]{1,0:T(8,128)(2,1)} %fusion.3), channel_id=1, source_target_pairs={{0,4},{2,6},{4,8},{6,10},{8,12},{10,14},{1,5},{3,7},{5,9},{7,11},{... | collective-permute-start | bytes 786440 | tf_op jit(solution)/shard_map/ppermute | solution.py:20
  28.8 3.4 %collective-permute-start.1 = (bf16[384,512]{1,0:T(8,128)(2,1)S(1)}, bf16[384,512]{1,0:T(8,128)(2,1)S(1)}, u32[]{:S(2)}, u32[]{:S(2)}) collective-permute-start(bf16[384,512]{1,0:T(8,128)(2,1)S(1)} %pad_maximum_fusion.5), channel_id=1, source_target_pairs={{0,2},{2,4},{4,6},{6,8},{8,10},{10,12},{12,14},{1,3},{3,5},{5,7},{... | collective-permute-start | bytes 1179656 | tf_op jit(solution)/shard_map/ppermute | solution.py:20
  32.8 1.6 %collective-permute-done = bf16[256,512]{1,0:T(8,128)(2,1)S(1)} collective-permute-done((bf16[256,512]{1,0:T(8,128)(2,1)}, bf16[256,512]{1,0:T(8,128)(2,1)S(1)}, u32[]{:S(2)}, u32[]{:S(2)}) %collective-permute-start) | collective-permute-done | bytes 262176 | tf_op jit(solution)/shard_map/ppermute | solution.py:20
  34.6 10.9 %shard_map.96 = (bf16[384,1024]{1,0:T(8,128)(2,1)S(1)}, f32[1024,256]{1,0:T(8,128)S(1)}, f32[1024,256]{1,0:T(8,128)S(1)}) custom-call(s32[384,1]{1,0:T(8,128)S(1)} %bitcast.19, s32[1,1024]{1,0:T(1,128)S(1)} %bitcast.21, bf16[384,7168]{1,0:T(8,128)(2,1)} %bitcast.24, bf16[384,7168]{1,0:T(8,128)(2,1)} %bitcast.25, bf16[384,7168]{1,0:T(8,128)(2,1)} %bitcast.26, ...), custom_call_target="tpu_custom_call" | custom-call | tf_op jit(solution)/shard_map/pallas_call | solution.py:85
  45.5 0.1 constant_dynamic-update-slice_fusion.3
  45.7 0.2 constant_dynamic-update-slice_fusion.2
  46.0 1.5 %collective-permute-start.6 = (bf16[384,512]{1,0:T(8,128)(2,1)S(1)}, bf16[384,512]{1,0:T(8,128)(2,1)S(1)}, u32[]{:S(2)}, u32[]{:S(2)}) collective-permute-start(bf16[384,512]{1,0:T(8,128)(2,1)S(1)} %slice.270), channel_id=1, source_target_pairs={{2,0},{4,2},{6,4},{8,6},{10,8},{12,10},{14,12},{3,1},{5,3},{7,5},{... | collective-permute-start | bytes 1179656 | tf_op jit(solution)/shard_map/ppermute | solution.py:20
  47.6 11.0 %shard_map.95 = (bf16[384,1024]{1,0:T(8,128)(2,1)S(1)}, f32[1024,256]{1,0:T(8,128)S(1)}, f32[1024,256]{1,0:T(8,128)S(1)}) custom-call(s32[384,1]{1,0:T(8,128)S(1)} %bitcast.20, s32[1,1024]{1,0:T(1,128)S(1)} %bitcast.22, bf16[384,7168]{1,0:T(8,128)(2,1)} %bitcast.27, bf16[384,7168]{1,0:T(8,128)(2,1)} %bitcast.28, bf16[384,7168]{1,0:T(8,128)(2,1)} %bitcast.29, ...), custom_call_target="tpu_custom_call" | custom-call | tf_op jit(solution)/shard_map/pallas_call | solution.py:85
  58.6 0.1 constant_dynamic-update-slice_fusion.1
  58.8 0.2 constant_dynamic-update-slice_fusion
  59.1 1.3 %collective-permute-start.7 = (bf16[256,512]{1,0:T(8,128)(2,1)S(1)}, bf16[256,512]{1,0:T(8,128)(2,1)S(1)}, u32[]{:S(2)}, u32[]{:S(2)}) collective-permute-start(bf16[256,512]{1,0:T(8,128)(2,1)S(1)} %slice.272), channel_id=1, source_target_pairs={{4,0},{6,2},{8,4},{10,6},{12,8},{14,10},{5,1},{7,3},{9,5},{11,7},{... | collective-permute-start | bytes 786440 | tf_op jit(solution)/shard_map/ppermute | solution.py:20
  60.4 1.3 %collective-permute-start.4 = (bf16[384,512]{1,0:T(8,128)(2,1)S(1)}, bf16[384,512]{1,0:T(8,128)(2,1)S(1)}, u32[]{:S(2)}, u32[]{:S(2)}) collective-permute-start(bf16[384,512]{1,0:T(8,128)(2,1)S(1)} %slice.265), channel_id=1, source_target_pairs={{2,0},{4,2},{6,4},{8,6},{10,8},{12,10},{14,12},{3,1},{5,3},{7,5},{... | collective-permute-start | bytes 1179656 | tf_op jit(solution)/shard_map/ppermute | solution.py:20
  61.7 1.3 %collective-permute-start.5 = (bf16[256,512]{1,0:T(8,128)(2,1)S(1)}, bf16[256,512]{1,0:T(8,128)(2,1)S(1)}, u32[]{:S(2)}, u32[]{:S(2)}) collective-permute-start(bf16[256,512]{1,0:T(8,128)(2,1)S(1)} %slice.267), channel_id=1, source_target_pairs={{4,0},{6,2},{8,4},{10,6},{12,8},{14,10},{5,1},{7,3},{9,5},{11,7},{... | collective-permute-start | bytes 786440 | tf_op jit(solution)/shard_map/ppermute | solution.py:20
  63.2 1.6 %collective-permute-done.6 = bf16[384,512]{1,0:T(8,128)(2,1)S(1)} collective-permute-done((bf16[384,512]{1,0:T(8,128)(2,1)S(1)}, bf16[384,512]{1,0:T(8,128)(2,1)S(1)}, u32[]{:S(2)}, u32[]{:S(2)}) %collective-permute-start.6) | collective-permute-done | bytes 393248 | tf_op jit(solution)/shard_map/ppermute | solution.py:20
  64.8 14.5 %collective-permute-done.7 = bf16[256,512]{1,0:T(8,128)(2,1)S(1)} collective-permute-done((bf16[256,512]{1,0:T(8,128)(2,1)S(1)}, bf16[256,512]{1,0:T(8,128)(2,1)S(1)}, u32[]{:S(2)}, u32[]{:S(2)}) %collective-permute-start.7) | collective-permute-done | bytes 262176 | tf_op jit(solution)/shard_map/ppermute | solution.py:20
  79.5 0.2 collective-permute-done.4
  79.9 11.0 %collective-permute-done.5 = bf16[256,512]{1,0:T(8,128)(2,1)S(1)} collective-permute-done((bf16[256,512]{1,0:T(8,128)(2,1)S(1)}, bf16[256,512]{1,0:T(8,128)(2,1)S(1)}, u32[]{:S(2)}, u32[]{:S(2)}) %collective-permute-start.5) | collective-permute-done | bytes 262176 | tf_op jit(solution)/shard_map/ppermute | solution.py:20
  91.2 5.6 %all_to_all.39 = bf16[2,192,3072]{2,1,0:T(8,128)(2,1)S(1)} all-to-all(bf16[2,192,3072]{2,1,0:T(8,128)(2,1)S(1)} %bitcast.35), channel_id=1, replica_groups=mesh['groups'=2,'ctx'=8,'head'=2] {'head'}, dimensions={0} | all-to-all | bytes 4718592 | tf_op jit(solution)/shard_map/all_to_all | solution.py:163
  96.8 0.2 copy.16
  97.2 0.8 pad_maximum_fusion.8
  98.0 0.8 pad_maximum_fusion.7
  98.8 1.3 %pad_maximum_fusion = bf16[192,4096]{1,0:T(8,128)(2,1)} fusion(bf16[192,2048]{1,0:T(8,128)(2,1)S(1)} %get-tuple-element.88, bf16[192,2048]{1,0:T(8,128)(2,1)S(1)} %get-tuple-element.87), kind=kLoop, calls=%fused_computation.1 | loop fusion | flops 3145728 | bytes 3145728 | tf_op jit(solution)/shard_map/concatenate | solution.py:167
  (59 shorter events, 2.5 us)
Async XLA Ops:
  0.6 2.7 %copy-start.3 = (bf16[192,4096]{1,0:T(8,128)(2,1)S(1)}, bf16[192,4096]{1,0:T(8,128)(2,1)}, u32[]{:S(2)}) copy-start(bf16[192,4096]{1,0:T(8,128)(2,1)} %param.21) | copy-start | bytes 4718596
  0.6 2.8 %copy-start.4 = (bf16[192,1024]{1,0:T(8,128)(2,1)S(1)}, bf16[192,1024]{1,0:T(8,128)(2,1)}, u32[]{:S(2)}) copy-start(bf16[192,1024]{1,0:T(8,128)(2,1)} %param.19) | copy-start | bytes 1179652
  0.7 2.8 %copy-start.5 = (bf16[192,1024]{1,0:T(8,128)(2,1)S(1)}, bf16[192,1024]{1,0:T(8,128)(2,1)}, u32[]{:S(2)}) copy-start(bf16[192,1024]{1,0:T(8,128)(2,1)} %param.20) | copy-start | bytes 1179652
  2.0 1.8 %copy-start.1 = (bf16[192,4096]{1,0:T(8,128)(2,1)S(1)}, bf16[192,4096]{1,0:T(8,128)(2,1)}, u32[]{:S(2)}) copy-start(bf16[192,4096]{1,0:T(8,128)(2,1)} %param.18) | copy-start | bytes 4718596
  3.4 1.5 %copy-start.2 = (bf16[192,4096]{1,0:T(8,128)(2,1)S(1)}, bf16[192,4096]{1,0:T(8,128)(2,1)}, u32[]{:S(2)}) copy-start(bf16[192,4096]{1,0:T(8,128)(2,1)} %param.22) | copy-start | bytes 4718596
  13.6 2.4 %copy-start = (bf16[192,2,7168]{2,0,1:T(8,128)(2,1)}, bf16[192,2,7168]{2,0,1:T(8,128)(2,1)S(1)}, u32[]{:S(2)}) copy-start(bf16[192,2,7168]{2,0,1:T(8,128)(2,1)S(1)} %all_to_all.38) | copy-start | bytes 16515076
  13.6 18.6 %copy-start.6 = (s32[24]{0:T(128)S(1)}, s32[24]{0:T(128)}, u32[]{:S(2)}) copy-start(s32[24]{0:T(128)} %param.23) | copy-start | bytes 292
  16.1 16.6 %collective-permute-start.2 = (bf16[256,512]{1,0:T(8,128)(2,1)S(1)}, bf16[256,512]{1,0:T(8,128)(2,1)S(1)}, u32[]{:S(2)}, u32[]{:S(2)}) collective-permute-start(bf16[256,512]{1,0:T(8,128)(2,1)S(1)} %fusion.2), channel_id=1, source_target_pairs={{0,4},{2,6},{4,8},{6,10},{8,12},{10,14},{1,5},{3,7},{5,9},{7,11},{... | collective-permute-start | bytes 786440 | tf_op jit(solution)/shard_map/ppermute | solution.py:20
  21.1 13.2 %collective-permute-start.3 = (bf16[384,512]{1,0:T(8,128)(2,1)S(1)}, bf16[384,512]{1,0:T(8,128)(2,1)S(1)}, u32[]{:S(2)}, u32[]{:S(2)}) collective-permute-start(bf16[384,512]{1,0:T(8,128)(2,1)S(1)} %pad_maximum_fusion.6), channel_id=1, source_target_pairs={{0,2},{2,4},{4,6},{6,8},{8,10},{10,12},{12,14},{1,3},{3,5},{5,7},{... | collective-permute-start | bytes 1179656 | tf_op jit(solution)/shard_map/ppermute | solution.py:20
  25.3 9.0 %collective-permute-start = (bf16[256,512]{1,0:T(8,128)(2,1)}, bf16[256,512]{1,0:T(8,128)(2,1)S(1)}, u32[]{:S(2)}, u32[]{:S(2)}) collective-permute-start(bf16[256,512]{1,0:T(8,128)(2,1)} %fusion.3), channel_id=1, source_target_pairs={{0,4},{2,6},{4,8},{6,10},{8,12},{10,14},{1,5},{3,7},{5,9},{7,11},{... | collective-permute-start | bytes 786440 | tf_op jit(solution)/shard_map/ppermute | solution.py:20
  28.8 18.7 %collective-permute-start.1 = (bf16[384,512]{1,0:T(8,128)(2,1)S(1)}, bf16[384,512]{1,0:T(8,128)(2,1)S(1)}, u32[]{:S(2)}, u32[]{:S(2)}) collective-permute-start(bf16[384,512]{1,0:T(8,128)(2,1)S(1)} %pad_maximum_fusion.5), channel_id=1, source_target_pairs={{0,2},{2,4},{4,6},{6,8},{8,10},{10,12},{12,14},{1,3},{3,5},{5,7},{... | collective-permute-start | bytes 1179656 | tf_op jit(solution)/shard_map/ppermute | solution.py:20
  46.0 18.7 %collective-permute-start.6 = (bf16[384,512]{1,0:T(8,128)(2,1)S(1)}, bf16[384,512]{1,0:T(8,128)(2,1)S(1)}, u32[]{:S(2)}, u32[]{:S(2)}) collective-permute-start(bf16[384,512]{1,0:T(8,128)(2,1)S(1)} %slice.270), channel_id=1, source_target_pairs={{2,0},{4,2},{6,4},{8,6},{10,8},{12,10},{14,12},{3,1},{5,3},{7,5},{... | collective-permute-start | bytes 1179656 | tf_op jit(solution)/shard_map/ppermute | solution.py:20
  59.1 20.2 %collective-permute-start.7 = (bf16[256,512]{1,0:T(8,128)(2,1)S(1)}, bf16[256,512]{1,0:T(8,128)(2,1)S(1)}, u32[]{:S(2)}, u32[]{:S(2)}) collective-permute-start(bf16[256,512]{1,0:T(8,128)(2,1)S(1)} %slice.272), channel_id=1, source_target_pairs={{4,0},{6,2},{8,4},{10,6},{12,8},{14,10},{5,1},{7,3},{9,5},{11,7},{... | collective-permute-start | bytes 786440 | tf_op jit(solution)/shard_map/ppermute | solution.py:20
  60.4 19.3 %collective-permute-start.4 = (bf16[384,512]{1,0:T(8,128)(2,1)S(1)}, bf16[384,512]{1,0:T(8,128)(2,1)S(1)}, u32[]{:S(2)}, u32[]{:S(2)}) collective-permute-start(bf16[384,512]{1,0:T(8,128)(2,1)S(1)} %slice.265), channel_id=1, source_target_pairs={{2,0},{4,2},{6,4},{8,6},{10,8},{12,10},{14,12},{3,1},{5,3},{7,5},{... | collective-permute-start | bytes 1179656 | tf_op jit(solution)/shard_map/ppermute | solution.py:20
  61.7 29.1 %collective-permute-start.5 = (bf16[256,512]{1,0:T(8,128)(2,1)S(1)}, bf16[256,512]{1,0:T(8,128)(2,1)S(1)}, u32[]{:S(2)}, u32[]{:S(2)}) collective-permute-start(bf16[256,512]{1,0:T(8,128)(2,1)S(1)} %slice.267), channel_id=1, source_target_pairs={{4,0},{6,2},{8,4},{10,6},{12,8},{14,10},{5,1},{7,3},{9,5},{11,7},{... | collective-permute-start | bytes 786440 | tf_op jit(solution)/shard_map/ppermute | solution.py:20
